TPU v7x, 128 devices: a whole 4x4x4 slice. The times are simulated.
128 devices in a mesh: box: 32 (over z, x_hi, y), dir: 4 (over x_lo, core).
Axes of the slice: x: 4 (x_hi: 2, x_lo: 2; x = x_hi * 2 + x_lo), y: 4, z: 4, core: 2. Of those that a mesh axis runs over, the one named last changes fastest.
Arguments:
- pattern: float32 [512, 8, 16384], P('dir', None, 'box'), may hold values from -6 to 6
- child_coef: float32 [2, 4, 512], P(None, None, 'dir'), may hold values from -3 to 3
- child_mask: int32 [4, 16384], P(None, 'box'), may hold values 0 or 1
- interp_index: int32 [16, 2048], replicated, may hold values from 0 to 511, as said below
- interp_weight: float32 [16, 2048], replicated, may hold values from -1.25 to 1.25
- phase_angle: float32 [8, 2048], replicated, may hold values from -3.140625 to 3.140625
- parent_coef: float32 [2, 32, 2048], replicated, may hold values from -3 to 3
- parent_mask: int32 [32, 2048], replicated, may hold values 0 or 1
Outputs:
- local_field: float32 [512, 8, 16384], P('dir', None, 'box')
Inputs may be any that keep to these rules, and one draw needn't show every extreme that they name: `interp_index`: child directions form a grid of 16 polar by 32 azimuthal angles, numbered as (azimuth % 4) * 128 + polar * 8 + azimuth // 4; each parent direction reads the 16 child directions of a 4 by 4 block of neighbouring angles, the azimuth wrapping round.
All inputs are finite; a program needn't handle non-finite values. No bound on the sum of `child_mask` on one device may be relied on, other than what follows from the above.
Results may differ from a plain program's by a relative error of at most 0.000053.
Values sent between devices are 32-bit elements; how exact they have to be, the bound alone decides.
No kernel may reach another device: no remote copies, remote signals or barrier semaphores. Data moves between devices by JAX's collectives and lax.ppermute only.
A program may use at most 192 MiB of HBM per device.

v0:
```python
import functools

import jax
import jax.numpy as jnp
from jax import lax
from jax.experimental import pallas as pl
from jax.experimental.pallas import tpu as pltpu
from jax.sharding import PartitionSpec as P

HIGHEST = lax.Precision.HIGHEST


def with_halo(block, sides, width):
    for axis, dim in sides:
        count = lax.axis_size(axis)
        forward = [(i, i + 1) for i in range(count - 1)]
        backward = [(target, source) for source, target in forward]
        low = lax.ppermute(
            lax.slice_in_dim(block, block.shape[dim] - width, None, axis=dim), axis, forward
        )
        high = lax.ppermute(lax.slice_in_dim(block, 0, width, axis=dim), axis, backward)
        block = jnp.concatenate([low, block, high], axis=dim)
    return block


def interp_matrix(index, weight, first_row, row_count):
    rows = first_row + lax.iota(jnp.int32, row_count)
    matrix = jnp.zeros((row_count, index.shape[1]), jnp.float32)
    for point in range(index.shape[0]):
        matrix = matrix + jnp.where(
            rows[:, None] == index[point][None, :], weight[point][None, :], jnp.float32(0.0)
        )
    return matrix


def translate_padded(padded, coef_real, coef_imag, mask, reach):
    count = padded.shape[2] - 2 * reach
    half = padded.shape[1] // 2
    offsets = list(range(-reach, 0)) + list(range(1, reach + 1))
    summed = jnp.zeros((padded.shape[0], padded.shape[1], count), jnp.float32)
    for position, offset in enumerate(offsets):
        source = padded[:, :, reach + offset : reach + offset + count]
        real_part = source[:, :half]
        imag_part = source[:, half:]
        scale_real = coef_real[position][:, None, None]
        scale_imag = coef_imag[position][:, None, None]
        weight = mask[position].astype(jnp.float32)[None, None, :]
        turned = jnp.concatenate(
            [
                scale_real * real_part - scale_imag * imag_part,
                scale_real * imag_part + scale_imag * real_part,
            ],
            axis=1,
        )
        summed = summed + weight * turned
    return summed


def upward_kernel(xt_ref, m_ref, cos_ref, sin_ref, out_ref):
    groups = xt_ref.shape[0]
    comps, slots, width = out_ref.shape[1:]
    half = comps // 2
    m = m_ref[...]
    acc_re = jnp.zeros((half, slots, width), jnp.float32)
    acc_im = jnp.zeros((half, slots, width), jnp.float32)
    for g in range(groups):
        r = jnp.dot(xt_ref[g], m, precision=HIGHEST, preferred_element_type=jnp.float32)
        r = r.reshape(comps, slots, width)
        c = cos_ref[pl.ds(g, 1), :].reshape(1, 1, width)
        s = sin_ref[pl.ds(g, 1), :].reshape(1, 1, width)
        re = r[:half]
        im = r[half:]
        acc_re = acc_re + (c * re - s * im)
        acc_im = acc_im + (c * im + s * re)
    out_ref[0, :half] = acc_re
    out_ref[0, half:] = acc_im


def upward(xt, m, cos, sin, parts):
    groups, rows, q = xt.shape
    total = m.shape[1]
    width = total // parts
    comps = 8
    slots = rows // comps
    return pl.pallas_call(
        upward_kernel,
        grid=(parts,),
        in_specs=[
            pl.BlockSpec((groups, rows, q), lambda j: (0, 0, 0)),
            pl.BlockSpec((q, width), lambda j: (0, j)),
            pl.BlockSpec((groups, width), lambda j: (0, j)),
            pl.BlockSpec((groups, width), lambda j: (0, j)),
        ],
        out_specs=pl.BlockSpec((1, comps, slots, width), lambda j: (j, 0, 0, 0)),
        out_shape=jax.ShapeDtypeStruct((parts, comps, slots, width), jnp.float32),
    )(xt, m, cos, sin)


def downward_kernel(pl_ref, m_ref, cos_ref, sin_ref, out_ref):
    g = pl.program_id(0)
    parts, comps, slots, width = pl_ref.shape
    half = comps // 2
    q = m_ref.shape[0]
    acc = jnp.zeros((q, comps * slots), jnp.float32)
    for d in range(parts):
        x = pl_ref[d]
        c = cos_ref[pl.ds(g, 1), pl.ds(d * width, width)].reshape(1, 1, width)
        s = sin_ref[pl.ds(g, 1), pl.ds(d * width, width)].reshape(1, 1, width)
        re = x[:half]
        im = x[half:]
        spread = jnp.concatenate([c * re + s * im, c * im - s * re], axis=0)
        spread = spread.reshape(comps * slots, width)
        acc = acc + lax.dot_general(
            m_ref[:, pl.ds(d * width, width)],
            spread,
            (((1,), (1,)), ((), ())),
            precision=HIGHEST,
            preferred_element_type=jnp.float32,
        )
    out_ref[0] = acc


def downward(parent_local, m, cos, sin):
    parts, comps, slots, width = parent_local.shape
    groups = cos.shape[0]
    q = m.shape[0]
    return pl.pallas_call(
        downward_kernel,
        grid=(groups,),
        in_specs=[
            pl.BlockSpec((parts, comps, slots, width), lambda g: (0, 0, 0, 0)),
            pl.BlockSpec((q, parts * width), lambda g: (0, 0)),
            pl.BlockSpec((groups, parts * width), lambda g: (0, 0)),
            pl.BlockSpec((groups, parts * width), lambda g: (0, 0)),
        ],
        out_specs=pl.BlockSpec((1, q, comps * slots), lambda g: (g, 0, 0)),
        out_shape=jax.ShapeDtypeStruct((groups, q, comps * slots), jnp.float32),
    )(parent_local, m, cos, sin)


def parent_translate(padded, coef_real, coef_imag, mask, reach):
    comps = padded.shape[0]
    half = comps // 2
    count = padded.shape[1] - 2 * reach
    offsets = list(range(-reach, 0)) + list(range(1, reach + 1))
    re_sum = jnp.zeros((half, count, padded.shape[2]), jnp.float32)
    im_sum = jnp.zeros((half, count, padded.shape[2]), jnp.float32)
    for position, offset in enumerate(offsets):
        source = padded[:, reach + offset : reach + offset + count]
        re = source[:half]
        im = source[half:]
        cr = coef_real[position][None, None, :]
        ci = coef_imag[position][None, None, :]
        weight = mask[position].astype(jnp.float32)[None, :, None]
        re_sum = re_sum + weight * (cr * re - ci * im)
        im_sum = im_sum + weight * (cr * im + ci * re)
    return jnp.concatenate([re_sum, im_sum], axis=0)


def body(
    pattern,
    child_coef,
    child_mask,
    interp_index,
    interp_weight,
    phase_angle,
    parent_coef,
    parent_mask,
):
    child_dev, comps, box_dev = pattern.shape
    dir_size = lax.axis_size("dir")
    parent_dirs = interp_index.shape[1]
    parent_dev = parent_dirs // dir_size
    groups = phase_angle.shape[0]
    slots = box_dev // groups
    dir_rank = lax.axis_index("dir")
    box_rank = lax.axis_index("box")
    child_first = dir_rank * child_dev
    parent_first = dir_rank * parent_dev
    cosine = jnp.cos(phase_angle)
    sine = jnp.sin(phase_angle)
    rows = interp_matrix(interp_index, interp_weight, child_first, child_dev)

    child_reach = child_coef.shape[1] // 2
    child_padded = with_halo(pattern, (("box", 2),), child_reach)
    child_local = translate_padded(
        child_padded, child_coef[0], child_coef[1], child_mask, child_reach
    )

    xt = pattern.reshape(child_dev, comps, slots, groups).transpose(3, 1, 2, 0)
    xt = xt.reshape(groups, comps * slots, child_dev)
    field = upward(xt, rows, cosine, sine, dir_size)
    field = lax.psum_scatter(field, "dir", scatter_dimension=0, tiled=True)[0]

    parent_reach = parent_coef.shape[1] // 2
    padded = with_halo(field, (("box", 1),), parent_reach)
    own_real = lax.dynamic_slice_in_dim(parent_coef[0], parent_first, parent_dev, 1)
    own_imag = lax.dynamic_slice_in_dim(parent_coef[1], parent_first, parent_dev, 1)
    own_mask = lax.dynamic_slice_in_dim(parent_mask, box_rank * slots, slots, 1)
    local = parent_translate(padded, own_real, own_imag, own_mask, parent_reach)
    local_all = lax.all_gather(local, "dir", axis=0, tiled=False)

    far = downward(local_all, rows, cosine, sine)
    far = far.reshape(groups, child_dev, comps, slots).transpose(1, 2, 3, 0)
    far = far.reshape(child_dev, comps, box_dev)
    return child_local + far


def solution(mesh):
    placed = (P("dir", None, "box"), P(None, None, "dir"), P(None, "box"), P(), P(), P(), P(), P())
    return jax.shard_map(
        body, mesh=mesh, in_specs=placed, out_specs=P("dir", None, "box"), check_vma=False
    )
```

profile of v0, /device:TPU:65, one launch (start us, length us, event | category | flops | bytes accessed | tf_op | source)
XLA Modules:
  0.0 238.7 jit_solution(5007793269111251437)
XLA Ops:
  6.5 2.0 copy.20
  8.6 1.7 copy.25
  10.3 0.1 fusion.109
  10.4 0.1 fusion.108
  10.5 0.9 fusion.110
  11.4 2.7 %select_add_fusion.m_ref = f32[128,2048]{1,0:T(8,128)} fusion(f32[2048]{0:T(1024)S(1)} %bitcast.212, s32[2048]{0:T(1024)S(1)} %bitcast.228, f32[2048]{0:T(1024)S(1)} %bitcast.213, s32[2048]{0:T(1024)S(1)} %bitcast.229, f32[2048]{0:T(1024)S(1)} %bitcast.199, s32[2048]{0:T(1024)S(1)} %bitcast.215, f32[2048]{0:T(1024)S(1)} %bitcast.200, ...), kind=kLoop, calls=%fused_computation.153 | loop fusion | flops 12320768 | bytes 1311232 | tf_op jit(solution)/shard_map/add | solution.py:30
  14.1 31.9 %shard_map.82 = f32[4,8,64,512]{3,2,1,0:T(8,128)} custom-call(f32[8,512,128]{2,1,0:T(8,128)} %bitcast.192, f32[128,2048]{1,0:T(8,128)} %select_add_fusion.m_ref, f32[8,2048]{1,0:T(8,128)} %get-tuple-element.152.cos_ref, f32[8,2048]{1,0:T(8,128)} %get-tuple-element.151.sin_ref), custom_call_target="tpu_custom_call" | custom-call | tf_op jit(solution)/shard_map/pallas_call | solution.py:85
  46.0 0.0 reduce-scatter.2.cloned.1.call-update
  46.0 0.0 all-gather.3.cloned.1.call-start
  46.0 1.2 fusion.73
  47.3 0.2 constant_dynamic-slice_fusion.60
  47.5 45.9 %reduce-scatter.2.cloned.1.call-done = f32[1,8,64,512]{3,2,1,0:T(8,128)} async-done(((f32[4,8,64,512]{3,2,1,0:T(8,128)}), f32[1,8,64,512]{3,2,1,0:T(8,128)}) %reduce-scatter.2.cloned.1.call-update) | async-done | bytes 1048592 | tf_op jit(solution)/shard_map/reduce_scatter | solution.py:193
  93.3 1.2 fusion.106
  94.5 3.1 %collective-permute-start.2 = (f32[8,16,512]{2,1,0:T(8,128)S(1)}, f32[8,16,512]{2,1,0:T(8,128)S(1)}, u32[]{:S(2)}, u32[]{:S(2)}) collective-permute-start(f32[8,16,512]{2,1,0:T(8,128)S(1)} %get-tuple-element.20), channel_id=1, source_target_pairs={{0,4},{4,8},{8,12},{12,16},{16,20},{20,24},{24,28},{28,32},{32,36}... | collective-permute-start | bytes 786440 | tf_op jit(solution)/shard_map/ppermute | solution.py:18
  97.6 6.9 %collective-permute-start.3 = (f32[8,16,512]{2,1,0:T(8,128)S(1)}, f32[8,16,512]{2,1,0:T(8,128)S(1)}, u32[]{:S(2)}, u32[]{:S(2)}) collective-permute-start(f32[8,16,512]{2,1,0:T(8,128)S(1)} %get-tuple-element.19), channel_id=1, source_target_pairs={{4,0},{8,4},{12,8},{16,12},{20,16},{24,20},{28,24},{32,28},{36,32}... | collective-permute-start | bytes 786440 | tf_op jit(solution)/shard_map/ppermute | solution.py:21
  104.5 1.1 fusion.104
  105.6 0.2 constant_dynamic-slice_fusion.61
  105.8 0.3 constant_dynamic-slice_fusion.58
  106.0 2.4 collective-permute-done.2
  108.4 0.9 collective-permute-done.3
  109.3 11.4 %multiply_add_fusion.4 = f32[4,64,512]{2,1,0:T(8,128)S(1)} fusion(f32[512]{0:T(512)S(1)} %bitcast.256, f32[512]{0:T(512)S(1)} %bitcast.258, f32[64]{0:T(128)S(1)} %get-tuple-element.90, f32[512]{0:T(512)S(1)} %bitcast.288, f32[512]{0:T(512)S(1)} %bitcast.324, f32[64]{0:T(128)S(1)} %get-tuple-element.24, f32[512]{0:T(512)S(1)} %bitcast.290, ...), kind=kLoop, calls=%fused_computation.226 | loop fusion | flops 29229056 | bytes 2236416 | tf_op jit(solution)/shard_map/add | solution.py:156
  120.8 11.7 %multiply_add_fusion.5 = f32[4,64,512]{2,1,0:T(8,128)S(1)} fusion(f32[512]{0:T(512)S(1)} %bitcast.257, f32[512]{0:T(512)S(1)} %bitcast.259, f32[64]{0:T(128)S(1)} %get-tuple-element.90, f32[512]{0:T(512)S(1)} %bitcast.289, f32[512]{0:T(512)S(1)} %bitcast.325, f32[64]{0:T(128)S(1)} %get-tuple-element.24, f32[512]{0:T(512)S(1)} %bitcast.291, ...), kind=kLoop, calls=%fused_computation.227 | loop fusion | flops 29229056 | bytes 2236416 | tf_op jit(solution)/shard_map/add | solution.py:155
  132.5 1.0 pad_maximum_fusion.2
  133.5 1.9 collective-permute-start
  135.5 8.8 %collective-permute-start.1 = (f32[128,8,2]{0,2,1:T(2,128)S(1)}, f32[128,8,2]{0,2,1:T(2,128)S(1)}, u32[]{:S(2)}, u32[]{:S(2)}) collective-permute-start(f32[128,8,2]{0,2,1:T(2,128)S(1)} %get-tuple-element.17), channel_id=1, source_target_pairs={{4,0},{8,4},{12,8},{16,12},{20,16},{24,20},{28,24},{32,28},{36,32}... | collective-permute-start | bytes 24584 | tf_op jit(solution)/shard_map/ppermute | solution.py:21
  144.4 2.0 multiply_subtract_fusion.2
  146.4 2.4 multiply_subtract_fusion
  148.8 35.3 %all-gather.3.cloned.1.call-done = f32[32,64,512]{2,1,0:T(8,128)} async-done(((f32[8,64,512]{2,1,0:T(8,128)}), f32[32,64,512]{2,1,0:T(8,128)}) %all-gather.3.cloned.1.call-update) | async-done | bytes 4194320 | tf_op jit(solution)/shard_map/all_gather | solution.py:201
  184.1 37.9 %shard_map.83 = f32[8,128,512]{2,1,0:T(8,128)} custom-call(f32[4,8,64,512]{3,2,1,0:T(8,128)} %bitcast.197, f32[128,2048]{1,0:T(8,128)} %select_add_fusion.m_ref, f32[8,2048]{1,0:T(8,128)} %get-tuple-element.152.cos_ref, f32[8,2048]{1,0:T(8,128)} %get-tuple-element.151.sin_ref), custom_call_target="tpu_custom_call" | custom-call | tf_op jit(solution)/shard_map/pallas_call | solution.py:127
  222.0 2.1 copy.29
  224.1 4.7 %fusion.3 = f32[128,8,512]{0,2,1:T(8,128)} fusion(f32[128,8,512]{0,2,1:T(8,128)S(1)} %bitcast.193, f32[128,4,512]{0,2,1:T(8,128)} %get-tuple-element.15, f32[128,4,512]{0,2,1:T(8,128)} %get-tuple-element.16, f32[128,4,512]{0,2,1:T(8,128)} %get-tuple-element.10, f32[128,4,512]{0,2,1:T(8,128)S(1)} %get-tuple-element.9, f32[128,4,512]{0,2,1:T(8,128)} %get-tuple-element.13, ...), kind=kLoop, calls=%fused_computation.134 | loop fusion | flops 6291456 | bytes 12591104 | tf_op jit(solution)/shard_map/add | solution.py:206
  228.8 3.0 %copy.28 = f32[128,8,512]{2,1,0:T(8,128)} copy(f32[128,8,512]{0,2,1:T(8,128)} %fusion.3) | data formatting | bytes 4194304 | tf_op jit(solution)/shard_map/add | solution.py:206
  (23 shorter events, 0.1 us)
Async XLA Ops:
  6.5 86.8 %reduce-scatter.2.cloned.1.call-start = ((), (), s32[]{:S(2)}) async-start(), calls=%async_computation.1 | async-start | bytes 5242880 | tf_op jit(solution)/shard_map/reduce_scatter | solution.py:193
  8.5 1.7 copy-start.2
  8.5 1.8 copy-start.3
  8.6 1.9 copy-start.4
  46.0 1.3 copy-start.1
  46.0 138.1 %all-gather.3.cloned.1.call-start = ((), (), s32[]{:S(2)}) async-start(), calls=%async_computation.2 | async-start | bytes 5242880 | tf_op jit(solution)/shard_map/all_gather | solution.py:201
  93.3 16.0 %copy-start = (f32[1,8,64,512]{3,2,1,0:T(8,128)S(1)}, f32[1,8,64,512]{3,2,1,0:T(8,128)}, u32[]{:S(2)}) copy-start(f32[1,8,64,512]{3,2,1,0:T(8,128)} %reduce-scatter.2.cloned.1.call-done) | copy-start | bytes 3145732
  94.5 13.9 %collective-permute-start.2 = (f32[8,16,512]{2,1,0:T(8,128)S(1)}, f32[8,16,512]{2,1,0:T(8,128)S(1)}, u32[]{:S(2)}, u32[]{:S(2)}) collective-permute-start(f32[8,16,512]{2,1,0:T(8,128)S(1)} %get-tuple-element.20), channel_id=1, source_target_pairs={{0,4},{4,8},{8,12},{12,16},{16,20},{20,24},{24,28},{28,32},{32,36}... | collective-permute-start | bytes 786440 | tf_op jit(solution)/shard_map/ppermute | solution.py:18
  97.6 11.7 %collective-permute-start.3 = (f32[8,16,512]{2,1,0:T(8,128)S(1)}, f32[8,16,512]{2,1,0:T(8,128)S(1)}, u32[]{:S(2)}, u32[]{:S(2)}) collective-permute-start(f32[8,16,512]{2,1,0:T(8,128)S(1)} %get-tuple-element.19), channel_id=1, source_target_pairs={{4,0},{8,4},{12,8},{16,12},{20,16},{24,20},{28,24},{32,28},{36,32}... | collective-permute-start | bytes 786440 | tf_op jit(solution)/shard_map/ppermute | solution.py:21
  132.4 11.9 %copy-start.5 = (s32[4,512]{1,0:T(4,128)S(1)}, s32[4,512]{1,0:T(4,128)}, u32[]{:S(2)}) copy-start(s32[4,512]{1,0:T(4,128)} %param.10) | copy-start | bytes 24580
  132.4 11.9 %copy-start.6 = (f32[2,4,128]{2,1,0:T(4,128)S(1)}, f32[2,4,128]{2,1,0:T(4,128)}, u32[]{:S(2)}) copy-start(f32[2,4,128]{2,1,0:T(4,128)} %param.9) | copy-start | bytes 12292
  133.5 10.8 %collective-permute-start = (f32[128,8,2]{0,2,1:T(2,128)S(1)}, f32[128,8,2]{0,2,1:T(2,128)S(1)}, u32[]{:S(2)}, u32[]{:S(2)}) collective-permute-start(f32[128,8,2]{0,2,1:T(2,128)S(1)} %get-tuple-element.18), channel_id=1, source_target_pairs={{0,4},{4,8},{8,12},{12,16},{16,20},{20,24},{24,28},{28,32},{32,36}... | collective-permute-start | bytes 24584 | tf_op jit(solution)/shard_map/ppermute | solution.py:18
  135.5 10.9 %collective-permute-start.1 = (f32[128,8,2]{0,2,1:T(2,128)S(1)}, f32[128,8,2]{0,2,1:T(2,128)S(1)}, u32[]{:S(2)}, u32[]{:S(2)}) collective-permute-start(f32[128,8,2]{0,2,1:T(2,128)S(1)} %get-tuple-element.17), channel_id=1, source_target_pairs={{4,0},{8,4},{12,8},{16,12},{20,16},{24,20},{28,24},{32,28},{36,32}... | collective-permute-start | bytes 24584 | tf_op jit(solution)/shard_map/ppermute | solution.py:21
Sparse Core Ops, SparseCore 0:
  46.1 47.1 reduce-scatter.1
  133.6 50.3 all-gather.2
where the time goes:
time: 241 us; the launch traced here: 239 us
  waiting for transfers between devices  84.5 us (35%)
  Pallas kernels  69.8 us (29%)
  other arithmetic  38.2 us (16%)
  starting transfers between devices  20.8 us (9%)
  between operations  13.7 us (6%)
  local copies, waits for them, and re-layouts  11.8 us (5%)
    reduce_scatter x1, waiting for transfers between devices, body(): field = lax.psum_scatter(field, 'dir', scatter_dimension=0, tiled=True)[0]  45.9 us
    pallas_call x1, Pallas kernels, downward(): pl.pallas_call(downward_kernel, grid=(groups,), in_specs=[pl.BlockSpec((p...  37.9 us
    all_gather x1, waiting for transfers between devices, body(): local_all = lax.all_gather(local, 'dir', axis=0, tiled=False)  35.3 us
    pallas_call x1, Pallas kernels, upward(): pl.pallas_call(upward_kernel, grid=(parts,), in_specs=[pl.BlockSpec((grou...  31.9 us
    ppermute x2, starting transfers between devices, with_halo(): lax.ppermute(lax.slice_in_dim(block, 0, width, axis=dim), axis, backward)  15.7 us
    add x1, other arithmetic, parent_translate(): re_sum = re_sum + weight * (cr * re - ci * im)  11.7 us
    add x1, other arithmetic, parent_translate(): im_sum = im_sum + weight * (cr * im + ci * re)  11.4 us
    ppermute x2, starting transfers between devices, with_halo(): lax.ppermute(lax.slice_in_dim(block, block.shape[dim] - width, None, axis...  5.05 us
  transfers between devices with their start and end apart: 6, of which 4 were waited for; matrix products, arithmetic and copies ran while one was open for 3% of the time, Pallas kernels for 0%

commit v1 on v0

--- a/solution.py
+++ b/solution.py
@@ -1,5 +1,3 @@
-import functools
-
 import jax
 import jax.numpy as jnp
 from jax import lax
@@ -8,6 +6,7 @@
 from jax.sharding import PartitionSpec as P
 
 HIGHEST = lax.Precision.HIGHEST
+CHUNKS = 2
 
 
 def with_halo(block, sides, width):
@@ -76,11 +75,10 @@
     out_ref[0, half:] = acc_im
 
 
-def upward(xt, m, cos, sin, parts):
+def upward(xt, m, cos, sin, parts, comps):
     groups, rows, q = xt.shape
     total = m.shape[1]
     width = total // parts
-    comps = 8
     slots = rows // comps
     return pl.pallas_call(
         upward_kernel,
@@ -187,21 +185,25 @@
         child_padded, child_coef[0], child_coef[1], child_mask, child_reach
     )
 
-    xt = pattern.reshape(child_dev, comps, slots, groups).transpose(3, 1, 2, 0)
-    xt = xt.reshape(groups, comps * slots, child_dev)
-    field = upward(xt, rows, cosine, sine, dir_size)
-    field = lax.psum_scatter(field, "dir", scatter_dimension=0, tiled=True)[0]
-
     parent_reach = parent_coef.shape[1] // 2
-    padded = with_halo(field, (("box", 1),), parent_reach)
     own_real = lax.dynamic_slice_in_dim(parent_coef[0], parent_first, parent_dev, 1)
     own_imag = lax.dynamic_slice_in_dim(parent_coef[1], parent_first, parent_dev, 1)
     own_mask = lax.dynamic_slice_in_dim(parent_mask, box_rank * slots, slots, 1)
-    local = parent_translate(padded, own_real, own_imag, own_mask, parent_reach)
-    local_all = lax.all_gather(local, "dir", axis=0, tiled=False)
-
-    far = downward(local_all, rows, cosine, sine)
-    far = far.reshape(groups, child_dev, comps, slots).transpose(1, 2, 3, 0)
+    rhs = comps // 2
+    step = rhs // CHUNKS
+    fars = []
+    for chunk in range(CHUNKS):
+        part = pattern.reshape(child_dev, 2, rhs, box_dev)[:, :, chunk * step : (chunk + 1) * step]
+        xt = part.reshape(child_dev, 2 * step, slots, groups).transpose(3, 1, 2, 0)
+        xt = xt.reshape(groups, 2 * step * slots, child_dev)
+        field = upward(xt, rows, cosine, sine, dir_size, 2 * step)
+        field = lax.psum_scatter(field, "dir", scatter_dimension=0, tiled=True)[0]
+        padded = with_halo(field, (("box", 1),), parent_reach)
+        local = parent_translate(padded, own_real, own_imag, own_mask, parent_reach)
+        local_all = lax.all_gather(local, "dir", axis=0, tiled=False)
+        far = downward(local_all, rows, cosine, sine)
+        fars.append(far.reshape(groups, child_dev, 2, step, slots))
+    far = jnp.concatenate(fars, axis=3).transpose(1, 2, 3, 4, 0)
     far = far.reshape(child_dev, comps, box_dev)
     return child_local + far
 

time: 241 us -> 208 us (0.86)
  the two profiles are of different devices: /device:TPU:65 before, /device:TPU:28 now
where the time goes in v1:
time: 208 us; the launch traced here: 207 us
  Pallas kernels  73.9 us (36%)
  other arithmetic  50.5 us (24%)
  waiting for transfers between devices  35 us (17%)
  starting transfers between devices  18.1 us (9%)
  local copies, waits for them, and re-layouts  16.3 us (8%)
  between operations  13.6 us (7%)
    pallas_call x2, Pallas kernels, downward(): pl.pallas_call(downward_kernel, grid=(groups,), in_specs=[pl.BlockSpec((p...  40.7 us
    pallas_call x2, Pallas kernels, upward(): pl.pallas_call(upward_kernel, grid=(parts,), in_specs=[pl.BlockSpec((grou...  33.1 us
    ppermute x3, waiting for transfers between devices, with_halo(): lax.ppermute(lax.slice_in_dim(block, 0, width, axis=dim), axis, backward)  23.3 us
    add x2, other arithmetic, parent_translate(): im_sum = im_sum + weight * (cr * im + ci * re)  21.6 us
    add x2, other arithmetic, parent_translate(): re_sum = re_sum + weight * (cr * re - ci * im)  16.7 us
    reduce_scatter x2, waiting for transfers between devices, body(): field = lax.psum_scatter(field, 'dir', scatter_dimension=0, tiled=True)[0]  10.5 us
    ppermute x3, starting transfers between devices, with_halo(): lax.ppermute(lax.slice_in_dim(block, 0, width, axis=dim), axis, backward)  10.4 us
    ppermute x3, starting transfers between devices, with_halo(): lax.ppermute(lax.slice_in_dim(block, block.shape[dim] - width, None, axis...  7.53 us
  transfers between devices with their start and end apart: 10, of which 6 were waited for; matrix products, arithmetic and copies ran while one was open for 25% of the time, Pallas kernels for 18%

profile of v1, /device:TPU:28, one launch (start us, length us, event | category | flops | bytes accessed | tf_op | source)
XLA Modules:
  0.0 207.3 jit_solution(2468516892435965292)
XLA Ops:
  6.5 2.0 copy.21
  8.7 1.2 copy.28
  11.0 2.7 %select_add_fusion.m_ref = f32[128,2048]{1,0:T(8,128)} fusion(f32[2048]{0:T(1024)S(1)} %bitcast.484, s32[2048]{0:T(1024)S(1)} %bitcast.500, f32[2048]{0:T(1024)S(1)} %bitcast.485, s32[2048]{0:T(1024)S(1)} %bitcast.501, f32[2048]{0:T(1024)S(1)} %bitcast.471, s32[2048]{0:T(1024)S(1)} %bitcast.487, f32[2048]{0:T(1024)S(1)} %bitcast.472, ...), kind=kLoop, calls=%fused_computation.277 | loop fusion | flops 12320768 | bytes 1311232 | tf_op jit(solution)/shard_map/add | solution.py:29
  13.7 16.6 %shard_map.84 = f32[4,4,64,512]{3,2,1,0:T(8,128)} custom-call(f32[8,256,128]{2,1,0:T(8,128)} %bitcast.201, f32[128,2048]{1,0:T(8,128)} %select_add_fusion.m_ref, f32[8,2048]{1,0:T(8,128)} %get-tuple-element.156.cos_ref, f32[8,2048]{1,0:T(8,128)} %get-tuple-element.155.sin_ref), custom_call_target="tpu_custom_call" | custom-call | tf_op jit(solution)/shard_map/pallas_call | solution.py:83
  30.3 1.2 copy.26
  31.5 16.6 %shard_map.82 = f32[4,4,64,512]{3,2,1,0:T(8,128)} custom-call(f32[8,256,128]{2,1,0:T(8,128)} %bitcast.205, f32[128,2048]{1,0:T(8,128)} %select_add_fusion.m_ref, f32[8,2048]{1,0:T(8,128)} %get-tuple-element.156.cos_ref, f32[8,2048]{1,0:T(8,128)} %get-tuple-element.155.sin_ref), custom_call_target="tpu_custom_call" | custom-call | tf_op jit(solution)/shard_map/pallas_call | solution.py:83
  48.2 1.2 fusion.135
  49.8 10.5 %reduce-scatter.5.cloned.1.call-done = f32[1,4,64,512]{3,2,1,0:T(8,128)} async-done(((f32[4,4,64,512]{3,2,1,0:T(8,128)}), f32[1,4,64,512]{3,2,1,0:T(8,128)}) %reduce-scatter.5.cloned.1.call-update) | async-done | bytes 524304 | tf_op jit(solution)/shard_map/reduce_scatter | solution.py:200
  60.3 1.0 fusion.170
  61.3 3.7 %collective-permute-start.4 = (f32[4,16,512]{2,1,0:T(8,128)S(1)}, f32[4,16,512]{2,1,0:T(8,128)S(1)}, u32[]{:S(2)}, u32[]{:S(2)}) collective-permute-start(f32[4,16,512]{2,1,0:T(8,128)S(1)} %get-tuple-element.24), channel_id=1, source_target_pairs={{0,4},{4,8},{8,12},{12,16},{16,20},{20,24},{24,28},{28,32},{32,36}... | collective-permute-start | bytes 393224 | tf_op jit(solution)/shard_map/ppermute | solution.py:17
  65.0 2.3 %collective-permute-start.5 = (f32[4,16,512]{2,1,0:T(8,128)S(1)}, f32[4,16,512]{2,1,0:T(8,128)S(1)}, u32[]{:S(2)}, u32[]{:S(2)}) collective-permute-start(f32[4,16,512]{2,1,0:T(8,128)S(1)} %get-tuple-element.23), channel_id=1, source_target_pairs={{4,0},{8,4},{12,8},{16,12},{20,16},{24,20},{28,24},{32,28},{36,32}... | collective-permute-start | bytes 393224 | tf_op jit(solution)/shard_map/ppermute | solution.py:20
  67.4 1.1 fusion.166
  68.8 10.9 %collective-permute-done.5 = f32[4,16,512]{2,1,0:T(8,128)S(1)} collective-permute-done((f32[4,16,512]{2,1,0:T(8,128)S(1)}, f32[4,16,512]{2,1,0:T(8,128)S(1)}, u32[]{:S(2)}, u32[]{:S(2)}) %collective-permute-start.5) | collective-permute-done | bytes 131104 | tf_op jit(solution)/shard_map/ppermute | solution.py:20
  79.7 11.0 %multiply_add_fusion.4 = f32[2,64,512]{2,1,0:T(8,128)S(1)} fusion(f32[512]{0:T(512)S(1)} %bitcast.266, f32[512]{0:T(512)S(1)} %bitcast.270, f32[64]{0:T(128)S(1)} %get-tuple-element.94, f32[512]{0:T(512)S(1)} %bitcast.330, f32[512]{0:T(512)S(1)} %bitcast.402, f32[64]{0:T(128)S(1)} %get-tuple-element.28, f32[512]{0:T(512)S(1)} %bitcast.334, ...), kind=kLoop, calls=%fused_computation.416 | loop fusion | flops 14614528 | bytes 1187840 | tf_op jit(solution)/shard_map/add | solution.py:154
  90.7 5.8 %multiply_add_fusion.5 = f32[2,64,512]{2,1,0:T(8,128)S(1)} fusion(f32[512]{0:T(512)S(1)} %bitcast.267, f32[512]{0:T(512)S(1)} %bitcast.271, f32[64]{0:T(128)S(1)} %get-tuple-element.94, f32[512]{0:T(512)S(1)} %bitcast.331, f32[512]{0:T(512)S(1)} %bitcast.403, f32[64]{0:T(128)S(1)} %get-tuple-element.28, f32[512]{0:T(512)S(1)} %bitcast.335, ...), kind=kLoop, calls=%fused_computation.417 | loop fusion | flops 14614528 | bytes 1187840 | tf_op jit(solution)/shard_map/add | solution.py:153
  98.5 1.9 collective-permute-start.2
  100.4 3.9 %collective-permute-start.3 = (f32[4,16,512]{2,1,0:T(8,128)S(1)}, f32[4,16,512]{2,1,0:T(8,128)S(1)}, u32[]{:S(2)}, u32[]{:S(2)}) collective-permute-start(f32[4,16,512]{2,1,0:T(8,128)S(1)} %get-tuple-element.21), channel_id=1, source_target_pairs={{4,0},{8,4},{12,8},{16,12},{20,16},{24,20},{28,24},{32,28},{36,32}... | collective-permute-start | bytes 393224 | tf_op jit(solution)/shard_map/ppermute | solution.py:20
  105.3 8.6 %collective-permute-done.3 = f32[4,16,512]{2,1,0:T(8,128)S(1)} collective-permute-done((f32[4,16,512]{2,1,0:T(8,128)S(1)}, f32[4,16,512]{2,1,0:T(8,128)S(1)}, u32[]{:S(2)}, u32[]{:S(2)}) %collective-permute-start.3) | collective-permute-done | bytes 131104 | tf_op jit(solution)/shard_map/ppermute | solution.py:20
  113.9 10.7 %multiply_add_fusion.6 = f32[2,64,512]{2,1,0:T(8,128)S(1)} fusion(f32[512]{0:T(512)S(1)} %bitcast.268, f32[512]{0:T(512)S(1)} %bitcast.272, f32[64]{0:T(128)S(1)} %get-tuple-element.94, f32[512]{0:T(512)S(1)} %bitcast.332, f32[512]{0:T(512)S(1)} %bitcast.404, f32[64]{0:T(128)S(1)} %get-tuple-element.28, f32[512]{0:T(512)S(1)} %bitcast.336, ...), kind=kLoop, calls=%fused_computation.418 | loop fusion | flops 14614528 | bytes 1187840 | tf_op jit(solution)/shard_map/add | solution.py:154
  124.6 10.9 %multiply_add_fusion.7 = f32[2,64,512]{2,1,0:T(8,128)S(1)} fusion(f32[512]{0:T(512)S(1)} %bitcast.269, f32[512]{0:T(512)S(1)} %bitcast.273, f32[64]{0:T(128)S(1)} %get-tuple-element.94, f32[512]{0:T(512)S(1)} %bitcast.333, f32[512]{0:T(512)S(1)} %bitcast.405, f32[64]{0:T(128)S(1)} %get-tuple-element.28, f32[512]{0:T(512)S(1)} %bitcast.337, ...), kind=kLoop, calls=%fused_computation.419 | loop fusion | flops 14614528 | bytes 1187840 | tf_op jit(solution)/shard_map/add | solution.py:153
  136.3 1.9 collective-permute-start
  138.3 4.1 %collective-permute-start.1 = (f32[128,8,2]{0,2,1:T(2,128)S(1)}, f32[128,8,2]{0,2,1:T(2,128)S(1)}, u32[]{:S(2)}, u32[]{:S(2)}) collective-permute-start(f32[128,8,2]{0,2,1:T(2,128)S(1)} %get-tuple-element.17), channel_id=1, source_target_pairs={{4,0},{8,4},{12,8},{16,12},{20,16},{24,20},{28,24},{32,28},{36,32}... | collective-permute-start | bytes 24584 | tf_op jit(solution)/shard_map/ppermute | solution.py:20
  142.5 2.0 multiply_subtract_fusion.2
  144.4 3.9 %collective-permute-done.1 = f32[128,8,2]{0,2,1:T(2,128)S(1)} collective-permute-done((f32[128,8,2]{0,2,1:T(2,128)S(1)}, f32[128,8,2]{0,2,1:T(2,128)S(1)}, u32[]{:S(2)}, u32[]{:S(2)}) %collective-permute-start.1) | collective-permute-done | bytes 8224 | tf_op jit(solution)/shard_map/ppermute | solution.py:20
  148.3 2.3 %multiply_subtract_fusion = (f32[128,4,512]{0,2,1:T(8,128)}, f32[128,4,512]{0,2,1:T(8,128)}, f32[128,4,512]{0,2,1:T(8,128)}, f32[128,4,512]{0,2,1:T(8,128)}) fusion(f32[128]{0:T(128)S(1)} %get-tuple-element.168, f32[128]{0:T(128)S(1)} %get-tuple-element.161, f32[128,8,2]{0,2,1:T(2,128)S(1)} %collective-permute-done.1, f32[128,8,512]{0,2,1:T(8,128)S(1)} %copy.21, ...), kind=kLoop, calls=%fused_computation.279 | loop fusion | flops 4980736 | bytes 6301696 | tf_op jit(solution)/shard_map/sub | solution.py:49
  150.6 20.4 %shard_map.85 = f32[8,128,256]{2,1,0:T(8,128)} custom-call(f32[4,4,64,512]{3,2,1,0:T(8,128)} %bitcast.212, f32[128,2048]{1,0:T(8,128)} %select_add_fusion.m_ref, f32[8,2048]{1,0:T(8,128)} %get-tuple-element.156.cos_ref, f32[8,2048]{1,0:T(8,128)} %get-tuple-element.155.sin_ref), custom_call_target="tpu_custom_call" | custom-call | tf_op jit(solution)/shard_map/pallas_call | solution.py:125
  171.0 1.5 copy.29
  172.6 20.4 %shard_map.83 = f32[8,128,256]{2,1,0:T(8,128)} custom-call(f32[4,4,64,512]{3,2,1,0:T(8,128)} %bitcast.213, f32[128,2048]{1,0:T(8,128)} %select_add_fusion.m_ref, f32[8,2048]{1,0:T(8,128)} %get-tuple-element.156.cos_ref, f32[8,2048]{1,0:T(8,128)} %get-tuple-element.155.sin_ref), custom_call_target="tpu_custom_call" | custom-call | tf_op jit(solution)/shard_map/pallas_call | solution.py:125
  193.0 1.5 copy.27
  194.7 1.2 copy.30
  197.7 1.2 fusion.3
  198.8 2.0 copy.31
  (58 shorter events, 7.8 us)
Async XLA Ops:
  6.5 53.7 %reduce-scatter.5.cloned.1.call-start = ((), (), s32[]{:S(2)}) async-start(), calls=%async_computation.3 | async-start | bytes 2621440 | tf_op jit(solution)/shard_map/reduce_scatter | solution.py:200
  8.7 1.2 copy-start.9
  8.7 1.3 copy-start.10
  8.7 1.4 copy-start.11
  30.3 67.2 %reduce-scatter.3.cloned.1.call-start = ((), (), s32[]{:S(2)}) async-start(), calls=%async_computation.2 | async-start | bytes 2621440 | tf_op jit(solution)/shard_map/reduce_scatter | solution.py:200
  48.1 1.3 copy-start.8
  48.1 102.5 %all-gather.7.cloned.1.call-start = ((), (), s32[]{:S(2)}) async-start(), calls=%async_computation.5 | async-start | bytes 2621440 | tf_op jit(solution)/shard_map/all_gather | solution.py:203
  60.3 30.4 %copy-start.7 = (f32[1,4,64,512]{3,2,1,0:T(8,128)S(1)}, f32[1,4,64,512]{3,2,1,0:T(8,128)}, u32[]{:S(2)}) copy-start(f32[1,4,64,512]{3,2,1,0:T(8,128)} %reduce-scatter.5.cloned.1.call-done) | copy-start | bytes 1572868
  61.3 7.5 %collective-permute-start.4 = (f32[4,16,512]{2,1,0:T(8,128)S(1)}, f32[4,16,512]{2,1,0:T(8,128)S(1)}, u32[]{:S(2)}, u32[]{:S(2)}) collective-permute-start(f32[4,16,512]{2,1,0:T(8,128)S(1)} %get-tuple-element.24), channel_id=1, source_target_pairs={{0,4},{4,8},{8,12},{12,16},{16,20},{20,24},{24,28},{28,32},{32,36}... | collective-permute-start | bytes 393224 | tf_op jit(solution)/shard_map/ppermute | solution.py:17
  65.0 14.6 %collective-permute-start.5 = (f32[4,16,512]{2,1,0:T(8,128)S(1)}, f32[4,16,512]{2,1,0:T(8,128)S(1)}, u32[]{:S(2)}, u32[]{:S(2)}) collective-permute-start(f32[4,16,512]{2,1,0:T(8,128)S(1)} %get-tuple-element.23), channel_id=1, source_target_pairs={{4,0},{8,4},{12,8},{16,12},{20,16},{24,20},{28,24},{32,28},{36,32}... | collective-permute-start | bytes 393224 | tf_op jit(solution)/shard_map/ppermute | solution.py:20
  97.4 75.2 %all-gather.5.cloned.1.call-start = ((), (), s32[]{:S(2)}) async-start(), calls=%async_computation.4 | async-start | bytes 2621440 | tf_op jit(solution)/shard_map/all_gather | solution.py:203
  98.4 44.0 %copy-start.12 = (s32[4,512]{1,0:T(4,128)S(1)}, s32[4,512]{1,0:T(4,128)}, u32[]{:S(2)}) copy-start(s32[4,512]{1,0:T(4,128)} %param.10) | copy-start | bytes 24580
  98.4 44.0 %copy-start.13 = (f32[2,4,128]{2,1,0:T(4,128)S(1)}, f32[2,4,128]{2,1,0:T(4,128)}, u32[]{:S(2)}) copy-start(f32[2,4,128]{2,1,0:T(4,128)} %param.9) | copy-start | bytes 12292
  98.5 6.9 %collective-permute-start.2 = (f32[4,16,512]{2,1,0:T(8,128)S(1)}, f32[4,16,512]{2,1,0:T(8,128)S(1)}, u32[]{:S(2)}, u32[]{:S(2)}) collective-permute-start(f32[4,16,512]{2,1,0:T(8,128)S(1)} %get-tuple-element.22), channel_id=1, source_target_pairs={{0,4},{4,8},{8,12},{12,16},{16,20},{20,24},{24,28},{28,32},{32,36}... | collective-permute-start | bytes 393224 | tf_op jit(solution)/shard_map/ppermute | solution.py:17
  100.4 13.5 %collective-permute-start.3 = (f32[4,16,512]{2,1,0:T(8,128)S(1)}, f32[4,16,512]{2,1,0:T(8,128)S(1)}, u32[]{:S(2)}, u32[]{:S(2)}) collective-permute-start(f32[4,16,512]{2,1,0:T(8,128)S(1)} %get-tuple-element.21), channel_id=1, source_target_pairs={{4,0},{8,4},{12,8},{16,12},{20,16},{24,20},{28,24},{32,28},{36,32}... | collective-permute-start | bytes 393224 | tf_op jit(solution)/shard_map/ppermute | solution.py:20
  136.3 6.1 %collective-permute-start = (f32[128,8,2]{0,2,1:T(2,128)S(1)}, f32[128,8,2]{0,2,1:T(2,128)S(1)}, u32[]{:S(2)}, u32[]{:S(2)}) collective-permute-start(f32[128,8,2]{0,2,1:T(2,128)S(1)} %get-tuple-element.18), channel_id=1, source_target_pairs={{0,4},{4,8},{8,12},{12,16},{16,20},{20,24},{24,28},{28,32},{32,36}... | collective-permute-start | bytes 24584 | tf_op jit(solution)/shard_map/ppermute | solution.py:17
  138.3 10.1 %collective-permute-start.1 = (f32[128,8,2]{0,2,1:T(2,128)S(1)}, f32[128,8,2]{0,2,1:T(2,128)S(1)}, u32[]{:S(2)}, u32[]{:S(2)}) collective-permute-start(f32[128,8,2]{0,2,1:T(2,128)S(1)} %get-tuple-element.17), channel_id=1, source_target_pairs={{4,0},{8,4},{12,8},{16,12},{20,16},{24,20},{28,24},{32,28},{36,32}... | collective-permute-start | bytes 24584 | tf_op jit(solution)/shard_map/ppermute | solution.py:20
  194.5 1.4 copy-start.4
  194.5 1.5 copy-start.5
  194.5 1.8 copy-start.6
  194.7 2.0 copy-start
  194.7 2.4 %copy-start.1 = (f32[128,4,512]{0,2,1:T(8,128)S(1)}, f32[128,4,512]{0,2,1:T(8,128)}, u32[]{:S(2)}) copy-start(f32[128,4,512]{0,2,1:T(8,128)} %get-tuple-element.15) | copy-start | bytes 3145732
  194.7 2.7 %copy-start.2 = (f32[128,4,512]{0,2,1:T(8,128)S(1)}, f32[128,4,512]{0,2,1:T(8,128)}, u32[]{:S(2)}) copy-start(f32[128,4,512]{0,2,1:T(8,128)} %get-tuple-element.16) | copy-start | bytes 3145732
  194.7 3.0 %copy-start.3 = (f32[128,4,512]{0,2,1:T(8,128)S(1)}, f32[128,4,512]{0,2,1:T(8,128)}, u32[]{:S(2)}) copy-start(f32[128,4,512]{0,2,1:T(8,128)} %get-tuple-element.5) | copy-start | bytes 3145732
Sparse Core Ops, SparseCore 0:
  30.4 29.8 reduce-scatter.4
  62.7 29.0 reduce-scatter.2
  97.5 29.1 all-gather.6
  136.4 29.1 all-gather.4

commit v2 on v1

--- a/solution.py
+++ b/solution.py
@@ -20,6 +20,32 @@
         high = lax.ppermute(lax.slice_in_dim(block, 0, width, axis=dim), axis, backward)
         block = jnp.concatenate([low, block, high], axis=dim)
     return block
+
+
+def dir_reduce_scatter(field):
+    rank = lax.axis_index("dir")
+    core = rank % 2
+    row = rank // 2
+    pairs = field.reshape((2, 2) + field.shape[1:])
+    keep = lax.dynamic_index_in_dim(pairs, core, 1, keepdims=False)
+    send = lax.dynamic_index_in_dim(pairs, 1 - core, 1, keepdims=False)
+    acc = keep + lax.ppermute(send, "dir", [(0, 1), (1, 0), (2, 3), (3, 2)])
+    keep = lax.dynamic_index_in_dim(acc, row, 0, keepdims=False)
+    send = lax.dynamic_index_in_dim(acc, 1 - row, 0, keepdims=False)
+    return keep + lax.ppermute(send, "dir", [(0, 2), (2, 0), (1, 3), (3, 1)])
+
+
+def dir_all_gather(local):
+    rank = lax.axis_index("dir")
+    core = rank % 2
+    row = rank // 2
+    other = lax.ppermute(local, "dir", [(0, 2), (2, 0), (1, 3), (3, 1)])
+    first = row == 0
+    pair = jnp.stack([jnp.where(first, local, other), jnp.where(first, other, local)], axis=0)
+    mate = lax.ppermute(pair, "dir", [(0, 1), (1, 0), (2, 3), (3, 2)])
+    low = core == 0
+    quad = jnp.stack([jnp.where(low, pair, mate), jnp.where(low, mate, pair)], axis=1)
+    return quad.reshape((4,) + local.shape)
 
 
 def interp_matrix(index, weight, first_row, row_count):
@@ -197,10 +223,10 @@
         xt = part.reshape(child_dev, 2 * step, slots, groups).transpose(3, 1, 2, 0)
         xt = xt.reshape(groups, 2 * step * slots, child_dev)
         field = upward(xt, rows, cosine, sine, dir_size, 2 * step)
-        field = lax.psum_scatter(field, "dir", scatter_dimension=0, tiled=True)[0]
+        field = dir_reduce_scatter(field)
         padded = with_halo(field, (("box", 1),), parent_reach)
         local = parent_translate(padded, own_real, own_imag, own_mask, parent_reach)
-        local_all = lax.all_gather(local, "dir", axis=0, tiled=False)
+        local_all = dir_all_gather(local)
         far = downward(local_all, rows, cosine, sine)
         fars.append(far.reshape(groups, child_dev, 2, step, slots))
     far = jnp.concatenate(fars, axis=3).transpose(1, 2, 3, 4, 0)

time: 208 us -> 197 us (0.947)
  the two profiles are of different devices: /device:TPU:28 before, /device:TPU:65 now
where the time goes in v2:
time: 197 us
  Pallas kernels  73.8 us (37%)
  other arithmetic  44.9 us (23%)
  starting transfers between devices  43.5 us (22%)
  local copies, waits for them, and re-layouts  24 us (12%)
  waiting for transfers between devices  9.93 us (5%)
    pallas_call x2, Pallas kernels, downward(): pl.pallas_call(downward_kernel, grid=(groups,), in_specs=[pl.BlockSpec((p...  40.7 us
    pallas_call x2, Pallas kernels, upward(): pl.pallas_call(upward_kernel, grid=(parts,), in_specs=[pl.BlockSpec((grou...  33.1 us
    ppermute x3, starting transfers between devices, with_halo(): lax.ppermute(lax.slice_in_dim(block, 0, width, axis=dim), axis, backward)  22.1 us
    add x2, other arithmetic, parent_translate(): re_sum = re_sum + weight * (cr * re - ci * im)  11.7 us
    add x2, other arithmetic, parent_translate(): im_sum = im_sum + weight * (cr * im + ci * re)  11.4 us
    ppermute x2, starting transfers between devices, dir_all_gather(): mate = lax.ppermute(pair, 'dir', [(0, 1), (1, 0), (2, 3), (3, 2)])  10.3 us
    ppermute x3, starting transfers between devices, with_halo(): lax.ppermute(lax.slice_in_dim(block, block.shape[dim] - width, None, axis...  7.03 us
    ppermute x2, waiting for transfers between devices, dir_reduce_scatter(): return keep + lax.ppermute(send, 'dir', [(0, 2), (2, 0), (1, 3), (3, 1)])  6.12 us
  transfers between devices with their start and end apart: 14, of which 4 were waited for; matrix products, arithmetic and copies ran while one was open for 24% of the time, Pallas kernels for 19%

profile of v2, /device:TPU:65, one launch (start us, length us, event | category | flops | bytes accessed | tf_op | source)
XLA Modules:
  0.0 196.7 jit_solution(1625663001806054995)
XLA Ops:
  0.0 2.0 %copy.12 = f32[128,8,512]{0,2,1:T(8,128)S(1)} copy(f32[128,8,512]{2,1,0:T(8,128)} %param.8) | data formatting | bytes 4194304 | tf_op args[0]
  4.5 2.6 %select_add_fusion.m_ref = f32[128,2048]{1,0:T(8,128)} fusion(f32[2048]{0:T(1024)S(1)} %bitcast.516, s32[2048]{0:T(1024)S(1)} %bitcast.532, f32[2048]{0:T(1024)S(1)} %bitcast.517, s32[2048]{0:T(1024)S(1)} %bitcast.533, f32[2048]{0:T(1024)S(1)} %bitcast.503, s32[2048]{0:T(1024)S(1)} %bitcast.519, f32[2048]{0:T(1024)S(1)} %bitcast.504, ...), kind=kLoop, calls=%fused_computation.289 | loop fusion | flops 12320768 | bytes 1311232 | tf_op jit(solution)/shard_map/add | solution.py:55
  7.1 16.6 %shard_map.84 = f32[4,4,64,512]{3,2,1,0:T(8,128)} custom-call(f32[8,256,128]{2,1,0:T(8,128)} %bitcast.241, f32[128,2048]{1,0:T(8,128)} %select_add_fusion.m_ref, f32[8,2048]{1,0:T(8,128)} %get-tuple-element.164.cos_ref, f32[8,2048]{1,0:T(8,128)} %get-tuple-element.163.sin_ref), custom_call_target="tpu_custom_call" | custom-call | tf_op jit(solution)/shard_map/pallas_call | solution.py:109
  23.7 2.3 %dynamic-slice_bitcast_fusion = f32[2,4,64,512]{3,2,1,0:T(8,128)} fusion(f32[2,2,4,64,512]{4,3,2,1,0:T(8,128)} %bitcast.235, s32[]{:T(128)S(6)} %select_n.157), kind=kLoop, calls=%fused_computation.285 | loop fusion | bytes 2097156 | tf_op jit(solution)/shard_map/jit(dynamic_index_in_dim)/squeeze | solution.py:31
  27.8 16.6 %shard_map.82 = f32[4,4,64,512]{3,2,1,0:T(8,128)} custom-call(f32[8,256,128]{2,1,0:T(8,128)} %bitcast.245, f32[128,2048]{1,0:T(8,128)} %select_add_fusion.m_ref, f32[8,2048]{1,0:T(8,128)} %get-tuple-element.164.cos_ref, f32[8,2048]{1,0:T(8,128)} %get-tuple-element.163.sin_ref), custom_call_target="tpu_custom_call" | custom-call | tf_op jit(solution)/shard_map/pallas_call | solution.py:109
  44.4 2.3 %dynamic-slice_bitcast_fusion.1 = f32[2,4,64,512]{3,2,1,0:T(8,128)} fusion(f32[2,2,4,64,512]{4,3,2,1,0:T(8,128)} %bitcast.233, s32[]{:T(128)S(6)} %select_n.157), kind=kLoop, calls=%fused_computation.288 | loop fusion | bytes 2097156 | tf_op jit(solution)/shard_map/jit(dynamic_index_in_dim)/squeeze | solution.py:31
  47.3 3.2 %collective-permute-start = (f32[128,8,2]{0,2,1:T(2,128)}, f32[128,8,2]{0,2,1:T(2,128)S(1)}, u32[]{:S(2)}, u32[]{:S(2)}) collective-permute-start(f32[128,8,2]{0,2,1:T(2,128)} %get-tuple-element.18), channel_id=1, source_target_pairs={{0,4},{4,8},{8,12},{12,16},{16,20},{20,24},{24,28},{28,32},{32,36}... | collective-permute-start | bytes 24584 | tf_op jit(solution)/shard_map/ppermute | solution.py:17
  50.5 6.6 %collective-permute-start.1 = (f32[128,8,2]{0,2,1:T(2,128)}, f32[128,8,2]{0,2,1:T(2,128)S(1)}, u32[]{:S(2)}, u32[]{:S(2)}) collective-permute-start(f32[128,8,2]{0,2,1:T(2,128)} %get-tuple-element.17), channel_id=1, source_target_pairs={{4,0},{8,4},{12,8},{16,12},{20,16},{24,20},{28,24},{32,28},{36,32}... | collective-permute-start | bytes 24584 | tf_op jit(solution)/shard_map/ppermute | solution.py:20
  58.5 2.0 bitcast_add_fusion
  68.1 5.8 %collective-permute-done.9 = f32[4,64,512]{2,1,0:T(8,128)} collective-permute-done((f32[4,64,512]{2,1,0:T(8,128)}, f32[4,64,512]{2,1,0:T(8,128)}, u32[]{:S(2)}, u32[]{:S(2)}) %collective-permute-start.9) | collective-permute-done | bytes 524320 | tf_op jit(solution)/shard_map/ppermute | solution.py:35
  75.1 1.9 collective-permute-start.10
  77.1 7.9 %collective-permute-start.11 = (f32[4,16,512]{2,1,0:T(8,128)S(1)}, f32[4,16,512]{2,1,0:T(8,128)S(1)}, u32[]{:S(2)}, u32[]{:S(2)}) collective-permute-start(f32[4,16,512]{2,1,0:T(8,128)S(1)} %get-tuple-element.31), channel_id=1, source_target_pairs={{4,0},{8,4},{12,8},{16,12},{20,16},{24,20},{28,24},{32,28},{36,32}... | collective-permute-start | bytes 393224 | tf_op jit(solution)/shard_map/ppermute | solution.py:20
  86.4 1.9 collective-permute-start.4
  88.6 7.6 %collective-permute-start.5 = (f32[4,16,512]{2,1,0:T(8,128)S(1)}, f32[4,16,512]{2,1,0:T(8,128)S(1)}, u32[]{:S(2)}, u32[]{:S(2)}) collective-permute-start(f32[4,16,512]{2,1,0:T(8,128)S(1)} %get-tuple-element.29), channel_id=1, source_target_pairs={{4,0},{8,4},{12,8},{16,12},{20,16},{24,20},{28,24},{32,28},{36,32}... | collective-permute-start | bytes 393224 | tf_op jit(solution)/shard_map/ppermute | solution.py:20
  96.2 5.8 %multiply_add_fusion.4 = f32[2,64,512]{2,1,0:T(8,128)S(1)} fusion(f32[512]{0:T(512)S(1)} %bitcast.298, f32[512]{0:T(512)S(1)} %bitcast.302, f32[64]{0:T(128)S(1)} %get-tuple-element.102, f32[512]{0:T(512)S(1)} %bitcast.362, f32[512]{0:T(512)S(1)} %bitcast.434, f32[64]{0:T(128)S(1)} %get-tuple-element.36, f32[512]{0:T(512)S(1)} %bitcast.366, ...), kind=kLoop, calls=%fused_computation.436 | loop fusion | flops 14614528 | bytes 1187840 | tf_op jit(solution)/shard_map/add | solution.py:180
  102.0 5.8 %multiply_add_fusion.5 = f32[2,64,512]{2,1,0:T(8,128)S(1)} fusion(f32[512]{0:T(512)S(1)} %bitcast.299, f32[512]{0:T(512)S(1)} %bitcast.303, f32[64]{0:T(128)S(1)} %get-tuple-element.102, f32[512]{0:T(512)S(1)} %bitcast.363, f32[512]{0:T(512)S(1)} %bitcast.435, f32[64]{0:T(128)S(1)} %get-tuple-element.36, f32[512]{0:T(512)S(1)} %bitcast.367, ...), kind=kLoop, calls=%fused_computation.437 | loop fusion | flops 14614528 | bytes 1187840 | tf_op jit(solution)/shard_map/add | solution.py:179
  107.9 1.5 collective-permute-start.12
  109.5 5.6 %multiply_add_fusion.6 = f32[2,64,512]{2,1,0:T(8,128)S(1)} fusion(f32[512]{0:T(512)S(1)} %bitcast.300, f32[512]{0:T(512)S(1)} %bitcast.304, f32[64]{0:T(128)S(1)} %get-tuple-element.102, f32[512]{0:T(512)S(1)} %bitcast.364, f32[512]{0:T(512)S(1)} %bitcast.436, f32[64]{0:T(128)S(1)} %get-tuple-element.36, f32[512]{0:T(512)S(1)} %bitcast.368, ...), kind=kLoop, calls=%fused_computation.438 | loop fusion | flops 14614528 | bytes 1187840 | tf_op jit(solution)/shard_map/add | solution.py:180
  115.1 5.8 %multiply_add_fusion.7 = f32[2,64,512]{2,1,0:T(8,128)S(1)} fusion(f32[512]{0:T(512)S(1)} %bitcast.301, f32[512]{0:T(512)S(1)} %bitcast.305, f32[64]{0:T(128)S(1)} %get-tuple-element.102, f32[512]{0:T(512)S(1)} %bitcast.365, f32[512]{0:T(512)S(1)} %bitcast.437, f32[64]{0:T(128)S(1)} %get-tuple-element.36, f32[512]{0:T(512)S(1)} %bitcast.369, ...), kind=kLoop, calls=%fused_computation.439 | loop fusion | flops 14614528 | bytes 1187840 | tf_op jit(solution)/shard_map/add | solution.py:179
  121.5 4.9 %collective-permute-start.13 = (f32[2,4,64,512]{3,2,1,0:T(8,128)S(1)}, f32[2,4,64,512]{3,2,1,0:T(8,128)S(1)}, u32[]{:S(2)}, u32[]{:S(2)}) collective-permute-start(f32[2,4,64,512]{3,2,1,0:T(8,128)S(1)} %pad_maximum_fusion.5), channel_id=1, source_target_pairs={{0,1},{1,0},{2,3},{3,2},{4,5},{5,4},{6,7},{7,6},{8,9},{9,8},{10,11... | collective-permute-start | bytes 3145736 | tf_op jit(solution)/shard_map/ppermute | solution.py:45
  126.4 3.5 %collective-permute-done.6 = f32[4,64,512]{2,1,0:T(8,128)S(1)} collective-permute-done((f32[4,64,512]{2,1,0:T(8,128)S(1)}, f32[4,64,512]{2,1,0:T(8,128)S(1)}, u32[]{:S(2)}, u32[]{:S(2)}) %collective-permute-start.6) | collective-permute-done | bytes 524320 | tf_op jit(solution)/shard_map/ppermute | solution.py:42
  131.2 5.4 %collective-permute-start.7 = (f32[2,4,64,512]{3,2,1,0:T(8,128)}, f32[2,4,64,512]{3,2,1,0:T(8,128)}, u32[]{:S(2)}, u32[]{:S(2)}) collective-permute-start(f32[2,4,64,512]{3,2,1,0:T(8,128)} %pad_maximum_fusion.4), channel_id=1, source_target_pairs={{0,1},{1,0},{2,3},{3,2},{4,5},{5,4},{6,7},{7,6},{8,9},{9,8},{10,11... | collective-permute-start | bytes 3145736 | tf_op jit(solution)/shard_map/ppermute | solution.py:45
  136.6 2.2 %multiply_subtract_fusion.2 = (f32[128,4,512]{0,2,1:T(8,128)}, f32[128,4,512]{0,2,1:T(8,128)}, f32[128,4,512]{0,2,1:T(8,128)}, f32[128,4,512]{0,2,1:T(8,128)}) fusion(f32[128]{0:T(128)S(1)} %get-tuple-element.172, f32[128]{0:T(128)S(1)} %get-tuple-element.173, f32[128,8,512]{0,2,1:T(8,128)S(1)} %copy.12, f32[128,8,2]{0,2,1:T(2,128)S(1)} %collective-permute-done, ...), kind=kLoop, calls=%fused_computation.295 | loop fusion | flops 4980736 | bytes 6301696 | tf_op jit(solution)/shard_map/sub | solution.py:75
  138.8 2.3 %multiply_subtract_fusion = (f32[128,4,512]{0,2,1:T(8,128)}, f32[128,4,512]{0,2,1:T(8,128)}, f32[128,4,512]{0,2,1:T(8,128)}, f32[128,4,512]{0,2,1:T(8,128)}) fusion(f32[128]{0:T(128)S(1)} %get-tuple-element.176, f32[128]{0:T(128)S(1)} %get-tuple-element.169, f32[128,8,2]{0,2,1:T(2,128)S(1)} %collective-permute-done.1, f32[128,8,512]{0,2,1:T(8,128)S(1)} %copy.12, ...), kind=kLoop, calls=%fused_computation.291 | loop fusion | flops 4980736 | bytes 6301696 | tf_op jit(solution)/shard_map/sub | solution.py:75
  141.4 1.5 pad_maximum_fusion.1
  143.0 20.3 %shard_map.85 = f32[8,128,256]{2,1,0:T(8,128)} custom-call(f32[4,4,64,512]{3,2,1,0:T(8,128)} %bitcast.238, f32[128,2048]{1,0:T(8,128)} %select_add_fusion.m_ref, f32[8,2048]{1,0:T(8,128)} %get-tuple-element.164.cos_ref, f32[8,2048]{1,0:T(8,128)} %get-tuple-element.163.sin_ref), custom_call_target="tpu_custom_call" | custom-call | tf_op jit(solution)/shard_map/pallas_call | solution.py:151
  163.3 1.5 copy.22
  164.9 1.5 select_bitcast_fusion.3
  166.6 1.5 copy.18
  168.1 20.3 %shard_map.83 = f32[8,128,256]{2,1,0:T(8,128)} custom-call(f32[4,4,64,512]{3,2,1,0:T(8,128)} %bitcast.237, f32[128,2048]{1,0:T(8,128)} %select_add_fusion.m_ref, f32[8,2048]{1,0:T(8,128)} %get-tuple-element.164.cos_ref, f32[8,2048]{1,0:T(8,128)} %get-tuple-element.163.sin_ref), custom_call_target="tpu_custom_call" | custom-call | tf_op jit(solution)/shard_map/pallas_call | solution.py:151
  188.4 1.5 copy.19
  194.7 2.0 %copy.24 = f32[128,8,512]{2,1,0:T(8,128)} copy(f32[128,8,512]{0,2,1:T(8,128)S(1)} %fusion.3) | data formatting | bytes 4194304 | tf_op jit(solution)/shard_map/add | solution.py:234
  (93 shorter events, 23.5 us)
Async XLA Ops:
  2.2 1.4 copy-start.14
  26.0 32.5 %collective-permute-start.8 = (f32[2,4,64,512]{3,2,1,0:T(8,128)}, f32[2,4,64,512]{3,2,1,0:T(8,128)}, u32[]{:S(2)}, u32[]{:S(2)}) collective-permute-start(f32[2,4,64,512]{3,2,1,0:T(8,128)} %dynamic-slice_bitcast_fusion), channel_id=1, source_target_pairs={{0,1},{1,0},{2,3},{3,2},{4,5},{5,4},{6,7},{7,6},{8,9},{9,8},{10,11... | collective-permute-start | bytes 3145736 | tf_op jit(solution)/shard_map/ppermute | solution.py:32
  44.4 12.8 %copy-start.11 = (f32[2,32,2048]{2,1,0:T(8,128)S(1)}, f32[2,32,2048]{2,1,0:T(8,128)}, u32[]{:S(2)}) copy-start(f32[2,32,2048]{2,1,0:T(8,128)} %param.14) | copy-start | bytes 1572868
  44.4 13.5 %copy-start.15 = (s32[4,512]{1,0:T(4,128)S(1)}, s32[4,512]{1,0:T(4,128)}, u32[]{:S(2)}) copy-start(s32[4,512]{1,0:T(4,128)} %param.10) | copy-start | bytes 24580
  46.7 16.9 %collective-permute-start.2 = (f32[2,4,64,512]{3,2,1,0:T(8,128)}, f32[2,4,64,512]{3,2,1,0:T(8,128)}, u32[]{:S(2)}, u32[]{:S(2)}) collective-permute-start(f32[2,4,64,512]{3,2,1,0:T(8,128)} %dynamic-slice_bitcast_fusion.1), channel_id=1, source_target_pairs={{0,1},{1,0},{2,3},{3,2},{4,5},{5,4},{6,7},{7,6},{8,9},{9,8},{10,11... | collective-permute-start | bytes 3145736 | tf_op jit(solution)/shard_map/ppermute | solution.py:32
  47.3 89.3 %collective-permute-start = (f32[128,8,2]{0,2,1:T(2,128)}, f32[128,8,2]{0,2,1:T(2,128)S(1)}, u32[]{:S(2)}, u32[]{:S(2)}) collective-permute-start(f32[128,8,2]{0,2,1:T(2,128)} %get-tuple-element.18), channel_id=1, source_target_pairs={{0,4},{4,8},{8,12},{12,16},{16,20},{20,24},{24,28},{28,32},{32,36}... | collective-permute-start | bytes 24584 | tf_op jit(solution)/shard_map/ppermute | solution.py:17
  50.5 88.3 %collective-permute-start.1 = (f32[128,8,2]{0,2,1:T(2,128)}, f32[128,8,2]{0,2,1:T(2,128)S(1)}, u32[]{:S(2)}, u32[]{:S(2)}) collective-permute-start(f32[128,8,2]{0,2,1:T(2,128)} %get-tuple-element.17), channel_id=1, source_target_pairs={{4,0},{8,4},{12,8},{16,12},{20,16},{24,20},{28,24},{32,28},{36,32}... | collective-permute-start | bytes 24584 | tf_op jit(solution)/shard_map/ppermute | solution.py:20
  58.5 5.1 %copy-start = (f32[4,4,64,512]{3,2,1,0:T(8,128)S(1)}, f32[4,4,64,512]{3,2,1,0:T(8,128)}, u32[]{:S(2)}) copy-start(f32[4,4,64,512]{3,2,1,0:T(8,128)} %shard_map.82) | copy-start | bytes 6291460
  61.3 12.7 %collective-permute-start.9 = (f32[4,64,512]{2,1,0:T(8,128)}, f32[4,64,512]{2,1,0:T(8,128)}, u32[]{:S(2)}, u32[]{:S(2)}) collective-permute-start(f32[4,64,512]{2,1,0:T(8,128)} %dynamic-slice_bitcast_fusion.2), channel_id=1, source_target_pairs={{0,2},{2,0},{1,3},{3,1},{4,6},{6,4},{5,7},{7,5},{8,10},{10,8},{9,1... | collective-permute-start | bytes 1572872 | tf_op jit(solution)/shard_map/ppermute | solution.py:35
  66.8 18.4 %collective-permute-start.3 = (f32[4,64,512]{2,1,0:T(8,128)}, f32[4,64,512]{2,1,0:T(8,128)}, u32[]{:S(2)}, u32[]{:S(2)}) collective-permute-start(f32[4,64,512]{2,1,0:T(8,128)} %dynamic-slice_bitcast_fusion.3), channel_id=1, source_target_pairs={{0,2},{2,0},{1,3},{3,1},{4,6},{6,4},{5,7},{7,5},{8,10},{10,8},{9,1... | collective-permute-start | bytes 1572872 | tf_op jit(solution)/shard_map/ppermute | solution.py:35
  68.1 17.1 %copy-start.2 = (f32[2,4,64,512]{3,2,1,0:T(8,128)S(1)}, f32[2,4,64,512]{3,2,1,0:T(8,128)}, u32[]{:S(2)}) copy-start(f32[2,4,64,512]{3,2,1,0:T(8,128)} %copy-done.1) | copy-start | bytes 3145732
  75.1 13.4 %collective-permute-start.10 = (f32[4,16,512]{2,1,0:T(8,128)S(1)}, f32[4,16,512]{2,1,0:T(8,128)S(1)}, u32[]{:S(2)}, u32[]{:S(2)}) collective-permute-start(f32[4,16,512]{2,1,0:T(8,128)S(1)} %get-tuple-element.32), channel_id=1, source_target_pairs={{0,4},{4,8},{8,12},{12,16},{16,20},{20,24},{24,28},{28,32},{32,36}... | collective-permute-start | bytes 393224 | tf_op jit(solution)/shard_map/ppermute | solution.py:17
  77.1 19.1 %collective-permute-start.11 = (f32[4,16,512]{2,1,0:T(8,128)S(1)}, f32[4,16,512]{2,1,0:T(8,128)S(1)}, u32[]{:S(2)}, u32[]{:S(2)}) collective-permute-start(f32[4,16,512]{2,1,0:T(8,128)S(1)} %get-tuple-element.31), channel_id=1, source_target_pairs={{4,0},{8,4},{12,8},{16,12},{20,16},{24,20},{28,24},{32,28},{36,32}... | collective-permute-start | bytes 393224 | tf_op jit(solution)/shard_map/ppermute | solution.py:20
  86.4 23.1 %collective-permute-start.4 = (f32[4,16,512]{2,1,0:T(8,128)S(1)}, f32[4,16,512]{2,1,0:T(8,128)S(1)}, u32[]{:S(2)}, u32[]{:S(2)}) collective-permute-start(f32[4,16,512]{2,1,0:T(8,128)S(1)} %get-tuple-element.30), channel_id=1, source_target_pairs={{0,4},{4,8},{8,12},{12,16},{16,20},{20,24},{24,28},{28,32},{32,36}... | collective-permute-start | bytes 393224 | tf_op jit(solution)/shard_map/ppermute | solution.py:17
  88.6 20.9 %collective-permute-start.5 = (f32[4,16,512]{2,1,0:T(8,128)S(1)}, f32[4,16,512]{2,1,0:T(8,128)S(1)}, u32[]{:S(2)}, u32[]{:S(2)}) collective-permute-start(f32[4,16,512]{2,1,0:T(8,128)S(1)} %get-tuple-element.29), channel_id=1, source_target_pairs={{4,0},{8,4},{12,8},{16,12},{20,16},{24,20},{28,24},{32,28},{36,32}... | collective-permute-start | bytes 393224 | tf_op jit(solution)/shard_map/ppermute | solution.py:20
  107.9 13.5 %copy-start.20 = (f32[2,4,128]{2,1,0:T(4,128)S(1)}, f32[2,4,128]{2,1,0:T(4,128)}, u32[]{:S(2)}) copy-start(f32[2,4,128]{2,1,0:T(4,128)} %param.9) | copy-start | bytes 12292
  107.9 13.4 %collective-permute-start.12 = (f32[4,64,512]{2,1,0:T(8,128)S(1)}, f32[4,64,512]{2,1,0:T(8,128)S(1)}, u32[]{:S(2)}, u32[]{:S(2)}) collective-permute-start(f32[4,64,512]{2,1,0:T(8,128)S(1)} %pad_maximum_fusion.7), channel_id=1, source_target_pairs={{0,2},{2,0},{1,3},{3,1},{4,6},{6,4},{5,7},{7,5},{8,10},{10,8},{9,1... | collective-permute-start | bytes 1572872 | tf_op jit(solution)/shard_map/ppermute | solution.py:42
  121.0 9.0 %collective-permute-start.6 = (f32[4,64,512]{2,1,0:T(8,128)S(1)}, f32[4,64,512]{2,1,0:T(8,128)S(1)}, u32[]{:S(2)}, u32[]{:S(2)}) collective-permute-start(f32[4,64,512]{2,1,0:T(8,128)S(1)} %pad_maximum_fusion.6), channel_id=1, source_target_pairs={{0,2},{2,0},{1,3},{3,1},{4,6},{6,4},{5,7},{7,5},{8,10},{10,8},{9,1... | collective-permute-start | bytes 1572872 | tf_op jit(solution)/shard_map/ppermute | solution.py:42
  121.5 19.6 %collective-permute-start.13 = (f32[2,4,64,512]{3,2,1,0:T(8,128)S(1)}, f32[2,4,64,512]{3,2,1,0:T(8,128)S(1)}, u32[]{:S(2)}, u32[]{:S(2)}) collective-permute-start(f32[2,4,64,512]{3,2,1,0:T(8,128)S(1)} %pad_maximum_fusion.5), channel_id=1, source_target_pairs={{0,1},{1,0},{2,3},{3,2},{4,5},{5,4},{6,7},{7,6},{8,9},{9,8},{10,11... | collective-permute-start | bytes 3145736 | tf_op jit(solution)/shard_map/ppermute | solution.py:45
  131.2 33.7 %collective-permute-start.7 = (f32[2,4,64,512]{3,2,1,0:T(8,128)}, f32[2,4,64,512]{3,2,1,0:T(8,128)}, u32[]{:S(2)}, u32[]{:S(2)}) collective-permute-start(f32[2,4,64,512]{3,2,1,0:T(8,128)} %pad_maximum_fusion.4), channel_id=1, source_target_pairs={{0,1},{1,0},{2,3},{3,2},{4,5},{5,4},{6,7},{7,6},{8,9},{9,8},{10,11... | collective-permute-start | bytes 3145736 | tf_op jit(solution)/shard_map/ppermute | solution.py:45
  190.0 1.5 copy-start.7
  190.0 1.5 copy-start.8
  190.0 1.8 copy-start.9
  190.0 2.2 %copy-start.10 = (f32[128,4,512]{0,2,1:T(8,128)S(1)}, f32[128,4,512]{0,2,1:T(8,128)}, u32[]{:S(2)}) copy-start(f32[128,4,512]{0,2,1:T(8,128)} %get-tuple-element.14) | copy-start | bytes 3145732
  190.2 2.4 %copy-start.3 = (f32[128,4,512]{0,2,1:T(8,128)S(1)}, f32[128,4,512]{0,2,1:T(8,128)}, u32[]{:S(2)}) copy-start(f32[128,4,512]{0,2,1:T(8,128)} %get-tuple-element.9) | copy-start | bytes 3145732
  190.2 2.7 %copy-start.4 = (f32[128,4,512]{0,2,1:T(8,128)S(1)}, f32[128,4,512]{0,2,1:T(8,128)}, u32[]{:S(2)}) copy-start(f32[128,4,512]{0,2,1:T(8,128)} %get-tuple-element.10) | copy-start | bytes 3145732
  190.2 3.0 %copy-start.5 = (f32[128,4,512]{0,2,1:T(8,128)S(1)}, f32[128,4,512]{0,2,1:T(8,128)}, u32[]{:S(2)}) copy-start(f32[128,4,512]{0,2,1:T(8,128)} %get-tuple-element.15) | copy-start | bytes 3145732
  190.2 3.2 %copy-start.6 = (f32[128,4,512]{0,2,1:T(8,128)S(1)}, f32[128,4,512]{0,2,1:T(8,128)}, u32[]{:S(2)}) copy-start(f32[128,4,512]{0,2,1:T(8,128)} %get-tuple-element.16) | copy-start | bytes 3145732
  190.2 3.2 %copy-start.16 = (f32[1,512]{1,0:T(1,128)S(1)}, f32[1,512]{1,0:T(1,128)}, u32[]{:S(2)}) copy-start(f32[1,512]{1,0:T(1,128)} %get-tuple-element.165) | copy-start | bytes 6148
  190.2 3.2 %copy-start.17 = (f32[1,512]{1,0:T(1,128)S(1)}, f32[1,512]{1,0:T(1,128)}, u32[]{:S(2)}) copy-start(f32[1,512]{1,0:T(1,128)} %get-tuple-element.166) | copy-start | bytes 6148
  190.2 3.2 %copy-start.18 = (f32[1,512]{1,0:T(1,128)S(1)}, f32[1,512]{1,0:T(1,128)}, u32[]{:S(2)}) copy-start(f32[1,512]{1,0:T(1,128)} %get-tuple-element.167) | copy-start | bytes 6148
  190.3 3.2 %copy-start.19 = (f32[1,512]{1,0:T(1,128)S(1)}, f32[1,512]{1,0:T(1,128)}, u32[]{:S(2)}) copy-start(f32[1,512]{1,0:T(1,128)} %get-tuple-element.168) | copy-start | bytes 6148
  (3 other events, 3.5 us)

commit v3 on v2

--- a/solution.py
+++ b/solution.py
@@ -5,7 +5,7 @@
 from jax.experimental.pallas import tpu as pltpu
 from jax.sharding import PartitionSpec as P
 
-HIGHEST = lax.Precision.HIGHEST
+HIGHEST = lax.Precision.HIGH
 CHUNKS = 2
 
 

time: 197 us -> 169 us (0.86)
  Pallas kernels: 73.8 us -> 45.4 us
    pallas_call x2, Pallas kernels: 40.7 us -> 24.9 us  [downward(): pl.pallas_call(downward_kernel, grid=(groups,), in_specs=[pl.BlockSpec((p...]
    pallas_call x2, Pallas kernels: 33.1 us -> 20.5 us  [upward(): pl.pallas_call(upward_kernel, grid=(parts,), in_specs=[pl.BlockSpec((grou...]
  transfers between devices with their start and end apart: 14 -> 14, of which waited for: 4 -> 4; matrix products, arithmetic and copies ran while one was open for 24% -> 28% of each run, Pallas kernels for 19% -> 13%
where the time goes in v3:
time: 169 us; the launch traced here: 168 us
  Pallas kernels  45.4 us (27%)
  other arithmetic  44.9 us (27%)
  starting transfers between devices  43.7 us (26%)
  local copies, waits for them, and re-layouts  24 us (14%)
  waiting for transfers between devices  9.91 us (6%)
    pallas_call x2, Pallas kernels, downward(): pl.pallas_call(downward_kernel, grid=(groups,), in_specs=[pl.BlockSpec((p...  24.9 us
    ppermute x3, starting transfers between devices, with_halo(): lax.ppermute(lax.slice_in_dim(block, 0, width, axis=dim), axis, backward)  22.3 us
    pallas_call x2, Pallas kernels, upward(): pl.pallas_call(upward_kernel, grid=(parts,), in_specs=[pl.BlockSpec((grou...  20.5 us
    add x2, other arithmetic, parent_translate(): re_sum = re_sum + weight * (cr * re - ci * im)  11.7 us
    add x2, other arithmetic, parent_translate(): im_sum = im_sum + weight * (cr * im + ci * re)  11.4 us
    ppermute x2, starting transfers between devices, dir_all_gather(): mate = lax.ppermute(pair, 'dir', [(0, 1), (1, 0), (2, 3), (3, 2)])  10.4 us
    ppermute x3, starting transfers between devices, with_halo(): lax.ppermute(lax.slice_in_dim(block, block.shape[dim] - width, None, axis...  7.03 us
    ppermute x2, waiting for transfers between devices, dir_reduce_scatter(): return keep + lax.ppermute(send, 'dir', [(0, 2), (2, 0), (1, 3), (3, 1)])  6.13 us
  transfers between devices with their start and end apart: 14, of which 4 were waited for; matrix products, arithmetic and copies ran while one was open for 28% of the time, Pallas kernels for 13%

profile of v3, /device:TPU:65, one launch (start us, length us, event | category | flops | bytes accessed | tf_op | source)
XLA Modules:
  0.0 168.4 jit_solution(2233085842220637099)
XLA Ops:
  0.0 2.0 %copy.12 = f32[128,8,512]{0,2,1:T(8,128)S(1)} copy(f32[128,8,512]{2,1,0:T(8,128)} %param.8) | data formatting | bytes 4194304 | tf_op args[0]
  4.5 2.6 %select_add_fusion.m_ref = f32[128,2048]{1,0:T(8,128)} fusion(f32[2048]{0:T(1024)S(1)} %bitcast.516, s32[2048]{0:T(1024)S(1)} %bitcast.532, f32[2048]{0:T(1024)S(1)} %bitcast.517, s32[2048]{0:T(1024)S(1)} %bitcast.533, f32[2048]{0:T(1024)S(1)} %bitcast.503, s32[2048]{0:T(1024)S(1)} %bitcast.519, f32[2048]{0:T(1024)S(1)} %bitcast.504, ...), kind=kLoop, calls=%fused_computation.289 | loop fusion | flops 12320768 | bytes 1311232 | tf_op jit(solution)/shard_map/add | solution.py:55
  7.1 10.2 %shard_map.84 = f32[4,4,64,512]{3,2,1,0:T(8,128)} custom-call(f32[8,256,128]{2,1,0:T(8,128)} %bitcast.241, f32[128,2048]{1,0:T(8,128)} %select_add_fusion.m_ref, f32[8,2048]{1,0:T(8,128)} %get-tuple-element.164.cos_ref, f32[8,2048]{1,0:T(8,128)} %get-tuple-element.163.sin_ref), custom_call_target="tpu_custom_call" | custom-call | tf_op jit(solution)/shard_map/pallas_call | solution.py:109
  17.4 2.3 %dynamic-slice_bitcast_fusion = f32[2,4,64,512]{3,2,1,0:T(8,128)} fusion(f32[2,2,4,64,512]{4,3,2,1,0:T(8,128)} %bitcast.235, s32[]{:T(128)S(6)} %select_n.157), kind=kLoop, calls=%fused_computation.285 | loop fusion | bytes 2097156 | tf_op jit(solution)/shard_map/jit(dynamic_index_in_dim)/squeeze | solution.py:31
  21.5 10.2 %shard_map.82 = f32[4,4,64,512]{3,2,1,0:T(8,128)} custom-call(f32[8,256,128]{2,1,0:T(8,128)} %bitcast.245, f32[128,2048]{1,0:T(8,128)} %select_add_fusion.m_ref, f32[8,2048]{1,0:T(8,128)} %get-tuple-element.164.cos_ref, f32[8,2048]{1,0:T(8,128)} %get-tuple-element.163.sin_ref), custom_call_target="tpu_custom_call" | custom-call | tf_op jit(solution)/shard_map/pallas_call | solution.py:109
  31.7 2.3 %dynamic-slice_bitcast_fusion.1 = f32[2,4,64,512]{3,2,1,0:T(8,128)} fusion(f32[2,2,4,64,512]{4,3,2,1,0:T(8,128)} %bitcast.233, s32[]{:T(128)S(6)} %select_n.157), kind=kLoop, calls=%fused_computation.288 | loop fusion | bytes 2097156 | tf_op jit(solution)/shard_map/jit(dynamic_index_in_dim)/squeeze | solution.py:31
  34.7 3.2 %collective-permute-start = (f32[128,8,2]{0,2,1:T(2,128)}, f32[128,8,2]{0,2,1:T(2,128)S(1)}, u32[]{:S(2)}, u32[]{:S(2)}) collective-permute-start(f32[128,8,2]{0,2,1:T(2,128)} %get-tuple-element.18), channel_id=1, source_target_pairs={{0,4},{4,8},{8,12},{12,16},{16,20},{20,24},{24,28},{28,32},{32,36}... | collective-permute-start | bytes 24584 | tf_op jit(solution)/shard_map/ppermute | solution.py:17
  37.9 6.6 %collective-permute-start.1 = (f32[128,8,2]{0,2,1:T(2,128)}, f32[128,8,2]{0,2,1:T(2,128)S(1)}, u32[]{:S(2)}, u32[]{:S(2)}) collective-permute-start(f32[128,8,2]{0,2,1:T(2,128)} %get-tuple-element.17), channel_id=1, source_target_pairs={{4,0},{8,4},{12,8},{16,12},{20,16},{24,20},{28,24},{32,28},{36,32}... | collective-permute-start | bytes 24584 | tf_op jit(solution)/shard_map/ppermute | solution.py:20
  45.8 2.0 %bitcast_add_fusion = f32[2,4,64,512]{3,2,1,0:T(8,128)S(1)} fusion(f32[2,4,64,512]{3,2,1,0:T(8,128)} %collective-permute-done.8, f32[2,2,4,64,512]{4,3,2,1,0:T(8,128)} %bitcast.236, s32[]{:T(128)S(6)} %select_n.156), kind=kLoop, calls=%fused_computation.281 | loop fusion | flops 262144 | bytes 3145732 | tf_op jit(solution)/shard_map/add | solution.py:32
  55.5 5.9 %collective-permute-done.9 = f32[4,64,512]{2,1,0:T(8,128)} collective-permute-done((f32[4,64,512]{2,1,0:T(8,128)}, f32[4,64,512]{2,1,0:T(8,128)}, u32[]{:S(2)}, u32[]{:S(2)}) %collective-permute-start.9) | collective-permute-done | bytes 524320 | tf_op jit(solution)/shard_map/ppermute | solution.py:35
  62.5 1.9 %collective-permute-start.10 = (f32[4,16,512]{2,1,0:T(8,128)S(1)}, f32[4,16,512]{2,1,0:T(8,128)S(1)}, u32[]{:S(2)}, u32[]{:S(2)}) collective-permute-start(f32[4,16,512]{2,1,0:T(8,128)S(1)} %get-tuple-element.32), channel_id=1, source_target_pairs={{0,4},{4,8},{8,12},{12,16},{16,20},{20,24},{24,28},{28,32},{32,36}... | collective-permute-start | bytes 393224 | tf_op jit(solution)/shard_map/ppermute | solution.py:17
  64.4 7.9 %collective-permute-start.11 = (f32[4,16,512]{2,1,0:T(8,128)S(1)}, f32[4,16,512]{2,1,0:T(8,128)S(1)}, u32[]{:S(2)}, u32[]{:S(2)}) collective-permute-start(f32[4,16,512]{2,1,0:T(8,128)S(1)} %get-tuple-element.31), channel_id=1, source_target_pairs={{4,0},{8,4},{12,8},{16,12},{20,16},{24,20},{28,24},{32,28},{36,32}... | collective-permute-start | bytes 393224 | tf_op jit(solution)/shard_map/ppermute | solution.py:20
  73.7 1.9 %collective-permute-start.4 = (f32[4,16,512]{2,1,0:T(8,128)S(1)}, f32[4,16,512]{2,1,0:T(8,128)S(1)}, u32[]{:S(2)}, u32[]{:S(2)}) collective-permute-start(f32[4,16,512]{2,1,0:T(8,128)S(1)} %get-tuple-element.30), channel_id=1, source_target_pairs={{0,4},{4,8},{8,12},{12,16},{16,20},{20,24},{24,28},{28,32},{32,36}... | collective-permute-start | bytes 393224 | tf_op jit(solution)/shard_map/ppermute | solution.py:17
  75.9 7.8 %collective-permute-start.5 = (f32[4,16,512]{2,1,0:T(8,128)S(1)}, f32[4,16,512]{2,1,0:T(8,128)S(1)}, u32[]{:S(2)}, u32[]{:S(2)}) collective-permute-start(f32[4,16,512]{2,1,0:T(8,128)S(1)} %get-tuple-element.29), channel_id=1, source_target_pairs={{4,0},{8,4},{12,8},{16,12},{20,16},{24,20},{28,24},{32,28},{36,32}... | collective-permute-start | bytes 393224 | tf_op jit(solution)/shard_map/ppermute | solution.py:20
  83.7 5.8 %multiply_add_fusion.4 = f32[2,64,512]{2,1,0:T(8,128)S(1)} fusion(f32[512]{0:T(512)S(1)} %bitcast.298, f32[512]{0:T(512)S(1)} %bitcast.302, f32[64]{0:T(128)S(1)} %get-tuple-element.102, f32[512]{0:T(512)S(1)} %bitcast.362, f32[512]{0:T(512)S(1)} %bitcast.434, f32[64]{0:T(128)S(1)} %get-tuple-element.36, f32[512]{0:T(512)S(1)} %bitcast.366, ...), kind=kLoop, calls=%fused_computation.436 | loop fusion | flops 14614528 | bytes 1187840 | tf_op jit(solution)/shard_map/add | solution.py:180
  89.6 5.8 %multiply_add_fusion.5 = f32[2,64,512]{2,1,0:T(8,128)S(1)} fusion(f32[512]{0:T(512)S(1)} %bitcast.299, f32[512]{0:T(512)S(1)} %bitcast.303, f32[64]{0:T(128)S(1)} %get-tuple-element.102, f32[512]{0:T(512)S(1)} %bitcast.363, f32[512]{0:T(512)S(1)} %bitcast.435, f32[64]{0:T(128)S(1)} %get-tuple-element.36, f32[512]{0:T(512)S(1)} %bitcast.367, ...), kind=kLoop, calls=%fused_computation.437 | loop fusion | flops 14614528 | bytes 1187840 | tf_op jit(solution)/shard_map/add | solution.py:179
  95.5 1.5 collective-permute-start.12
  97.0 5.6 %multiply_add_fusion.6 = f32[2,64,512]{2,1,0:T(8,128)S(1)} fusion(f32[512]{0:T(512)S(1)} %bitcast.300, f32[512]{0:T(512)S(1)} %bitcast.304, f32[64]{0:T(128)S(1)} %get-tuple-element.102, f32[512]{0:T(512)S(1)} %bitcast.364, f32[512]{0:T(512)S(1)} %bitcast.436, f32[64]{0:T(128)S(1)} %get-tuple-element.36, f32[512]{0:T(512)S(1)} %bitcast.368, ...), kind=kLoop, calls=%fused_computation.438 | loop fusion | flops 14614528 | bytes 1187840 | tf_op jit(solution)/shard_map/add | solution.py:180
  102.6 5.8 %multiply_add_fusion.7 = f32[2,64,512]{2,1,0:T(8,128)S(1)} fusion(f32[512]{0:T(512)S(1)} %bitcast.301, f32[512]{0:T(512)S(1)} %bitcast.305, f32[64]{0:T(128)S(1)} %get-tuple-element.102, f32[512]{0:T(512)S(1)} %bitcast.365, f32[512]{0:T(512)S(1)} %bitcast.437, f32[64]{0:T(128)S(1)} %get-tuple-element.36, f32[512]{0:T(512)S(1)} %bitcast.369, ...), kind=kLoop, calls=%fused_computation.439 | loop fusion | flops 14614528 | bytes 1187840 | tf_op jit(solution)/shard_map/add | solution.py:179
  109.1 4.9 %collective-permute-start.13 = (f32[2,4,64,512]{3,2,1,0:T(8,128)S(1)}, f32[2,4,64,512]{3,2,1,0:T(8,128)S(1)}, u32[]{:S(2)}, u32[]{:S(2)}) collective-permute-start(f32[2,4,64,512]{3,2,1,0:T(8,128)S(1)} %pad_maximum_fusion.5), channel_id=1, source_target_pairs={{0,1},{1,0},{2,3},{3,2},{4,5},{5,4},{6,7},{7,6},{8,9},{9,8},{10,11... | collective-permute-start | bytes 3145736 | tf_op jit(solution)/shard_map/ppermute | solution.py:45
  114.0 3.5 %collective-permute-done.6 = f32[4,64,512]{2,1,0:T(8,128)S(1)} collective-permute-done((f32[4,64,512]{2,1,0:T(8,128)S(1)}, f32[4,64,512]{2,1,0:T(8,128)S(1)}, u32[]{:S(2)}, u32[]{:S(2)}) %collective-permute-start.6) | collective-permute-done | bytes 524320 | tf_op jit(solution)/shard_map/ppermute | solution.py:42
  118.7 5.4 %collective-permute-start.7 = (f32[2,4,64,512]{3,2,1,0:T(8,128)}, f32[2,4,64,512]{3,2,1,0:T(8,128)}, u32[]{:S(2)}, u32[]{:S(2)}) collective-permute-start(f32[2,4,64,512]{3,2,1,0:T(8,128)} %pad_maximum_fusion.4), channel_id=1, source_target_pairs={{0,1},{1,0},{2,3},{3,2},{4,5},{5,4},{6,7},{7,6},{8,9},{9,8},{10,11... | collective-permute-start | bytes 3145736 | tf_op jit(solution)/shard_map/ppermute | solution.py:45
  124.1 2.2 %multiply_subtract_fusion.2 = (f32[128,4,512]{0,2,1:T(8,128)}, f32[128,4,512]{0,2,1:T(8,128)}, f32[128,4,512]{0,2,1:T(8,128)}, f32[128,4,512]{0,2,1:T(8,128)}) fusion(f32[128]{0:T(128)S(1)} %get-tuple-element.172, f32[128]{0:T(128)S(1)} %get-tuple-element.173, f32[128,8,512]{0,2,1:T(8,128)S(1)} %copy.12, f32[128,8,2]{0,2,1:T(2,128)S(1)} %collective-permute-done, ...), kind=kLoop, calls=%fused_computation.295 | loop fusion | flops 4980736 | bytes 6301696 | tf_op jit(solution)/shard_map/sub | solution.py:75
  126.3 2.3 %multiply_subtract_fusion = (f32[128,4,512]{0,2,1:T(8,128)}, f32[128,4,512]{0,2,1:T(8,128)}, f32[128,4,512]{0,2,1:T(8,128)}, f32[128,4,512]{0,2,1:T(8,128)}) fusion(f32[128]{0:T(128)S(1)} %get-tuple-element.176, f32[128]{0:T(128)S(1)} %get-tuple-element.169, f32[128,8,2]{0,2,1:T(2,128)S(1)} %collective-permute-done.1, f32[128,8,512]{0,2,1:T(8,128)S(1)} %copy.12, ...), kind=kLoop, calls=%fused_computation.291 | loop fusion | flops 4980736 | bytes 6301696 | tf_op jit(solution)/shard_map/sub | solution.py:75
  128.9 1.5 pad_maximum_fusion.1
  130.5 12.5 %shard_map.85 = f32[8,128,256]{2,1,0:T(8,128)} custom-call(f32[4,4,64,512]{3,2,1,0:T(8,128)} %bitcast.238, f32[128,2048]{1,0:T(8,128)} %select_add_fusion.m_ref, f32[8,2048]{1,0:T(8,128)} %get-tuple-element.164.cos_ref, f32[8,2048]{1,0:T(8,128)} %get-tuple-element.163.sin_ref), custom_call_target="tpu_custom_call" | custom-call | tf_op jit(solution)/shard_map/pallas_call | solution.py:151
  142.9 1.5 copy.22
  144.5 1.5 select_bitcast_fusion.3
  146.2 1.5 copy.18
  147.7 12.5 %shard_map.83 = f32[8,128,256]{2,1,0:T(8,128)} custom-call(f32[4,4,64,512]{3,2,1,0:T(8,128)} %bitcast.237, f32[128,2048]{1,0:T(8,128)} %select_add_fusion.m_ref, f32[8,2048]{1,0:T(8,128)} %get-tuple-element.164.cos_ref, f32[8,2048]{1,0:T(8,128)} %get-tuple-element.163.sin_ref), custom_call_target="tpu_custom_call" | custom-call | tf_op jit(solution)/shard_map/pallas_call | solution.py:151
  160.2 1.5 copy.19
  166.4 2.0 %copy.24 = f32[128,8,512]{2,1,0:T(8,128)} copy(f32[128,8,512]{0,2,1:T(8,128)S(1)} %fusion.3) | data formatting | bytes 4194304 | tf_op jit(solution)/shard_map/add | solution.py:234
  (93 shorter events, 23.5 us)
Async XLA Ops:
  2.2 1.4 copy-start.14
  19.6 26.2 %collective-permute-start.8 = (f32[2,4,64,512]{3,2,1,0:T(8,128)}, f32[2,4,64,512]{3,2,1,0:T(8,128)}, u32[]{:S(2)}, u32[]{:S(2)}) collective-permute-start(f32[2,4,64,512]{3,2,1,0:T(8,128)} %dynamic-slice_bitcast_fusion), channel_id=1, source_target_pairs={{0,1},{1,0},{2,3},{3,2},{4,5},{5,4},{6,7},{7,6},{8,9},{9,8},{10,11... | collective-permute-start | bytes 3145736 | tf_op jit(solution)/shard_map/ppermute | solution.py:32
  31.7 12.8 %copy-start.11 = (f32[2,32,2048]{2,1,0:T(8,128)S(1)}, f32[2,32,2048]{2,1,0:T(8,128)}, u32[]{:S(2)}) copy-start(f32[2,32,2048]{2,1,0:T(8,128)} %param.14) | copy-start | bytes 1572868
  31.7 13.5 %copy-start.15 = (s32[4,512]{1,0:T(4,128)S(1)}, s32[4,512]{1,0:T(4,128)}, u32[]{:S(2)}) copy-start(s32[4,512]{1,0:T(4,128)} %param.10) | copy-start | bytes 24580
  34.0 16.9 %collective-permute-start.2 = (f32[2,4,64,512]{3,2,1,0:T(8,128)}, f32[2,4,64,512]{3,2,1,0:T(8,128)}, u32[]{:S(2)}, u32[]{:S(2)}) collective-permute-start(f32[2,4,64,512]{3,2,1,0:T(8,128)} %dynamic-slice_bitcast_fusion.1), channel_id=1, source_target_pairs={{0,1},{1,0},{2,3},{3,2},{4,5},{5,4},{6,7},{7,6},{8,9},{9,8},{10,11... | collective-permute-start | bytes 3145736 | tf_op jit(solution)/shard_map/ppermute | solution.py:32
  34.7 89.5 %collective-permute-start = (f32[128,8,2]{0,2,1:T(2,128)}, f32[128,8,2]{0,2,1:T(2,128)S(1)}, u32[]{:S(2)}, u32[]{:S(2)}) collective-permute-start(f32[128,8,2]{0,2,1:T(2,128)} %get-tuple-element.18), channel_id=1, source_target_pairs={{0,4},{4,8},{8,12},{12,16},{16,20},{20,24},{24,28},{28,32},{32,36}... | collective-permute-start | bytes 24584 | tf_op jit(solution)/shard_map/ppermute | solution.py:17
  37.9 88.5 %collective-permute-start.1 = (f32[128,8,2]{0,2,1:T(2,128)}, f32[128,8,2]{0,2,1:T(2,128)S(1)}, u32[]{:S(2)}, u32[]{:S(2)}) collective-permute-start(f32[128,8,2]{0,2,1:T(2,128)} %get-tuple-element.17), channel_id=1, source_target_pairs={{4,0},{8,4},{12,8},{16,12},{20,16},{24,20},{28,24},{32,28},{36,32}... | collective-permute-start | bytes 24584 | tf_op jit(solution)/shard_map/ppermute | solution.py:20
  45.8 5.1 %copy-start = (f32[4,4,64,512]{3,2,1,0:T(8,128)S(1)}, f32[4,4,64,512]{3,2,1,0:T(8,128)}, u32[]{:S(2)}) copy-start(f32[4,4,64,512]{3,2,1,0:T(8,128)} %shard_map.82) | copy-start | bytes 6291460
  48.6 12.7 %collective-permute-start.9 = (f32[4,64,512]{2,1,0:T(8,128)}, f32[4,64,512]{2,1,0:T(8,128)}, u32[]{:S(2)}, u32[]{:S(2)}) collective-permute-start(f32[4,64,512]{2,1,0:T(8,128)} %dynamic-slice_bitcast_fusion.2), channel_id=1, source_target_pairs={{0,2},{2,0},{1,3},{3,1},{4,6},{6,4},{5,7},{7,5},{8,10},{10,8},{9,1... | collective-permute-start | bytes 1572872 | tf_op jit(solution)/shard_map/ppermute | solution.py:35
  54.2 18.4 %collective-permute-start.3 = (f32[4,64,512]{2,1,0:T(8,128)}, f32[4,64,512]{2,1,0:T(8,128)}, u32[]{:S(2)}, u32[]{:S(2)}) collective-permute-start(f32[4,64,512]{2,1,0:T(8,128)} %dynamic-slice_bitcast_fusion.3), channel_id=1, source_target_pairs={{0,2},{2,0},{1,3},{3,1},{4,6},{6,4},{5,7},{7,5},{8,10},{10,8},{9,1... | collective-permute-start | bytes 1572872 | tf_op jit(solution)/shard_map/ppermute | solution.py:35
  55.5 17.1 %copy-start.2 = (f32[2,4,64,512]{3,2,1,0:T(8,128)S(1)}, f32[2,4,64,512]{3,2,1,0:T(8,128)}, u32[]{:S(2)}) copy-start(f32[2,4,64,512]{3,2,1,0:T(8,128)} %copy-done.1) | copy-start | bytes 3145732
  62.5 13.4 %collective-permute-start.10 = (f32[4,16,512]{2,1,0:T(8,128)S(1)}, f32[4,16,512]{2,1,0:T(8,128)S(1)}, u32[]{:S(2)}, u32[]{:S(2)}) collective-permute-start(f32[4,16,512]{2,1,0:T(8,128)S(1)} %get-tuple-element.32), channel_id=1, source_target_pairs={{0,4},{4,8},{8,12},{12,16},{16,20},{20,24},{24,28},{28,32},{32,36}... | collective-permute-start | bytes 393224 | tf_op jit(solution)/shard_map/ppermute | solution.py:17
  64.4 19.3 %collective-permute-start.11 = (f32[4,16,512]{2,1,0:T(8,128)S(1)}, f32[4,16,512]{2,1,0:T(8,128)S(1)}, u32[]{:S(2)}, u32[]{:S(2)}) collective-permute-start(f32[4,16,512]{2,1,0:T(8,128)S(1)} %get-tuple-element.31), channel_id=1, source_target_pairs={{4,0},{8,4},{12,8},{16,12},{20,16},{24,20},{28,24},{32,28},{36,32}... | collective-permute-start | bytes 393224 | tf_op jit(solution)/shard_map/ppermute | solution.py:20
  73.7 23.3 %collective-permute-start.4 = (f32[4,16,512]{2,1,0:T(8,128)S(1)}, f32[4,16,512]{2,1,0:T(8,128)S(1)}, u32[]{:S(2)}, u32[]{:S(2)}) collective-permute-start(f32[4,16,512]{2,1,0:T(8,128)S(1)} %get-tuple-element.30), channel_id=1, source_target_pairs={{0,4},{4,8},{8,12},{12,16},{16,20},{20,24},{24,28},{28,32},{32,36}... | collective-permute-start | bytes 393224 | tf_op jit(solution)/shard_map/ppermute | solution.py:17
  75.9 21.1 %collective-permute-start.5 = (f32[4,16,512]{2,1,0:T(8,128)S(1)}, f32[4,16,512]{2,1,0:T(8,128)S(1)}, u32[]{:S(2)}, u32[]{:S(2)}) collective-permute-start(f32[4,16,512]{2,1,0:T(8,128)S(1)} %get-tuple-element.29), channel_id=1, source_target_pairs={{4,0},{8,4},{12,8},{16,12},{20,16},{24,20},{28,24},{32,28},{36,32}... | collective-permute-start | bytes 393224 | tf_op jit(solution)/shard_map/ppermute | solution.py:20
  95.4 13.4 %copy-start.20 = (f32[2,4,128]{2,1,0:T(4,128)S(1)}, f32[2,4,128]{2,1,0:T(4,128)}, u32[]{:S(2)}) copy-start(f32[2,4,128]{2,1,0:T(4,128)} %param.9) | copy-start | bytes 12292
  95.5 13.4 %collective-permute-start.12 = (f32[4,64,512]{2,1,0:T(8,128)S(1)}, f32[4,64,512]{2,1,0:T(8,128)S(1)}, u32[]{:S(2)}, u32[]{:S(2)}) collective-permute-start(f32[4,64,512]{2,1,0:T(8,128)S(1)} %pad_maximum_fusion.7), channel_id=1, source_target_pairs={{0,2},{2,0},{1,3},{3,1},{4,6},{6,4},{5,7},{7,5},{8,10},{10,8},{9,1... | collective-permute-start | bytes 1572872 | tf_op jit(solution)/shard_map/ppermute | solution.py:42
  108.5 9.0 %collective-permute-start.6 = (f32[4,64,512]{2,1,0:T(8,128)S(1)}, f32[4,64,512]{2,1,0:T(8,128)S(1)}, u32[]{:S(2)}, u32[]{:S(2)}) collective-permute-start(f32[4,64,512]{2,1,0:T(8,128)S(1)} %pad_maximum_fusion.6), channel_id=1, source_target_pairs={{0,2},{2,0},{1,3},{3,1},{4,6},{6,4},{5,7},{7,5},{8,10},{10,8},{9,1... | collective-permute-start | bytes 1572872 | tf_op jit(solution)/shard_map/ppermute | solution.py:42
  109.1 19.6 %collective-permute-start.13 = (f32[2,4,64,512]{3,2,1,0:T(8,128)S(1)}, f32[2,4,64,512]{3,2,1,0:T(8,128)S(1)}, u32[]{:S(2)}, u32[]{:S(2)}) collective-permute-start(f32[2,4,64,512]{3,2,1,0:T(8,128)S(1)} %pad_maximum_fusion.5), channel_id=1, source_target_pairs={{0,1},{1,0},{2,3},{3,2},{4,5},{5,4},{6,7},{7,6},{8,9},{9,8},{10,11... | collective-permute-start | bytes 3145736 | tf_op jit(solution)/shard_map/ppermute | solution.py:45
  118.7 25.8 %collective-permute-start.7 = (f32[2,4,64,512]{3,2,1,0:T(8,128)}, f32[2,4,64,512]{3,2,1,0:T(8,128)}, u32[]{:S(2)}, u32[]{:S(2)}) collective-permute-start(f32[2,4,64,512]{3,2,1,0:T(8,128)} %pad_maximum_fusion.4), channel_id=1, source_target_pairs={{0,1},{1,0},{2,3},{3,2},{4,5},{5,4},{6,7},{7,6},{8,9},{9,8},{10,11... | collective-permute-start | bytes 3145736 | tf_op jit(solution)/shard_map/ppermute | solution.py:45
  161.8 1.5 copy-start.7
  161.8 1.5 copy-start.8
  161.8 1.8 %copy-start.9 = (f32[128,4,512]{0,2,1:T(8,128)S(1)}, f32[128,4,512]{0,2,1:T(8,128)}, u32[]{:S(2)}) copy-start(f32[128,4,512]{0,2,1:T(8,128)} %get-tuple-element.13) | copy-start | bytes 3145732
  161.8 2.2 %copy-start.10 = (f32[128,4,512]{0,2,1:T(8,128)S(1)}, f32[128,4,512]{0,2,1:T(8,128)}, u32[]{:S(2)}) copy-start(f32[128,4,512]{0,2,1:T(8,128)} %get-tuple-element.14) | copy-start | bytes 3145732
  161.9 2.4 %copy-start.3 = (f32[128,4,512]{0,2,1:T(8,128)S(1)}, f32[128,4,512]{0,2,1:T(8,128)}, u32[]{:S(2)}) copy-start(f32[128,4,512]{0,2,1:T(8,128)} %get-tuple-element.9) | copy-start | bytes 3145732
  161.9 2.7 %copy-start.4 = (f32[128,4,512]{0,2,1:T(8,128)S(1)}, f32[128,4,512]{0,2,1:T(8,128)}, u32[]{:S(2)}) copy-start(f32[128,4,512]{0,2,1:T(8,128)} %get-tuple-element.10) | copy-start | bytes 3145732
  162.0 3.0 %copy-start.5 = (f32[128,4,512]{0,2,1:T(8,128)S(1)}, f32[128,4,512]{0,2,1:T(8,128)}, u32[]{:S(2)}) copy-start(f32[128,4,512]{0,2,1:T(8,128)} %get-tuple-element.15) | copy-start | bytes 3145732
  162.0 3.2 %copy-start.6 = (f32[128,4,512]{0,2,1:T(8,128)S(1)}, f32[128,4,512]{0,2,1:T(8,128)}, u32[]{:S(2)}) copy-start(f32[128,4,512]{0,2,1:T(8,128)} %get-tuple-element.16) | copy-start | bytes 3145732
  162.0 3.2 %copy-start.16 = (f32[1,512]{1,0:T(1,128)S(1)}, f32[1,512]{1,0:T(1,128)}, u32[]{:S(2)}) copy-start(f32[1,512]{1,0:T(1,128)} %get-tuple-element.165) | copy-start | bytes 6148
  162.0 3.2 %copy-start.17 = (f32[1,512]{1,0:T(1,128)S(1)}, f32[1,512]{1,0:T(1,128)}, u32[]{:S(2)}) copy-start(f32[1,512]{1,0:T(1,128)} %get-tuple-element.166) | copy-start | bytes 6148
  162.0 3.2 %copy-start.18 = (f32[1,512]{1,0:T(1,128)S(1)}, f32[1,512]{1,0:T(1,128)}, u32[]{:S(2)}) copy-start(f32[1,512]{1,0:T(1,128)} %get-tuple-element.167) | copy-start | bytes 6148
  162.0 3.2 %copy-start.19 = (f32[1,512]{1,0:T(1,128)S(1)}, f32[1,512]{1,0:T(1,128)}, u32[]{:S(2)}) copy-start(f32[1,512]{1,0:T(1,128)} %get-tuple-element.168) | copy-start | bytes 6148
  (3 other events, 3.5 us)

commit v4 on v3

--- a/solution.py
+++ b/solution.py
@@ -6,7 +6,7 @@
 from jax.sharding import PartitionSpec as P
 
 HIGHEST = lax.Precision.HIGH
-CHUNKS = 2
+CHUNKS = 4
 
 
 def with_halo(block, sides, width):

time: 169 us -> 200 us (1.18)
  starting transfers between devices: 43.7 us -> 66.1 us
  Pallas kernels: 45.4 us -> 54.7 us
  local copies, waits for them, and re-layouts: 24 us -> 33.1 us
  waiting for transfers between devices: 9.91 us -> 2.01 us
  other arithmetic: 44.9 us -> 41.7 us
    ppermute x3 -> x5, starting transfers between devices: 22.3 us -> 36.7 us  [with_halo(): lax.ppermute(lax.slice_in_dim(block, 0, width, axis=dim), axis, backward)]
    ppermute x2 -> x4, waiting for transfers between devices: 6.13 us -> 0.2 us  [dir_reduce_scatter(): return keep + lax.ppermute(send, 'dir', [(0, 2), (2, 0), (1, 3), (3, 1)])]
    pallas_call x2 -> x4, Pallas kernels: 24.9 us -> 29.6 us  [downward(): pl.pallas_call(downward_kernel, grid=(groups,), in_specs=[pl.BlockSpec((p...]
    pallas_call x2 -> x4, Pallas kernels: 20.5 us -> 25.1 us  [upward(): pl.pallas_call(upward_kernel, grid=(parts,), in_specs=[pl.BlockSpec((grou...]
    ppermute x3 -> x5, starting transfers between devices: 7.03 us -> 10.9 us  [with_halo(): lax.ppermute(lax.slice_in_dim(block, block.shape[dim] - width, None, axis...]
    ppermute x2 -> x4, waiting for transfers between devices: 3.49 us -> 0.01 us  [dir_all_gather(): other = lax.ppermute(local, 'dir', [(0, 2), (2, 0), (1, 3), (3, 1)])]
    add x2 -> x4, other arithmetic: 11.4 us -> 8.36 us  [parent_translate(): im_sum = im_sum + weight * (cr * im + ci * re)]
    squeeze x2 -> x4, local copies, waits for them, and re-layouts: 4.59 us -> 7.52 us  [dir_reduce_scatter(): send = lax.dynamic_index_in_dim(pairs, 1 - core, 1, keepdims=False)]
  transfers between devices with their start and end apart: 14 -> 26, of which waited for: 4 -> 2; matrix products, arithmetic and copies ran while one was open for 28% -> 28% of each run, Pallas kernels for 13% -> 21%
where the time goes in v4:
time: 200 us; the launch traced here: 199 us
  starting transfers between devices  66.1 us (33%)
  Pallas kernels  54.7 us (27%)
  other arithmetic  41.7 us (21%)
  local copies, waits for them, and re-layouts  33.1 us (17%)
  waiting for transfers between devices  2.01 us (1%)
    ppermute x5, starting transfers between devices, with_halo(): lax.ppermute(lax.slice_in_dim(block, 0, width, axis=dim), axis, backward)  36.7 us
    pallas_call x4, Pallas kernels, downward(): pl.pallas_call(downward_kernel, grid=(groups,), in_specs=[pl.BlockSpec((p...  29.6 us
    pallas_call x4, Pallas kernels, upward(): pl.pallas_call(upward_kernel, grid=(parts,), in_specs=[pl.BlockSpec((grou...  25.1 us
    ppermute x5, starting transfers between devices, with_halo(): lax.ppermute(lax.slice_in_dim(block, block.shape[dim] - width, None, axis...  10.9 us
    ppermute x4, starting transfers between devices, dir_all_gather(): mate = lax.ppermute(pair, 'dir', [(0, 1), (1, 0), (2, 3), (3, 2)])  10.6 us
    add x4, other arithmetic, parent_translate(): re_sum = re_sum + weight * (cr * re - ci * im)  9.04 us
    add x4, other arithmetic, parent_translate(): im_sum = im_sum + weight * (cr * im + ci * re)  8.36 us
    squeeze x4, local copies, waits for them, and re-layouts, dir_reduce_scatter(): send = lax.dynamic_index_in_dim(pairs, 1 - core, 1, keepdims=False)  7.52 us
  transfers between devices with their start and end apart: 26, of which 2 were waited for; matrix products, arithmetic and copies ran while one was open for 28% of the time, Pallas kernels for 21%

profile of v4, /device:TPU:65, one launch (start us, length us, event | category | flops | bytes accessed | tf_op | source)
XLA Modules:
  0.0 198.5 jit_solution(350318725866150148)
XLA Ops:
  0.0 2.8 %copy.36 = f32[128,8,512]{2,0,1:T(8,128)S(1)} copy(f32[128,8,512]{2,1,0:T(8,128)} %param.8) | data formatting | bytes 4194304 | tf_op args[0]
  5.3 2.6 %select_add_fusion.m_ref = f32[128,2048]{1,0:T(8,128)} fusion(f32[2048]{0:T(1024)S(1)} %bitcast.830, s32[2048]{0:T(1024)S(1)} %bitcast.846, f32[2048]{0:T(1024)S(1)} %bitcast.831, s32[2048]{0:T(1024)S(1)} %bitcast.847, f32[2048]{0:T(1024)S(1)} %bitcast.817, s32[2048]{0:T(1024)S(1)} %bitcast.833, f32[2048]{0:T(1024)S(1)} %bitcast.818, ...), kind=kLoop, calls=%fused_computation.281 | loop fusion | flops 12320768 | bytes 1311232 | tf_op jit(solution)/shard_map/add | solution.py:55
  7.9 6.3 %shard_map.88 = f32[4,2,64,512]{3,2,1,0:T(8,128)} custom-call(f32[8,128,128]{2,1,0:T(8,128)} %bitcast.296, f32[128,2048]{1,0:T(8,128)} %select_add_fusion.m_ref, f32[8,2048]{1,0:T(8,128)} %get-tuple-element.178.cos_ref, f32[8,2048]{1,0:T(8,128)} %get-tuple-element.177.sin_ref), custom_call_target="tpu_custom_call" | custom-call | tf_op jit(solution)/shard_map/pallas_call | solution.py:109
  17.9 6.3 %shard_map.86 = f32[4,2,64,512]{3,2,1,0:T(8,128)} custom-call(f32[8,128,128]{2,1,0:T(8,128)} %bitcast.297, f32[128,2048]{1,0:T(8,128)} %select_add_fusion.m_ref, f32[8,2048]{1,0:T(8,128)} %get-tuple-element.178.cos_ref, f32[8,2048]{1,0:T(8,128)} %get-tuple-element.177.sin_ref), custom_call_target="tpu_custom_call" | custom-call | tf_op jit(solution)/shard_map/pallas_call | solution.py:109
  27.2 6.3 %shard_map.84 = f32[4,2,64,512]{3,2,1,0:T(8,128)} custom-call(f32[8,128,128]{2,1,0:T(8,128)} %bitcast.298, f32[128,2048]{1,0:T(8,128)} %select_add_fusion.m_ref, f32[8,2048]{1,0:T(8,128)} %get-tuple-element.178.cos_ref, f32[8,2048]{1,0:T(8,128)} %get-tuple-element.177.sin_ref), custom_call_target="tpu_custom_call" | custom-call | tf_op jit(solution)/shard_map/pallas_call | solution.py:109
  37.0 6.3 %shard_map.82 = f32[4,2,64,512]{3,2,1,0:T(8,128)} custom-call(f32[8,128,128]{2,1,0:T(8,128)} %bitcast.299, f32[128,2048]{1,0:T(8,128)} %select_add_fusion.m_ref, f32[8,2048]{1,0:T(8,128)} %get-tuple-element.178.cos_ref, f32[8,2048]{1,0:T(8,128)} %get-tuple-element.177.sin_ref), custom_call_target="tpu_custom_call" | custom-call | tf_op jit(solution)/shard_map/pallas_call | solution.py:109
  45.1 2.0 %copy.32 = f32[128,8,512]{0,2,1:T(8,128)S(1)} copy(f32[128,8,512]{2,1,0:T(8,128)} %param.8) | data formatting | bytes 4194304 | tf_op args[0]
  47.8 3.2 %collective-permute-start = (f32[128,8,2]{0,2,1:T(2,128)}, f32[128,8,2]{0,2,1:T(2,128)S(1)}, u32[]{:S(2)}, u32[]{:S(2)}) collective-permute-start(f32[128,8,2]{0,2,1:T(2,128)} %get-tuple-element.18), channel_id=1, source_target_pairs={{0,4},{4,8},{8,12},{12,16},{16,20},{20,24},{24,28},{28,32},{32,36}... | collective-permute-start | bytes 24584 | tf_op jit(solution)/shard_map/ppermute | solution.py:17
  56.9 5.2 %collective-permute-start.1 = (f32[128,8,2]{0,2,1:T(2,128)S(1)}, f32[128,8,2]{0,2,1:T(2,128)S(1)}, u32[]{:S(2)}, u32[]{:S(2)}) collective-permute-start(f32[128,8,2]{0,2,1:T(2,128)S(1)} %get-tuple-element.17), channel_id=1, source_target_pairs={{4,0},{8,4},{12,8},{16,12},{20,16},{24,20},{28,24},{32,28},{36,32}... | collective-permute-start | bytes 24584 | tf_op jit(solution)/shard_map/ppermute | solution.py:20
  62.1 2.6 %multiply_subtract_fusion.2 = (f32[128,4,512]{0,2,1:T(8,128)S(1)}, f32[128,4,512]{0,2,1:T(8,128)}, f32[128,4,512]{0,2,1:T(8,128)}, f32[128,4,512]{0,2,1:T(8,128)}) fusion(f32[128]{0:T(128)} %get-tuple-element.186, f32[128]{0:T(128)} %get-tuple-element.187, f32[128,8,512]{0,2,1:T(8,128)S(1)} %copy.32, f32[128,8,2]{0,2,1:T(2,128)S(1)} %collective-permute-done, ...), kind=kLoop, calls=%fused_computation.287 | loop fusion | flops 4980736 | bytes 6301696 | tf_op jit(solution)/shard_map/sub | solution.py:75
  64.8 2.4 %multiply_subtract_fusion = (f32[128,4,512]{0,2,1:T(8,128)}, f32[128,4,512]{0,2,1:T(8,128)}, f32[128,4,512]{0,2,1:T(8,128)}, f32[128,4,512]{0,2,1:T(8,128)}) fusion(f32[128]{0:T(128)S(1)} %copy-done.24, f32[128]{0:T(128)S(1)} %copy-done.21, f32[128,8,2]{0,2,1:T(2,128)S(1)} %collective-permute-done.1, f32[128,8,512]{0,2,1:T(8,128)S(1)} %copy.32, ...), kind=kLoop, calls=%fused_computation.283 | loop fusion | flops 4980736 | bytes 6301696 | tf_op jit(solution)/shard_map/sub | solution.py:75
  75.5 1.9 collective-permute-start.22
  77.5 7.9 %collective-permute-start.23 = (f32[2,16,512]{2,1,0:T(8,128)S(1)}, f32[2,16,512]{2,1,0:T(8,128)S(1)}, u32[]{:S(2)}, u32[]{:S(2)}) collective-permute-start(f32[2,16,512]{2,1,0:T(8,128)S(1)} %get-tuple-element.47), channel_id=1, source_target_pairs={{4,0},{8,4},{12,8},{16,12},{20,16},{24,20},{28,24},{32,28},{36,32}... | collective-permute-start | bytes 196616 | tf_op jit(solution)/shard_map/ppermute | solution.py:20
  85.4 1.9 collective-permute-start.16
  87.4 7.9 %collective-permute-start.17 = (f32[2,16,512]{2,1,0:T(8,128)S(1)}, f32[2,16,512]{2,1,0:T(8,128)S(1)}, u32[]{:S(2)}, u32[]{:S(2)}) collective-permute-start(f32[2,16,512]{2,1,0:T(8,128)S(1)} %get-tuple-element.45), channel_id=1, source_target_pairs={{4,0},{8,4},{12,8},{16,12},{20,16},{24,20},{28,24},{32,28},{36,32}... | collective-permute-start | bytes 196616 | tf_op jit(solution)/shard_map/ppermute | solution.py:20
  97.3 7.9 %collective-permute-start.11 = (f32[2,16,512]{2,1,0:T(8,128)S(1)}, f32[2,16,512]{2,1,0:T(8,128)S(1)}, u32[]{:S(2)}, u32[]{:S(2)}) collective-permute-start(f32[2,16,512]{2,1,0:T(8,128)S(1)} %get-tuple-element.43), channel_id=1, source_target_pairs={{4,0},{8,4},{12,8},{16,12},{20,16},{24,20},{28,24},{32,28},{36,32}... | collective-permute-start | bytes 196616 | tf_op jit(solution)/shard_map/ppermute | solution.py:20
  107.1 2.3 %multiply_add_fusion.4 = f32[1,64,512]{2,1,0:T(8,128)S(1)} fusion(f32[512]{0:T(512)S(1)} %bitcast.408, f32[512]{0:T(512)S(1)} %bitcast.416, f32[64]{0:T(128)S(1)} %get-tuple-element.116, f32[512]{0:T(512)S(1)} %bitcast.536, f32[512]{0:T(512)S(1)} %bitcast.680, f32[64]{0:T(128)S(1)} %get-tuple-element.50, f32[512]{0:T(512)S(1)} %bitcast.544, ...), kind=kLoop, calls=%fused_computation.834 | loop fusion | flops 7307264 | bytes 663552 | tf_op jit(solution)/shard_map/add | solution.py:180
  109.4 2.3 %multiply_add_fusion.5 = f32[1,64,512]{2,1,0:T(8,128)S(1)} fusion(f32[512]{0:T(512)S(1)} %bitcast.409, f32[512]{0:T(512)S(1)} %bitcast.417, f32[64]{0:T(128)S(1)} %get-tuple-element.116, f32[512]{0:T(512)S(1)} %bitcast.537, f32[512]{0:T(512)S(1)} %bitcast.681, f32[64]{0:T(128)S(1)} %get-tuple-element.50, f32[512]{0:T(512)S(1)} %bitcast.545, ...), kind=kLoop, calls=%fused_computation.835 | loop fusion | flops 7307264 | bytes 663552 | tf_op jit(solution)/shard_map/add | solution.py:179
  111.7 7.9 %collective-permute-start.5 = (f32[2,16,512]{2,1,0:T(8,128)S(1)}, f32[2,16,512]{2,1,0:T(8,128)S(1)}, u32[]{:S(2)}, u32[]{:S(2)}) collective-permute-start(f32[2,16,512]{2,1,0:T(8,128)S(1)} %get-tuple-element.41), channel_id=1, source_target_pairs={{4,0},{8,4},{12,8},{16,12},{20,16},{24,20},{28,24},{32,28},{36,32}... | collective-permute-start | bytes 196616 | tf_op jit(solution)/shard_map/ppermute | solution.py:20
  120.9 2.0 %multiply_add_fusion.6 = f32[1,64,512]{2,1,0:T(8,128)S(1)} fusion(f32[512]{0:T(512)S(1)} %bitcast.410, f32[512]{0:T(512)S(1)} %bitcast.418, f32[64]{0:T(128)S(1)} %get-tuple-element.116, f32[512]{0:T(512)S(1)} %bitcast.538, f32[512]{0:T(512)S(1)} %bitcast.682, f32[64]{0:T(128)S(1)} %get-tuple-element.50, f32[512]{0:T(512)S(1)} %bitcast.546, ...), kind=kLoop, calls=%fused_computation.836 | loop fusion | flops 7307264 | bytes 663552 | tf_op jit(solution)/shard_map/add | solution.py:180
  122.9 2.3 %multiply_add_fusion.7 = f32[1,64,512]{2,1,0:T(8,128)S(1)} fusion(f32[512]{0:T(512)S(1)} %bitcast.411, f32[512]{0:T(512)S(1)} %bitcast.419, f32[64]{0:T(128)S(1)} %get-tuple-element.116, f32[512]{0:T(512)S(1)} %bitcast.539, f32[512]{0:T(512)S(1)} %bitcast.683, f32[64]{0:T(128)S(1)} %get-tuple-element.50, f32[512]{0:T(512)S(1)} %bitcast.547, ...), kind=kLoop, calls=%fused_computation.837 | loop fusion | flops 7307264 | bytes 663552 | tf_op jit(solution)/shard_map/add | solution.py:179
  125.6 2.0 %multiply_add_fusion.8 = f32[1,64,512]{2,1,0:T(8,128)S(1)} fusion(f32[512]{0:T(512)S(1)} %bitcast.412, f32[512]{0:T(512)S(1)} %bitcast.420, f32[64]{0:T(128)S(1)} %get-tuple-element.116, f32[512]{0:T(512)S(1)} %bitcast.540, f32[512]{0:T(512)S(1)} %bitcast.684, f32[64]{0:T(128)S(1)} %get-tuple-element.50, f32[512]{0:T(512)S(1)} %bitcast.548, ...), kind=kLoop, calls=%fused_computation.838 | loop fusion | flops 7307264 | bytes 663552 | tf_op jit(solution)/shard_map/add | solution.py:180
  127.6 2.3 %multiply_add_fusion.9 = f32[1,64,512]{2,1,0:T(8,128)S(1)} fusion(f32[512]{0:T(512)S(1)} %bitcast.413, f32[512]{0:T(512)S(1)} %bitcast.421, f32[64]{0:T(128)S(1)} %get-tuple-element.116, f32[512]{0:T(512)S(1)} %bitcast.541, f32[512]{0:T(512)S(1)} %bitcast.685, f32[64]{0:T(128)S(1)} %get-tuple-element.50, f32[512]{0:T(512)S(1)} %bitcast.549, ...), kind=kLoop, calls=%fused_computation.839 | loop fusion | flops 7307264 | bytes 663552 | tf_op jit(solution)/shard_map/add | solution.py:179
  131.4 2.0 %multiply_add_fusion.10 = f32[1,64,512]{2,1,0:T(8,128)S(1)} fusion(f32[512]{0:T(512)S(1)} %bitcast.414, f32[512]{0:T(512)S(1)} %bitcast.422, f32[64]{0:T(128)S(1)} %get-tuple-element.116, f32[512]{0:T(512)S(1)} %bitcast.542, f32[512]{0:T(512)S(1)} %bitcast.686, f32[64]{0:T(128)S(1)} %get-tuple-element.50, f32[512]{0:T(512)S(1)} %bitcast.550, ...), kind=kLoop, calls=%fused_computation.840 | loop fusion | flops 7307264 | bytes 663552 | tf_op jit(solution)/shard_map/add | solution.py:180
  133.5 2.3 %multiply_add_fusion.11 = f32[1,64,512]{2,1,0:T(8,128)S(1)} fusion(f32[512]{0:T(512)S(1)} %bitcast.415, f32[512]{0:T(512)S(1)} %bitcast.423, f32[64]{0:T(128)S(1)} %get-tuple-element.116, f32[512]{0:T(512)S(1)} %bitcast.543, f32[512]{0:T(512)S(1)} %bitcast.687, f32[64]{0:T(128)S(1)} %get-tuple-element.50, f32[512]{0:T(512)S(1)} %bitcast.551, ...), kind=kLoop, calls=%fused_computation.841 | loop fusion | flops 7307264 | bytes 663552 | tf_op jit(solution)/shard_map/add | solution.py:179
  136.2 6.7 %collective-permute-start.25 = (f32[2,2,64,512]{3,2,1,0:T(8,128)S(1)}, f32[2,2,64,512]{3,2,1,0:T(8,128)S(1)}, u32[]{:S(2)}, u32[]{:S(2)}) collective-permute-start(f32[2,2,64,512]{3,2,1,0:T(8,128)S(1)} %pad_maximum_fusion.9), channel_id=1, source_target_pairs={{0,1},{1,0},{2,3},{3,2},{4,5},{5,4},{6,7},{7,6},{8,9},{9,8},{10,11... | collective-permute-start | bytes 1572872 | tf_op jit(solution)/shard_map/ppermute | solution.py:45
  147.5 2.0 %collective-permute-start.7 = (f32[2,2,64,512]{3,2,1,0:T(8,128)}, f32[2,2,64,512]{3,2,1,0:T(8,128)}, u32[]{:S(2)}, u32[]{:S(2)}) collective-permute-start(f32[2,2,64,512]{3,2,1,0:T(8,128)} %pad_maximum_fusion.6), channel_id=1, source_target_pairs={{0,1},{1,0},{2,3},{3,2},{4,5},{5,4},{6,7},{7,6},{8,9},{9,8},{10,11... | collective-permute-start | bytes 1572872 | tf_op jit(solution)/shard_map/ppermute | solution.py:45
  150.7 7.4 %shard_map.89 = f32[8,128,128]{2,1,0:T(8,128)} custom-call(f32[4,2,64,512]{3,2,1,0:T(8,128)} %bitcast.289, f32[128,2048]{1,0:T(8,128)} %select_add_fusion.m_ref, f32[8,2048]{1,0:T(8,128)} %get-tuple-element.178.cos_ref, f32[8,2048]{1,0:T(8,128)} %get-tuple-element.177.sin_ref), custom_call_target="tpu_custom_call" | custom-call | tf_op jit(solution)/shard_map/pallas_call | solution.py:151
  161.6 7.4 %shard_map.87 = f32[8,128,128]{2,1,0:T(8,128)} custom-call(f32[4,2,64,512]{3,2,1,0:T(8,128)} %bitcast.290, f32[128,2048]{1,0:T(8,128)} %select_add_fusion.m_ref, f32[8,2048]{1,0:T(8,128)} %get-tuple-element.178.cos_ref, f32[8,2048]{1,0:T(8,128)} %get-tuple-element.177.sin_ref), custom_call_target="tpu_custom_call" | custom-call | tf_op jit(solution)/shard_map/pallas_call | solution.py:151
  172.6 7.4 %shard_map.85 = f32[8,128,128]{2,1,0:T(8,128)} custom-call(f32[4,2,64,512]{3,2,1,0:T(8,128)} %bitcast.291, f32[128,2048]{1,0:T(8,128)} %select_add_fusion.m_ref, f32[8,2048]{1,0:T(8,128)} %get-tuple-element.178.cos_ref, f32[8,2048]{1,0:T(8,128)} %get-tuple-element.177.sin_ref), custom_call_target="tpu_custom_call" | custom-call | tf_op jit(solution)/shard_map/pallas_call | solution.py:151
  183.5 7.4 %shard_map.83 = f32[8,128,128]{2,1,0:T(8,128)} custom-call(f32[4,2,64,512]{3,2,1,0:T(8,128)} %bitcast.288, f32[128,2048]{1,0:T(8,128)} %select_add_fusion.m_ref, f32[8,2048]{1,0:T(8,128)} %get-tuple-element.178.cos_ref, f32[8,2048]{1,0:T(8,128)} %get-tuple-element.177.sin_ref), custom_call_target="tpu_custom_call" | custom-call | tf_op jit(solution)/shard_map/pallas_call | solution.py:151
  196.6 2.0 copy.54
  (164 shorter events, 58.6 us)
Async XLA Ops:
  16.1 51.1 %collective-permute-start.20 = (f32[2,2,64,512]{3,2,1,0:T(8,128)}, f32[2,2,64,512]{3,2,1,0:T(8,128)}, u32[]{:S(2)}, u32[]{:S(2)}) collective-permute-start(f32[2,2,64,512]{3,2,1,0:T(8,128)} %dynamic-slice_bitcast_fusion), channel_id=1, source_target_pairs={{0,1},{1,0},{2,3},{3,2},{4,5},{5,4},{6,7},{7,6},{8,9},{9,8},{10,11... | collective-permute-start | bytes 1572872 | tf_op jit(solution)/shard_map/ppermute | solution.py:32
  26.0 43.8 %collective-permute-start.14 = (f32[2,2,64,512]{3,2,1,0:T(8,128)}, f32[2,2,64,512]{3,2,1,0:T(8,128)}, u32[]{:S(2)}, u32[]{:S(2)}) collective-permute-start(f32[2,2,64,512]{3,2,1,0:T(8,128)} %dynamic-slice_bitcast_fusion.1), channel_id=1, source_target_pairs={{0,1},{1,0},{2,3},{3,2},{4,5},{5,4},{6,7},{7,6},{8,9},{9,8},{10,11... | collective-permute-start | bytes 1572872 | tf_op jit(solution)/shard_map/ppermute | solution.py:32
  35.3 36.0 %collective-permute-start.8 = (f32[2,2,64,512]{3,2,1,0:T(8,128)}, f32[2,2,64,512]{3,2,1,0:T(8,128)}, u32[]{:S(2)}, u32[]{:S(2)}) collective-permute-start(f32[2,2,64,512]{3,2,1,0:T(8,128)} %dynamic-slice_bitcast_fusion.2), channel_id=1, source_target_pairs={{0,1},{1,0},{2,3},{3,2},{4,5},{5,4},{6,7},{7,6},{8,9},{9,8},{10,11... | collective-permute-start | bytes 1572872 | tf_op jit(solution)/shard_map/ppermute | solution.py:32
  45.1 5.9 %copy-start.11 = (f32[2,32,2048]{2,1,0:T(8,128)S(1)}, f32[2,32,2048]{2,1,0:T(8,128)}, u32[]{:S(2)}) copy-start(f32[2,32,2048]{2,1,0:T(8,128)} %param.14) | copy-start | bytes 1572868
  45.1 6.3 %copy-start.20 = (f32[2,4,128]{2,1,0:T(4,128)S(1)}, f32[2,4,128]{2,1,0:T(4,128)}, u32[]{:S(2)}) copy-start(f32[2,4,128]{2,1,0:T(4,128)} %param.9) | copy-start | bytes 12292
  45.1 6.9 %copy-start.15 = (s32[4,512]{1,0:T(4,128)S(1)}, s32[4,512]{1,0:T(4,128)}, u32[]{:S(2)}) copy-start(s32[4,512]{1,0:T(4,128)} %param.10) | copy-start | bytes 24580
  45.1 28.6 %collective-permute-start.2 = (f32[2,2,64,512]{3,2,1,0:T(8,128)}, f32[2,2,64,512]{3,2,1,0:T(8,128)}, u32[]{:S(2)}, u32[]{:S(2)}) collective-permute-start(f32[2,2,64,512]{3,2,1,0:T(8,128)} %dynamic-slice_bitcast_fusion.3), channel_id=1, source_target_pairs={{0,1},{1,0},{2,3},{3,2},{4,5},{5,4},{6,7},{7,6},{8,9},{9,8},{10,11... | collective-permute-start | bytes 1572872 | tf_op jit(solution)/shard_map/ppermute | solution.py:32
  47.8 9.1 %collective-permute-start = (f32[128,8,2]{0,2,1:T(2,128)}, f32[128,8,2]{0,2,1:T(2,128)S(1)}, u32[]{:S(2)}, u32[]{:S(2)}) collective-permute-start(f32[128,8,2]{0,2,1:T(2,128)} %get-tuple-element.18), channel_id=1, source_target_pairs={{0,4},{4,8},{8,12},{12,16},{16,20},{20,24},{24,28},{28,32},{32,36}... | collective-permute-start | bytes 24584 | tf_op jit(solution)/shard_map/ppermute | solution.py:17
  56.9 7.9 %collective-permute-start.1 = (f32[128,8,2]{0,2,1:T(2,128)S(1)}, f32[128,8,2]{0,2,1:T(2,128)S(1)}, u32[]{:S(2)}, u32[]{:S(2)}) collective-permute-start(f32[128,8,2]{0,2,1:T(2,128)S(1)} %get-tuple-element.17), channel_id=1, source_target_pairs={{4,0},{8,4},{12,8},{16,12},{20,16},{24,20},{28,24},{32,28},{36,32}... | collective-permute-start | bytes 24584 | tf_op jit(solution)/shard_map/ppermute | solution.py:20
  67.2 4.1 %copy-start = (f32[4,2,64,512]{3,2,1,0:T(8,128)S(1)}, f32[4,2,64,512]{3,2,1,0:T(8,128)}, u32[]{:S(2)}) copy-start(f32[4,2,64,512]{3,2,1,0:T(8,128)} %shard_map.84) | copy-start | bytes 3145732
  68.5 5.3 %copy-start.1 = (f32[4,2,64,512]{3,2,1,0:T(8,128)S(1)}, f32[4,2,64,512]{3,2,1,0:T(8,128)}, u32[]{:S(2)}) copy-start(f32[4,2,64,512]{3,2,1,0:T(8,128)} %shard_map.82) | copy-start | bytes 3145732
  68.5 6.9 %collective-permute-start.21 = (f32[2,64,512]{2,1,0:T(8,128)S(1)}, f32[2,64,512]{2,1,0:T(8,128)S(1)}, u32[]{:S(2)}, u32[]{:S(2)}) collective-permute-start(f32[2,64,512]{2,1,0:T(8,128)S(1)} %dynamic-slice_bitcast_fusion.4), channel_id=1, source_target_pairs={{0,2},{2,0},{1,3},{3,1},{4,6},{6,4},{5,7},{7,5},{8,10},{10,8},{9,1... | collective-permute-start | bytes 786440 | tf_op jit(solution)/shard_map/ppermute | solution.py:35
  71.0 14.4 %collective-permute-start.15 = (f32[2,64,512]{2,1,0:T(8,128)S(1)}, f32[2,64,512]{2,1,0:T(8,128)S(1)}, u32[]{:S(2)}, u32[]{:S(2)}) collective-permute-start(f32[2,64,512]{2,1,0:T(8,128)S(1)} %dynamic-slice_bitcast_fusion.5), channel_id=1, source_target_pairs={{0,2},{2,0},{1,3},{3,1},{4,6},{6,4},{5,7},{7,5},{8,10},{10,8},{9,1... | collective-permute-start | bytes 786440 | tf_op jit(solution)/shard_map/ppermute | solution.py:35
  72.5 14.9 %collective-permute-start.9 = (f32[2,64,512]{2,1,0:T(8,128)S(1)}, f32[2,64,512]{2,1,0:T(8,128)S(1)}, u32[]{:S(2)}, u32[]{:S(2)}) collective-permute-start(f32[2,64,512]{2,1,0:T(8,128)S(1)} %dynamic-slice_bitcast_fusion.6), channel_id=1, source_target_pairs={{0,2},{2,0},{1,3},{3,1},{4,6},{6,4},{5,7},{7,5},{8,10},{10,8},{9,1... | collective-permute-start | bytes 786440 | tf_op jit(solution)/shard_map/ppermute | solution.py:35
  74.9 20.4 %collective-permute-start.3 = (f32[2,64,512]{2,1,0:T(8,128)S(1)}, f32[2,64,512]{2,1,0:T(8,128)S(1)}, u32[]{:S(2)}, u32[]{:S(2)}) collective-permute-start(f32[2,64,512]{2,1,0:T(8,128)S(1)} %dynamic-slice_bitcast_fusion.7), channel_id=1, source_target_pairs={{0,2},{2,0},{1,3},{3,1},{4,6},{6,4},{5,7},{7,5},{8,10},{10,8},{9,1... | collective-permute-start | bytes 786440 | tf_op jit(solution)/shard_map/ppermute | solution.py:35
  75.5 21.8 %collective-permute-start.22 = (f32[2,16,512]{2,1,0:T(8,128)S(1)}, f32[2,16,512]{2,1,0:T(8,128)S(1)}, u32[]{:S(2)}, u32[]{:S(2)}) collective-permute-start(f32[2,16,512]{2,1,0:T(8,128)S(1)} %get-tuple-element.48), channel_id=1, source_target_pairs={{0,4},{4,8},{8,12},{12,16},{16,20},{20,24},{24,28},{28,32},{32,36}... | collective-permute-start | bytes 196616 | tf_op jit(solution)/shard_map/ppermute | solution.py:17
  77.5 27.7 %collective-permute-start.23 = (f32[2,16,512]{2,1,0:T(8,128)S(1)}, f32[2,16,512]{2,1,0:T(8,128)S(1)}, u32[]{:S(2)}, u32[]{:S(2)}) collective-permute-start(f32[2,16,512]{2,1,0:T(8,128)S(1)} %get-tuple-element.47), channel_id=1, source_target_pairs={{4,0},{8,4},{12,8},{16,12},{20,16},{24,20},{28,24},{32,28},{36,32}... | collective-permute-start | bytes 196616 | tf_op jit(solution)/shard_map/ppermute | solution.py:20
  85.4 26.3 %collective-permute-start.16 = (f32[2,16,512]{2,1,0:T(8,128)S(1)}, f32[2,16,512]{2,1,0:T(8,128)S(1)}, u32[]{:S(2)}, u32[]{:S(2)}) collective-permute-start(f32[2,16,512]{2,1,0:T(8,128)S(1)} %get-tuple-element.46), channel_id=1, source_target_pairs={{0,4},{4,8},{8,12},{12,16},{16,20},{20,24},{24,28},{28,32},{32,36}... | collective-permute-start | bytes 196616 | tf_op jit(solution)/shard_map/ppermute | solution.py:17
  87.4 32.2 %collective-permute-start.17 = (f32[2,16,512]{2,1,0:T(8,128)S(1)}, f32[2,16,512]{2,1,0:T(8,128)S(1)}, u32[]{:S(2)}, u32[]{:S(2)}) collective-permute-start(f32[2,16,512]{2,1,0:T(8,128)S(1)} %get-tuple-element.45), channel_id=1, source_target_pairs={{4,0},{8,4},{12,8},{16,12},{20,16},{24,20},{28,24},{32,28},{36,32}... | collective-permute-start | bytes 196616 | tf_op jit(solution)/shard_map/ppermute | solution.py:20
  95.3 29.9 %collective-permute-start.10 = (f32[2,16,512]{2,1,0:T(8,128)S(1)}, f32[2,16,512]{2,1,0:T(8,128)S(1)}, u32[]{:S(2)}, u32[]{:S(2)}) collective-permute-start(f32[2,16,512]{2,1,0:T(8,128)S(1)} %get-tuple-element.44), channel_id=1, source_target_pairs={{0,4},{4,8},{8,12},{12,16},{16,20},{20,24},{24,28},{28,32},{32,36}... | collective-permute-start | bytes 196616 | tf_op jit(solution)/shard_map/ppermute | solution.py:17
  97.3 28.3 %collective-permute-start.11 = (f32[2,16,512]{2,1,0:T(8,128)S(1)}, f32[2,16,512]{2,1,0:T(8,128)S(1)}, u32[]{:S(2)}, u32[]{:S(2)}) collective-permute-start(f32[2,16,512]{2,1,0:T(8,128)S(1)} %get-tuple-element.43), channel_id=1, source_target_pairs={{4,0},{8,4},{12,8},{16,12},{20,16},{24,20},{28,24},{32,28},{36,32}... | collective-permute-start | bytes 196616 | tf_op jit(solution)/shard_map/ppermute | solution.py:20
  105.2 26.2 %collective-permute-start.4 = (f32[2,16,512]{2,1,0:T(8,128)S(1)}, f32[2,16,512]{2,1,0:T(8,128)S(1)}, u32[]{:S(2)}, u32[]{:S(2)}) collective-permute-start(f32[2,16,512]{2,1,0:T(8,128)S(1)} %get-tuple-element.42), channel_id=1, source_target_pairs={{0,4},{4,8},{8,12},{12,16},{16,20},{20,24},{24,28},{28,32},{32,36}... | collective-permute-start | bytes 196616 | tf_op jit(solution)/shard_map/ppermute | solution.py:17
  111.7 19.7 %collective-permute-start.5 = (f32[2,16,512]{2,1,0:T(8,128)S(1)}, f32[2,16,512]{2,1,0:T(8,128)S(1)}, u32[]{:S(2)}, u32[]{:S(2)}) collective-permute-start(f32[2,16,512]{2,1,0:T(8,128)S(1)} %get-tuple-element.41), channel_id=1, source_target_pairs={{4,0},{8,4},{12,8},{16,12},{20,16},{24,20},{28,24},{32,28},{36,32}... | collective-permute-start | bytes 196616 | tf_op jit(solution)/shard_map/ppermute | solution.py:20
  119.6 16.5 %collective-permute-start.24 = (f32[2,64,512]{2,1,0:T(8,128)S(1)}, f32[2,64,512]{2,1,0:T(8,128)S(1)}, u32[]{:S(2)}, u32[]{:S(2)}) collective-permute-start(f32[2,64,512]{2,1,0:T(8,128)S(1)} %pad_maximum_fusion.13), channel_id=1, source_target_pairs={{0,2},{2,0},{1,3},{3,1},{4,6},{6,4},{5,7},{7,5},{8,10},{10,8},{9,1... | collective-permute-start | bytes 786440 | tf_op jit(solution)/shard_map/ppermute | solution.py:42
  125.2 17.7 %collective-permute-start.18 = (f32[2,64,512]{2,1,0:T(8,128)S(1)}, f32[2,64,512]{2,1,0:T(8,128)S(1)}, u32[]{:S(2)}, u32[]{:S(2)}) collective-permute-start(f32[2,64,512]{2,1,0:T(8,128)S(1)} %pad_maximum_fusion.12), channel_id=1, source_target_pairs={{0,2},{2,0},{1,3},{3,1},{4,6},{6,4},{5,7},{7,5},{8,10},{10,8},{9,1... | collective-permute-start | bytes 786440 | tf_op jit(solution)/shard_map/ppermute | solution.py:42
  129.9 14.0 %collective-permute-start.12 = (f32[2,64,512]{2,1,0:T(8,128)S(1)}, f32[2,64,512]{2,1,0:T(8,128)S(1)}, u32[]{:S(2)}, u32[]{:S(2)}) collective-permute-start(f32[2,64,512]{2,1,0:T(8,128)S(1)} %pad_maximum_fusion.11), channel_id=1, source_target_pairs={{0,2},{2,0},{1,3},{3,1},{4,6},{6,4},{5,7},{7,5},{8,10},{10,8},{9,1... | collective-permute-start | bytes 786440 | tf_op jit(solution)/shard_map/ppermute | solution.py:42
  135.8 10.8 %collective-permute-start.6 = (f32[2,64,512]{2,1,0:T(8,128)S(1)}, f32[2,64,512]{2,1,0:T(8,128)S(1)}, u32[]{:S(2)}, u32[]{:S(2)}) collective-permute-start(f32[2,64,512]{2,1,0:T(8,128)S(1)} %pad_maximum_fusion.10), channel_id=1, source_target_pairs={{0,2},{2,0},{1,3},{3,1},{4,6},{6,4},{5,7},{7,5},{8,10},{10,8},{9,1... | collective-permute-start | bytes 786440 | tf_op jit(solution)/shard_map/ppermute | solution.py:42
  136.2 13.3 %collective-permute-start.25 = (f32[2,2,64,512]{3,2,1,0:T(8,128)S(1)}, f32[2,2,64,512]{3,2,1,0:T(8,128)S(1)}, u32[]{:S(2)}, u32[]{:S(2)}) collective-permute-start(f32[2,2,64,512]{3,2,1,0:T(8,128)S(1)} %pad_maximum_fusion.9), channel_id=1, source_target_pairs={{0,1},{1,0},{2,3},{3,2},{4,5},{5,4},{6,7},{7,6},{8,9},{9,8},{10,11... | collective-permute-start | bytes 1572872 | tf_op jit(solution)/shard_map/ppermute | solution.py:45
  143.9 15.5 %collective-permute-start.19 = (f32[2,2,64,512]{3,2,1,0:T(8,128)}, f32[2,2,64,512]{3,2,1,0:T(8,128)}, u32[]{:S(2)}, u32[]{:S(2)}) collective-permute-start(f32[2,2,64,512]{3,2,1,0:T(8,128)} %pad_maximum_fusion.8), channel_id=1, source_target_pairs={{0,1},{1,0},{2,3},{3,2},{4,5},{5,4},{6,7},{7,6},{8,9},{9,8},{10,11... | collective-permute-start | bytes 1572872 | tf_op jit(solution)/shard_map/ppermute | solution.py:45
  144.8 25.5 %collective-permute-start.13 = (f32[2,2,64,512]{3,2,1,0:T(8,128)}, f32[2,2,64,512]{3,2,1,0:T(8,128)}, u32[]{:S(2)}, u32[]{:S(2)}) collective-permute-start(f32[2,2,64,512]{3,2,1,0:T(8,128)} %pad_maximum_fusion.7), channel_id=1, source_target_pairs={{0,1},{1,0},{2,3},{3,2},{4,5},{5,4},{6,7},{7,6},{8,9},{9,8},{10,11... | collective-permute-start | bytes 1572872 | tf_op jit(solution)/shard_map/ppermute | solution.py:45
  147.5 33.7 %collective-permute-start.7 = (f32[2,2,64,512]{3,2,1,0:T(8,128)}, f32[2,2,64,512]{3,2,1,0:T(8,128)}, u32[]{:S(2)}, u32[]{:S(2)}) collective-permute-start(f32[2,2,64,512]{3,2,1,0:T(8,128)} %pad_maximum_fusion.6), channel_id=1, source_target_pairs={{0,1},{1,0},{2,3},{3,2},{4,5},{5,4},{6,7},{7,6},{8,9},{9,8},{10,11... | collective-permute-start | bytes 1572872 | tf_op jit(solution)/shard_map/ppermute | solution.py:45
  192.5 2.9 %copy-start.7 = (f32[128,4,512]{0,2,1:T(8,128)S(1)}, f32[128,4,512]{0,2,1:T(8,128)}, u32[]{:S(2)}) copy-start(f32[128,4,512]{0,2,1:T(8,128)} %get-tuple-element.5) | copy-start | bytes 3145732
  (19 other events, 42.6 us)

commit v5 on v1

--- a/solution.py
+++ b/solution.py
@@ -5,8 +5,7 @@
 from jax.experimental.pallas import tpu as pltpu
 from jax.sharding import PartitionSpec as P
 
-HIGHEST = lax.Precision.HIGHEST
-CHUNKS = 2
+HIGHEST = lax.Precision.HIGH
 
 
 def with_halo(block, sides, width):
@@ -20,6 +19,35 @@
         high = lax.ppermute(lax.slice_in_dim(block, 0, width, axis=dim), axis, backward)
         block = jnp.concatenate([low, block, high], axis=dim)
     return block
+
+
+CORE_SWAP = [(0, 1), (1, 0), (2, 3), (3, 2)]
+ROW_SWAP = [(0, 2), (2, 0), (1, 3), (3, 1)]
+
+
+def reduce_cores(field):
+    core = lax.axis_index("dir") % 2
+    pairs = field.reshape((2, 2) + field.shape[1:])
+    keep = lax.dynamic_index_in_dim(pairs, core, 1, keepdims=False)
+    send = lax.dynamic_index_in_dim(pairs, 1 - core, 1, keepdims=False)
+    return keep + lax.ppermute(send, "dir", CORE_SWAP)
+
+
+def split_rows(acc):
+    row = lax.axis_index("dir") // 2
+    keep = lax.dynamic_index_in_dim(acc, row, 0, keepdims=False)
+    send = lax.dynamic_index_in_dim(acc, 1 - row, 0, keepdims=False)
+    return keep, send
+
+
+def gather_cores(local, other):
+    rank = lax.axis_index("dir")
+    first = rank // 2 == 0
+    pair = jnp.stack([jnp.where(first, local, other), jnp.where(first, other, local)], axis=0)
+    mate = lax.ppermute(pair, "dir", CORE_SWAP)
+    low = rank % 2 == 0
+    quad = jnp.stack([jnp.where(low, pair, mate), jnp.where(low, mate, pair)], axis=1)
+    return quad.reshape((4,) + local.shape)
 
 
 def interp_matrix(index, weight, first_row, row_count):
@@ -190,19 +218,41 @@
     own_imag = lax.dynamic_slice_in_dim(parent_coef[1], parent_first, parent_dev, 1)
     own_mask = lax.dynamic_slice_in_dim(parent_mask, box_rank * slots, slots, 1)
     rhs = comps // 2
-    step = rhs // CHUNKS
-    fars = []
-    for chunk in range(CHUNKS):
+    step = rhs // 2
+
+    def chunk_xt(chunk):
         part = pattern.reshape(child_dev, 2, rhs, box_dev)[:, :, chunk * step : (chunk + 1) * step]
         xt = part.reshape(child_dev, 2 * step, slots, groups).transpose(3, 1, 2, 0)
-        xt = xt.reshape(groups, 2 * step * slots, child_dev)
-        field = upward(xt, rows, cosine, sine, dir_size, 2 * step)
-        field = lax.psum_scatter(field, "dir", scatter_dimension=0, tiled=True)[0]
+        return xt.reshape(groups, 2 * step * slots, child_dev)
+
+    def translate(field):
         padded = with_halo(field, (("box", 1),), parent_reach)
-        local = parent_translate(padded, own_real, own_imag, own_mask, parent_reach)
-        local_all = lax.all_gather(local, "dir", axis=0, tiled=False)
-        far = downward(local_all, rows, cosine, sine)
-        fars.append(far.reshape(groups, child_dev, 2, step, slots))
+        return parent_translate(padded, own_real, own_imag, own_mask, parent_reach)
+
+    acc_a = reduce_cores(upward(chunk_xt(0), rows, cosine, sine, dir_size, 2 * step))
+    acc_a, xt_b = lax.optimization_barrier((acc_a, chunk_xt(1)))
+    keep_a, send_a = split_rows(acc_a)
+    recv_a = lax.ppermute(send_a, "dir", ROW_SWAP)
+    field_b = upward(xt_b, rows, cosine, sine, dir_size, 2 * step)
+    field_b, recv_a = lax.optimization_barrier((field_b, recv_a))
+    sum_a = keep_a + recv_a
+    acc_b = reduce_cores(field_b)
+    sum_a, acc_b = lax.optimization_barrier((sum_a, acc_b))
+    keep_b, send_b = split_rows(acc_b)
+    recv_b = lax.ppermute(send_b, "dir", ROW_SWAP)
+    local_a = translate(sum_a)
+    local_a, recv_b = lax.optimization_barrier((local_a, recv_b))
+    sum_b = keep_b + recv_b
+    other_a = lax.ppermute(local_a, "dir", ROW_SWAP)
+    local_b = translate(sum_b)
+    other_a, local_b = lax.optimization_barrier((other_a, local_b))
+    all_a = gather_cores(local_a, other_a)
+    all_a, local_b = lax.optimization_barrier((all_a, local_b))
+    other_b = lax.ppermute(local_b, "dir", ROW_SWAP)
+    far_a = downward(all_a, rows, cosine, sine)
+    far_a, other_b = lax.optimization_barrier((far_a, other_b))
+    far_b = downward(gather_cores(local_b, other_b), rows, cosine, sine)
+    fars = [far.reshape(groups, child_dev, 2, step, slots) for far in (far_a, far_b)]
     far = jnp.concatenate(fars, axis=3).transpose(1, 2, 3, 4, 0)
     far = far.reshape(child_dev, comps, box_dev)
     return child_local + far

time: 208 us -> 169 us (0.81)
  the two profiles are of different devices: /device:TPU:28 before, /device:TPU:65 now
where the time goes in v5:
time: 169 us; the launch traced here: 168 us
  other arithmetic  47.1 us (28%)
  Pallas kernels  45.5 us (27%)
  starting transfers between devices  40.6 us (24%)
  local copies, waits for them, and re-layouts  22.9 us (14%)
  waiting for transfers between devices  11.2 us (7%)
    pallas_call x2, Pallas kernels, downward(): pl.pallas_call(downward_kernel, grid=(groups,), in_specs=[pl.BlockSpec((p...  25 us
    ppermute x3, starting transfers between devices, with_halo(): lax.ppermute(lax.slice_in_dim(block, 0, width, axis=dim), axis, backward)  23.7 us
    pallas_call x2, Pallas kernels, upward(): pl.pallas_call(upward_kernel, grid=(parts,), in_specs=[pl.BlockSpec((grou...  20.5 us
    add x2, other arithmetic, parent_translate(): re_sum = re_sum + weight * (cr * re - ci * im)  11 us
    add x2, other arithmetic, parent_translate(): im_sum = im_sum + weight * (cr * im + ci * re)  10.7 us
    ppermute x3, starting transfers between devices, with_halo(): lax.ppermute(lax.slice_in_dim(block, block.shape[dim] - width, None, axis...  7.03 us
    another operation x4, other arithmetic, gather_cores(): jnp.stack([jnp.where(low, pair, mate), jnp.where(low, mate, pair)], axis=1)  4.74 us
    another operation x4, other arithmetic, gather_cores(): jnp.stack([jnp.where(first, local, other), jnp.where(first, other, local)...  4.67 us
  transfers between devices with their start and end apart: 14, of which 7 were waited for; matrix products, arithmetic and copies ran while one was open for 23% of the time, Pallas kernels for 14%

profile of v5, /device:TPU:65, one launch (start us, length us, event | category | flops | bytes accessed | tf_op | source)
XLA Modules:
  0.0 168.4 jit_solution(81600760544213466)
XLA Ops:
  0.0 2.0 %copy.12 = f32[128,8,512]{0,2,1:T(8,128)S(1)} copy(f32[128,8,512]{2,1,0:T(8,128)} %param.8) | data formatting | bytes 4194304 | tf_op args[0]
  4.5 2.6 %select_add_fusion.m_ref = f32[128,2048]{1,0:T(8,128)} fusion(f32[2048]{0:T(1024)S(1)} %bitcast.432, s32[2048]{0:T(1024)S(1)} %bitcast.448, f32[2048]{0:T(1024)S(1)} %bitcast.433, s32[2048]{0:T(1024)S(1)} %bitcast.449, f32[2048]{0:T(1024)S(1)} %bitcast.419, s32[2048]{0:T(1024)S(1)} %bitcast.435, f32[2048]{0:T(1024)S(1)} %bitcast.420, ...), kind=kLoop, calls=%fused_computation.165 | loop fusion | flops 12320768 | bytes 1311232 | tf_op jit(solution)/shard_map/add | solution.py:57
  7.1 10.2 %shard_map.82 = f32[4,4,64,512]{3,2,1,0:T(8,128)} custom-call(f32[8,256,128]{2,1,0:T(8,128)} %bitcast.242, f32[128,2048]{1,0:T(8,128)} %select_add_fusion.m_ref, f32[8,2048]{1,0:T(8,128)} %get-tuple-element.194.cos_ref, f32[8,2048]{1,0:T(8,128)} %get-tuple-element.193.sin_ref), custom_call_target="tpu_custom_call" | custom-call | tf_op jit(solution)/shard_map/pallas_call | solution.py:111
  17.3 2.2 %dynamic-slice_bitcast_fusion.1 = f32[2,4,64,512]{3,2,1,0:T(8,128)} fusion(f32[2,2,4,64,512]{4,3,2,1,0:T(8,128)} %bitcast.235, s32[]{:T(128)S(6)} %select_n.157), kind=kLoop, calls=%fused_computation.164 | loop fusion | bytes 2097156 | tf_op jit(solution)/shard_map/jit(dynamic_index_in_dim)/squeeze | solution.py:32
  22.9 1.8 %bitcast_add_fusion.1 = f32[2,4,64,512]{3,2,1,0:T(8,128)S(1)} fusion(f32[2,4,64,512]{3,2,1,0:T(8,128)} %collective-permute-done.2, f32[2,2,4,64,512]{4,3,2,1,0:T(8,128)} %bitcast.236, s32[]{:T(128)S(6)} %select_n.156), kind=kLoop, calls=%fused_computation.158 | loop fusion | flops 262144 | bytes 3145732 | tf_op jit(solution)/shard_map/add | solution.py:33
  26.7 1.7 %fusion.73 = (f32[64]{0:T(128)}, f32[64]{0:T(128)}, f32[64]{0:T(128)}, f32[64]{0:T(128)}, f32[64]{0:T(128)}, /*index=5*/f32[64]{0:T(128)}, f32[64]{0:T(128)}, f3...) fusion(s32[32,2048]{1,0:T(8,128)} %param.15, ...), kind=kLoop, calls=%fused_computation.326 | loop fusion | flops 1152 | bytes 9288 | tf_op jit(solution)/shard_map/convert_element_type | solution.py:180
  28.5 10.3 %shard_map.83 = f32[4,4,64,512]{3,2,1,0:T(8,128)} custom-call(f32[8,256,128]{2,1,0:T(8,128)} %bitcast.240, f32[128,2048]{1,0:T(8,128)} %select_add_fusion.m_ref, f32[8,2048]{1,0:T(8,128)} %get-tuple-element.194.cos_ref, f32[8,2048]{1,0:T(8,128)} %get-tuple-element.193.sin_ref), custom_call_target="tpu_custom_call" | custom-call | tf_op jit(solution)/shard_map/pallas_call | solution.py:111
  45.4 3.2 %collective-permute-start.5 = (f32[4,16,512]{2,1,0:T(8,128)S(1)}, f32[4,16,512]{2,1,0:T(8,128)S(1)}, u32[]{:S(2)}, u32[]{:S(2)}) collective-permute-start(f32[4,16,512]{2,1,0:T(8,128)S(1)} %get-tuple-element.63), channel_id=1, source_target_pairs={{0,4},{4,8},{8,12},{12,16},{16,20},{20,24},{24,28},{28,32},{32,36}... | collective-permute-start | bytes 393224 | tf_op jit(solution)/shard_map/ppermute | solution.py:16
  48.6 1.7 %fusion.104 = (f32[64]{0:T(128)}, f32[64]{0:T(128)}, f32[64]{0:T(128)}, f32[64]{0:T(128)}, f32[64]{0:T(128)}, /*index=5*/f32[64]{0:T(128)}, f32[64]{0:T(128)}, f...) fusion(s32[32,2048]{1,0:T(8,128)} %param.15, ...), kind=kLoop, calls=%fused_computation.388 | loop fusion | flops 896 | bytes 7228 | tf_op jit(solution)/shard_map/convert_element_type | solution.py:180
  50.3 6.6 %collective-permute-start.6 = (f32[4,16,512]{2,1,0:T(8,128)S(1)}, f32[4,16,512]{2,1,0:T(8,128)S(1)}, u32[]{:S(2)}, u32[]{:S(2)}) collective-permute-start(f32[4,16,512]{2,1,0:T(8,128)S(1)} %get-tuple-element.64), channel_id=1, source_target_pairs={{4,0},{8,4},{12,8},{16,12},{20,16},{24,20},{28,24},{32,28},{36,32}... | collective-permute-start | bytes 393224 | tf_op jit(solution)/shard_map/ppermute | solution.py:19
  57.0 1.5 collective-permute-start.7
  59.5 4.1 %multiply_add_fusion.6 = f32[2,64,512]{2,1,0:T(8,128)S(1)} fusion(f32[4,80,512]{2,1,0:T(8,128)S(1)} %constant_dynamic-update-slice_fusion.2, f32[4,80,512]{2,1,0:T(8,128)S(1)} %get-tuple-element.61, f32[512]{0:T(512)S(1)} %bitcast.298, f32[512]{0:T(512)S(1)} %bitcast.302, f32[64]{0:T(128)} %get-tuple-element.132, f32[512]{0:T(512)S(1)} %bitcast.362, ...), kind=kLoop, calls=%fused_computation.250 | loop fusion | flops 10420224 | bytes 17178624 | tf_op jit(solution)/shard_map/add | solution.py:182
  64.0 4.1 %multiply_add_fusion.7 = f32[2,64,512]{2,1,0:T(8,128)S(1)} fusion(f32[4,80,512]{2,1,0:T(8,128)S(1)} %constant_dynamic-update-slice_fusion.2, f32[4,80,512]{2,1,0:T(8,128)S(1)} %get-tuple-element.61, f32[512]{0:T(512)S(1)} %bitcast.299, f32[512]{0:T(512)S(1)} %bitcast.303, f32[64]{0:T(128)} %get-tuple-element.132, f32[512]{0:T(512)S(1)} %bitcast.363, ...), kind=kLoop, calls=%fused_computation.251 | loop fusion | flops 10420224 | bytes 17178624 | tf_op jit(solution)/shard_map/add | solution.py:181
  68.2 4.5 %collective-permute-done.7 = f32[4,64,512]{2,1,0:T(8,128)S(1)} collective-permute-done((f32[4,64,512]{2,1,0:T(8,128)S(1)}, f32[4,64,512]{2,1,0:T(8,128)S(1)}, u32[]{:S(2)}, u32[]{:S(2)}) %collective-permute-start.7) | collective-permute-done | bytes 524320 | tf_op jit(solution)/shard_map/ppermute | solution.py:242
  73.4 1.9 %collective-permute-start.9 = (f32[4,16,512]{2,1,0:T(8,128)}, f32[4,16,512]{2,1,0:T(8,128)S(1)}, u32[]{:S(2)}, u32[]{:S(2)}) collective-permute-start(f32[4,16,512]{2,1,0:T(8,128)} %get-tuple-element.58), channel_id=1, source_target_pairs={{0,4},{4,8},{8,12},{12,16},{16,20},{20,24},{24,28},{28,32},{32,36}... | collective-permute-start | bytes 393224 | tf_op jit(solution)/shard_map/ppermute | solution.py:16
  75.3 7.9 %collective-permute-start.10 = (f32[4,16,512]{2,1,0:T(8,128)S(1)}, f32[4,16,512]{2,1,0:T(8,128)S(1)}, u32[]{:S(2)}, u32[]{:S(2)}) collective-permute-start(f32[4,16,512]{2,1,0:T(8,128)S(1)} %get-tuple-element.57), channel_id=1, source_target_pairs={{4,0},{8,4},{12,8},{16,12},{20,16},{24,20},{28,24},{32,28},{36,32}... | collective-permute-start | bytes 393224 | tf_op jit(solution)/shard_map/ppermute | solution.py:19
  85.1 6.6 %multiply_add_fusion.4 = f32[2,64,512]{2,1,0:T(8,128)S(1)} fusion(f32[512]{0:T(512)} %bitcast.300, f32[512]{0:T(512)} %bitcast.304, f32[64]{0:T(128)} %get-tuple-element.132, f32[512]{0:T(512)} %bitcast.364, f32[512]{0:T(512)} %bitcast.150, f32[64]{0:T(128)} %get-tuple-element.66, f32[512]{0:T(512)} %bitcast.368, f32[512]{0:T(512)} %bitcast.147, ...), kind=kLoop, calls=%fused_computation.248 | loop fusion | flops 14614528 | bytes 1187840 | tf_op jit(solution)/shard_map/add | solution.py:182
  91.7 6.9 %multiply_add_fusion.5 = f32[2,64,512]{2,1,0:T(8,128)S(1)} fusion(f32[512]{0:T(512)} %bitcast.301, f32[512]{0:T(512)} %bitcast.305, f32[64]{0:T(128)} %get-tuple-element.132, f32[512]{0:T(512)} %bitcast.365, f32[512]{0:T(512)} %bitcast.150, f32[64]{0:T(128)} %get-tuple-element.66, f32[512]{0:T(512)} %bitcast.369, f32[512]{0:T(512)} %bitcast.147, ...), kind=kLoop, calls=%fused_computation.249 | loop fusion | flops 14614528 | bytes 1187840 | tf_op jit(solution)/shard_map/add | solution.py:181
  101.6 3.7 %collective-permute-start.11 = (f32[2,4,64,512]{3,2,1,0:T(8,128)}, f32[2,4,64,512]{3,2,1,0:T(8,128)}, u32[]{:S(2)}, u32[]{:S(2)}) collective-permute-start(f32[2,4,64,512]{3,2,1,0:T(8,128)} %pad_maximum_fusion.4), channel_id=1, source_target_pairs={{0,1},{1,0},{2,3},{3,2},{4,5},{5,4},{6,7},{7,6},{8,9},{9,8},{10,11... | collective-permute-start | bytes 3145736 | tf_op jit(solution)/shard_map/ppermute | solution.py:47
  105.3 2.6 %collective-permute-done.11 = f32[2,4,64,512]{3,2,1,0:T(8,128)} collective-permute-done((f32[2,4,64,512]{3,2,1,0:T(8,128)}, f32[2,4,64,512]{3,2,1,0:T(8,128)}, u32[]{:S(2)}, u32[]{:S(2)}) %collective-permute-start.11) | collective-permute-done | bytes 1048608 | tf_op jit(solution)/shard_map/ppermute | solution.py:47
  107.9 1.5 select_bitcast_fusion.3
  109.7 1.5 copy.19
  111.5 1.9 %collective-permute-start = (f32[128,8,2]{0,2,1:T(2,128)S(1)}, f32[128,8,2]{0,2,1:T(2,128)S(1)}, u32[]{:S(2)}, u32[]{:S(2)}) collective-permute-start(f32[128,8,2]{0,2,1:T(2,128)S(1)} %get-tuple-element.46), channel_id=1, source_target_pairs={{0,4},{4,8},{8,12},{12,16},{16,20},{20,24},{24,28},{28,32},{32,36}... | collective-permute-start | bytes 24584 | tf_op jit(solution)/shard_map/ppermute | solution.py:16
  113.4 9.2 %collective-permute-start.1 = (f32[128,8,2]{0,2,1:T(2,128)S(1)}, f32[128,8,2]{0,2,1:T(2,128)S(1)}, u32[]{:S(2)}, u32[]{:S(2)}) collective-permute-start(f32[128,8,2]{0,2,1:T(2,128)S(1)} %get-tuple-element.45), channel_id=1, source_target_pairs={{4,0},{8,4},{12,8},{16,12},{20,16},{24,20},{28,24},{32,28},{36,32}... | collective-permute-start | bytes 24584 | tf_op jit(solution)/shard_map/ppermute | solution.py:19
  122.6 12.5 %shard_map.84 = f32[8,128,256]{2,1,0:T(8,128)} custom-call(f32[4,4,64,512]{3,2,1,0:T(8,128)} %bitcast.237, f32[128,2048]{1,0:T(8,128)} %select_add_fusion.m_ref, f32[8,2048]{1,0:T(8,128)} %get-tuple-element.194.cos_ref, f32[8,2048]{1,0:T(8,128)} %get-tuple-element.193.sin_ref), custom_call_target="tpu_custom_call" | custom-call | tf_op jit(solution)/shard_map/pallas_call | solution.py:153
  138.6 2.3 %multiply_subtract_fusion.2 = (f32[128,4,512]{0,2,1:T(8,128)}, f32[128,4,512]{0,2,1:T(8,128)}, f32[128,4,512]{0,2,1:T(8,128)}, f32[128,4,512]{0,2,1:T(8,128)}) fusion(f32[128]{0:T(128)S(1)} %get-tuple-element.202, f32[128]{0:T(128)S(1)} %get-tuple-element.203, f32[128,8,512]{0,2,1:T(8,128)S(1)} %copy.12, f32[128,8,2]{0,2,1:T(2,128)S(1)} %collective-permute-done, ...), kind=kLoop, calls=%fused_computation.171 | loop fusion | flops 4980736 | bytes 6301696 | tf_op jit(solution)/shard_map/sub | solution.py:77
  140.9 2.3 %multiply_subtract_fusion = (f32[128,4,512]{0,2,1:T(8,128)}, f32[128,4,512]{0,2,1:T(8,128)}, f32[128,4,512]{0,2,1:T(8,128)}, f32[128,4,512]{0,2,1:T(8,128)}) fusion(f32[128]{0:T(128)S(1)} %get-tuple-element.206, f32[128]{0:T(128)S(1)} %get-tuple-element.199, f32[128,8,2]{0,2,1:T(2,128)S(1)} %collective-permute-done.1, f32[128,8,512]{0,2,1:T(8,128)S(1)} %copy.12, ...), kind=kLoop, calls=%fused_computation.167 | loop fusion | flops 4980736 | bytes 6301696 | tf_op jit(solution)/shard_map/sub | solution.py:77
  143.2 1.5 copy.20
  146.2 1.6 pad_maximum_fusion.1
  147.8 12.5 %shard_map.85 = f32[8,128,256]{2,1,0:T(8,128)} custom-call(f32[4,4,64,512]{3,2,1,0:T(8,128)} %bitcast.238, f32[128,2048]{1,0:T(8,128)} %select_add_fusion.m_ref, f32[8,2048]{1,0:T(8,128)} %get-tuple-element.194.cos_ref, f32[8,2048]{1,0:T(8,128)} %get-tuple-element.193.sin_ref), custom_call_target="tpu_custom_call" | custom-call | tf_op jit(solution)/shard_map/pallas_call | solution.py:153
  160.2 1.5 copy.22
  166.4 2.0 %copy.24 = f32[128,8,512]{2,1,0:T(8,128)} copy(f32[128,8,512]{0,2,1:T(8,128)S(1)} %fusion.3) | data formatting | bytes 4194304 | tf_op jit(solution)/shard_map/add | solution.py:258
  (166 shorter events, 30.9 us)
Async XLA Ops:
  19.6 3.3 %collective-permute-start.2 = (f32[2,4,64,512]{3,2,1,0:T(8,128)}, f32[2,4,64,512]{3,2,1,0:T(8,128)}, u32[]{:S(2)}, u32[]{:S(2)}) collective-permute-start(f32[2,4,64,512]{3,2,1,0:T(8,128)} %dynamic-slice_bitcast_fusion.1), channel_id=1, source_target_pairs={{0,1},{1,0},{2,3},{3,2},{4,5},{5,4},{6,7},{7,6},{8,9},{9,8},{10,11... | collective-permute-start | bytes 3145736 | tf_op jit(solution)/shard_map/ppermute | solution.py:33
  25.5 13.4 %collective-permute-start.3 = (f32[4,64,512]{2,1,0:T(8,128)}, f32[4,64,512]{2,1,0:T(8,128)}, u32[]{:S(2)}, u32[]{:S(2)}) collective-permute-start(f32[4,64,512]{2,1,0:T(8,128)} %dynamic-slice_bitcast_fusion.3), channel_id=1, source_target_pairs={{0,2},{2,0},{1,3},{3,1},{4,6},{6,4},{5,7},{7,5},{8,10},{10,8},{9,1... | collective-permute-start | bytes 1572872 | tf_op jit(solution)/shard_map/ppermute | solution.py:235
  40.4 4.7 %collective-permute-start.4 = (f32[2,4,64,512]{3,2,1,0:T(8,128)S(1)}, f32[2,4,64,512]{3,2,1,0:T(8,128)S(1)}, u32[]{:S(2)}, u32[]{:S(2)}) collective-permute-start(f32[2,4,64,512]{3,2,1,0:T(8,128)S(1)} %dynamic-slice_bitcast_fusion), channel_id=1, source_target_pairs={{0,1},{1,0},{2,3},{3,2},{4,5},{5,4},{6,7},{7,6},{8,9},{9,8},{10,11... | collective-permute-start | bytes 3145736 | tf_op jit(solution)/shard_map/ppermute | solution.py:33
  42.5 21.1 %copy-start.39 = (f32[1,1,512]{2,1,0:T(1,128)}, f32[1,1,512]{2,1,0:T(1,128)S(1)}, u32[]{:S(2)}) copy-start(f32[1,1,512]{2,1,0:T(1,128)S(1)} %get-tuple-element.101) | copy-start | bytes 6148
  42.5 21.1 %copy-start.40 = (f32[1,1,512]{2,1,0:T(1,128)}, f32[1,1,512]{2,1,0:T(1,128)S(1)}, u32[]{:S(2)}) copy-start(f32[1,1,512]{2,1,0:T(1,128)S(1)} %get-tuple-element.102) | copy-start | bytes 6148
  42.5 21.1 %copy-start.41 = (f32[1,1,512]{2,1,0:T(1,128)}, f32[1,1,512]{2,1,0:T(1,128)S(1)}, u32[]{:S(2)}) copy-start(f32[1,1,512]{2,1,0:T(1,128)S(1)} %get-tuple-element.103) | copy-start | bytes 6148
  42.5 21.1 %copy-start.42 = (f32[1,1,512]{2,1,0:T(1,128)}, f32[1,1,512]{2,1,0:T(1,128)S(1)}, u32[]{:S(2)}) copy-start(f32[1,1,512]{2,1,0:T(1,128)S(1)} %get-tuple-element.104) | copy-start | bytes 6148
  42.5 21.1 %copy-start.43 = (f32[1,1,512]{2,1,0:T(1,128)}, f32[1,1,512]{2,1,0:T(1,128)S(1)}, u32[]{:S(2)}) copy-start(f32[1,1,512]{2,1,0:T(1,128)S(1)} %get-tuple-element.105) | copy-start | bytes 6148
  42.6 21.1 %copy-start.44 = (f32[1,1,512]{2,1,0:T(1,128)}, f32[1,1,512]{2,1,0:T(1,128)S(1)}, u32[]{:S(2)}) copy-start(f32[1,1,512]{2,1,0:T(1,128)S(1)} %get-tuple-element.106) | copy-start | bytes 6148
  42.6 21.1 %copy-start.45 = (f32[1,1,512]{2,1,0:T(1,128)}, f32[1,1,512]{2,1,0:T(1,128)S(1)}, u32[]{:S(2)}) copy-start(f32[1,1,512]{2,1,0:T(1,128)S(1)} %get-tuple-element.107) | copy-start | bytes 6148
  42.6 21.1 %copy-start.46 = (f32[1,1,512]{2,1,0:T(1,128)}, f32[1,1,512]{2,1,0:T(1,128)S(1)}, u32[]{:S(2)}) copy-start(f32[1,1,512]{2,1,0:T(1,128)S(1)} %get-tuple-element.108) | copy-start | bytes 6148
  42.6 21.1 %copy-start.47 = (f32[1,1,512]{2,1,0:T(1,128)}, f32[1,1,512]{2,1,0:T(1,128)S(1)}, u32[]{:S(2)}) copy-start(f32[1,1,512]{2,1,0:T(1,128)S(1)} %get-tuple-element.109) | copy-start | bytes 6148
  42.6 21.1 %copy-start.48 = (f32[1,1,512]{2,1,0:T(1,128)}, f32[1,1,512]{2,1,0:T(1,128)S(1)}, u32[]{:S(2)}) copy-start(f32[1,1,512]{2,1,0:T(1,128)S(1)} %get-tuple-element.110) | copy-start | bytes 6148
  42.6 21.1 %copy-start.49 = (f32[1,1,512]{2,1,0:T(1,128)}, f32[1,1,512]{2,1,0:T(1,128)S(1)}, u32[]{:S(2)}) copy-start(f32[1,1,512]{2,1,0:T(1,128)S(1)} %get-tuple-element.111) | copy-start | bytes 6148
  42.6 21.1 %copy-start.50 = (f32[1,1,512]{2,1,0:T(1,128)}, f32[1,1,512]{2,1,0:T(1,128)S(1)}, u32[]{:S(2)}) copy-start(f32[1,1,512]{2,1,0:T(1,128)S(1)} %get-tuple-element.112) | copy-start | bytes 6148
  42.6 21.1 %copy-start.51 = (f32[1,1,512]{2,1,0:T(1,128)}, f32[1,1,512]{2,1,0:T(1,128)S(1)}, u32[]{:S(2)}) copy-start(f32[1,1,512]{2,1,0:T(1,128)S(1)} %get-tuple-element.113) | copy-start | bytes 6148
  42.6 21.1 %copy-start.52 = (f32[1,1,512]{2,1,0:T(1,128)}, f32[1,1,512]{2,1,0:T(1,128)S(1)}, u32[]{:S(2)}) copy-start(f32[1,1,512]{2,1,0:T(1,128)S(1)} %get-tuple-element.114) | copy-start | bytes 6148
  42.6 21.1 %copy-start.53 = (f32[1,1,512]{2,1,0:T(1,128)}, f32[1,1,512]{2,1,0:T(1,128)S(1)}, u32[]{:S(2)}) copy-start(f32[1,1,512]{2,1,0:T(1,128)S(1)} %get-tuple-element.115) | copy-start | bytes 6148
  43.7 20.0 %copy-start.15 = (f32[1,1,512]{2,1,0:T(1,128)}, f32[1,1,512]{2,1,0:T(1,128)S(1)}, u32[]{:S(2)}) copy-start(f32[1,1,512]{2,1,0:T(1,128)S(1)} %get-tuple-element.151) | copy-start | bytes 6148
  43.8 20.0 %copy-start.16 = (f32[1,1,512]{2,1,0:T(1,128)}, f32[1,1,512]{2,1,0:T(1,128)S(1)}, u32[]{:S(2)}) copy-start(f32[1,1,512]{2,1,0:T(1,128)S(1)} %get-tuple-element.152) | copy-start | bytes 6148
  45.4 13.1 %collective-permute-start.5 = (f32[4,16,512]{2,1,0:T(8,128)S(1)}, f32[4,16,512]{2,1,0:T(8,128)S(1)}, u32[]{:S(2)}, u32[]{:S(2)}) collective-permute-start(f32[4,16,512]{2,1,0:T(8,128)S(1)} %get-tuple-element.63), channel_id=1, source_target_pairs={{0,4},{4,8},{8,12},{12,16},{16,20},{20,24},{24,28},{28,32},{32,36}... | collective-permute-start | bytes 393224 | tf_op jit(solution)/shard_map/ppermute | solution.py:16
  50.3 9.1 %collective-permute-start.6 = (f32[4,16,512]{2,1,0:T(8,128)S(1)}, f32[4,16,512]{2,1,0:T(8,128)S(1)}, u32[]{:S(2)}, u32[]{:S(2)}) collective-permute-start(f32[4,16,512]{2,1,0:T(8,128)S(1)} %get-tuple-element.64), channel_id=1, source_target_pairs={{4,0},{8,4},{12,8},{16,12},{20,16},{24,20},{28,24},{32,28},{36,32}... | collective-permute-start | bytes 393224 | tf_op jit(solution)/shard_map/ppermute | solution.py:19
  57.0 15.7 %collective-permute-start.7 = (f32[4,64,512]{2,1,0:T(8,128)S(1)}, f32[4,64,512]{2,1,0:T(8,128)S(1)}, u32[]{:S(2)}, u32[]{:S(2)}) collective-permute-start(f32[4,64,512]{2,1,0:T(8,128)S(1)} %dynamic-slice_bitcast_fusion.2), channel_id=1, source_target_pairs={{0,2},{2,0},{1,3},{3,1},{4,6},{6,4},{5,7},{7,5},{8,10},{10,8},{9,1... | collective-permute-start | bytes 1572872 | tf_op jit(solution)/shard_map/ppermute | solution.py:242
  68.2 30.4 %copy-start.9 = (f32[4,64,512]{2,1,0:T(8,128)}, f32[4,64,512]{2,1,0:T(8,128)S(1)}, u32[]{:S(2)}) copy-start(f32[4,64,512]{2,1,0:T(8,128)S(1)} %pad_maximum_fusion.6) | copy-start | bytes 1572868
  73.4 10.4 %collective-permute-start.9 = (f32[4,16,512]{2,1,0:T(8,128)}, f32[4,16,512]{2,1,0:T(8,128)S(1)}, u32[]{:S(2)}, u32[]{:S(2)}) collective-permute-start(f32[4,16,512]{2,1,0:T(8,128)} %get-tuple-element.58), channel_id=1, source_target_pairs={{0,4},{4,8},{8,12},{12,16},{16,20},{20,24},{24,28},{28,32},{32,36}... | collective-permute-start | bytes 393224 | tf_op jit(solution)/shard_map/ppermute | solution.py:16
  75.3 9.8 %collective-permute-start.10 = (f32[4,16,512]{2,1,0:T(8,128)S(1)}, f32[4,16,512]{2,1,0:T(8,128)S(1)}, u32[]{:S(2)}, u32[]{:S(2)}) collective-permute-start(f32[4,16,512]{2,1,0:T(8,128)S(1)} %get-tuple-element.57), channel_id=1, source_target_pairs={{4,0},{8,4},{12,8},{16,12},{20,16},{24,20},{28,24},{32,28},{36,32}... | collective-permute-start | bytes 393224 | tf_op jit(solution)/shard_map/ppermute | solution.py:19
  83.2 16.2 %collective-permute-start.8 = (f32[4,64,512]{2,1,0:T(8,128)S(1)}, f32[4,64,512]{2,1,0:T(8,128)S(1)}, u32[]{:S(2)}, u32[]{:S(2)}) collective-permute-start(f32[4,64,512]{2,1,0:T(8,128)S(1)} %pad_maximum_fusion.6), channel_id=1, source_target_pairs={{0,2},{2,0},{1,3},{3,1},{4,6},{6,4},{5,7},{7,5},{8,10},{10,8},{9,1... | collective-permute-start | bytes 1572872 | tf_op jit(solution)/shard_map/ppermute | solution.py:246
  101.6 6.3 %collective-permute-start.11 = (f32[2,4,64,512]{3,2,1,0:T(8,128)}, f32[2,4,64,512]{3,2,1,0:T(8,128)}, u32[]{:S(2)}, u32[]{:S(2)}) collective-permute-start(f32[2,4,64,512]{3,2,1,0:T(8,128)} %pad_maximum_fusion.4), channel_id=1, source_target_pairs={{0,1},{1,0},{2,3},{3,2},{4,5},{5,4},{6,7},{7,6},{8,9},{9,8},{10,11... | collective-permute-start | bytes 3145736 | tf_op jit(solution)/shard_map/ppermute | solution.py:47
  111.2 23.9 %collective-permute-start.12 = (f32[4,64,512]{2,1,0:T(8,128)S(1)}, f32[4,64,512]{2,1,0:T(8,128)}, u32[]{:S(2)}, u32[]{:S(2)}) collective-permute-start(f32[4,64,512]{2,1,0:T(8,128)S(1)} %copy-done.10), channel_id=1, source_target_pairs={{0,2},{2,0},{1,3},{3,1},{4,6},{6,4},{5,7},{7,5},{8,10},{10,8},{9,1... | collective-permute-start | bytes 1572872 | tf_op jit(solution)/shard_map/ppermute | solution.py:251
  111.5 27.1 %collective-permute-start = (f32[128,8,2]{0,2,1:T(2,128)S(1)}, f32[128,8,2]{0,2,1:T(2,128)S(1)}, u32[]{:S(2)}, u32[]{:S(2)}) collective-permute-start(f32[128,8,2]{0,2,1:T(2,128)S(1)} %get-tuple-element.46), channel_id=1, source_target_pairs={{0,4},{4,8},{8,12},{12,16},{16,20},{20,24},{24,28},{28,32},{32,36}... | collective-permute-start | bytes 24584 | tf_op jit(solution)/shard_map/ppermute | solution.py:16
  113.4 27.5 %collective-permute-start.1 = (f32[128,8,2]{0,2,1:T(2,128)S(1)}, f32[128,8,2]{0,2,1:T(2,128)S(1)}, u32[]{:S(2)}, u32[]{:S(2)}) collective-permute-start(f32[128,8,2]{0,2,1:T(2,128)S(1)} %get-tuple-element.45), channel_id=1, source_target_pairs={{4,0},{8,4},{12,8},{16,12},{20,16},{24,20},{28,24},{32,28},{36,32}... | collective-permute-start | bytes 24584 | tf_op jit(solution)/shard_map/ppermute | solution.py:19
  137.6 7.1 %collective-permute-start.13 = (f32[2,4,64,512]{3,2,1,0:T(8,128)}, f32[2,4,64,512]{3,2,1,0:T(8,128)}, u32[]{:S(2)}, u32[]{:S(2)}) collective-permute-start(f32[2,4,64,512]{3,2,1,0:T(8,128)} %pad_maximum_fusion.5), channel_id=1, source_target_pairs={{0,1},{1,0},{2,3},{3,2},{4,5},{5,4},{6,7},{7,6},{8,9},{9,8},{10,11... | collective-permute-start | bytes 3145736 | tf_op jit(solution)/shard_map/ppermute | solution.py:47
  (38 other events, 479.4 us)

commit v6 on v5

--- a/solution.py
+++ b/solution.py
@@ -48,6 +48,18 @@
     low = rank % 2 == 0
     quad = jnp.stack([jnp.where(low, pair, mate), jnp.where(low, mate, pair)], axis=1)
     return quad.reshape((4,) + local.shape)
+
+
+def pack(pieces):
+    return jnp.concatenate([piece.reshape(-1) for piece in pieces])
+
+
+def unpack(flat, like):
+    out, first = [], 0
+    for piece in like:
+        out.append(flat[first : first + piece.size].reshape(piece.shape))
+        first += piece.size
+    return out
 
 
 def interp_matrix(index, weight, first_row, row_count):
@@ -208,10 +220,6 @@
     rows = interp_matrix(interp_index, interp_weight, child_first, child_dev)
 
     child_reach = child_coef.shape[1] // 2
-    child_padded = with_halo(pattern, (("box", 2),), child_reach)
-    child_local = translate_padded(
-        child_padded, child_coef[0], child_coef[1], child_mask, child_reach
-    )
 
     parent_reach = parent_coef.shape[1] // 2
     own_real = lax.dynamic_slice_in_dim(parent_coef[0], parent_first, parent_dev, 1)
@@ -240,7 +248,19 @@
     sum_a, acc_b = lax.optimization_barrier((sum_a, acc_b))
     keep_b, send_b = split_rows(acc_b)
     recv_b = lax.ppermute(send_b, "dir", ROW_SWAP)
-    local_a = translate(sum_a)
+    box_size = lax.axis_size("box")
+    forward = [(i, i + 1) for i in range(box_size - 1)]
+    backward = [(i + 1, i) for i in range(box_size - 1)]
+    pieces_up = (pattern[:, :, box_dev - child_reach :], sum_a[:, slots - parent_reach :])
+    pieces_down = (pattern[:, :, :child_reach], sum_a[:, :parent_reach])
+    got_up = unpack(lax.ppermute(pack(pieces_up), "box", forward), pieces_up)
+    got_down = unpack(lax.ppermute(pack(pieces_down), "box", backward), pieces_down)
+    child_padded = jnp.concatenate([got_up[0], pattern, got_down[0]], axis=2)
+    child_local = translate_padded(
+        child_padded, child_coef[0], child_coef[1], child_mask, child_reach
+    )
+    padded_a = jnp.concatenate([got_up[1], sum_a, got_down[1]], axis=1)
+    local_a = parent_translate(padded_a, own_real, own_imag, own_mask, parent_reach)
     local_a, recv_b = lax.optimization_barrier((local_a, recv_b))
     sum_b = keep_b + recv_b
     other_a = lax.ppermute(local_a, "dir", ROW_SWAP)

time: 169 us -> 176 us (1.041)
  the two profiles are of different devices: /device:TPU:65 before, /device:TPU:31 now
where the time goes in v6:
time: 176 us; the launch traced here: 175 us
  other arithmetic  50.8 us (29%)
  Pallas kernels  45.4 us (26%)
  local copies, waits for them, and re-layouts  40.2 us (23%)
  starting transfers between devices  19.6 us (11%)
  waiting for transfers between devices  18 us (10%)
    pallas_call x2, Pallas kernels, downward(): pl.pallas_call(downward_kernel, grid=(groups,), in_specs=[pl.BlockSpec((p...  24.9 us
    pallas_call x2, Pallas kernels, upward(): pl.pallas_call(upward_kernel, grid=(parts,), in_specs=[pl.BlockSpec((grou...  20.5 us
    add x2, other arithmetic, parent_translate(): re_sum = re_sum + weight * (cr * re - ci * im)  10.9 us
    add x2, other arithmetic, parent_translate(): im_sum = im_sum + weight * (cr * im + ci * re)  10.8 us
    ppermute x1, waiting for transfers between devices, with_halo(): lax.ppermute(lax.slice_in_dim(block, 0, width, axis=dim), axis, backward)  7.07 us
    ppermute x1, waiting for transfers between devices, body(): lax.ppermute(pack(pieces_down), 'box', backward)  6.28 us
    slice x10, local copies, waits for them, and re-layouts, unpack(): out.append(flat[first:first + piece.size].reshape(piece.shape))  5.7 us
    ppermute x2, starting transfers between devices, gather_cores(): mate = lax.ppermute(pair, 'dir', CORE_SWAP)  5.22 us
  transfers between devices with their start and end apart: 12, of which 5 were waited for; matrix products, arithmetic and copies ran while one was open for 30% of the time, Pallas kernels for 13%

profile of v6, /device:TPU:31, one launch (start us, length us, event | category | flops | bytes accessed | tf_op | source)
XLA Modules:
  0.0 175.2 jit_solution(11366078021463264316)
XLA Ops:
  0.0 2.0 %copy.12 = f32[128,8,512]{0,2,1:T(8,128)S(1)} copy(f32[128,8,512]{2,1,0:T(8,128)} %param.8) | data formatting | bytes 4194304 | tf_op args[0]
  4.5 2.6 %select_add_fusion.m_ref = f32[128,2048]{1,0:T(8,128)} fusion(f32[2048]{0:T(1024)S(1)} %bitcast.524, s32[2048]{0:T(1024)S(1)} %bitcast.540, f32[2048]{0:T(1024)S(1)} %bitcast.525, s32[2048]{0:T(1024)S(1)} %bitcast.541, f32[2048]{0:T(1024)S(1)} %bitcast.511, s32[2048]{0:T(1024)S(1)} %bitcast.527, f32[2048]{0:T(1024)S(1)} %bitcast.512, ...), kind=kLoop, calls=%fused_computation.173 | loop fusion | flops 12320768 | bytes 1311232 | tf_op jit(solution)/shard_map/add | solution.py:69
  7.1 10.2 %shard_map.82 = f32[4,4,64,512]{3,2,1,0:T(8,128)} custom-call(f32[8,256,128]{2,1,0:T(8,128)} %bitcast.246, f32[128,2048]{1,0:T(8,128)} %select_add_fusion.m_ref, f32[8,2048]{1,0:T(8,128)} %get-tuple-element.194.cos_ref, f32[8,2048]{1,0:T(8,128)} %get-tuple-element.193.sin_ref), custom_call_target="tpu_custom_call" | custom-call | tf_op jit(solution)/shard_map/pallas_call | solution.py:123
  17.3 2.3 %dynamic-slice_bitcast_fusion.1 = f32[2,4,64,512]{3,2,1,0:T(8,128)} fusion(f32[2,2,4,64,512]{4,3,2,1,0:T(8,128)} %bitcast.239, s32[]{:T(128)S(6)} %select_n.152), kind=kLoop, calls=%fused_computation.172 | loop fusion | bytes 2097156 | tf_op jit(solution)/shard_map/jit(dynamic_index_in_dim)/squeeze | solution.py:32
  22.9 1.8 %bitcast_add_fusion.1 = f32[2,4,64,512]{3,2,1,0:T(8,128)S(1)} fusion(f32[2,4,64,512]{3,2,1,0:T(8,128)} %collective-permute-done, f32[2,2,4,64,512]{4,3,2,1,0:T(8,128)} %bitcast.240, s32[]{:T(128)S(6)} %select_n.151), kind=kLoop, calls=%fused_computation.158 | loop fusion | flops 262144 | bytes 3145732 | tf_op jit(solution)/shard_map/add | solution.py:33
  26.1 2.3 %fusion.105 = (f32[128,8,2]{2,1,0:T(8,128)}, f32[128,8,2]{2,1,0:T(8,128)}) fusion(f32[128,8,512]{2,1,0:T(8,128)} %param.8), kind=kLoop, calls=%fused_computation.400 | loop fusion | bytes 32768 | tf_op jit(solution)/shard_map/slice | solution.py:254
  31.1 1.9 %fusion.104 = (f32[64]{0:T(128)}, f32[64]{0:T(128)}, f32[64]{0:T(128)}, f32[64]{0:T(128)}, f32[64]{0:T(128)}, /*index=5*/f32[64]{0:T(128)}, f32[64]{0:T(128)}, f...) fusion(s32[32,2048]{1,0:T(8,128)} %param.15, ...), kind=kLoop, calls=%fused_computation.390 | loop fusion | flops 896 | bytes 7228 | tf_op jit(solution)/shard_map/convert_element_type | solution.py:192
  32.9 1.8 %fusion.73 = (f32[64]{0:T(128)}, f32[64]{0:T(128)}, f32[64]{0:T(128)}, f32[64]{0:T(128)}, f32[64]{0:T(128)}, /*index=5*/f32[64]{0:T(128)}, f32[64]{0:T(128)}, f3...) fusion(s32[32,2048]{1,0:T(8,128)} %param.15, ...), kind=kLoop, calls=%fused_computation.328 | loop fusion | flops 1152 | bytes 9288 | tf_op jit(solution)/shard_map/convert_element_type | solution.py:192
  34.8 10.3 %shard_map.83 = f32[4,4,64,512]{3,2,1,0:T(8,128)} custom-call(f32[8,256,128]{2,1,0:T(8,128)} %bitcast.244, f32[128,2048]{1,0:T(8,128)} %select_add_fusion.m_ref, f32[8,2048]{1,0:T(8,128)} %get-tuple-element.194.cos_ref, f32[8,2048]{1,0:T(8,128)} %get-tuple-element.193.sin_ref), custom_call_target="tpu_custom_call" | custom-call | tf_op jit(solution)/shard_map/pallas_call | solution.py:123
  51.9 3.7 %collective-permute-start.3 = (f32[34816]{0:T(1024)S(1)}, f32[34816]{0:T(1024)S(1)}, u32[]{:S(2)}, u32[]{:S(2)}) collective-permute-start(f32[34816]{0:T(1024)S(1)} %pad_maximum_fusion.10), channel_id=1, source_target_pairs={{0,4},{4,8},{8,12},{12,16},{16,20},{20,24},{24,28},{28,32},{32,36}... | collective-permute-start | bytes 417800 | tf_op jit(solution)/shard_map/ppermute | solution.py:256
  56.3 1.9 %collective-permute-start.4 = (f32[34816]{0:T(1024)}, f32[34816]{0:T(1024)S(1)}, u32[]{:S(2)}, u32[]{:S(2)}) collective-permute-start(f32[34816]{0:T(1024)} %pad_maximum_fusion.11), channel_id=1, source_target_pairs={{4,0},{8,4},{12,8},{16,12},{20,16},{24,20},{28,24},{32,28},{36,32}... | collective-permute-start | bytes 417800 | tf_op jit(solution)/shard_map/ppermute | solution.py:257
  61.6 6.3 %collective-permute-done.4 = f32[34816]{0:T(1024)S(1)} collective-permute-done((f32[34816]{0:T(1024)}, f32[34816]{0:T(1024)S(1)}, u32[]{:S(2)}, u32[]{:S(2)}) %collective-permute-start.4) | collective-permute-done | bytes 139296 | tf_op jit(solution)/shard_map/ppermute | solution.py:257
  70.5 4.2 %multiply_add_fusion.6 = f32[2,64,512]{2,1,0:T(8,128)S(1)} fusion(f32[4,80,512]{2,1,0:T(8,128)S(1)} %constant_dynamic-update-slice_fusion.2, f32[4,80,512]{2,1,0:T(8,128)S(1)} %get-tuple-element.61, f32[512]{0:T(512)} %bitcast.306, f32[512]{0:T(512)} %bitcast.310, f32[64]{0:T(128)} %get-tuple-element.132, f32[512]{0:T(512)} %bitcast.370, f32[512]{0:T(512)} %bitcast.442, ...), kind=kLoop, calls=%fused_computation.250 | loop fusion | flops 10420224 | bytes 17178624 | tf_op jit(solution)/shard_map/add | solution.py:194
  75.2 4.1 %multiply_add_fusion.7 = f32[2,64,512]{2,1,0:T(8,128)S(1)} fusion(f32[4,80,512]{2,1,0:T(8,128)S(1)} %constant_dynamic-update-slice_fusion.2, f32[4,80,512]{2,1,0:T(8,128)S(1)} %get-tuple-element.61, f32[512]{0:T(512)S(1)} %bitcast.309, f32[512]{0:T(512)S(1)} %bitcast.313, f32[64]{0:T(128)} %get-tuple-element.132, f32[512]{0:T(512)S(1)} %bitcast.373, ...), kind=kLoop, calls=%fused_computation.251 | loop fusion | flops 10420224 | bytes 17178624 | tf_op jit(solution)/shard_map/add | solution.py:193
  81.3 2.8 %collective-permute-start.7 = (f32[4,16,512]{2,1,0:T(8,128)}, f32[4,16,512]{2,1,0:T(8,128)S(1)}, u32[]{:S(2)}, u32[]{:S(2)}) collective-permute-start(f32[4,16,512]{2,1,0:T(8,128)} %get-tuple-element.58), channel_id=1, source_target_pairs={{0,4},{4,8},{8,12},{12,16},{16,20},{20,24},{24,28},{28,32},{32,36}... | collective-permute-start | bytes 393224 | tf_op jit(solution)/shard_map/ppermute | solution.py:16
  84.1 2.5 %collective-permute-start.8 = (f32[4,16,512]{2,1,0:T(8,128)S(1)}, f32[4,16,512]{2,1,0:T(8,128)S(1)}, u32[]{:S(2)}, u32[]{:S(2)}) collective-permute-start(f32[4,16,512]{2,1,0:T(8,128)S(1)} %get-tuple-element.57), channel_id=1, source_target_pairs={{4,0},{8,4},{12,8},{16,12},{20,16},{24,20},{28,24},{32,28},{36,32}... | collective-permute-start | bytes 393224 | tf_op jit(solution)/shard_map/ppermute | solution.py:19
  87.3 7.1 %collective-permute-done.8 = f32[4,16,512]{2,1,0:T(8,128)S(1)} collective-permute-done((f32[4,16,512]{2,1,0:T(8,128)S(1)}, f32[4,16,512]{2,1,0:T(8,128)S(1)}, u32[]{:S(2)}, u32[]{:S(2)}) %collective-permute-start.8) | collective-permute-done | bytes 131104 | tf_op jit(solution)/shard_map/ppermute | solution.py:19
  94.4 6.6 %multiply_add_fusion.4 = f32[2,64,512]{2,1,0:T(8,128)S(1)} fusion(f32[512]{0:T(512)} %bitcast.307, f32[512]{0:T(512)} %bitcast.311, f32[64]{0:T(128)} %get-tuple-element.132, f32[512]{0:T(512)} %bitcast.371, f32[512]{0:T(512)} %bitcast.444, f32[64]{0:T(128)} %get-tuple-element.66, f32[512]{0:T(512)} %bitcast.375, f32[512]{0:T(512)} %bitcast.448, ...), kind=kLoop, calls=%fused_computation.248 | loop fusion | flops 14614528 | bytes 1187840 | tf_op jit(solution)/shard_map/add | solution.py:194
  100.9 6.9 %multiply_add_fusion.5 = f32[2,64,512]{2,1,0:T(8,128)S(1)} fusion(f32[512]{0:T(512)} %bitcast.308, f32[512]{0:T(512)} %bitcast.312, f32[64]{0:T(128)} %get-tuple-element.132, f32[512]{0:T(512)} %bitcast.372, f32[512]{0:T(512)} %bitcast.445, f32[64]{0:T(128)} %get-tuple-element.66, f32[512]{0:T(512)} %bitcast.376, f32[512]{0:T(512)} %bitcast.449, ...), kind=kLoop, calls=%fused_computation.249 | loop fusion | flops 14614528 | bytes 1187840 | tf_op jit(solution)/shard_map/add | solution.py:193
  110.9 4.0 %collective-permute-start.9 = (f32[2,4,64,512]{3,2,1,0:T(8,128)}, f32[2,4,64,512]{3,2,1,0:T(8,128)}, u32[]{:S(2)}, u32[]{:S(2)}) collective-permute-start(f32[2,4,64,512]{3,2,1,0:T(8,128)} %pad_maximum_fusion.4), channel_id=1, source_target_pairs={{0,1},{1,0},{2,3},{3,2},{4,5},{5,4},{6,7},{7,6},{8,9},{9,8},{10,11... | collective-permute-start | bytes 3145736 | tf_op jit(solution)/shard_map/ppermute | solution.py:47
  114.9 2.6 %collective-permute-done.9 = f32[2,4,64,512]{3,2,1,0:T(8,128)} collective-permute-done((f32[2,4,64,512]{3,2,1,0:T(8,128)}, f32[2,4,64,512]{3,2,1,0:T(8,128)}, u32[]{:S(2)}, u32[]{:S(2)}) %collective-permute-start.9) | collective-permute-done | bytes 1048608 | tf_op jit(solution)/shard_map/ppermute | solution.py:47
  119.2 1.5 copy.19
  121.0 12.5 %shard_map.84 = f32[8,128,256]{2,1,0:T(8,128)} custom-call(f32[4,4,64,512]{3,2,1,0:T(8,128)} %bitcast.241, f32[128,2048]{1,0:T(8,128)} %select_add_fusion.m_ref, f32[8,2048]{1,0:T(8,128)} %get-tuple-element.194.cos_ref, f32[8,2048]{1,0:T(8,128)} %get-tuple-element.193.sin_ref), custom_call_target="tpu_custom_call" | custom-call | tf_op jit(solution)/shard_map/pallas_call | solution.py:165
  142.7 2.3 %multiply_subtract_fusion.2 = (f32[128,4,512]{0,2,1:T(8,128)}, f32[128,4,512]{0,2,1:T(8,128)}, f32[128,4,512]{0,2,1:T(8,128)}, f32[128,4,512]{0,2,1:T(8,128)}) fusion(f32[128]{0:T(128)S(1)} %get-tuple-element.202, f32[128]{0:T(128)S(1)} %get-tuple-element.203, f32[128,8,512]{0,2,1:T(8,128)S(1)} %copy.12, f32[128,8,2]{0,2,1:T(2,128)S(1)} %copy.15, ...), kind=kLoop, calls=%fused_computation.168 | loop fusion | flops 4980736 | bytes 6301696 | tf_op jit(solution)/shard_map/sub | solution.py:89
  145.0 2.3 %multiply_subtract_fusion = (f32[128,4,512]{0,2,1:T(8,128)}, f32[128,4,512]{0,2,1:T(8,128)}, f32[128,4,512]{0,2,1:T(8,128)}, f32[128,4,512]{0,2,1:T(8,128)}) fusion(f32[128]{0:T(128)S(1)} %get-tuple-element.206, f32[128]{0:T(128)S(1)} %get-tuple-element.199, f32[128,8,2]{0,2,1:T(2,128)S(1)} %copy.18, f32[128,8,512]{0,2,1:T(8,128)S(1)} %copy.12, ...), kind=kLoop, calls=%fused_computation.164 | loop fusion | flops 4980736 | bytes 6301696 | tf_op jit(solution)/shard_map/sub | solution.py:89
  147.3 2.6 %copy.20 = f32[8,128,256]{1,2,0:T(8,128)} copy(f32[8,128,256]{2,1,0:T(8,128)} %shard_map.84) | data formatting | bytes 2097152 | tf_op jit(solution)/shard_map/optimization_barrier | solution.py:273
  149.9 1.6 select_bitcast_fusion.1
  151.4 1.6 pad_maximum_fusion.1
  153.0 12.5 %shard_map.85 = f32[8,128,256]{2,1,0:T(8,128)} custom-call(f32[4,4,64,512]{3,2,1,0:T(8,128)} %bitcast.242, f32[128,2048]{1,0:T(8,128)} %select_add_fusion.m_ref, f32[8,2048]{1,0:T(8,128)} %get-tuple-element.194.cos_ref, f32[8,2048]{1,0:T(8,128)} %get-tuple-element.193.sin_ref), custom_call_target="tpu_custom_call" | custom-call | tf_op jit(solution)/shard_map/pallas_call | solution.py:165
  165.4 2.6 %copy.22 = f32[8,128,256]{1,2,0:T(8,128)} copy(f32[8,128,256]{2,1,0:T(8,128)} %shard_map.85) | data formatting | bytes 2097152 | tf_op jit(solution)/shard_map/pallas_call | solution.py:165
  168.1 1.6 maximum_bitcast_fusion
  173.2 2.0 %copy.24 = f32[128,8,512]{2,1,0:T(8,128)} copy(f32[128,8,512]{0,2,1:T(8,128)S(1)} %fusion.3) | data formatting | bytes 4194304 | tf_op jit(solution)/shard_map/add | solution.py:278
  (192 shorter events, 43.3 us)
Async XLA Ops:
  19.6 3.3 %collective-permute-start = (f32[2,4,64,512]{3,2,1,0:T(8,128)}, f32[2,4,64,512]{3,2,1,0:T(8,128)}, u32[]{:S(2)}, u32[]{:S(2)}) collective-permute-start(f32[2,4,64,512]{3,2,1,0:T(8,128)} %dynamic-slice_bitcast_fusion.1), channel_id=1, source_target_pairs={{0,1},{1,0},{2,3},{3,2},{4,5},{5,4},{6,7},{7,6},{8,9},{9,8},{10,11... | collective-permute-start | bytes 3145736 | tf_op jit(solution)/shard_map/ppermute | solution.py:33
  25.6 19.5 %collective-permute-start.1 = (f32[4,64,512]{2,1,0:T(8,128)}, f32[4,64,512]{2,1,0:T(8,128)}, u32[]{:S(2)}, u32[]{:S(2)}) collective-permute-start(f32[4,64,512]{2,1,0:T(8,128)} %dynamic-slice_bitcast_fusion.3), channel_id=1, source_target_pairs={{0,2},{2,0},{1,3},{3,1},{4,6},{6,4},{5,7},{7,5},{8,10},{10,8},{9,1... | collective-permute-start | bytes 1572872 | tf_op jit(solution)/shard_map/ppermute | solution.py:243
  45.0 6.1 %copy-start = (f32[4,4,64,512]{3,2,1,0:T(8,128)S(1)}, f32[4,4,64,512]{3,2,1,0:T(8,128)}, u32[]{:S(2)}) copy-start(f32[4,4,64,512]{3,2,1,0:T(8,128)} %shard_map.83) | copy-start | bytes 6291460
  46.5 4.6 %collective-permute-start.2 = (f32[2,4,64,512]{3,2,1,0:T(8,128)S(1)}, f32[2,4,64,512]{3,2,1,0:T(8,128)S(1)}, u32[]{:S(2)}, u32[]{:S(2)}) collective-permute-start(f32[2,4,64,512]{3,2,1,0:T(8,128)S(1)} %dynamic-slice_bitcast_fusion), channel_id=1, source_target_pairs={{0,1},{1,0},{2,3},{3,2},{4,5},{5,4},{6,7},{7,6},{8,9},{9,8},{10,11... | collective-permute-start | bytes 3145736 | tf_op jit(solution)/shard_map/ppermute | solution.py:33
  51.3 6.9 %copy-start.1 = (f32[2,4,64,512]{3,2,1,0:T(8,128)}, f32[2,4,64,512]{3,2,1,0:T(8,128)S(1)}, u32[]{:S(2)}) copy-start(f32[2,4,64,512]{3,2,1,0:T(8,128)S(1)} %bitcast_add_fusion) | copy-start | bytes 3145732
  51.9 7.8 %collective-permute-start.3 = (f32[34816]{0:T(1024)S(1)}, f32[34816]{0:T(1024)S(1)}, u32[]{:S(2)}, u32[]{:S(2)}) collective-permute-start(f32[34816]{0:T(1024)S(1)} %pad_maximum_fusion.10), channel_id=1, source_target_pairs={{0,4},{4,8},{8,12},{12,16},{16,20},{20,24},{24,28},{28,32},{32,36}... | collective-permute-start | bytes 417800 | tf_op jit(solution)/shard_map/ppermute | solution.py:256
  56.3 11.5 %collective-permute-start.4 = (f32[34816]{0:T(1024)}, f32[34816]{0:T(1024)S(1)}, u32[]{:S(2)}, u32[]{:S(2)}) collective-permute-start(f32[34816]{0:T(1024)} %pad_maximum_fusion.11), channel_id=1, source_target_pairs={{4,0},{8,4},{12,8},{16,12},{20,16},{24,20},{28,24},{32,28},{36,32}... | collective-permute-start | bytes 417800 | tf_op jit(solution)/shard_map/ppermute | solution.py:257
  59.1 20.2 %collective-permute-start.5 = (f32[4,64,512]{2,1,0:T(8,128)}, f32[4,64,512]{2,1,0:T(8,128)}, u32[]{:S(2)}, u32[]{:S(2)}) collective-permute-start(f32[4,64,512]{2,1,0:T(8,128)} %dynamic-slice_bitcast_fusion.2), channel_id=1, source_target_pairs={{0,2},{2,0},{1,3},{3,1},{4,6},{6,4},{5,7},{7,5},{8,10},{10,8},{9,1... | collective-permute-start | bytes 1572872 | tf_op jit(solution)/shard_map/ppermute | solution.py:250
  70.1 4.6 %copy-start.21 = (f32[1,1,512]{2,1,0:T(1,128)S(1)}, f32[1,1,512]{2,1,0:T(1,128)}, u32[]{:S(2)}) copy-start(f32[1,1,512]{2,1,0:T(1,128)} %get-tuple-element.149) | copy-start | bytes 6148
  70.1 4.6 %copy-start.22 = (f32[1,1,512]{2,1,0:T(1,128)S(1)}, f32[1,1,512]{2,1,0:T(1,128)}, u32[]{:S(2)}) copy-start(f32[1,1,512]{2,1,0:T(1,128)} %get-tuple-element.150) | copy-start | bytes 6148
  70.1 4.6 %copy-start.23 = (f32[1,1,512]{2,1,0:T(1,128)S(1)}, f32[1,1,512]{2,1,0:T(1,128)}, u32[]{:S(2)}) copy-start(f32[1,1,512]{2,1,0:T(1,128)} %get-tuple-element.151) | copy-start | bytes 6148
  70.2 4.6 %copy-start.24 = (f32[1,1,512]{2,1,0:T(1,128)S(1)}, f32[1,1,512]{2,1,0:T(1,128)}, u32[]{:S(2)}) copy-start(f32[1,1,512]{2,1,0:T(1,128)} %get-tuple-element.152) | copy-start | bytes 6148
  70.2 4.6 %copy-start.25 = (f32[1,1,512]{2,1,0:T(1,128)S(1)}, f32[1,1,512]{2,1,0:T(1,128)}, u32[]{:S(2)}) copy-start(f32[1,1,512]{2,1,0:T(1,128)} %get-tuple-element.153) | copy-start | bytes 6148
  70.2 4.6 %copy-start.26 = (f32[1,1,512]{2,1,0:T(1,128)S(1)}, f32[1,1,512]{2,1,0:T(1,128)}, u32[]{:S(2)}) copy-start(f32[1,1,512]{2,1,0:T(1,128)} %get-tuple-element.154) | copy-start | bytes 6148
  70.2 4.6 %copy-start.27 = (f32[1,1,512]{2,1,0:T(1,128)S(1)}, f32[1,1,512]{2,1,0:T(1,128)}, u32[]{:S(2)}) copy-start(f32[1,1,512]{2,1,0:T(1,128)} %get-tuple-element.155) | copy-start | bytes 6148
  70.2 4.6 %copy-start.28 = (f32[1,1,512]{2,1,0:T(1,128)S(1)}, f32[1,1,512]{2,1,0:T(1,128)}, u32[]{:S(2)}) copy-start(f32[1,1,512]{2,1,0:T(1,128)} %get-tuple-element.156) | copy-start | bytes 6148
  70.2 4.6 %copy-start.29 = (f32[1,1,512]{2,1,0:T(1,128)S(1)}, f32[1,1,512]{2,1,0:T(1,128)}, u32[]{:S(2)}) copy-start(f32[1,1,512]{2,1,0:T(1,128)} %get-tuple-element.157) | copy-start | bytes 6148
  70.2 4.6 %copy-start.30 = (f32[1,1,512]{2,1,0:T(1,128)S(1)}, f32[1,1,512]{2,1,0:T(1,128)}, u32[]{:S(2)}) copy-start(f32[1,1,512]{2,1,0:T(1,128)} %get-tuple-element.158) | copy-start | bytes 6148
  70.2 4.6 %copy-start.31 = (f32[1,1,512]{2,1,0:T(1,128)S(1)}, f32[1,1,512]{2,1,0:T(1,128)}, u32[]{:S(2)}) copy-start(f32[1,1,512]{2,1,0:T(1,128)} %get-tuple-element.159) | copy-start | bytes 6148
  70.2 4.6 %copy-start.32 = (f32[1,1,512]{2,1,0:T(1,128)S(1)}, f32[1,1,512]{2,1,0:T(1,128)}, u32[]{:S(2)}) copy-start(f32[1,1,512]{2,1,0:T(1,128)} %get-tuple-element.160) | copy-start | bytes 6148
  70.2 4.6 %copy-start.33 = (f32[1,1,512]{2,1,0:T(1,128)S(1)}, f32[1,1,512]{2,1,0:T(1,128)}, u32[]{:S(2)}) copy-start(f32[1,1,512]{2,1,0:T(1,128)} %get-tuple-element.207) | copy-start | bytes 6148
  70.3 4.6 %copy-start.34 = (f32[1,1,512]{2,1,0:T(1,128)S(1)}, f32[1,1,512]{2,1,0:T(1,128)}, u32[]{:S(2)}) copy-start(f32[1,1,512]{2,1,0:T(1,128)} %get-tuple-element.208) | copy-start | bytes 6148
  70.3 4.6 %copy-start.35 = (f32[1,1,512]{2,1,0:T(1,128)S(1)}, f32[1,1,512]{2,1,0:T(1,128)}, u32[]{:S(2)}) copy-start(f32[1,1,512]{2,1,0:T(1,128)} %get-tuple-element.209) | copy-start | bytes 6148
  70.3 4.6 %copy-start.36 = (f32[1,1,512]{2,1,0:T(1,128)S(1)}, f32[1,1,512]{2,1,0:T(1,128)}, u32[]{:S(2)}) copy-start(f32[1,1,512]{2,1,0:T(1,128)} %get-tuple-element.210) | copy-start | bytes 6148
  79.3 28.5 %copy-start.13 = (f32[4,64,512]{2,1,0:T(8,128)}, f32[4,64,512]{2,1,0:T(8,128)S(1)}, u32[]{:S(2)}) copy-start(f32[4,64,512]{2,1,0:T(8,128)S(1)} %pad_maximum_fusion.6) | copy-start | bytes 1572868
  81.3 6.0 %collective-permute-start.7 = (f32[4,16,512]{2,1,0:T(8,128)}, f32[4,16,512]{2,1,0:T(8,128)S(1)}, u32[]{:S(2)}, u32[]{:S(2)}) collective-permute-start(f32[4,16,512]{2,1,0:T(8,128)} %get-tuple-element.58), channel_id=1, source_target_pairs={{0,4},{4,8},{8,12},{12,16},{16,20},{20,24},{24,28},{28,32},{32,36}... | collective-permute-start | bytes 393224 | tf_op jit(solution)/shard_map/ppermute | solution.py:16
  84.1 10.2 %collective-permute-start.8 = (f32[4,16,512]{2,1,0:T(8,128)S(1)}, f32[4,16,512]{2,1,0:T(8,128)S(1)}, u32[]{:S(2)}, u32[]{:S(2)}) collective-permute-start(f32[4,16,512]{2,1,0:T(8,128)S(1)} %get-tuple-element.57), channel_id=1, source_target_pairs={{4,0},{8,4},{12,8},{16,12},{20,16},{24,20},{28,24},{32,28},{36,32}... | collective-permute-start | bytes 393224 | tf_op jit(solution)/shard_map/ppermute | solution.py:19
  86.6 22.0 %collective-permute-start.6 = (f32[4,64,512]{2,1,0:T(8,128)S(1)}, f32[4,64,512]{2,1,0:T(8,128)S(1)}, u32[]{:S(2)}, u32[]{:S(2)}) collective-permute-start(f32[4,64,512]{2,1,0:T(8,128)S(1)} %pad_maximum_fusion.6), channel_id=1, source_target_pairs={{0,2},{2,0},{1,3},{3,1},{4,6},{6,4},{5,7},{7,5},{8,10},{10,8},{9,1... | collective-permute-start | bytes 1572872 | tf_op jit(solution)/shard_map/ppermute | solution.py:266
  110.9 6.6 %collective-permute-start.9 = (f32[2,4,64,512]{3,2,1,0:T(8,128)}, f32[2,4,64,512]{3,2,1,0:T(8,128)}, u32[]{:S(2)}, u32[]{:S(2)}) collective-permute-start(f32[2,4,64,512]{3,2,1,0:T(8,128)} %pad_maximum_fusion.4), channel_id=1, source_target_pairs={{0,1},{1,0},{2,3},{3,2},{4,5},{5,4},{6,7},{7,6},{8,9},{9,8},{10,11... | collective-permute-start | bytes 3145736 | tf_op jit(solution)/shard_map/ppermute | solution.py:47
  120.8 13.2 %collective-permute-start.10 = (f32[4,64,512]{2,1,0:T(8,128)S(1)}, f32[4,64,512]{2,1,0:T(8,128)}, u32[]{:S(2)}, u32[]{:S(2)}) collective-permute-start(f32[4,64,512]{2,1,0:T(8,128)S(1)} %copy-done.14), channel_id=1, source_target_pairs={{0,2},{2,0},{1,3},{3,1},{4,6},{6,4},{5,7},{7,5},{8,10},{10,8},{9,1... | collective-permute-start | bytes 1572872 | tf_op jit(solution)/shard_map/ppermute | solution.py:271
  135.3 4.9 %slice-start.1 = ((f32[34816]{0:T(1024)}), f32[2048]{0:T(1024)S(1)}, s32[]{:S(2)}) async-start(f32[34816]{0:T(1024)} %copy-done.17), calls=%async_computation.1 | async-start | bytes 16384 | tf_op jit(solution)/shard_map/slice | solution.py:60
  136.4 13.4 %collective-permute-start.11 = (f32[2,4,64,512]{3,2,1,0:T(8,128)}, f32[2,4,64,512]{3,2,1,0:T(8,128)}, u32[]{:S(2)}, u32[]{:S(2)}) collective-permute-start(f32[2,4,64,512]{3,2,1,0:T(8,128)} %pad_maximum_fusion.5), channel_id=1, source_target_pairs={{0,1},{1,0},{2,3},{3,2},{4,5},{5,4},{6,7},{7,6},{8,9},{9,8},{10,11... | collective-permute-start | bytes 3145736 | tf_op jit(solution)/shard_map/ppermute | solution.py:47
  (44 other events, 155.2 us)

commit v7 on v5

--- a/solution.py
+++ b/solution.py
@@ -181,6 +181,45 @@
         re_sum = re_sum + weight * (cr * re - ci * im)
         im_sum = im_sum + weight * (cr * im + ci * re)
     return jnp.concatenate([re_sum, im_sum], axis=0)
+
+
+def translate_kernel(low_ref, keep_ref, recv_ref, high_ref, cr_ref, ci_ref, mask_ref, out_ref, pad_ref):
+    comps, slots, width = keep_ref.shape
+    reach = low_ref.shape[1]
+    half = comps // 2
+    pad_ref[:, :reach] = low_ref[...]
+    pad_ref[:, reach : reach + slots] = keep_ref[...] + recv_ref[...]
+    pad_ref[:, reach + slots :] = high_ref[...]
+    offsets = list(range(-reach, 0)) + list(range(1, reach + 1))
+
+    def lane_block(lb, carry):
+        lanes = pl.ds(pl.multiple_of(lb * 128, 128), 128)
+        for h in range(half):
+            acc_re = jnp.zeros((slots, 128), jnp.float32)
+            acc_im = jnp.zeros((slots, 128), jnp.float32)
+            for k, t in enumerate(offsets):
+                m = mask_ref[k]
+                a = m * cr_ref[pl.ds(k, 1), lanes]
+                b = m * ci_ref[pl.ds(k, 1), lanes]
+                xr = pad_ref[h, pl.ds(reach + t, slots), lanes]
+                xi = pad_ref[h + half, pl.ds(reach + t, slots), lanes]
+                acc_re = acc_re + (a * xr - b * xi)
+                acc_im = acc_im + (a * xi + b * xr)
+            out_ref[h, :, lanes] = acc_re
+            out_ref[h + half, :, lanes] = acc_im
+        return carry
+
+    lax.fori_loop(0, width // 128, lane_block, 0)
+
+
+def translate_call(low, keep, recv, high, cr, ci, mask_b):
+    comps, slots, width = keep.shape
+    reach = low.shape[1]
+    return pl.pallas_call(
+        translate_kernel,
+        out_shape=jax.ShapeDtypeStruct(keep.shape, jnp.float32),
+        scratch_shapes=[pltpu.VMEM((comps, slots + 2 * reach, width), jnp.float32)],
+    )(low, keep, recv, high, cr, ci, mask_b)
 
 
 def body(
@@ -225,9 +264,19 @@
         xt = part.reshape(child_dev, 2 * step, slots, groups).transpose(3, 1, 2, 0)
         return xt.reshape(groups, 2 * step * slots, child_dev)
 
-    def translate(field):
-        padded = with_halo(field, (("box", 1),), parent_reach)
-        return parent_translate(padded, own_real, own_imag, own_mask, parent_reach)
+    box_size = lax.axis_size("box")
+    forward = [(i, i + 1) for i in range(box_size - 1)]
+    backward = [(i + 1, i) for i in range(box_size - 1)]
+    mask_lanes = jnp.broadcast_to(
+        own_mask.astype(jnp.float32)[:, :, None], own_mask.shape + (128,)
+    )
+
+    def translate(keep, recv):
+        low = keep[:, slots - parent_reach :] + recv[:, slots - parent_reach :]
+        high = keep[:, :parent_reach] + recv[:, :parent_reach]
+        low = lax.ppermute(low, "box", forward)
+        high = lax.ppermute(high, "box", backward)
+        return translate_call(low, keep, recv, high, own_real, own_imag, mask_lanes)
 
     acc_a = reduce_cores(upward(chunk_xt(0), rows, cosine, sine, dir_size, 2 * step))
     acc_a, xt_b = lax.optimization_barrier((acc_a, chunk_xt(1)))
@@ -235,16 +284,14 @@
     recv_a = lax.ppermute(send_a, "dir", ROW_SWAP)
     field_b = upward(xt_b, rows, cosine, sine, dir_size, 2 * step)
     field_b, recv_a = lax.optimization_barrier((field_b, recv_a))
-    sum_a = keep_a + recv_a
     acc_b = reduce_cores(field_b)
-    sum_a, acc_b = lax.optimization_barrier((sum_a, acc_b))
+    keep_a, recv_a, acc_b = lax.optimization_barrier((keep_a, recv_a, acc_b))
     keep_b, send_b = split_rows(acc_b)
     recv_b = lax.ppermute(send_b, "dir", ROW_SWAP)
-    local_a = translate(sum_a)
+    local_a = translate(keep_a, recv_a)
     local_a, recv_b = lax.optimization_barrier((local_a, recv_b))
-    sum_b = keep_b + recv_b
     other_a = lax.ppermute(local_a, "dir", ROW_SWAP)
-    local_b = translate(sum_b)
+    local_b = translate(keep_b, recv_b)
     other_a, local_b = lax.optimization_barrier((other_a, local_b))
     all_a = gather_cores(local_a, other_a)
     all_a, local_b = lax.optimization_barrier((all_a, local_b))

time: 169 us -> 167 us (0.988)
  other arithmetic: 47.1 us -> 23.8 us
  Pallas kernels: 45.5 us -> 58 us
  waiting for transfers between devices: 11.2 us -> 17.3 us
  local copies, waits for them, and re-layouts: 22.9 us -> 28.7 us
  starting transfers between devices: 40.6 us -> 38.1 us
    add x6 -> x2, other arithmetic: 22.9 us -> 2.68 us  [translate(): high = keep[:, :parent_reach] + recv[:, :parent_reach]]
    ppermute x0 -> x4, starting transfers between devices: none -> 19.8 us  [the longest x2 14.6 us: translate(): high = lax.ppermute(high, 'box', backward)]
    ppermute x3 -> x1, starting transfers between devices: 23.7 us -> 7.87 us  [with_halo(): lax.ppermute(lax.slice_in_dim(block, 0, width, axis=dim), axis, backward)]
    pallas_call x0 -> x2, Pallas kernels: none -> 12.6 us  [translate_call(): pl.pallas_call(translate_kernel, out_shape=jax.ShapeDtypeStruct(keep.shap...]
    ppermute x0 -> x4, waiting for transfers between devices: none -> 9.07 us  [the longest x2 9.07 us: translate(): low = lax.ppermute(low, 'box', forward)]
    ppermute x3 -> x1, starting transfers between devices: 7.03 us -> 1.92 us  [with_halo(): lax.ppermute(lax.slice_in_dim(block, block.shape[dim] - width, None, axis...]
    ppermute x1, waiting for transfers between devices: 4.47 us -> 0.01 us  [body(): recv_b = lax.ppermute(send_b, 'dir', ROW_SWAP)]
    convert_element_type x2 -> x1, other arithmetic: 3.46 us -> 0.8 us  [body(): own_mask.astype(jnp.float32)[:, :, None]]
  transfers between devices with their start and end apart: 14 -> 14, of which waited for: 7 -> 6; matrix products, arithmetic and copies ran while one was open for 23% -> 11% of each run, Pallas kernels for 14% -> 21%
where the time goes in v7:
time: 167 us; the launch traced here: 166 us
  Pallas kernels  58 us (35%)
  starting transfers between devices  38.1 us (23%)
  local copies, waits for them, and re-layouts  28.7 us (17%)
  other arithmetic  23.8 us (14%)
  waiting for transfers between devices  17.3 us (10%)
    pallas_call x2, Pallas kernels, downward(): pl.pallas_call(downward_kernel, grid=(groups,), in_specs=[pl.BlockSpec((p...  25 us
    pallas_call x2, Pallas kernels, upward(): pl.pallas_call(upward_kernel, grid=(parts,), in_specs=[pl.BlockSpec((grou...  20.5 us
    ppermute x2, starting transfers between devices, translate(): high = lax.ppermute(high, 'box', backward)  14.6 us
    pallas_call x2, Pallas kernels, translate_call(): pl.pallas_call(translate_kernel, out_shape=jax.ShapeDtypeStruct(keep.shap...  12.6 us
    ppermute x2, waiting for transfers between devices, translate(): low = lax.ppermute(low, 'box', forward)  9.07 us
    ppermute x1, starting transfers between devices, with_halo(): lax.ppermute(lax.slice_in_dim(block, 0, width, axis=dim), axis, backward)  7.87 us
    ppermute x2, starting transfers between devices, translate(): low = lax.ppermute(low, 'box', forward)  5.12 us
    another operation x4, other arithmetic, gather_cores(): jnp.stack([jnp.where(first, local, other), jnp.where(first, other, local)...  4.85 us
  transfers between devices with their start and end apart: 14, of which 6 were waited for; matrix products, arithmetic and copies ran while one was open for 11% of the time, Pallas kernels for 21%

profile of v7, /device:TPU:65, one launch (start us, length us, event | category | flops | bytes accessed | tf_op | source)
XLA Modules:
  0.0 166.3 jit_solution(11682604537407766135)
XLA Ops:
  0.0 2.0 %copy.12 = f32[128,8,512]{0,2,1:T(8,128)S(1)} copy(f32[128,8,512]{2,1,0:T(8,128)} %param.8) | data formatting | bytes 4194304 | tf_op args[0]
  4.5 2.7 %select_add_fusion.m_ref = f32[128,2048]{1,0:T(8,128)} fusion(f32[2048]{0:T(1024)S(1)} %bitcast.134, s32[2048]{0:T(1024)S(1)} %bitcast.150, f32[2048]{0:T(1024)S(1)} %bitcast.135, s32[2048]{0:T(1024)S(1)} %bitcast.151, f32[2048]{0:T(1024)S(1)} %bitcast.121, s32[2048]{0:T(1024)S(1)} %bitcast.137, f32[2048]{0:T(1024)S(1)} %bitcast.122, s32[2048]{0:T(1024)S(1)} %bitcast.138, ...), kind=kLoop, calls=%fused_computation.41 | loop fusion | flops 12320768 | bytes 1311232 | tf_op jit(solution)/shard_map/add | solution.py:57
  7.1 10.2 %shard_map.82 = f32[4,4,64,512]{3,2,1,0:T(8,128)} custom-call(f32[8,256,128]{2,1,0:T(8,128)} %bitcast.115, f32[128,2048]{1,0:T(8,128)} %select_add_fusion.m_ref, f32[8,2048]{1,0:T(8,128)} %get-tuple-element.102.cos_ref, f32[8,2048]{1,0:T(8,128)} %get-tuple-element.101.sin_ref), custom_call_target="tpu_custom_call" | custom-call | tf_op jit(solution)/shard_map/pallas_call | solution.py:111
  17.4 2.3 %dynamic-slice_bitcast_fusion.1 = f32[2,4,64,512]{3,2,1,0:T(8,128)} fusion(f32[2,2,4,64,512]{4,3,2,1,0:T(8,128)} %bitcast.107, s32[]{:T(128)S(6)} %select_n.155), kind=kLoop, calls=%fused_computation.40 | loop fusion | bytes 2097156 | tf_op jit(solution)/shard_map/jit(dynamic_index_in_dim)/squeeze | solution.py:32
  23.0 1.8 %bitcast_add_fusion.1 = f32[2,4,64,512]{3,2,1,0:T(8,128)S(1)} fusion(f32[2,4,64,512]{3,2,1,0:T(8,128)} %collective-permute-done.2, f32[2,2,4,64,512]{4,3,2,1,0:T(8,128)} %bitcast.108, s32[]{:T(128)S(6)} %select_n.154), kind=kLoop, calls=%fused_computation.34 | loop fusion | flops 262144 | bytes 3145732 | tf_op jit(solution)/shard_map/add | solution.py:33
  26.9 10.2 %shard_map.83 = f32[4,4,64,512]{3,2,1,0:T(8,128)} custom-call(f32[8,256,128]{2,1,0:T(8,128)} %bitcast.116, f32[128,2048]{1,0:T(8,128)} %select_add_fusion.m_ref, f32[8,2048]{1,0:T(8,128)} %get-tuple-element.102.cos_ref, f32[8,2048]{1,0:T(8,128)} %get-tuple-element.101.sin_ref), custom_call_target="tpu_custom_call" | custom-call | tf_op jit(solution)/shard_map/pallas_call | solution.py:111
  37.1 1.9 %collective-permute-done.3.recv_ref = f32[4,64,512]{2,1,0:T(8,128)S(1)} collective-permute-done((f32[4,64,512]{2,1,0:T(8,128)}, f32[4,64,512]{2,1,0:T(8,128)S(1)}, u32[]{:S(2)}, u32[]{:S(2)}) %collective-permute-start.3) | collective-permute-done | bytes 524320 | tf_op jit(solution)/shard_map/ppermute | solution.py:284
  41.8 2.3 %collective-permute-done.4 = f32[2,4,64,512]{3,2,1,0:T(8,128)S(1)} collective-permute-done((f32[2,4,64,512]{3,2,1,0:T(8,128)S(1)}, f32[2,4,64,512]{3,2,1,0:T(8,128)S(1)}, u32[]{:S(2)}, u32[]{:S(2)}) %collective-permute-start.4) | collective-permute-done | bytes 1048608 | tf_op jit(solution)/shard_map/ppermute | solution.py:33
  47.2 1.7 %slice_add_fusion.2 = (f32[4,16,512]{2,1,0:T(8,128)S(1)}, f32[4,16,512]{2,1,0:T(8,128)}) fusion(f32[4,64,512]{2,1,0:T(8,128)} %copy-done.13, f32[4,64,512]{2,1,0:T(8,128)S(1)} %get-tuple-element.24.keep_ref), kind=kLoop, calls=%fused_computation.60 | loop fusion | flops 65536 | bytes 786432 | tf_op jit(solution)/shard_map/add | solution.py:276
  48.8 3.2 %collective-permute-start.5 = (f32[4,16,512]{2,1,0:T(8,128)}, f32[4,16,512]{2,1,0:T(8,128)S(1)}, u32[]{:S(2)}, u32[]{:S(2)}) collective-permute-start(f32[4,16,512]{2,1,0:T(8,128)} %get-tuple-element.64), channel_id=1, source_target_pairs={{0,4},{4,8},{8,12},{12,16},{16,20},{20,24},{24,28},{28,32},{32,36}... | collective-permute-start | bytes 393224 | tf_op jit(solution)/shard_map/ppermute | solution.py:277
  52.1 6.6 %collective-permute-start.6 = (f32[4,16,512]{2,1,0:T(8,128)S(1)}, f32[4,16,512]{2,1,0:T(8,128)S(1)}, u32[]{:S(2)}, u32[]{:S(2)}) collective-permute-start(f32[4,16,512]{2,1,0:T(8,128)S(1)} %get-tuple-element.63), channel_id=1, source_target_pairs={{4,0},{8,4},{12,8},{16,12},{20,16},{24,20},{28,24},{32,28},{36,32}... | collective-permute-start | bytes 393224 | tf_op jit(solution)/shard_map/ppermute | solution.py:278
  59.4 1.5 dynamic-slice_bitcast_fusion.6
  61.0 4.6 %collective-permute-done.5.low_ref = f32[4,16,512]{2,1,0:T(8,128)S(1)} collective-permute-done((f32[4,16,512]{2,1,0:T(8,128)}, f32[4,16,512]{2,1,0:T(8,128)S(1)}, u32[]{:S(2)}, u32[]{:S(2)}) %collective-permute-start.5) | collective-permute-done | bytes 131104 | tf_op jit(solution)/shard_map/ppermute | solution.py:277
  66.9 6.3 %shard_map.84 = f32[4,64,512]{2,1,0:T(8,128)} custom-call(f32[4,16,512]{2,1,0:T(8,128)} %copy-done.15, f32[4,64,512]{2,1,0:T(8,128)} %copy-done.11, f32[4,64,512]{2,1,0:T(8,128)} %copy-done.13, f32[4,16,512]{2,1,0:T(8,128)} %copy-done.16, f32[32,512]{1,0:T(8,128)} %get-tuple-element.116.cr_ref, f32[32,512]{1,0:T(8,128)} %get-tuple-element.115.ci_ref, ...), custom_call_target="tpu_custom_call" | custom-call | tf_op jit(solution)/shard_map/pallas_call | solution.py:218
  74.2 1.9 %collective-permute-start.9 = (f32[4,16,512]{2,1,0:T(8,128)S(1)}, f32[4,16,512]{2,1,0:T(8,128)S(1)}, u32[]{:S(2)}, u32[]{:S(2)}) collective-permute-start(f32[4,16,512]{2,1,0:T(8,128)S(1)} %get-tuple-element.60), channel_id=1, source_target_pairs={{0,4},{4,8},{8,12},{12,16},{16,20},{20,24},{24,28},{28,32},{32,36}... | collective-permute-start | bytes 393224 | tf_op jit(solution)/shard_map/ppermute | solution.py:277
  76.1 8.1 %collective-permute-start.10 = (f32[4,16,512]{2,1,0:T(8,128)S(1)}, f32[4,16,512]{2,1,0:T(8,128)S(1)}, u32[]{:S(2)}, u32[]{:S(2)}) collective-permute-start(f32[4,16,512]{2,1,0:T(8,128)S(1)} %get-tuple-element.59), channel_id=1, source_target_pairs={{4,0},{8,4},{12,8},{16,12},{20,16},{24,20},{28,24},{32,28},{36,32}... | collective-permute-start | bytes 393224 | tf_op jit(solution)/shard_map/ppermute | solution.py:278
  84.2 4.5 %collective-permute-done.9.low_ref = f32[4,16,512]{2,1,0:T(8,128)S(1)} collective-permute-done((f32[4,16,512]{2,1,0:T(8,128)S(1)}, f32[4,16,512]{2,1,0:T(8,128)S(1)}, u32[]{:S(2)}, u32[]{:S(2)}) %collective-permute-start.9) | collective-permute-done | bytes 131104 | tf_op jit(solution)/shard_map/ppermute | solution.py:277
  90.0 6.3 %shard_map.85 = f32[4,64,512]{2,1,0:T(8,128)} custom-call(f32[4,16,512]{2,1,0:T(8,128)} %copy-done.17, f32[4,64,512]{2,1,0:T(8,128)} %copy-done.10, f32[4,64,512]{2,1,0:T(8,128)} %collective-permute-done.7.recv_ref, f32[4,16,512]{2,1,0:T(8,128)} %copy-done.18, f32[32,512]{1,0:T(8,128)} %get-tuple-element.116.cr_ref, f32[32,512]{1,0:T(8,128)} %get-tuple-element.115.ci_ref, ...), custom_call_target="tpu_custom_call" | custom-call | tf_op jit(solution)/shard_map/pallas_call | solution.py:218
  98.7 2.9 %collective-permute-start.11 = (f32[2,4,64,512]{3,2,1,0:T(8,128)}, f32[2,4,64,512]{3,2,1,0:T(8,128)}, u32[]{:S(2)}, u32[]{:S(2)}) collective-permute-start(f32[2,4,64,512]{3,2,1,0:T(8,128)} %pad_maximum_fusion.4), channel_id=1, source_target_pairs={{0,1},{1,0},{2,3},{3,2},{4,5},{5,4},{6,7},{7,6},{8,9},{9,8},{10,11... | collective-permute-start | bytes 3145736 | tf_op jit(solution)/shard_map/ppermute | solution.py:47
  101.6 2.6 %collective-permute-done.11 = f32[2,4,64,512]{3,2,1,0:T(8,128)} collective-permute-done((f32[2,4,64,512]{3,2,1,0:T(8,128)}, f32[2,4,64,512]{3,2,1,0:T(8,128)}, u32[]{:S(2)}, u32[]{:S(2)}) %collective-permute-start.11) | collective-permute-done | bytes 1048608 | tf_op jit(solution)/shard_map/ppermute | solution.py:47
  106.0 1.5 copy.19
  107.6 1.9 %collective-permute-start = (f32[128,8,2]{0,2,1:T(2,128)S(1)}, f32[128,8,2]{0,2,1:T(2,128)S(1)}, u32[]{:S(2)}, u32[]{:S(2)}) collective-permute-start(f32[128,8,2]{0,2,1:T(2,128)S(1)} %get-tuple-element.48), channel_id=1, source_target_pairs={{0,4},{4,8},{8,12},{12,16},{16,20},{20,24},{24,28},{28,32},{32,36}... | collective-permute-start | bytes 24584 | tf_op jit(solution)/shard_map/ppermute | solution.py:16
  109.5 7.9 %collective-permute-start.1 = (f32[128,8,2]{0,2,1:T(2,128)S(1)}, f32[128,8,2]{0,2,1:T(2,128)S(1)}, u32[]{:S(2)}, u32[]{:S(2)}) collective-permute-start(f32[128,8,2]{0,2,1:T(2,128)S(1)} %get-tuple-element.47), channel_id=1, source_target_pairs={{4,0},{8,4},{12,8},{16,12},{20,16},{24,20},{28,24},{32,28},{36,32}... | collective-permute-start | bytes 24584 | tf_op jit(solution)/shard_map/ppermute | solution.py:19
  117.4 12.5 %shard_map.86 = f32[8,128,256]{2,1,0:T(8,128)} custom-call(f32[4,4,64,512]{3,2,1,0:T(8,128)} %bitcast.109, f32[128,2048]{1,0:T(8,128)} %select_add_fusion.m_ref, f32[8,2048]{1,0:T(8,128)} %get-tuple-element.102.cos_ref, f32[8,2048]{1,0:T(8,128)} %get-tuple-element.101.sin_ref), custom_call_target="tpu_custom_call" | custom-call | tf_op jit(solution)/shard_map/pallas_call | solution.py:153
  133.6 2.3 %multiply_subtract_fusion.2 = (f32[128,4,512]{0,2,1:T(8,128)}, f32[128,4,512]{0,2,1:T(8,128)}, f32[128,4,512]{0,2,1:T(8,128)}, f32[128,4,512]{0,2,1:T(8,128)}) fusion(f32[128]{0:T(128)S(1)} %get-tuple-element.110, f32[128]{0:T(128)S(1)} %get-tuple-element.111, f32[128,8,512]{0,2,1:T(8,128)S(1)} %copy.12, f32[128,8,2]{0,2,1:T(2,128)S(1)} %collective-permute-done, ...), kind=kLoop, calls=%fused_computation.47 | loop fusion | flops 4980736 | bytes 6301696 | tf_op jit(solution)/shard_map/sub | solution.py:77
  135.9 2.3 %multiply_subtract_fusion = (f32[128,4,512]{0,2,1:T(8,128)}, f32[128,4,512]{0,2,1:T(8,128)}, f32[128,4,512]{0,2,1:T(8,128)}, f32[128,4,512]{0,2,1:T(8,128)}) fusion(f32[128]{0:T(128)S(1)} %get-tuple-element.114, f32[128]{0:T(128)S(1)} %get-tuple-element.107, f32[128,8,2]{0,2,1:T(2,128)S(1)} %collective-permute-done.1, f32[128,8,512]{0,2,1:T(8,128)S(1)} %copy.12, ...), kind=kLoop, calls=%fused_computation.43 | loop fusion | flops 4980736 | bytes 6301696 | tf_op jit(solution)/shard_map/sub | solution.py:77
  138.2 2.6 %copy.20 = f32[8,128,256]{1,2,0:T(8,128)} copy(f32[8,128,256]{2,1,0:T(8,128)} %shard_map.86) | data formatting | bytes 2097152 | tf_op jit(solution)/shard_map/optimization_barrier | solution.py:300
  142.6 1.6 copy.21
  144.1 12.5 %shard_map.87 = f32[8,128,256]{2,1,0:T(8,128)} custom-call(f32[4,4,64,512]{3,2,1,0:T(8,128)} %bitcast.112, f32[128,2048]{1,0:T(8,128)} %select_add_fusion.m_ref, f32[8,2048]{1,0:T(8,128)} %get-tuple-element.102.cos_ref, f32[8,2048]{1,0:T(8,128)} %get-tuple-element.101.sin_ref), custom_call_target="tpu_custom_call" | custom-call | tf_op jit(solution)/shard_map/pallas_call | solution.py:153
  156.6 2.6 %copy.22 = f32[8,128,256]{1,2,0:T(8,128)} copy(f32[8,128,256]{2,1,0:T(8,128)} %shard_map.87) | data formatting | bytes 2097152 | tf_op jit(solution)/shard_map/pallas_call | solution.py:153
  159.2 1.6 maximum_bitcast_fusion
  164.4 2.0 %copy.24 = f32[128,8,512]{2,1,0:T(8,128)} copy(f32[128,8,512]{0,2,1:T(8,128)S(1)} %fusion.3) | data formatting | bytes 4194304 | tf_op jit(solution)/shard_map/add | solution.py:305
  (92 shorter events, 31.2 us)
Async XLA Ops:
  2.2 1.4 copy-start.21
  19.7 3.3 %collective-permute-start.2 = (f32[2,4,64,512]{3,2,1,0:T(8,128)}, f32[2,4,64,512]{3,2,1,0:T(8,128)}, u32[]{:S(2)}, u32[]{:S(2)}) collective-permute-start(f32[2,4,64,512]{3,2,1,0:T(8,128)} %dynamic-slice_bitcast_fusion.1), channel_id=1, source_target_pairs={{0,1},{1,0},{2,3},{3,2},{4,5},{5,4},{6,7},{7,6},{8,9},{9,8},{10,11... | collective-permute-start | bytes 3145736 | tf_op jit(solution)/shard_map/ppermute | solution.py:33
  25.7 21.5 %copy-start.11 = (f32[4,64,512]{2,1,0:T(8,128)}, f32[4,64,512]{2,1,0:T(8,128)S(1)}, u32[]{:S(2)}) copy-start(f32[4,64,512]{2,1,0:T(8,128)S(1)} %get-tuple-element.24.keep_ref) | copy-start | bytes 1572868
  25.7 13.3 %collective-permute-start.3 = (f32[4,64,512]{2,1,0:T(8,128)}, f32[4,64,512]{2,1,0:T(8,128)S(1)}, u32[]{:S(2)}, u32[]{:S(2)}) collective-permute-start(f32[4,64,512]{2,1,0:T(8,128)} %get-tuple-element.65), channel_id=1, source_target_pairs={{0,2},{2,0},{1,3},{3,1},{4,6},{6,4},{5,7},{7,5},{8,10},{10,8},{9,1... | collective-permute-start | bytes 1572872 | tf_op jit(solution)/shard_map/ppermute | solution.py:284
  37.1 7.0 %copy-start = (f32[4,4,64,512]{3,2,1,0:T(8,128)S(1)}, f32[4,4,64,512]{3,2,1,0:T(8,128)}, u32[]{:S(2)}) copy-start(f32[4,4,64,512]{3,2,1,0:T(8,128)} %shard_map.83) | copy-start | bytes 6291460
  39.0 5.3 %copy-start.13 = (f32[4,64,512]{2,1,0:T(8,128)}, f32[4,64,512]{2,1,0:T(8,128)S(1)}, u32[]{:S(2)}) copy-start(f32[4,64,512]{2,1,0:T(8,128)S(1)} %collective-permute-done.3.recv_ref) | copy-start | bytes 1572868
  40.5 5.9 %copy-start.14 = (f32[2,32,2048]{2,1,0:T(8,128)S(1)}, f32[2,32,2048]{2,1,0:T(8,128)}, u32[]{:S(2)}) copy-start(f32[2,32,2048]{2,1,0:T(8,128)} %param.14) | copy-start | bytes 1572868
  40.5 3.6 %collective-permute-start.4 = (f32[2,4,64,512]{3,2,1,0:T(8,128)S(1)}, f32[2,4,64,512]{3,2,1,0:T(8,128)S(1)}, u32[]{:S(2)}, u32[]{:S(2)}) collective-permute-start(f32[2,4,64,512]{3,2,1,0:T(8,128)S(1)} %dynamic-slice_bitcast_fusion), channel_id=1, source_target_pairs={{0,1},{1,0},{2,3},{3,2},{4,5},{5,4},{6,7},{7,6},{8,9},{9,8},{10,11... | collective-permute-start | bytes 3145736 | tf_op jit(solution)/shard_map/ppermute | solution.py:33
  45.2 27.9 %copy-start.10 = (f32[4,64,512]{2,1,0:T(8,128)}, f32[4,64,512]{2,1,0:T(8,128)S(1)}, u32[]{:S(2)}) copy-start(f32[4,64,512]{2,1,0:T(8,128)S(1)} %get-tuple-element.61.keep_ref) | copy-start | bytes 1572868
  45.2 27.9 %collective-permute-start.7 = (f32[4,64,512]{2,1,0:T(8,128)}, f32[4,64,512]{2,1,0:T(8,128)}, u32[]{:S(2)}, u32[]{:S(2)}) collective-permute-start(f32[4,64,512]{2,1,0:T(8,128)} %get-tuple-element.62), channel_id=1, source_target_pairs={{0,2},{2,0},{1,3},{3,1},{4,6},{6,4},{5,7},{7,5},{8,10},{10,8},{9,1... | collective-permute-start | bytes 1572872 | tf_op jit(solution)/shard_map/ppermute | solution.py:290
  48.8 16.7 %collective-permute-start.5 = (f32[4,16,512]{2,1,0:T(8,128)}, f32[4,16,512]{2,1,0:T(8,128)S(1)}, u32[]{:S(2)}, u32[]{:S(2)}) collective-permute-start(f32[4,16,512]{2,1,0:T(8,128)} %get-tuple-element.64), channel_id=1, source_target_pairs={{0,4},{4,8},{8,12},{12,16},{16,20},{20,24},{24,28},{28,32},{32,36}... | collective-permute-start | bytes 393224 | tf_op jit(solution)/shard_map/ppermute | solution.py:277
  52.1 13.5 %collective-permute-start.6 = (f32[4,16,512]{2,1,0:T(8,128)S(1)}, f32[4,16,512]{2,1,0:T(8,128)S(1)}, u32[]{:S(2)}, u32[]{:S(2)}) collective-permute-start(f32[4,16,512]{2,1,0:T(8,128)S(1)} %get-tuple-element.63), channel_id=1, source_target_pairs={{4,0},{8,4},{12,8},{16,12},{20,16},{24,20},{28,24},{32,28},{36,32}... | collective-permute-start | bytes 393224 | tf_op jit(solution)/shard_map/ppermute | solution.py:278
  73.1 23.1 %collective-permute-start.8 = (f32[4,64,512]{2,1,0:T(8,128)}, f32[4,64,512]{2,1,0:T(8,128)}, u32[]{:S(2)}, u32[]{:S(2)}) collective-permute-start(f32[4,64,512]{2,1,0:T(8,128)} %shard_map.84), channel_id=1, source_target_pairs={{0,2},{2,0},{1,3},{3,1},{4,6},{6,4},{5,7},{7,5},{8,10},{10,8},{9,1... | collective-permute-start | bytes 1572872 | tf_op jit(solution)/shard_map/ppermute | solution.py:293
  74.2 14.5 %collective-permute-start.9 = (f32[4,16,512]{2,1,0:T(8,128)S(1)}, f32[4,16,512]{2,1,0:T(8,128)S(1)}, u32[]{:S(2)}, u32[]{:S(2)}) collective-permute-start(f32[4,16,512]{2,1,0:T(8,128)S(1)} %get-tuple-element.60), channel_id=1, source_target_pairs={{0,4},{4,8},{8,12},{12,16},{16,20},{20,24},{24,28},{28,32},{32,36}... | collective-permute-start | bytes 393224 | tf_op jit(solution)/shard_map/ppermute | solution.py:277
  76.1 12.6 %collective-permute-start.10 = (f32[4,16,512]{2,1,0:T(8,128)S(1)}, f32[4,16,512]{2,1,0:T(8,128)S(1)}, u32[]{:S(2)}, u32[]{:S(2)}) collective-permute-start(f32[4,16,512]{2,1,0:T(8,128)S(1)} %get-tuple-element.59), channel_id=1, source_target_pairs={{4,0},{8,4},{12,8},{16,12},{20,16},{24,20},{28,24},{32,28},{36,32}... | collective-permute-start | bytes 393224 | tf_op jit(solution)/shard_map/ppermute | solution.py:278
  98.7 5.6 %collective-permute-start.11 = (f32[2,4,64,512]{3,2,1,0:T(8,128)}, f32[2,4,64,512]{3,2,1,0:T(8,128)}, u32[]{:S(2)}, u32[]{:S(2)}) collective-permute-start(f32[2,4,64,512]{3,2,1,0:T(8,128)} %pad_maximum_fusion.4), channel_id=1, source_target_pairs={{0,1},{1,0},{2,3},{3,2},{4,5},{5,4},{6,7},{7,6},{8,9},{9,8},{10,11... | collective-permute-start | bytes 3145736 | tf_op jit(solution)/shard_map/ppermute | solution.py:47
  106.0 1.6 copy-start.12
  107.6 22.3 %collective-permute-start.12 = (f32[4,64,512]{2,1,0:T(8,128)S(1)}, f32[4,64,512]{2,1,0:T(8,128)}, u32[]{:S(2)}, u32[]{:S(2)}) collective-permute-start(f32[4,64,512]{2,1,0:T(8,128)S(1)} %copy-done.12), channel_id=1, source_target_pairs={{0,2},{2,0},{1,3},{3,1},{4,6},{6,4},{5,7},{7,5},{8,10},{10,8},{9,1... | collective-permute-start | bytes 1572872 | tf_op jit(solution)/shard_map/ppermute | solution.py:298
  107.6 26.0 %collective-permute-start = (f32[128,8,2]{0,2,1:T(2,128)S(1)}, f32[128,8,2]{0,2,1:T(2,128)S(1)}, u32[]{:S(2)}, u32[]{:S(2)}) collective-permute-start(f32[128,8,2]{0,2,1:T(2,128)S(1)} %get-tuple-element.48), channel_id=1, source_target_pairs={{0,4},{4,8},{8,12},{12,16},{16,20},{20,24},{24,28},{28,32},{32,36}... | collective-permute-start | bytes 24584 | tf_op jit(solution)/shard_map/ppermute | solution.py:16
  109.5 26.4 %collective-permute-start.1 = (f32[128,8,2]{0,2,1:T(2,128)S(1)}, f32[128,8,2]{0,2,1:T(2,128)S(1)}, u32[]{:S(2)}, u32[]{:S(2)}) collective-permute-start(f32[128,8,2]{0,2,1:T(2,128)S(1)} %get-tuple-element.47), channel_id=1, source_target_pairs={{4,0},{8,4},{12,8},{16,12},{20,16},{24,20},{28,24},{32,28},{36,32}... | collective-permute-start | bytes 24584 | tf_op jit(solution)/shard_map/ppermute | solution.py:19
  129.9 3.7 %copy-start.22 = (s32[4,512]{1,0:T(4,128)S(1)}, s32[4,512]{1,0:T(4,128)}, u32[]{:S(2)}) copy-start(s32[4,512]{1,0:T(4,128)} %param.10) | copy-start | bytes 24580
  129.9 3.7 %copy-start.23 = (f32[2,4,128]{2,1,0:T(4,128)S(1)}, f32[2,4,128]{2,1,0:T(4,128)}, u32[]{:S(2)}) copy-start(f32[2,4,128]{2,1,0:T(4,128)} %param.9) | copy-start | bytes 12292
  132.4 8.5 %collective-permute-start.13 = (f32[2,4,64,512]{3,2,1,0:T(8,128)}, f32[2,4,64,512]{3,2,1,0:T(8,128)}, u32[]{:S(2)}, u32[]{:S(2)}) collective-permute-start(f32[2,4,64,512]{3,2,1,0:T(8,128)} %pad_maximum_fusion.5), channel_id=1, source_target_pairs={{0,1},{1,0},{2,3},{3,2},{4,5},{5,4},{6,7},{7,6},{8,9},{9,8},{10,11... | collective-permute-start | bytes 3145736 | tf_op jit(solution)/shard_map/ppermute | solution.py:47
  156.6 2.6 %copy-start.1 = (f32[8,128,256]{1,2,0:T(8,128)S(1)}, f32[8,128,256]{1,2,0:T(8,128)}, u32[]{:S(2)}) copy-start(f32[8,128,256]{1,2,0:T(8,128)} %copy.20) | copy-start | bytes 3145732
  159.2 2.8 %copy-start.6 = (f32[128,4,512]{0,2,1:T(8,128)S(1)}, f32[128,4,512]{0,2,1:T(8,128)}, u32[]{:S(2)}) copy-start(f32[128,4,512]{0,2,1:T(8,128)} %get-tuple-element.35) | copy-start | bytes 3145732
  159.2 2.8 %copy-start.7 = (f32[128,4,512]{0,2,1:T(8,128)S(1)}, f32[128,4,512]{0,2,1:T(8,128)}, u32[]{:S(2)}) copy-start(f32[128,4,512]{0,2,1:T(8,128)} %get-tuple-element.36) | copy-start | bytes 3145732
  159.2 2.9 %copy-start.8 = (f32[128,4,512]{0,2,1:T(8,128)S(1)}, f32[128,4,512]{0,2,1:T(8,128)}, u32[]{:S(2)}) copy-start(f32[128,4,512]{0,2,1:T(8,128)} %get-tuple-element.43) | copy-start | bytes 3145732
  159.2 2.9 %copy-start.9 = (f32[128,4,512]{0,2,1:T(8,128)S(1)}, f32[128,4,512]{0,2,1:T(8,128)}, u32[]{:S(2)}) copy-start(f32[128,4,512]{0,2,1:T(8,128)} %get-tuple-element.44) | copy-start | bytes 3145732
  160.8 1.5 copy-start.2
  160.8 1.8 %copy-start.3 = (f32[128,4,512]{0,2,1:T(8,128)S(1)}, f32[128,4,512]{0,2,1:T(8,128)}, u32[]{:S(2)}) copy-start(f32[128,4,512]{0,2,1:T(8,128)} %get-tuple-element.40) | copy-start | bytes 3145732
  160.8 2.1 %copy-start.4 = (f32[128,4,512]{0,2,1:T(8,128)S(1)}, f32[128,4,512]{0,2,1:T(8,128)}, u32[]{:S(2)}) copy-start(f32[128,4,512]{0,2,1:T(8,128)} %get-tuple-element.45) | copy-start | bytes 3145732
  160.8 2.3 %copy-start.5 = (f32[128,4,512]{0,2,1:T(8,128)S(1)}, f32[128,4,512]{0,2,1:T(8,128)}, u32[]{:S(2)}) copy-start(f32[128,4,512]{0,2,1:T(8,128)} %get-tuple-element.46) | copy-start | bytes 3145732
  (6 other events, 6.5 us)

commit v8 on v7

--- a/solution.py
+++ b/solution.py
@@ -247,7 +247,23 @@
     rows = interp_matrix(interp_index, interp_weight, child_first, child_dev)
 
     child_reach = child_coef.shape[1] // 2
-    child_padded = with_halo(pattern, (("box", 2),), child_reach)
+    box_count = lax.axis_size("box")
+    edge_up = [(i, i + 1) for i in range(box_count - 1)]
+    edge_down = [(i + 1, i) for i in range(box_count - 1)]
+
+    def edge_send(piece, pairs):
+        flat = piece.transpose(2, 0, 1).reshape(piece.shape[2], -1)
+        got = lax.ppermute(flat, "box", pairs)
+        return got.reshape(piece.shape[2], child_dev, comps).transpose(1, 2, 0)
+
+    child_padded = jnp.concatenate(
+        [
+            edge_send(pattern[:, :, box_dev - child_reach :], edge_up),
+            pattern,
+            edge_send(pattern[:, :, :child_reach], edge_down),
+        ],
+        axis=2,
+    )
     child_local = translate_padded(
         child_padded, child_coef[0], child_coef[1], child_mask, child_reach
     )

time: 167 us -> 171 us (1.024)
  local copies, waits for them, and re-layouts: 28.7 us -> 32.3 us
    reshape x0 -> x5, local copies, waits for them, and re-layouts: none -> 2.62 us  [the longest x3 2.4 us: edge_send(): flat = piece.transpose(2, 0, 1).reshape(piece.shape[2], -1)]
    unnamed x49 -> x51, local copies, waits for them, and re-layouts: 4.48 us -> 5.42 us
  transfers between devices with their start and end apart: 14 -> 14, of which waited for: 6 -> 6; matrix products, arithmetic and copies ran while one was open for 11% -> 12% of each run, Pallas kernels for 21% -> 21%
where the time goes in v8:
time: 171 us; the launch traced here: 170 us
  Pallas kernels  58 us (34%)
  starting transfers between devices  37.8 us (22%)
  local copies, waits for them, and re-layouts  32.3 us (19%)
  other arithmetic  23.7 us (14%)
  waiting for transfers between devices  17.4 us (10%)
    pallas_call x2, Pallas kernels, downward(): pl.pallas_call(downward_kernel, grid=(groups,), in_specs=[pl.BlockSpec((p...  25 us
    pallas_call x2, Pallas kernels, upward(): pl.pallas_call(upward_kernel, grid=(parts,), in_specs=[pl.BlockSpec((grou...  20.5 us
    ppermute x2, starting transfers between devices, translate(): high = lax.ppermute(high, 'box', backward)  14.6 us
    pallas_call x2, Pallas kernels, translate_call(): pl.pallas_call(translate_kernel, out_shape=jax.ShapeDtypeStruct(keep.shap...  12.5 us
    ppermute x2, starting transfers between devices, edge_send(): got = lax.ppermute(flat, 'box', pairs)  9.8 us
    ppermute x2, waiting for transfers between devices, translate(): low = lax.ppermute(low, 'box', forward)  9.09 us
    unnamed x51, local copies, waits for them, and re-layouts  5.42 us
    ppermute x2, starting transfers between devices, translate(): low = lax.ppermute(low, 'box', forward)  5.11 us
  transfers between devices with their start and end apart: 14, of which 6 were waited for; matrix products, arithmetic and copies ran while one was open for 12% of the time, Pallas kernels for 21%

profile of v8, /device:TPU:65, one launch (start us, length us, event | category | flops | bytes accessed | tf_op | source)
XLA Modules:
  0.0 169.6 jit_solution(4573535123603144698)
XLA Ops:
  0.0 2.0 %copy.25 = f32[128,8,512]{0,2,1:T(8,128)S(1)} copy(f32[128,8,512]{2,1,0:T(8,128)} %param.8) | data formatting | bytes 4194304 | tf_op args[0]
  4.5 2.7 %select_add_fusion.m_ref = f32[128,2048]{1,0:T(8,128)} fusion(f32[2048]{0:T(1024)S(1)} %bitcast.146, s32[2048]{0:T(1024)S(1)} %bitcast.162, f32[2048]{0:T(1024)S(1)} %bitcast.147, s32[2048]{0:T(1024)S(1)} %bitcast.163, f32[2048]{0:T(1024)S(1)} %bitcast.133, s32[2048]{0:T(1024)S(1)} %bitcast.149, f32[2048]{0:T(1024)S(1)} %bitcast.134, s32[2048]{0:T(1024)S(1)} %bitcast.150, ...), kind=kLoop, calls=%fused_computation.41 | loop fusion | flops 12320768 | bytes 1311232 | tf_op jit(solution)/shard_map/add | solution.py:57
  7.1 10.2 %shard_map.82 = f32[4,4,64,512]{3,2,1,0:T(8,128)} custom-call(f32[8,256,128]{2,1,0:T(8,128)} %bitcast.125, f32[128,2048]{1,0:T(8,128)} %select_add_fusion.m_ref, f32[8,2048]{1,0:T(8,128)} %get-tuple-element.102.cos_ref, f32[8,2048]{1,0:T(8,128)} %get-tuple-element.101.sin_ref), custom_call_target="tpu_custom_call" | custom-call | tf_op jit(solution)/shard_map/pallas_call | solution.py:111
  17.4 2.3 %dynamic-slice_bitcast_fusion.1 = f32[2,4,64,512]{3,2,1,0:T(8,128)} fusion(f32[2,2,4,64,512]{4,3,2,1,0:T(8,128)} %bitcast.117, s32[]{:T(128)S(6)} %select_n.155), kind=kLoop, calls=%fused_computation.40 | loop fusion | bytes 2097156 | tf_op jit(solution)/shard_map/jit(dynamic_index_in_dim)/squeeze | solution.py:32
  23.0 1.8 %bitcast_add_fusion.1 = f32[2,4,64,512]{3,2,1,0:T(8,128)S(1)} fusion(f32[2,4,64,512]{3,2,1,0:T(8,128)} %collective-permute-done.2, f32[2,2,4,64,512]{4,3,2,1,0:T(8,128)} %bitcast.118, s32[]{:T(128)S(6)} %select_n.154), kind=kLoop, calls=%fused_computation.34 | loop fusion | flops 262144 | bytes 3145732 | tf_op jit(solution)/shard_map/add | solution.py:33
  26.9 10.2 %shard_map.83 = f32[4,4,64,512]{3,2,1,0:T(8,128)} custom-call(f32[8,256,128]{2,1,0:T(8,128)} %bitcast.126, f32[128,2048]{1,0:T(8,128)} %select_add_fusion.m_ref, f32[8,2048]{1,0:T(8,128)} %get-tuple-element.102.cos_ref, f32[8,2048]{1,0:T(8,128)} %get-tuple-element.101.sin_ref), custom_call_target="tpu_custom_call" | custom-call | tf_op jit(solution)/shard_map/pallas_call | solution.py:111
  37.1 1.9 %collective-permute-done.3.recv_ref = f32[4,64,512]{2,1,0:T(8,128)S(1)} collective-permute-done((f32[4,64,512]{2,1,0:T(8,128)}, f32[4,64,512]{2,1,0:T(8,128)S(1)}, u32[]{:S(2)}, u32[]{:S(2)}) %collective-permute-start.3) | collective-permute-done | bytes 524320 | tf_op jit(solution)/shard_map/ppermute | solution.py:300
  41.8 2.3 %collective-permute-done.4 = f32[2,4,64,512]{3,2,1,0:T(8,128)S(1)} collective-permute-done((f32[2,4,64,512]{3,2,1,0:T(8,128)S(1)}, f32[2,4,64,512]{3,2,1,0:T(8,128)S(1)}, u32[]{:S(2)}, u32[]{:S(2)}) %collective-permute-start.4) | collective-permute-done | bytes 1048608 | tf_op jit(solution)/shard_map/ppermute | solution.py:33
  47.1 1.7 slice_add_fusion.2
  48.8 3.2 %collective-permute-start.5 = (f32[4,16,512]{2,1,0:T(8,128)}, f32[4,16,512]{2,1,0:T(8,128)S(1)}, u32[]{:S(2)}, u32[]{:S(2)}) collective-permute-start(f32[4,16,512]{2,1,0:T(8,128)} %get-tuple-element.64), channel_id=1, source_target_pairs={{0,4},{4,8},{8,12},{12,16},{16,20},{20,24},{24,28},{28,32},{32,36}... | collective-permute-start | bytes 393224 | tf_op jit(solution)/shard_map/ppermute | solution.py:293
  52.0 6.6 %collective-permute-start.6 = (f32[4,16,512]{2,1,0:T(8,128)S(1)}, f32[4,16,512]{2,1,0:T(8,128)S(1)}, u32[]{:S(2)}, u32[]{:S(2)}) collective-permute-start(f32[4,16,512]{2,1,0:T(8,128)S(1)} %get-tuple-element.63), channel_id=1, source_target_pairs={{4,0},{8,4},{12,8},{16,12},{20,16},{24,20},{28,24},{32,28},{36,32}... | collective-permute-start | bytes 393224 | tf_op jit(solution)/shard_map/ppermute | solution.py:294
  59.4 1.5 dynamic-slice_bitcast_fusion.6
  60.9 4.6 %collective-permute-done.5.low_ref = f32[4,16,512]{2,1,0:T(8,128)S(1)} collective-permute-done((f32[4,16,512]{2,1,0:T(8,128)}, f32[4,16,512]{2,1,0:T(8,128)S(1)}, u32[]{:S(2)}, u32[]{:S(2)}) %collective-permute-start.5) | collective-permute-done | bytes 131104 | tf_op jit(solution)/shard_map/ppermute | solution.py:293
  66.8 6.3 %shard_map.84 = f32[4,64,512]{2,1,0:T(8,128)} custom-call(f32[4,16,512]{2,1,0:T(8,128)} %copy-done.16, f32[4,64,512]{2,1,0:T(8,128)} %copy-done.12, f32[4,64,512]{2,1,0:T(8,128)} %copy-done.14, f32[4,16,512]{2,1,0:T(8,128)} %copy-done.17, f32[32,512]{1,0:T(8,128)} %get-tuple-element.116.cr_ref, f32[32,512]{1,0:T(8,128)} %get-tuple-element.115.ci_ref, ...), custom_call_target="tpu_custom_call" | custom-call | tf_op jit(solution)/shard_map/pallas_call | solution.py:218
  74.1 1.9 %collective-permute-start.9 = (f32[4,16,512]{2,1,0:T(8,128)S(1)}, f32[4,16,512]{2,1,0:T(8,128)S(1)}, u32[]{:S(2)}, u32[]{:S(2)}) collective-permute-start(f32[4,16,512]{2,1,0:T(8,128)S(1)} %get-tuple-element.60), channel_id=1, source_target_pairs={{0,4},{4,8},{8,12},{12,16},{16,20},{20,24},{24,28},{28,32},{32,36}... | collective-permute-start | bytes 393224 | tf_op jit(solution)/shard_map/ppermute | solution.py:293
  76.1 8.1 %collective-permute-start.10 = (f32[4,16,512]{2,1,0:T(8,128)S(1)}, f32[4,16,512]{2,1,0:T(8,128)S(1)}, u32[]{:S(2)}, u32[]{:S(2)}) collective-permute-start(f32[4,16,512]{2,1,0:T(8,128)S(1)} %get-tuple-element.59), channel_id=1, source_target_pairs={{4,0},{8,4},{12,8},{16,12},{20,16},{24,20},{28,24},{32,28},{36,32}... | collective-permute-start | bytes 393224 | tf_op jit(solution)/shard_map/ppermute | solution.py:294
  84.1 4.5 %collective-permute-done.9.low_ref = f32[4,16,512]{2,1,0:T(8,128)S(1)} collective-permute-done((f32[4,16,512]{2,1,0:T(8,128)S(1)}, f32[4,16,512]{2,1,0:T(8,128)S(1)}, u32[]{:S(2)}, u32[]{:S(2)}) %collective-permute-start.9) | collective-permute-done | bytes 131104 | tf_op jit(solution)/shard_map/ppermute | solution.py:293
  89.9 6.3 %shard_map.85 = f32[4,64,512]{2,1,0:T(8,128)} custom-call(f32[4,16,512]{2,1,0:T(8,128)} %copy-done.18, f32[4,64,512]{2,1,0:T(8,128)} %copy-done.11, f32[4,64,512]{2,1,0:T(8,128)} %collective-permute-done.7.recv_ref, f32[4,16,512]{2,1,0:T(8,128)} %copy-done.19, f32[32,512]{1,0:T(8,128)} %get-tuple-element.116.cr_ref, f32[32,512]{1,0:T(8,128)} %get-tuple-element.115.ci_ref, ...), custom_call_target="tpu_custom_call" | custom-call | tf_op jit(solution)/shard_map/pallas_call | solution.py:218
  98.6 2.9 %collective-permute-start.11 = (f32[2,4,64,512]{3,2,1,0:T(8,128)}, f32[2,4,64,512]{3,2,1,0:T(8,128)}, u32[]{:S(2)}, u32[]{:S(2)}) collective-permute-start(f32[2,4,64,512]{3,2,1,0:T(8,128)} %pad_maximum_fusion.4), channel_id=1, source_target_pairs={{0,1},{1,0},{2,3},{3,2},{4,5},{5,4},{6,7},{7,6},{8,9},{9,8},{10,11... | collective-permute-start | bytes 3145736 | tf_op jit(solution)/shard_map/ppermute | solution.py:47
  101.6 2.6 %collective-permute-done.11 = f32[2,4,64,512]{3,2,1,0:T(8,128)} collective-permute-done((f32[2,4,64,512]{3,2,1,0:T(8,128)}, f32[2,4,64,512]{3,2,1,0:T(8,128)}, u32[]{:S(2)}, u32[]{:S(2)}) %collective-permute-start.11) | collective-permute-done | bytes 1048608 | tf_op jit(solution)/shard_map/ppermute | solution.py:47
  106.0 1.5 copy.32
  110.7 1.9 %collective-permute-start = (f32[2,1024]{1,0:T(2,128)S(1)}, f32[2,1024]{1,0:T(2,128)S(1)}, u32[]{:S(2)}, u32[]{:S(2)}) collective-permute-start(f32[2,1024]{1,0:T(2,128)S(1)} %copy.23), channel_id=1, source_target_pairs={{0,4},{4,8},{8,12},{12,16},{16,20},{20,24},{24,28},{28,32},{32,36}... | collective-permute-start | bytes 24584 | tf_op jit(solution)/shard_map/ppermute | solution.py:256
  112.8 7.9 %collective-permute-start.1 = (f32[2,1024]{1,0:T(2,128)S(1)}, f32[2,1024]{1,0:T(2,128)S(1)}, u32[]{:S(2)}, u32[]{:S(2)}) collective-permute-start(f32[2,1024]{1,0:T(2,128)S(1)} %copy.26), channel_id=1, source_target_pairs={{4,0},{8,4},{12,8},{16,12},{20,16},{24,20},{28,24},{32,28},{36,32}... | collective-permute-start | bytes 24584 | tf_op jit(solution)/shard_map/ppermute | solution.py:256
  120.7 12.5 %shard_map.86 = f32[8,128,256]{2,1,0:T(8,128)} custom-call(f32[4,4,64,512]{3,2,1,0:T(8,128)} %bitcast.119, f32[128,2048]{1,0:T(8,128)} %select_add_fusion.m_ref, f32[8,2048]{1,0:T(8,128)} %get-tuple-element.102.cos_ref, f32[8,2048]{1,0:T(8,128)} %get-tuple-element.101.sin_ref), custom_call_target="tpu_custom_call" | custom-call | tf_op jit(solution)/shard_map/pallas_call | solution.py:153
  137.0 2.2 %multiply_subtract_fusion.2 = (f32[128,4,512]{0,2,1:T(8,128)}, f32[128,4,512]{0,2,1:T(8,128)}, f32[128,4,512]{0,2,1:T(8,128)}, f32[128,4,512]{0,2,1:T(8,128)}) fusion(f32[128]{0:T(128)S(1)} %get-tuple-element.110, f32[128]{0:T(128)S(1)} %get-tuple-element.111, f32[128,8,512]{0,2,1:T(8,128)S(1)} %copy.25, f32[128,8,2]{0,2,1:T(2,128)S(1)} %copy.24, ...), kind=kLoop, calls=%fused_computation.47 | loop fusion | flops 4980736 | bytes 6301696 | tf_op jit(solution)/shard_map/sub | solution.py:77
  139.2 2.3 %multiply_subtract_fusion = (f32[128,4,512]{0,2,1:T(8,128)}, f32[128,4,512]{0,2,1:T(8,128)}, f32[128,4,512]{0,2,1:T(8,128)}, f32[128,4,512]{0,2,1:T(8,128)}) fusion(f32[128]{0:T(128)S(1)} %get-tuple-element.114, f32[128]{0:T(128)S(1)} %get-tuple-element.107, f32[128,8,2]{0,2,1:T(2,128)S(1)} %copy.28, f32[128,8,512]{0,2,1:T(8,128)S(1)} %copy.25, ...), kind=kLoop, calls=%fused_computation.43 | loop fusion | flops 4980736 | bytes 6301696 | tf_op jit(solution)/shard_map/sub | solution.py:77
  141.5 2.6 %copy.33 = f32[8,128,256]{1,2,0:T(8,128)} copy(f32[8,128,256]{2,1,0:T(8,128)} %shard_map.86) | data formatting | bytes 2097152 | tf_op jit(solution)/shard_map/optimization_barrier | solution.py:316
  145.9 1.6 copy.34
  147.4 12.5 %shard_map.87 = f32[8,128,256]{2,1,0:T(8,128)} custom-call(f32[4,4,64,512]{3,2,1,0:T(8,128)} %bitcast.122, f32[128,2048]{1,0:T(8,128)} %select_add_fusion.m_ref, f32[8,2048]{1,0:T(8,128)} %get-tuple-element.102.cos_ref, f32[8,2048]{1,0:T(8,128)} %get-tuple-element.101.sin_ref), custom_call_target="tpu_custom_call" | custom-call | tf_op jit(solution)/shard_map/pallas_call | solution.py:153
  159.9 2.6 %copy.35 = f32[8,128,256]{1,2,0:T(8,128)} copy(f32[8,128,256]{2,1,0:T(8,128)} %shard_map.87) | data formatting | bytes 2097152 | tf_op jit(solution)/shard_map/pallas_call | solution.py:153
  162.5 1.6 maximum_bitcast_fusion
  167.6 2.0 %copy.37 = f32[128,8,512]{2,1,0:T(8,128)} copy(f32[128,8,512]{0,2,1:T(8,128)S(1)} %fusion.3) | data formatting | bytes 4194304 | tf_op jit(solution)/shard_map/add | solution.py:321
  (100 shorter events, 34.5 us)
Async XLA Ops:
  19.7 3.3 %collective-permute-start.2 = (f32[2,4,64,512]{3,2,1,0:T(8,128)}, f32[2,4,64,512]{3,2,1,0:T(8,128)}, u32[]{:S(2)}, u32[]{:S(2)}) collective-permute-start(f32[2,4,64,512]{3,2,1,0:T(8,128)} %dynamic-slice_bitcast_fusion.1), channel_id=1, source_target_pairs={{0,1},{1,0},{2,3},{3,2},{4,5},{5,4},{6,7},{7,6},{8,9},{9,8},{10,11... | collective-permute-start | bytes 3145736 | tf_op jit(solution)/shard_map/ppermute | solution.py:33
  25.7 21.5 %copy-start.12 = (f32[4,64,512]{2,1,0:T(8,128)}, f32[4,64,512]{2,1,0:T(8,128)S(1)}, u32[]{:S(2)}) copy-start(f32[4,64,512]{2,1,0:T(8,128)S(1)} %get-tuple-element.24.keep_ref) | copy-start | bytes 1572868
  25.7 13.3 %collective-permute-start.3 = (f32[4,64,512]{2,1,0:T(8,128)}, f32[4,64,512]{2,1,0:T(8,128)S(1)}, u32[]{:S(2)}, u32[]{:S(2)}) collective-permute-start(f32[4,64,512]{2,1,0:T(8,128)} %get-tuple-element.65), channel_id=1, source_target_pairs={{0,2},{2,0},{1,3},{3,1},{4,6},{6,4},{5,7},{7,5},{8,10},{10,8},{9,1... | collective-permute-start | bytes 1572872 | tf_op jit(solution)/shard_map/ppermute | solution.py:300
  37.1 7.0 %copy-start = (f32[4,4,64,512]{3,2,1,0:T(8,128)S(1)}, f32[4,4,64,512]{3,2,1,0:T(8,128)}, u32[]{:S(2)}) copy-start(f32[4,4,64,512]{3,2,1,0:T(8,128)} %shard_map.83) | copy-start | bytes 6291460
  39.0 5.3 %copy-start.14 = (f32[4,64,512]{2,1,0:T(8,128)}, f32[4,64,512]{2,1,0:T(8,128)S(1)}, u32[]{:S(2)}) copy-start(f32[4,64,512]{2,1,0:T(8,128)S(1)} %collective-permute-done.3.recv_ref) | copy-start | bytes 1572868
  40.5 5.9 %copy-start.15 = (f32[2,32,2048]{2,1,0:T(8,128)S(1)}, f32[2,32,2048]{2,1,0:T(8,128)}, u32[]{:S(2)}) copy-start(f32[2,32,2048]{2,1,0:T(8,128)} %param.14) | copy-start | bytes 1572868
  40.5 3.6 %collective-permute-start.4 = (f32[2,4,64,512]{3,2,1,0:T(8,128)S(1)}, f32[2,4,64,512]{3,2,1,0:T(8,128)S(1)}, u32[]{:S(2)}, u32[]{:S(2)}) collective-permute-start(f32[2,4,64,512]{3,2,1,0:T(8,128)S(1)} %dynamic-slice_bitcast_fusion), channel_id=1, source_target_pairs={{0,1},{1,0},{2,3},{3,2},{4,5},{5,4},{6,7},{7,6},{8,9},{9,8},{10,11... | collective-permute-start | bytes 3145736 | tf_op jit(solution)/shard_map/ppermute | solution.py:33
  45.2 27.9 %copy-start.11 = (f32[4,64,512]{2,1,0:T(8,128)}, f32[4,64,512]{2,1,0:T(8,128)S(1)}, u32[]{:S(2)}) copy-start(f32[4,64,512]{2,1,0:T(8,128)S(1)} %get-tuple-element.61.keep_ref) | copy-start | bytes 1572868
  45.2 27.9 %collective-permute-start.7 = (f32[4,64,512]{2,1,0:T(8,128)}, f32[4,64,512]{2,1,0:T(8,128)}, u32[]{:S(2)}, u32[]{:S(2)}) collective-permute-start(f32[4,64,512]{2,1,0:T(8,128)} %get-tuple-element.62), channel_id=1, source_target_pairs={{0,2},{2,0},{1,3},{3,1},{4,6},{6,4},{5,7},{7,5},{8,10},{10,8},{9,1... | collective-permute-start | bytes 1572872 | tf_op jit(solution)/shard_map/ppermute | solution.py:306
  48.8 16.7 %collective-permute-start.5 = (f32[4,16,512]{2,1,0:T(8,128)}, f32[4,16,512]{2,1,0:T(8,128)S(1)}, u32[]{:S(2)}, u32[]{:S(2)}) collective-permute-start(f32[4,16,512]{2,1,0:T(8,128)} %get-tuple-element.64), channel_id=1, source_target_pairs={{0,4},{4,8},{8,12},{12,16},{16,20},{20,24},{24,28},{28,32},{32,36}... | collective-permute-start | bytes 393224 | tf_op jit(solution)/shard_map/ppermute | solution.py:293
  52.0 13.5 %collective-permute-start.6 = (f32[4,16,512]{2,1,0:T(8,128)S(1)}, f32[4,16,512]{2,1,0:T(8,128)S(1)}, u32[]{:S(2)}, u32[]{:S(2)}) collective-permute-start(f32[4,16,512]{2,1,0:T(8,128)S(1)} %get-tuple-element.63), channel_id=1, source_target_pairs={{4,0},{8,4},{12,8},{16,12},{20,16},{24,20},{28,24},{32,28},{36,32}... | collective-permute-start | bytes 393224 | tf_op jit(solution)/shard_map/ppermute | solution.py:294
  73.1 23.1 %collective-permute-start.8 = (f32[4,64,512]{2,1,0:T(8,128)}, f32[4,64,512]{2,1,0:T(8,128)}, u32[]{:S(2)}, u32[]{:S(2)}) collective-permute-start(f32[4,64,512]{2,1,0:T(8,128)} %shard_map.84), channel_id=1, source_target_pairs={{0,2},{2,0},{1,3},{3,1},{4,6},{6,4},{5,7},{7,5},{8,10},{10,8},{9,1... | collective-permute-start | bytes 1572872 | tf_op jit(solution)/shard_map/ppermute | solution.py:309
  74.1 14.5 %collective-permute-start.9 = (f32[4,16,512]{2,1,0:T(8,128)S(1)}, f32[4,16,512]{2,1,0:T(8,128)S(1)}, u32[]{:S(2)}, u32[]{:S(2)}) collective-permute-start(f32[4,16,512]{2,1,0:T(8,128)S(1)} %get-tuple-element.60), channel_id=1, source_target_pairs={{0,4},{4,8},{8,12},{12,16},{16,20},{20,24},{24,28},{28,32},{32,36}... | collective-permute-start | bytes 393224 | tf_op jit(solution)/shard_map/ppermute | solution.py:293
  76.1 12.6 %collective-permute-start.10 = (f32[4,16,512]{2,1,0:T(8,128)S(1)}, f32[4,16,512]{2,1,0:T(8,128)S(1)}, u32[]{:S(2)}, u32[]{:S(2)}) collective-permute-start(f32[4,16,512]{2,1,0:T(8,128)S(1)} %get-tuple-element.59), channel_id=1, source_target_pairs={{4,0},{8,4},{12,8},{16,12},{20,16},{24,20},{28,24},{32,28},{36,32}... | collective-permute-start | bytes 393224 | tf_op jit(solution)/shard_map/ppermute | solution.py:294
  98.6 5.6 %collective-permute-start.11 = (f32[2,4,64,512]{3,2,1,0:T(8,128)}, f32[2,4,64,512]{3,2,1,0:T(8,128)}, u32[]{:S(2)}, u32[]{:S(2)}) collective-permute-start(f32[2,4,64,512]{3,2,1,0:T(8,128)} %pad_maximum_fusion.4), channel_id=1, source_target_pairs={{0,1},{1,0},{2,3},{3,2},{4,5},{5,4},{6,7},{7,6},{8,9},{9,8},{10,11... | collective-permute-start | bytes 3145736 | tf_op jit(solution)/shard_map/ppermute | solution.py:47
  105.9 1.6 copy-start.13
  105.9 2.5 %copy-start.1 = (f32[128,8,512]{2,1,0:T(8,128)S(1)}, f32[128,8,512]{2,1,0:T(8,128)}, u32[]{:S(2)}) copy-start(f32[128,8,512]{2,1,0:T(8,128)} %param.8) | copy-start | bytes 6291460
  107.5 25.7 %collective-permute-start.12 = (f32[4,64,512]{2,1,0:T(8,128)S(1)}, f32[4,64,512]{2,1,0:T(8,128)}, u32[]{:S(2)}, u32[]{:S(2)}) collective-permute-start(f32[4,64,512]{2,1,0:T(8,128)S(1)} %copy-done.13), channel_id=1, source_target_pairs={{0,2},{2,0},{1,3},{3,1},{4,6},{6,4},{5,7},{7,5},{8,10},{10,8},{9,1... | collective-permute-start | bytes 1572872 | tf_op jit(solution)/shard_map/ppermute | solution.py:314
  110.7 25.9 %collective-permute-start = (f32[2,1024]{1,0:T(2,128)S(1)}, f32[2,1024]{1,0:T(2,128)S(1)}, u32[]{:S(2)}, u32[]{:S(2)}) collective-permute-start(f32[2,1024]{1,0:T(2,128)S(1)} %copy.23), channel_id=1, source_target_pairs={{0,4},{4,8},{8,12},{12,16},{16,20},{20,24},{24,28},{28,32},{32,36}... | collective-permute-start | bytes 24584 | tf_op jit(solution)/shard_map/ppermute | solution.py:256
  112.8 24.0 %collective-permute-start.1 = (f32[2,1024]{1,0:T(2,128)S(1)}, f32[2,1024]{1,0:T(2,128)S(1)}, u32[]{:S(2)}, u32[]{:S(2)}) collective-permute-start(f32[2,1024]{1,0:T(2,128)S(1)} %copy.26), channel_id=1, source_target_pairs={{4,0},{8,4},{12,8},{16,12},{20,16},{24,20},{28,24},{32,28},{36,32}... | collective-permute-start | bytes 24584 | tf_op jit(solution)/shard_map/ppermute | solution.py:256
  133.2 3.4 %copy-start.23 = (s32[4,512]{1,0:T(4,128)S(1)}, s32[4,512]{1,0:T(4,128)}, u32[]{:S(2)}) copy-start(s32[4,512]{1,0:T(4,128)} %param.10) | copy-start | bytes 24580
  133.2 3.4 %copy-start.24 = (f32[2,4,128]{2,1,0:T(4,128)S(1)}, f32[2,4,128]{2,1,0:T(4,128)}, u32[]{:S(2)}) copy-start(f32[2,4,128]{2,1,0:T(4,128)} %param.9) | copy-start | bytes 12292
  135.6 8.5 %collective-permute-start.13 = (f32[2,4,64,512]{3,2,1,0:T(8,128)}, f32[2,4,64,512]{3,2,1,0:T(8,128)}, u32[]{:S(2)}, u32[]{:S(2)}) collective-permute-start(f32[2,4,64,512]{3,2,1,0:T(8,128)} %pad_maximum_fusion.5), channel_id=1, source_target_pairs={{0,1},{1,0},{2,3},{3,2},{4,5},{5,4},{6,7},{7,6},{8,9},{9,8},{10,11... | collective-permute-start | bytes 3145736 | tf_op jit(solution)/shard_map/ppermute | solution.py:47
  159.9 2.6 %copy-start.2 = (f32[8,128,256]{1,2,0:T(8,128)S(1)}, f32[8,128,256]{1,2,0:T(8,128)}, u32[]{:S(2)}) copy-start(f32[8,128,256]{1,2,0:T(8,128)} %copy.33) | copy-start | bytes 3145732
  162.5 2.8 %copy-start.7 = (f32[128,4,512]{0,2,1:T(8,128)S(1)}, f32[128,4,512]{0,2,1:T(8,128)}, u32[]{:S(2)}) copy-start(f32[128,4,512]{0,2,1:T(8,128)} %get-tuple-element.35) | copy-start | bytes 3145732
  162.5 2.8 %copy-start.8 = (f32[128,4,512]{0,2,1:T(8,128)S(1)}, f32[128,4,512]{0,2,1:T(8,128)}, u32[]{:S(2)}) copy-start(f32[128,4,512]{0,2,1:T(8,128)} %get-tuple-element.36) | copy-start | bytes 3145732
  162.5 2.9 %copy-start.9 = (f32[128,4,512]{0,2,1:T(8,128)S(1)}, f32[128,4,512]{0,2,1:T(8,128)}, u32[]{:S(2)}) copy-start(f32[128,4,512]{0,2,1:T(8,128)} %get-tuple-element.43) | copy-start | bytes 3145732
  162.5 2.9 %copy-start.10 = (f32[128,4,512]{0,2,1:T(8,128)S(1)}, f32[128,4,512]{0,2,1:T(8,128)}, u32[]{:S(2)}) copy-start(f32[128,4,512]{0,2,1:T(8,128)} %get-tuple-element.44) | copy-start | bytes 3145732
  164.1 1.5 copy-start.3
  164.1 1.8 %copy-start.4 = (f32[128,4,512]{0,2,1:T(8,128)S(1)}, f32[128,4,512]{0,2,1:T(8,128)}, u32[]{:S(2)}) copy-start(f32[128,4,512]{0,2,1:T(8,128)} %get-tuple-element.40) | copy-start | bytes 3145732
  164.1 2.1 %copy-start.5 = (f32[128,4,512]{0,2,1:T(8,128)S(1)}, f32[128,4,512]{0,2,1:T(8,128)}, u32[]{:S(2)}) copy-start(f32[128,4,512]{0,2,1:T(8,128)} %get-tuple-element.45) | copy-start | bytes 3145732
  164.1 2.3 %copy-start.6 = (f32[128,4,512]{0,2,1:T(8,128)S(1)}, f32[128,4,512]{0,2,1:T(8,128)}, u32[]{:S(2)}) copy-start(f32[128,4,512]{0,2,1:T(8,128)} %get-tuple-element.46) | copy-start | bytes 3145732
  (7 other events, 7.8 us)

commit v9 on v7

--- a/solution.py
+++ b/solution.py
@@ -248,9 +248,6 @@
 
     child_reach = child_coef.shape[1] // 2
     child_padded = with_halo(pattern, (("box", 2),), child_reach)
-    child_local = translate_padded(
-        child_padded, child_coef[0], child_coef[1], child_mask, child_reach
-    )
 
     parent_reach = parent_coef.shape[1] // 2
     own_real = lax.dynamic_slice_in_dim(parent_coef[0], parent_first, parent_dev, 1)
@@ -278,7 +275,13 @@
         high = lax.ppermute(high, "box", backward)
         return translate_call(low, keep, recv, high, own_real, own_imag, mask_lanes)
 
-    acc_a = reduce_cores(upward(chunk_xt(0), rows, cosine, sine, dir_size, 2 * step))
+    field_a, child_padded = lax.optimization_barrier(
+        (upward(chunk_xt(0), rows, cosine, sine, dir_size, 2 * step), child_padded)
+    )
+    acc_a = reduce_cores(field_a)
+    child_local = translate_padded(
+        child_padded, child_coef[0], child_coef[1], child_mask, child_reach
+    )
     acc_a, xt_b = lax.optimization_barrier((acc_a, chunk_xt(1)))
     keep_a, send_a = split_rows(acc_a)
     recv_a = lax.ppermute(send_a, "dir", ROW_SWAP)

time: 167 us -> 170 us (1.018)
    ppermute x2, starting transfers between devices: 14.6 us -> 16.7 us  [translate(): high = lax.ppermute(high, 'box', backward)]
    concatenate x0 -> x1, other arithmetic: none -> 1.89 us  [with_halo(): block = jnp.concatenate([low, block, high], axis=dim)]
    unnamed x49 -> x51, local copies, waits for them, and re-layouts: 4.48 us -> 5.1 us
  transfers between devices with their start and end apart: 14 -> 14, of which waited for: 6 -> 8; matrix products, arithmetic and copies ran while one was open for 11% -> 13% of each run, Pallas kernels for 21% -> 27%
where the time goes in v9:
time: 170 us; the launch traced here: 169 us
  Pallas kernels  58 us (34%)
  starting transfers between devices  39.5 us (23%)
  local copies, waits for them, and re-layouts  28.2 us (17%)
  other arithmetic  24.8 us (15%)
  waiting for transfers between devices  18.2 us (11%)
    pallas_call x2, Pallas kernels, downward(): pl.pallas_call(downward_kernel, grid=(groups,), in_specs=[pl.BlockSpec((p...  24.9 us
    pallas_call x2, Pallas kernels, upward(): pl.pallas_call(upward_kernel, grid=(parts,), in_specs=[pl.BlockSpec((grou...  20.5 us
    ppermute x2, starting transfers between devices, translate(): high = lax.ppermute(high, 'box', backward)  16.7 us
    pallas_call x2, Pallas kernels, translate_call(): pl.pallas_call(translate_kernel, out_shape=jax.ShapeDtypeStruct(keep.shap...  12.6 us
    ppermute x2, waiting for transfers between devices, translate(): low = lax.ppermute(low, 'box', forward)  8.04 us
    ppermute x1, starting transfers between devices, with_halo(): lax.ppermute(lax.slice_in_dim(block, 0, width, axis=dim), axis, backward)  6.59 us
    sub x2, other arithmetic, translate_padded(): scale_real * real_part - scale_imag * imag_part  5.18 us
    unnamed x51, local copies, waits for them, and re-layouts  5.1 us
  transfers between devices with their start and end apart: 14, of which 8 were waited for; matrix products, arithmetic and copies ran while one was open for 13% of the time, Pallas kernels for 27%

profile of v9, /device:TPU:65, one launch (start us, length us, event | category | flops | bytes accessed | tf_op | source)
XLA Modules:
  0.0 169.1 jit_solution(3340143735038184659)
XLA Ops:
  0.0 2.0 %copy.12 = f32[128,8,512]{0,2,1:T(8,128)S(1)} copy(f32[128,8,512]{2,1,0:T(8,128)} %param.8) | data formatting | bytes 4194304 | tf_op args[0]
  2.1 3.2 %collective-permute-start = (f32[128,8,2]{0,2,1:T(2,128)S(1)}, f32[128,8,2]{0,2,1:T(2,128)S(1)}, u32[]{:S(2)}, u32[]{:S(2)}) collective-permute-start(f32[128,8,2]{0,2,1:T(2,128)S(1)} %get-tuple-element.57), channel_id=1, source_target_pairs={{0,4},{4,8},{8,12},{12,16},{16,20},{20,24},{24,28},{28,32},{32,36}... | collective-permute-start | bytes 24584 | tf_op jit(solution)/shard_map/ppermute | solution.py:16
  5.3 6.6 %collective-permute-start.1 = (f32[128,8,2]{0,2,1:T(2,128)S(1)}, f32[128,8,2]{0,2,1:T(2,128)S(1)}, u32[]{:S(2)}, u32[]{:S(2)}) collective-permute-start(f32[128,8,2]{0,2,1:T(2,128)S(1)} %get-tuple-element.58), channel_id=1, source_target_pairs={{4,0},{8,4},{12,8},{16,12},{20,16},{24,20},{28,24},{32,28},{36,32}... | collective-permute-start | bytes 24584 | tf_op jit(solution)/shard_map/ppermute | solution.py:19
  13.0 2.6 %select_add_fusion.m_ref = f32[128,2048]{1,0:T(8,128)} fusion(f32[2048]{0:T(1024)S(1)} %bitcast.150, s32[2048]{0:T(1024)S(1)} %bitcast.134, f32[2048]{0:T(1024)S(1)} %bitcast.151, s32[2048]{0:T(1024)S(1)} %bitcast.135, f32[2048]{0:T(1024)S(1)} %bitcast.137, s32[2048]{0:T(1024)S(1)} %bitcast.121, f32[2048]{0:T(1024)S(1)} %bitcast.138, s32[2048]{0:T(1024)S(1)} %bitcast.122, ...), kind=kLoop, calls=%fused_computation.30 | loop fusion | flops 12320768 | bytes 1311232 | tf_op jit(solution)/shard_map/add | solution.py:57
  16.8 2.4 %copy.13 = f32[8,4,64,128]{3,2,1,0:T(8,128)} copy(f32[8,4,64,128]{3,0,2,1:T(8,128)} %bitcast.118) | data formatting | bytes 2097152 | tf_op jit(solution)/shard_map/transpose | solution.py:261
  19.2 10.2 %shard_map.82 = f32[4,4,64,512]{3,2,1,0:T(8,128)} custom-call(f32[8,256,128]{2,1,0:T(8,128)} %bitcast.117, f32[128,2048]{1,0:T(8,128)} %select_add_fusion.m_ref, f32[8,2048]{1,0:T(8,128)} %get-tuple-element.106.cos_ref, f32[8,2048]{1,0:T(8,128)} %get-tuple-element.105.sin_ref), custom_call_target="tpu_custom_call" | custom-call | tf_op jit(solution)/shard_map/pallas_call | solution.py:111
  29.5 1.9 %pad_maximum_fusion = f32[128,8,516]{0,2,1:T(8,128)S(1)} fusion(f32[128,8,2]{0,2,1:T(2,128)S(1)} %collective-permute-done.1, f32[128,8,512]{0,2,1:T(8,128)} %copy-done, f32[128,8,2]{0,2,1:T(2,128)S(1)} %collective-permute-done), kind=kLoop, calls=%fused_computation | loop fusion | flops 1056768 | bytes 4227072 | tf_op jit(solution)/shard_map/concatenate | solution.py:20
  36.6 1.8 %bitcast_add_fusion.1 = f32[2,4,64,512]{3,2,1,0:T(8,128)S(1)} fusion(f32[2,4,64,512]{3,2,1,0:T(8,128)} %collective-permute-done.2, f32[2,2,4,64,512]{4,3,2,1,0:T(8,128)} %bitcast.107, s32[]{:T(128)S(6)} %select_n.154), kind=kLoop, calls=%fused_computation.15 | loop fusion | flops 262144 | bytes 3145732 | tf_op jit(solution)/shard_map/add | solution.py:33
  40.5 10.2 %shard_map.83 = f32[4,4,64,512]{3,2,1,0:T(8,128)} custom-call(f32[8,256,128]{2,1,0:T(8,128)} %bitcast.115, f32[128,2048]{1,0:T(8,128)} %select_add_fusion.m_ref, f32[8,2048]{1,0:T(8,128)} %get-tuple-element.106.cos_ref, f32[8,2048]{1,0:T(8,128)} %get-tuple-element.105.sin_ref), custom_call_target="tpu_custom_call" | custom-call | tf_op jit(solution)/shard_map/pallas_call | solution.py:111
  50.8 1.9 %collective-permute-done.3.recv_ref = f32[4,64,512]{2,1,0:T(8,128)S(1)} collective-permute-done((f32[4,64,512]{2,1,0:T(8,128)}, f32[4,64,512]{2,1,0:T(8,128)S(1)}, u32[]{:S(2)}, u32[]{:S(2)}) %collective-permute-start.3) | collective-permute-done | bytes 524320 | tf_op jit(solution)/shard_map/ppermute | solution.py:287
  55.5 2.3 %collective-permute-done.4 = f32[2,4,64,512]{3,2,1,0:T(8,128)S(1)} collective-permute-done((f32[2,4,64,512]{3,2,1,0:T(8,128)S(1)}, f32[2,4,64,512]{3,2,1,0:T(8,128)S(1)}, u32[]{:S(2)}, u32[]{:S(2)}) %collective-permute-start.4) | collective-permute-done | bytes 1048608 | tf_op jit(solution)/shard_map/ppermute | solution.py:33
  60.8 1.7 %slice_add_fusion.2 = (f32[4,16,512]{2,1,0:T(8,128)}, f32[4,16,512]{2,1,0:T(8,128)}) fusion(f32[4,64,512]{2,1,0:T(8,128)} %copy-done.14, f32[4,64,512]{2,1,0:T(8,128)S(1)} %get-tuple-element.28.keep_ref), kind=kLoop, calls=%fused_computation.41 | loop fusion | flops 65536 | bytes 786432 | tf_op jit(solution)/shard_map/add | solution.py:273
  62.5 1.9 %collective-permute-start.5 = (f32[4,16,512]{2,1,0:T(8,128)}, f32[4,16,512]{2,1,0:T(8,128)S(1)}, u32[]{:S(2)}, u32[]{:S(2)}) collective-permute-start(f32[4,16,512]{2,1,0:T(8,128)} %get-tuple-element.68), channel_id=1, source_target_pairs={{0,4},{4,8},{8,12},{12,16},{16,20},{20,24},{24,28},{28,32},{32,36}... | collective-permute-start | bytes 393224 | tf_op jit(solution)/shard_map/ppermute | solution.py:274
  64.4 7.9 %collective-permute-start.6 = (f32[4,16,512]{2,1,0:T(8,128)}, f32[4,16,512]{2,1,0:T(8,128)S(1)}, u32[]{:S(2)}, u32[]{:S(2)}) collective-permute-start(f32[4,16,512]{2,1,0:T(8,128)} %get-tuple-element.67), channel_id=1, source_target_pairs={{4,0},{8,4},{12,8},{16,12},{20,16},{24,20},{28,24},{32,28},{36,32}... | collective-permute-start | bytes 393224 | tf_op jit(solution)/shard_map/ppermute | solution.py:275
  73.1 1.5 dynamic-slice_bitcast_fusion.6
  76.4 6.3 %shard_map.84 = f32[4,64,512]{2,1,0:T(8,128)} custom-call(f32[4,16,512]{2,1,0:T(8,128)} %copy-done.16, f32[4,64,512]{2,1,0:T(8,128)} %copy-done.12, f32[4,64,512]{2,1,0:T(8,128)} %copy-done.14, f32[4,16,512]{2,1,0:T(8,128)} %copy-done.17, f32[32,512]{1,0:T(8,128)} %get-tuple-element.120.cr_ref, f32[32,512]{1,0:T(8,128)} %get-tuple-element.119.ci_ref, ...), custom_call_target="tpu_custom_call" | custom-call | tf_op jit(solution)/shard_map/pallas_call | solution.py:218
  83.7 8.8 %collective-permute-start.10 = (f32[4,16,512]{2,1,0:T(8,128)S(1)}, f32[4,16,512]{2,1,0:T(8,128)S(1)}, u32[]{:S(2)}, u32[]{:S(2)}) collective-permute-start(f32[4,16,512]{2,1,0:T(8,128)S(1)} %get-tuple-element.63), channel_id=1, source_target_pairs={{4,0},{8,4},{12,8},{16,12},{20,16},{24,20},{28,24},{32,28},{36,32}... | collective-permute-start | bytes 393224 | tf_op jit(solution)/shard_map/ppermute | solution.py:275
  92.5 2.1 %collective-permute-start.9 = (f32[4,16,512]{2,1,0:T(8,128)S(1)}, f32[4,16,512]{2,1,0:T(8,128)S(1)}, u32[]{:S(2)}, u32[]{:S(2)}) collective-permute-start(f32[4,16,512]{2,1,0:T(8,128)S(1)} %get-tuple-element.64), channel_id=1, source_target_pairs={{0,4},{4,8},{8,12},{12,16},{16,20},{20,24},{24,28},{28,32},{32,36}... | collective-permute-start | bytes 393224 | tf_op jit(solution)/shard_map/ppermute | solution.py:274
  95.8 7.6 %collective-permute-done.9.low_ref = f32[4,16,512]{2,1,0:T(8,128)S(1)} collective-permute-done((f32[4,16,512]{2,1,0:T(8,128)S(1)}, f32[4,16,512]{2,1,0:T(8,128)S(1)}, u32[]{:S(2)}, u32[]{:S(2)}) %collective-permute-start.9) | collective-permute-done | bytes 131104 | tf_op jit(solution)/shard_map/ppermute | solution.py:274
  104.0 6.3 %shard_map.85 = f32[4,64,512]{2,1,0:T(8,128)} custom-call(f32[4,16,512]{2,1,0:T(8,128)} %copy-done.19, f32[4,64,512]{2,1,0:T(8,128)} %copy-done.11, f32[4,64,512]{2,1,0:T(8,128)} %collective-permute-done.7.recv_ref, f32[4,16,512]{2,1,0:T(8,128)} %copy-done.18, f32[32,512]{1,0:T(8,128)} %get-tuple-element.120.cr_ref, f32[32,512]{1,0:T(8,128)} %get-tuple-element.119.ci_ref, ...), custom_call_target="tpu_custom_call" | custom-call | tf_op jit(solution)/shard_map/pallas_call | solution.py:218
  112.7 2.9 %collective-permute-start.11 = (f32[2,4,64,512]{3,2,1,0:T(8,128)}, f32[2,4,64,512]{3,2,1,0:T(8,128)}, u32[]{:S(2)}, u32[]{:S(2)}) collective-permute-start(f32[2,4,64,512]{3,2,1,0:T(8,128)} %pad_maximum_fusion.3), channel_id=1, source_target_pairs={{0,1},{1,0},{2,3},{3,2},{4,5},{5,4},{6,7},{7,6},{8,9},{9,8},{10,11... | collective-permute-start | bytes 3145736 | tf_op jit(solution)/shard_map/ppermute | solution.py:47
  115.6 2.6 %collective-permute-done.11 = f32[2,4,64,512]{3,2,1,0:T(8,128)} collective-permute-done((f32[2,4,64,512]{3,2,1,0:T(8,128)}, f32[2,4,64,512]{3,2,1,0:T(8,128)}, u32[]{:S(2)}, u32[]{:S(2)}) %collective-permute-start.11) | collective-permute-done | bytes 1048608 | tf_op jit(solution)/shard_map/ppermute | solution.py:47
  120.0 1.5 copy.18
  121.5 12.5 %shard_map.86 = f32[8,128,256]{2,1,0:T(8,128)} custom-call(f32[4,4,64,512]{3,2,1,0:T(8,128)} %bitcast.111, f32[128,2048]{1,0:T(8,128)} %select_add_fusion.m_ref, f32[8,2048]{1,0:T(8,128)} %get-tuple-element.106.cos_ref, f32[8,2048]{1,0:T(8,128)} %get-tuple-element.105.sin_ref), custom_call_target="tpu_custom_call" | custom-call | tf_op jit(solution)/shard_map/pallas_call | solution.py:153
  138.4 1.6 multiply_subtract_fusion.3
  140.0 3.6 %multiply_subtract_fusion = (f32[128,4,512]{0,2,1:T(8,128)}, f32[128,4,512]{0,2,1:T(8,128)}, f32[128,4,512]{0,2,1:T(8,128)}, f32[128,4,512]{0,2,1:T(8,128)}, f32[128,4,512]{0,2,1:T(8,128)}, /*index=5*/f32[128,4,512]{0,2,1:T(8,128)}) fusion(f32[128,8,516]{0,2,1:T(8,128)S(1)} %pad_maximum_fusion, f32[128]{0:T(128)S(1)} %get-tuple-element.118, ...), kind=kLoop, calls=%fused_computation.23 | loop fusion | flops 4718592 | bytes 12585984 | tf_op jit(solution)/shard_map/sub | solution.py:77
  143.6 1.5 copy.19
  145.2 1.5 select_bitcast_fusion.1
  146.9 1.5 copy.20
  148.5 12.5 %shard_map.87 = f32[8,128,256]{2,1,0:T(8,128)} custom-call(f32[4,4,64,512]{3,2,1,0:T(8,128)} %bitcast.112, f32[128,2048]{1,0:T(8,128)} %select_add_fusion.m_ref, f32[8,2048]{1,0:T(8,128)} %get-tuple-element.106.cos_ref, f32[8,2048]{1,0:T(8,128)} %get-tuple-element.105.sin_ref), custom_call_target="tpu_custom_call" | custom-call | tf_op jit(solution)/shard_map/pallas_call | solution.py:153
  160.9 1.5 copy.21
  167.1 2.0 %copy.23 = f32[128,8,512]{2,1,0:T(8,128)} copy(f32[128,8,512]{0,2,1:T(8,128)S(1)} %fusion.3) | data formatting | bytes 4194304 | tf_op jit(solution)/shard_map/add | solution.py:308
  (95 shorter events, 34.2 us)
Async XLA Ops:
  0.0 11.9 %copy-start.20 = (s32[16,2048]{1,0:T(8,128)S(1)}, s32[16,2048]{1,0:T(8,128)}, u32[]{:S(2)}) copy-start(s32[16,2048]{1,0:T(8,128)} %param.11) | copy-start | bytes 393220
  0.0 12.0 %copy-start.21 = (f32[16,2048]{1,0:T(8,128)S(1)}, f32[16,2048]{1,0:T(8,128)}, u32[]{:S(2)}) copy-start(f32[16,2048]{1,0:T(8,128)} %param.12) | copy-start | bytes 393220
  0.0 12.1 %copy-start.22 = (f32[8,2048]{1,0:T(8,128)S(1)}, f32[8,2048]{1,0:T(8,128)}, u32[]{:S(2)}) copy-start(f32[8,2048]{1,0:T(8,128)} %param.13) | copy-start | bytes 196612
  2.1 14.7 %copy-start = (f32[128,8,512]{0,2,1:T(8,128)}, f32[128,8,512]{0,2,1:T(8,128)S(1)}, u32[]{:S(2)}) copy-start(f32[128,8,512]{0,2,1:T(8,128)S(1)} %copy.12) | copy-start | bytes 6291460
  2.1 27.4 %collective-permute-start = (f32[128,8,2]{0,2,1:T(2,128)S(1)}, f32[128,8,2]{0,2,1:T(2,128)S(1)}, u32[]{:S(2)}, u32[]{:S(2)}) collective-permute-start(f32[128,8,2]{0,2,1:T(2,128)S(1)} %get-tuple-element.57), channel_id=1, source_target_pairs={{0,4},{4,8},{8,12},{12,16},{16,20},{20,24},{24,28},{28,32},{32,36}... | collective-permute-start | bytes 24584 | tf_op jit(solution)/shard_map/ppermute | solution.py:16
  5.3 24.2 %collective-permute-start.1 = (f32[128,8,2]{0,2,1:T(2,128)S(1)}, f32[128,8,2]{0,2,1:T(2,128)S(1)}, u32[]{:S(2)}, u32[]{:S(2)}) collective-permute-start(f32[128,8,2]{0,2,1:T(2,128)S(1)} %get-tuple-element.58), channel_id=1, source_target_pairs={{4,0},{8,4},{12,8},{16,12},{20,16},{24,20},{28,24},{32,28},{36,32}... | collective-permute-start | bytes 24584 | tf_op jit(solution)/shard_map/ppermute | solution.py:19
  29.4 2.2 %copy-start.1 = (f32[4,4,64,512]{3,2,1,0:T(8,128)S(1)}, f32[4,4,64,512]{3,2,1,0:T(8,128)}, u32[]{:S(2)}) copy-start(f32[4,4,64,512]{3,2,1,0:T(8,128)} %shard_map.82) | copy-start | bytes 6291460
  32.7 3.9 %collective-permute-start.2 = (f32[2,4,64,512]{3,2,1,0:T(8,128)}, f32[2,4,64,512]{3,2,1,0:T(8,128)}, u32[]{:S(2)}, u32[]{:S(2)}) collective-permute-start(f32[2,4,64,512]{3,2,1,0:T(8,128)} %dynamic-slice_bitcast_fusion.1), channel_id=1, source_target_pairs={{0,1},{1,0},{2,3},{3,2},{4,5},{5,4},{6,7},{7,6},{8,9},{9,8},{10,11... | collective-permute-start | bytes 3145736 | tf_op jit(solution)/shard_map/ppermute | solution.py:33
  39.3 21.5 %copy-start.12 = (f32[4,64,512]{2,1,0:T(8,128)}, f32[4,64,512]{2,1,0:T(8,128)S(1)}, u32[]{:S(2)}) copy-start(f32[4,64,512]{2,1,0:T(8,128)S(1)} %get-tuple-element.28.keep_ref) | copy-start | bytes 1572868
  39.3 13.3 %collective-permute-start.3 = (f32[4,64,512]{2,1,0:T(8,128)}, f32[4,64,512]{2,1,0:T(8,128)S(1)}, u32[]{:S(2)}, u32[]{:S(2)}) collective-permute-start(f32[4,64,512]{2,1,0:T(8,128)} %get-tuple-element.69), channel_id=1, source_target_pairs={{0,2},{2,0},{1,3},{3,1},{4,6},{6,4},{5,7},{7,5},{8,10},{10,8},{9,1... | collective-permute-start | bytes 1572872 | tf_op jit(solution)/shard_map/ppermute | solution.py:287
  50.8 7.0 %copy-start.2 = (f32[4,4,64,512]{3,2,1,0:T(8,128)S(1)}, f32[4,4,64,512]{3,2,1,0:T(8,128)}, u32[]{:S(2)}) copy-start(f32[4,4,64,512]{3,2,1,0:T(8,128)} %shard_map.83) | copy-start | bytes 6291460
  52.6 5.3 %copy-start.14 = (f32[4,64,512]{2,1,0:T(8,128)}, f32[4,64,512]{2,1,0:T(8,128)S(1)}, u32[]{:S(2)}) copy-start(f32[4,64,512]{2,1,0:T(8,128)S(1)} %collective-permute-done.3.recv_ref) | copy-start | bytes 1572868
  54.1 6.0 %copy-start.15 = (f32[2,32,2048]{2,1,0:T(8,128)S(1)}, f32[2,32,2048]{2,1,0:T(8,128)}, u32[]{:S(2)}) copy-start(f32[2,32,2048]{2,1,0:T(8,128)} %param.14) | copy-start | bytes 1572868
  54.1 3.6 %collective-permute-start.4 = (f32[2,4,64,512]{3,2,1,0:T(8,128)S(1)}, f32[2,4,64,512]{3,2,1,0:T(8,128)S(1)}, u32[]{:S(2)}, u32[]{:S(2)}) collective-permute-start(f32[2,4,64,512]{3,2,1,0:T(8,128)S(1)} %dynamic-slice_bitcast_fusion), channel_id=1, source_target_pairs={{0,1},{1,0},{2,3},{3,2},{4,5},{5,4},{6,7},{7,6},{8,9},{9,8},{10,11... | collective-permute-start | bytes 3145736 | tf_op jit(solution)/shard_map/ppermute | solution.py:33
  58.9 23.8 %copy-start.11 = (f32[4,64,512]{2,1,0:T(8,128)}, f32[4,64,512]{2,1,0:T(8,128)S(1)}, u32[]{:S(2)}) copy-start(f32[4,64,512]{2,1,0:T(8,128)S(1)} %get-tuple-element.65.keep_ref) | copy-start | bytes 1572868
  58.9 23.8 %collective-permute-start.7 = (f32[4,64,512]{2,1,0:T(8,128)}, f32[4,64,512]{2,1,0:T(8,128)}, u32[]{:S(2)}, u32[]{:S(2)}) collective-permute-start(f32[4,64,512]{2,1,0:T(8,128)} %get-tuple-element.66), channel_id=1, source_target_pairs={{0,2},{2,0},{1,3},{3,1},{4,6},{6,4},{5,7},{7,5},{8,10},{10,8},{9,1... | collective-permute-start | bytes 1572872 | tf_op jit(solution)/shard_map/ppermute | solution.py:293
  62.5 12.6 %collective-permute-start.5 = (f32[4,16,512]{2,1,0:T(8,128)}, f32[4,16,512]{2,1,0:T(8,128)S(1)}, u32[]{:S(2)}, u32[]{:S(2)}) collective-permute-start(f32[4,16,512]{2,1,0:T(8,128)} %get-tuple-element.68), channel_id=1, source_target_pairs={{0,4},{4,8},{8,12},{12,16},{16,20},{20,24},{24,28},{28,32},{32,36}... | collective-permute-start | bytes 393224 | tf_op jit(solution)/shard_map/ppermute | solution.py:274
  64.4 10.6 %collective-permute-start.6 = (f32[4,16,512]{2,1,0:T(8,128)}, f32[4,16,512]{2,1,0:T(8,128)S(1)}, u32[]{:S(2)}, u32[]{:S(2)}) collective-permute-start(f32[4,16,512]{2,1,0:T(8,128)} %get-tuple-element.67), channel_id=1, source_target_pairs={{4,0},{8,4},{12,8},{16,12},{20,16},{24,20},{28,24},{32,28},{36,32}... | collective-permute-start | bytes 393224 | tf_op jit(solution)/shard_map/ppermute | solution.py:275
  82.7 27.7 %collective-permute-start.8 = (f32[4,64,512]{2,1,0:T(8,128)}, f32[4,64,512]{2,1,0:T(8,128)}, u32[]{:S(2)}, u32[]{:S(2)}) collective-permute-start(f32[4,64,512]{2,1,0:T(8,128)} %shard_map.84), channel_id=1, source_target_pairs={{0,2},{2,0},{1,3},{3,1},{4,6},{6,4},{5,7},{7,5},{8,10},{10,8},{9,1... | collective-permute-start | bytes 1572872 | tf_op jit(solution)/shard_map/ppermute | solution.py:296
  83.7 12.1 %collective-permute-start.10 = (f32[4,16,512]{2,1,0:T(8,128)S(1)}, f32[4,16,512]{2,1,0:T(8,128)S(1)}, u32[]{:S(2)}, u32[]{:S(2)}) collective-permute-start(f32[4,16,512]{2,1,0:T(8,128)S(1)} %get-tuple-element.63), channel_id=1, source_target_pairs={{4,0},{8,4},{12,8},{16,12},{20,16},{24,20},{28,24},{32,28},{36,32}... | collective-permute-start | bytes 393224 | tf_op jit(solution)/shard_map/ppermute | solution.py:275
  92.5 10.9 %collective-permute-start.9 = (f32[4,16,512]{2,1,0:T(8,128)S(1)}, f32[4,16,512]{2,1,0:T(8,128)S(1)}, u32[]{:S(2)}, u32[]{:S(2)}) collective-permute-start(f32[4,16,512]{2,1,0:T(8,128)S(1)} %get-tuple-element.64), channel_id=1, source_target_pairs={{0,4},{4,8},{8,12},{12,16},{16,20},{20,24},{24,28},{28,32},{32,36}... | collective-permute-start | bytes 393224 | tf_op jit(solution)/shard_map/ppermute | solution.py:274
  95.8 7.6 %copy-start.18 = (f32[4,16,512]{2,1,0:T(8,128)}, f32[4,16,512]{2,1,0:T(8,128)S(1)}, u32[]{:S(2)}) copy-start(f32[4,16,512]{2,1,0:T(8,128)S(1)} %collective-permute-done.10.high_ref) | copy-start | bytes 393220
  112.7 5.5 %collective-permute-start.11 = (f32[2,4,64,512]{3,2,1,0:T(8,128)}, f32[2,4,64,512]{3,2,1,0:T(8,128)}, u32[]{:S(2)}, u32[]{:S(2)}) collective-permute-start(f32[2,4,64,512]{3,2,1,0:T(8,128)} %pad_maximum_fusion.3), channel_id=1, source_target_pairs={{0,1},{1,0},{2,3},{3,2},{4,5},{5,4},{6,7},{7,6},{8,9},{9,8},{10,11... | collective-permute-start | bytes 3145736 | tf_op jit(solution)/shard_map/ppermute | solution.py:47
  121.5 13.2 %collective-permute-start.12 = (f32[4,64,512]{2,1,0:T(8,128)S(1)}, f32[4,64,512]{2,1,0:T(8,128)}, u32[]{:S(2)}, u32[]{:S(2)}) collective-permute-start(f32[4,64,512]{2,1,0:T(8,128)S(1)} %copy-done.13), channel_id=1, source_target_pairs={{0,2},{2,0},{1,3},{3,1},{4,6},{6,4},{5,7},{7,5},{8,10},{10,8},{9,1... | collective-permute-start | bytes 1572872 | tf_op jit(solution)/shard_map/ppermute | solution.py:301
  134.0 4.4 %copy-start.24 = (f32[2,4,128]{2,1,0:T(4,128)S(1)}, f32[2,4,128]{2,1,0:T(4,128)}, u32[]{:S(2)}) copy-start(f32[2,4,128]{2,1,0:T(4,128)} %param.9) | copy-start | bytes 12292
  134.0 4.4 %copy-start.23 = (s32[4,512]{1,0:T(4,128)S(1)}, s32[4,512]{1,0:T(4,128)}, u32[]{:S(2)}) copy-start(s32[4,512]{1,0:T(4,128)} %param.10) | copy-start | bytes 24580
  137.2 8.0 %collective-permute-start.13 = (f32[2,4,64,512]{3,2,1,0:T(8,128)}, f32[2,4,64,512]{3,2,1,0:T(8,128)}, u32[]{:S(2)}, u32[]{:S(2)}) collective-permute-start(f32[2,4,64,512]{3,2,1,0:T(8,128)} %pad_maximum_fusion.4), channel_id=1, source_target_pairs={{0,1},{1,0},{2,3},{3,2},{4,5},{5,4},{6,7},{7,6},{8,9},{9,8},{10,11... | collective-permute-start | bytes 3145736 | tf_op jit(solution)/shard_map/ppermute | solution.py:47
  162.5 2.2 %copy-start.10 = (f32[128,4,512]{0,2,1:T(8,128)S(1)}, f32[128,4,512]{0,2,1:T(8,128)}, u32[]{:S(2)}) copy-start(f32[128,4,512]{0,2,1:T(8,128)} %get-tuple-element.50) | copy-start | bytes 3145732
  162.7 2.4 %copy-start.3 = (f32[128,4,512]{0,2,1:T(8,128)S(1)}, f32[128,4,512]{0,2,1:T(8,128)}, u32[]{:S(2)}) copy-start(f32[128,4,512]{0,2,1:T(8,128)} %get-tuple-element.45) | copy-start | bytes 3145732
  162.7 2.7 %copy-start.4 = (f32[128,4,512]{0,2,1:T(8,128)S(1)}, f32[128,4,512]{0,2,1:T(8,128)}, u32[]{:S(2)}) copy-start(f32[128,4,512]{0,2,1:T(8,128)} %get-tuple-element.46) | copy-start | bytes 3145732
  162.7 3.0 %copy-start.5 = (f32[128,4,512]{0,2,1:T(8,128)S(1)}, f32[128,4,512]{0,2,1:T(8,128)}, u32[]{:S(2)}) copy-start(f32[128,4,512]{0,2,1:T(8,128)} %get-tuple-element.39) | copy-start | bytes 3145732
  162.7 3.2 %copy-start.6 = (f32[128,4,512]{0,2,1:T(8,128)S(1)}, f32[128,4,512]{0,2,1:T(8,128)}, u32[]{:S(2)}) copy-start(f32[128,4,512]{0,2,1:T(8,128)} %get-tuple-element.40) | copy-start | bytes 3145732
  (7 other events, 9.7 us)

commit v10 on v7

--- a/solution.py
+++ b/solution.py
@@ -26,28 +26,12 @@
 
 
 def reduce_cores(field):
-    core = lax.axis_index("dir") % 2
-    pairs = field.reshape((2, 2) + field.shape[1:])
-    keep = lax.dynamic_index_in_dim(pairs, core, 1, keepdims=False)
-    send = lax.dynamic_index_in_dim(pairs, 1 - core, 1, keepdims=False)
-    return keep + lax.ppermute(send, "dir", CORE_SWAP)
-
-
-def split_rows(acc):
-    row = lax.axis_index("dir") // 2
-    keep = lax.dynamic_index_in_dim(acc, row, 0, keepdims=False)
-    send = lax.dynamic_index_in_dim(acc, 1 - row, 0, keepdims=False)
-    return keep, send
-
-
-def gather_cores(local, other):
-    rank = lax.axis_index("dir")
-    first = rank // 2 == 0
-    pair = jnp.stack([jnp.where(first, local, other), jnp.where(first, other, local)], axis=0)
-    mate = lax.ppermute(pair, "dir", CORE_SWAP)
-    low = rank % 2 == 0
-    quad = jnp.stack([jnp.where(low, pair, mate), jnp.where(low, mate, pair)], axis=1)
-    return quad.reshape((4,) + local.shape)
+    return field[:2] + lax.ppermute(field[2:], "dir", CORE_SWAP)
+
+
+def gather_blocks(local, other):
+    mate_local, mate_other = lax.ppermute((local, other), "dir", CORE_SWAP)
+    return (local, other, mate_local, mate_other)
 
 
 def interp_matrix(index, weight, first_row, row_count):
@@ -83,18 +67,24 @@
     return summed
 
 
+def slot_part(slot):
+    rank = lax.axis_index("dir")
+    return ((rank // 2 + slot % 2) % 2) * 2 + (rank % 2 + slot // 2) % 2
+
+
 def upward_kernel(xt_ref, m_ref, cos_ref, sin_ref, out_ref):
     groups = xt_ref.shape[0]
     comps, slots, width = out_ref.shape[1:]
     half = comps // 2
-    m = m_ref[...]
+    first = pl.multiple_of(slot_part(pl.program_id(0)) * width, 128)
+    m = m_ref[:, pl.ds(first, width)]
     acc_re = jnp.zeros((half, slots, width), jnp.float32)
     acc_im = jnp.zeros((half, slots, width), jnp.float32)
     for g in range(groups):
         r = jnp.dot(xt_ref[g], m, precision=HIGHEST, preferred_element_type=jnp.float32)
         r = r.reshape(comps, slots, width)
-        c = cos_ref[pl.ds(g, 1), :].reshape(1, 1, width)
-        s = sin_ref[pl.ds(g, 1), :].reshape(1, 1, width)
+        c = cos_ref[pl.ds(g, 1), pl.ds(first, width)].reshape(1, 1, width)
+        s = sin_ref[pl.ds(g, 1), pl.ds(first, width)].reshape(1, 1, width)
         re = r[:half]
         im = r[half:]
         acc_re = acc_re + (c * re - s * im)
@@ -113,31 +103,34 @@
         grid=(parts,),
         in_specs=[
             pl.BlockSpec((groups, rows, q), lambda j: (0, 0, 0)),
-            pl.BlockSpec((q, width), lambda j: (0, j)),
-            pl.BlockSpec((groups, width), lambda j: (0, j)),
-            pl.BlockSpec((groups, width), lambda j: (0, j)),
+            pl.BlockSpec((q, total), lambda j: (0, 0)),
+            pl.BlockSpec((groups, total), lambda j: (0, 0)),
+            pl.BlockSpec((groups, total), lambda j: (0, 0)),
         ],
         out_specs=pl.BlockSpec((1, comps, slots, width), lambda j: (j, 0, 0, 0)),
         out_shape=jax.ShapeDtypeStruct((parts, comps, slots, width), jnp.float32),
     )(xt, m, cos, sin)
 
 
-def downward_kernel(pl_ref, m_ref, cos_ref, sin_ref, out_ref):
+def downward_kernel(b0_ref, b1_ref, b2_ref, b3_ref, m_ref, cos_ref, sin_ref, out_ref):
     g = pl.program_id(0)
-    parts, comps, slots, width = pl_ref.shape
+    comps, slots, width = b0_ref.shape
     half = comps // 2
     q = m_ref.shape[0]
     acc = jnp.zeros((q, comps * slots), jnp.float32)
-    for d in range(parts):
-        x = pl_ref[d]
-        c = cos_ref[pl.ds(g, 1), pl.ds(d * width, width)].reshape(1, 1, width)
-        s = sin_ref[pl.ds(g, 1), pl.ds(d * width, width)].reshape(1, 1, width)
+    rank = lax.axis_index("dir")
+    for code, ref in zip((0, 2, 1, 3), (b0_ref, b1_ref, b2_ref, b3_ref)):
+        part = ((rank // 2 + code // 2) % 2) * 2 + (rank % 2 + code % 2) % 2
+        first = pl.multiple_of(part * width, 128)
+        x = ref[...]
+        c = cos_ref[pl.ds(g, 1), pl.ds(first, width)].reshape(1, 1, width)
+        s = sin_ref[pl.ds(g, 1), pl.ds(first, width)].reshape(1, 1, width)
         re = x[:half]
         im = x[half:]
         spread = jnp.concatenate([c * re + s * im, c * im - s * re], axis=0)
         spread = spread.reshape(comps * slots, width)
         acc = acc + lax.dot_general(
-            m_ref[:, pl.ds(d * width, width)],
+            m_ref[:, pl.ds(first, width)],
             spread,
             (((1,), (1,)), ((), ())),
             precision=HIGHEST,
@@ -146,22 +139,23 @@
     out_ref[0] = acc
 
 
-def downward(parent_local, m, cos, sin):
-    parts, comps, slots, width = parent_local.shape
+def downward(blocks, m, cos, sin):
+    comps, slots, width = blocks[0].shape
     groups = cos.shape[0]
-    q = m.shape[0]
+    q, total = m.shape
+    block = pl.BlockSpec((comps, slots, width), lambda g: (0, 0, 0))
     return pl.pallas_call(
         downward_kernel,
         grid=(groups,),
-        in_specs=[
-            pl.BlockSpec((parts, comps, slots, width), lambda g: (0, 0, 0, 0)),
-            pl.BlockSpec((q, parts * width), lambda g: (0, 0)),
-            pl.BlockSpec((groups, parts * width), lambda g: (0, 0)),
-            pl.BlockSpec((groups, parts * width), lambda g: (0, 0)),
+        in_specs=[block] * 4
+        + [
+            pl.BlockSpec((q, total), lambda g: (0, 0)),
+            pl.BlockSpec((groups, total), lambda g: (0, 0)),
+            pl.BlockSpec((groups, total), lambda g: (0, 0)),
         ],
         out_specs=pl.BlockSpec((1, q, comps * slots), lambda g: (g, 0, 0)),
         out_shape=jax.ShapeDtypeStruct((groups, q, comps * slots), jnp.float32),
-    )(parent_local, m, cos, sin)
+    )(*blocks, m, cos, sin)
 
 
 def parent_translate(padded, coef_real, coef_imag, mask, reach):
@@ -280,25 +274,25 @@
 
     acc_a = reduce_cores(upward(chunk_xt(0), rows, cosine, sine, dir_size, 2 * step))
     acc_a, xt_b = lax.optimization_barrier((acc_a, chunk_xt(1)))
-    keep_a, send_a = split_rows(acc_a)
+    keep_a, send_a = acc_a[0], acc_a[1]
     recv_a = lax.ppermute(send_a, "dir", ROW_SWAP)
     field_b = upward(xt_b, rows, cosine, sine, dir_size, 2 * step)
     field_b, recv_a = lax.optimization_barrier((field_b, recv_a))
     acc_b = reduce_cores(field_b)
     keep_a, recv_a, acc_b = lax.optimization_barrier((keep_a, recv_a, acc_b))
-    keep_b, send_b = split_rows(acc_b)
+    keep_b, send_b = acc_b[0], acc_b[1]
     recv_b = lax.ppermute(send_b, "dir", ROW_SWAP)
     local_a = translate(keep_a, recv_a)
     local_a, recv_b = lax.optimization_barrier((local_a, recv_b))
     other_a = lax.ppermute(local_a, "dir", ROW_SWAP)
     local_b = translate(keep_b, recv_b)
     other_a, local_b = lax.optimization_barrier((other_a, local_b))
-    all_a = gather_cores(local_a, other_a)
+    all_a = gather_blocks(local_a, other_a)
     all_a, local_b = lax.optimization_barrier((all_a, local_b))
     other_b = lax.ppermute(local_b, "dir", ROW_SWAP)
     far_a = downward(all_a, rows, cosine, sine)
     far_a, other_b = lax.optimization_barrier((far_a, other_b))
-    far_b = downward(gather_cores(local_b, other_b), rows, cosine, sine)
+    far_b = downward(gather_blocks(local_b, other_b), rows, cosine, sine)
     fars = [far.reshape(groups, child_dev, 2, step, slots) for far in (far_a, far_b)]
     far = jnp.concatenate(fars, axis=3).transpose(1, 2, 3, 4, 0)
     far = far.reshape(child_dev, comps, box_dev)

time: 167 us -> 152 us (0.910)
  other arithmetic: 23.8 us -> 13.9 us
  local copies, waits for them, and re-layouts: 28.7 us -> 24.3 us
  waiting for transfers between devices: 17.3 us -> 13.7 us
  starting transfers between devices: 38.1 us -> 40.5 us
    another operation x8 -> x0, other arithmetic: 8.28 us -> none  [the longest x4 4.85 us: gather_cores(): jnp.stack([jnp.where(first, local, other), jnp.where(first, other, local)...]
    squeeze x4 -> x2, local copies, waits for them, and re-layouts: 5.57 us -> 1.79 us  [the longest x1 0.9 us: body(): keep_a, send_a = (acc_a[0], acc_a[1])]
    another operation x2 -> x0, local copies, waits for them, and re-layouts: 3.1 us -> none  [gather_cores(): jnp.stack([jnp.where(low, pair, mate), jnp.where(low, mate, pair)], axis=1)]
    slice x0 -> x2, local copies, waits for them, and re-layouts: none -> 2.99 us  [reduce_cores(): return field[:2] + lax.ppermute(field[2:], 'dir', CORE_SWAP)]
    ppermute x4 -> x6, starting transfers between devices: 6.14 us -> 8.59 us  [the longest x4 6.52 us: gather_blocks(): mate_local, mate_other = lax.ppermute((local, other), 'dir', CORE_SWAP)]
    ppermute x2, waiting for transfers between devices: 9.07 us -> 7.02 us  [translate(): low = lax.ppermute(low, 'box', forward)]
    ppermute x4 -> x6, waiting for transfers between devices: 6.38 us -> 4.95 us  [the longest x2 3.41 us: reduce_cores(): return field[:2] + lax.ppermute(field[2:], 'dir', CORE_SWAP)]
    unnamed x49 -> x57, local copies, waits for them, and re-layouts: 4.48 us -> 5.27 us
  transfers between devices with their start and end apart: 14 -> 16, of which waited for: 6 -> 6; matrix products, arithmetic and copies ran while one was open for 11% -> 9% of each run, Pallas kernels for 21% -> 24%
where the time goes in v10:
time: 152 us; the launch traced here: 151 us
  Pallas kernels  58.7 us (39%)
  starting transfers between devices  40.5 us (27%)
  local copies, waits for them, and re-layouts  24.3 us (16%)
  other arithmetic  13.9 us (9%)
  waiting for transfers between devices  13.7 us (9%)
    pallas_call x2, Pallas kernels, downward(): pl.pallas_call(downward_kernel, grid=(groups,), in_specs=[block] * 4 + [p...  25.3 us
    pallas_call x2, Pallas kernels, upward(): pl.pallas_call(upward_kernel, grid=(parts,), in_specs=[pl.BlockSpec((grou...  20.8 us
    ppermute x2, starting transfers between devices, translate(): high = lax.ppermute(high, 'box', backward)  14.5 us
    pallas_call x2, Pallas kernels, translate_call(): pl.pallas_call(translate_kernel, out_shape=jax.ShapeDtypeStruct(keep.shap...  12.6 us
    ppermute x1, starting transfers between devices, with_halo(): lax.ppermute(lax.slice_in_dim(block, 0, width, axis=dim), axis, backward)  7.87 us
    ppermute x2, waiting for transfers between devices, translate(): low = lax.ppermute(low, 'box', forward)  7.02 us
    ppermute x4, starting transfers between devices, gather_blocks(): mate_local, mate_other = lax.ppermute((local, other), 'dir', CORE_SWAP)  6.52 us
    unnamed x57, local copies, waits for them, and re-layouts  5.27 us
  transfers between devices with their start and end apart: 16, of which 6 were waited for; matrix products, arithmetic and copies ran while one was open for 9% of the time, Pallas kernels for 24%

profile of v10, /device:TPU:65, one launch (start us, length us, event | category | flops | bytes accessed | tf_op | source)
XLA Modules:
  0.0 151.4 jit_solution(13724145717808567224)
XLA Ops:
  0.0 2.0 %copy.10 = f32[128,8,512]{0,2,1:T(8,128)S(1)} copy(f32[128,8,512]{2,1,0:T(8,128)} %param.8) | data formatting | bytes 4194304 | tf_op args[0]
  4.5 2.7 %select_add_fusion.m_ref = f32[128,2048]{1,0:T(8,128)} fusion(f32[2048]{0:T(1024)S(1)} %bitcast.100, s32[2048]{0:T(1024)S(1)} %bitcast.116, f32[2048]{0:T(1024)S(1)} %bitcast.101, s32[2048]{0:T(1024)S(1)} %bitcast.117, f32[2048]{0:T(1024)S(1)} %bitcast.87, s32[2048]{0:T(1024)S(1)} %bitcast.103, f32[2048]{0:T(1024)S(1)} %bitcast.88, s32[2048]{0:T(1024)S(1)} %bitcast.104, ...), kind=kLoop, calls=%fused_computation.31 | loop fusion | flops 12320768 | bytes 1311232 | tf_op jit(solution)/shard_map/add | solution.py:41
  7.1 10.4 %shard_map.82 = f32[4,4,64,512]{3,2,1,0:T(8,128)} custom-call(f32[8,256,128]{2,1,0:T(8,128)} %bitcast.81, f32[128,2048]{1,0:T(8,128)} %select_add_fusion.m_ref, f32[8,2048]{1,0:T(8,128)} %get-tuple-element.100.cos_ref, f32[8,2048]{1,0:T(8,128)} %get-tuple-element.99.sin_ref), custom_call_target="tpu_custom_call" | custom-call | tf_op jit(solution)/shard_map/pallas_call | solution.py:101
  17.6 1.5 slice.346
  24.4 10.4 %shard_map.83 = f32[4,4,64,512]{3,2,1,0:T(8,128)} custom-call(f32[8,256,128]{2,1,0:T(8,128)} %bitcast.83, f32[128,2048]{1,0:T(8,128)} %select_add_fusion.m_ref, f32[8,2048]{1,0:T(8,128)} %get-tuple-element.100.cos_ref, f32[8,2048]{1,0:T(8,128)} %get-tuple-element.99.sin_ref), custom_call_target="tpu_custom_call" | custom-call | tf_op jit(solution)/shard_map/pallas_call | solution.py:101
  34.8 1.7 %collective-permute-done.3.recv_ref = f32[4,64,512]{2,1,0:T(8,128)S(1)} collective-permute-done((f32[4,64,512]{2,1,0:T(8,128)}, f32[4,64,512]{2,1,0:T(8,128)S(1)}, u32[]{:S(2)}, u32[]{:S(2)}) %collective-permute-start.3) | collective-permute-done | bytes 524320 | tf_op jit(solution)/shard_map/ppermute | solution.py:278
  36.5 1.5 %slice.317 = f32[2,4,64,512]{3,2,1,0:T(8,128)S(1)} slice(f32[4,4,64,512]{3,2,1,0:T(8,128)} %shard_map.83), slice={[2:4], [0:4], [0:64], [0:512]} | slice | bytes 2097152 | tf_op jit(solution)/shard_map/slice | solution.py:29
  38.1 1.3 collective-permute-start.4
  39.4 2.3 %collective-permute-done.4 = f32[2,4,64,512]{3,2,1,0:T(8,128)S(1)} collective-permute-done((f32[2,4,64,512]{3,2,1,0:T(8,128)S(1)}, f32[2,4,64,512]{3,2,1,0:T(8,128)S(1)}, u32[]{:S(2)}, u32[]{:S(2)}) %collective-permute-start.4) | collective-permute-done | bytes 1048608 | tf_op jit(solution)/shard_map/ppermute | solution.py:29
  44.7 1.6 %slice_add_fusion.4 = (f32[4,16,512]{2,1,0:T(8,128)S(1)}, f32[4,16,512]{2,1,0:T(8,128)}) fusion(f32[4,64,512]{2,1,0:T(8,128)} %copy-done.14, f32[4,64,512]{2,1,0:T(8,128)S(1)} %get-tuple-element.27.keep_ref), kind=kLoop, calls=%fused_computation.46 | loop fusion | flops 65536 | bytes 786432 | tf_op jit(solution)/shard_map/add | solution.py:270
  46.4 3.2 %collective-permute-start.5 = (f32[4,16,512]{2,1,0:T(8,128)}, f32[4,16,512]{2,1,0:T(8,128)S(1)}, u32[]{:S(2)}, u32[]{:S(2)}) collective-permute-start(f32[4,16,512]{2,1,0:T(8,128)} %get-tuple-element.62), channel_id=1, source_target_pairs={{0,4},{4,8},{8,12},{12,16},{16,20},{20,24},{24,28},{28,32},{32,36}... | collective-permute-start | bytes 393224 | tf_op jit(solution)/shard_map/ppermute | solution.py:271
  49.6 6.6 %collective-permute-start.6 = (f32[4,16,512]{2,1,0:T(8,128)S(1)}, f32[4,16,512]{2,1,0:T(8,128)S(1)}, u32[]{:S(2)}, u32[]{:S(2)}) collective-permute-start(f32[4,16,512]{2,1,0:T(8,128)S(1)} %get-tuple-element.61), channel_id=1, source_target_pairs={{4,0},{8,4},{12,8},{16,12},{20,16},{24,20},{28,24},{32,28},{36,32}... | collective-permute-start | bytes 393224 | tf_op jit(solution)/shard_map/ppermute | solution.py:272
  57.0 1.5 dynamic-slice_bitcast_fusion
  58.5 4.6 %collective-permute-done.5.low_ref = f32[4,16,512]{2,1,0:T(8,128)S(1)} collective-permute-done((f32[4,16,512]{2,1,0:T(8,128)}, f32[4,16,512]{2,1,0:T(8,128)S(1)}, u32[]{:S(2)}, u32[]{:S(2)}) %collective-permute-start.5) | collective-permute-done | bytes 131104 | tf_op jit(solution)/shard_map/ppermute | solution.py:271
  64.4 6.3 %shard_map.84.b0_ref = f32[4,64,512]{2,1,0:T(8,128)} custom-call(f32[4,16,512]{2,1,0:T(8,128)} %copy-done.19, f32[4,64,512]{2,1,0:T(8,128)} %copy-done.13, f32[4,64,512]{2,1,0:T(8,128)} %copy-done.14, f32[4,16,512]{2,1,0:T(8,128)} %copy-done.20, f32[32,512]{1,0:T(8,128)} %get-tuple-element.114.cr_ref, f32[32,512]{1,0:T(8,128)} %get-tuple-element.113.ci_ref, ...), custom_call_target="tpu_custom_call" | custom-call | tf_op jit(solution)/shard_map/pallas_call | solution.py:212
  71.8 1.9 %collective-permute-start.9 = (f32[4,16,512]{2,1,0:T(8,128)S(1)}, f32[4,16,512]{2,1,0:T(8,128)S(1)}, u32[]{:S(2)}, u32[]{:S(2)}) collective-permute-start(f32[4,16,512]{2,1,0:T(8,128)S(1)} %get-tuple-element.58), channel_id=1, source_target_pairs={{0,4},{4,8},{8,12},{12,16},{16,20},{20,24},{24,28},{28,32},{32,36}... | collective-permute-start | bytes 393224 | tf_op jit(solution)/shard_map/ppermute | solution.py:271
  73.7 7.9 %collective-permute-start.10 = (f32[4,16,512]{2,1,0:T(8,128)S(1)}, f32[4,16,512]{2,1,0:T(8,128)S(1)}, u32[]{:S(2)}, u32[]{:S(2)}) collective-permute-start(f32[4,16,512]{2,1,0:T(8,128)S(1)} %get-tuple-element.57), channel_id=1, source_target_pairs={{4,0},{8,4},{12,8},{16,12},{20,16},{24,20},{28,24},{32,28},{36,32}... | collective-permute-start | bytes 393224 | tf_op jit(solution)/shard_map/ppermute | solution.py:272
  81.6 2.2 %collective-permute-start.11 = (f32[4,64,512]{2,1,0:T(8,128)}, f32[4,64,512]{2,1,0:T(8,128)S(1)}, u32[]{:S(2)}, u32[]{:S(2)}) collective-permute-start(f32[4,64,512]{2,1,0:T(8,128)} %shard_map.84.b0_ref), channel_id=1, source_target_pairs={{0,1},{1,0},{2,3},{3,2},{4,5},{5,4},{6,7},{7,6},{8,9},{9,8},{10,11... | collective-permute-start | bytes 1572872 | tf_op jit(solution)/shard_map/ppermute | solution.py:33
  83.9 2.4 %collective-permute-done.9.low_ref = f32[4,16,512]{2,1,0:T(8,128)S(1)} collective-permute-done((f32[4,16,512]{2,1,0:T(8,128)S(1)}, f32[4,16,512]{2,1,0:T(8,128)S(1)}, u32[]{:S(2)}, u32[]{:S(2)}) %collective-permute-start.9) | collective-permute-done | bytes 131104 | tf_op jit(solution)/shard_map/ppermute | solution.py:271
  87.6 6.3 %shard_map.85.b0_ref = f32[4,64,512]{2,1,0:T(8,128)} custom-call(f32[4,16,512]{2,1,0:T(8,128)} %copy-done.21, f32[4,64,512]{2,1,0:T(8,128)} %copy-done.12, f32[4,64,512]{2,1,0:T(8,128)} %collective-permute-done.7.recv_ref, f32[4,16,512]{2,1,0:T(8,128)} %copy-done.22, f32[32,512]{1,0:T(8,128)} %get-tuple-element.114.cr_ref, ...), custom_call_target="tpu_custom_call" | custom-call | tf_op jit(solution)/shard_map/pallas_call | solution.py:212
  93.9 2.9 %collective-permute-start.12 = (f32[4,64,512]{2,1,0:T(8,128)S(1)}, f32[4,64,512]{2,1,0:T(8,128)S(1)}, u32[]{:S(2)}, u32[]{:S(2)}) collective-permute-start(f32[4,64,512]{2,1,0:T(8,128)S(1)} %collective-permute-done.8.b1_ref), channel_id=1, source_target_pairs={{0,1},{1,0},{2,3},{3,2},{4,5},{5,4},{6,7},{7,6},{8,9},{9,8},{10,11... | collective-permute-start | bytes 1572872 | tf_op jit(solution)/shard_map/ppermute | solution.py:33
  96.8 1.5 %collective-permute-done.12.b3_ref = f32[4,64,512]{2,1,0:T(8,128)S(1)} collective-permute-done((f32[4,64,512]{2,1,0:T(8,128)S(1)}, f32[4,64,512]{2,1,0:T(8,128)S(1)}, u32[]{:S(2)}, u32[]{:S(2)}) %collective-permute-start.12) | collective-permute-done | bytes 524320 | tf_op jit(solution)/shard_map/ppermute | solution.py:33
  99.2 1.9 %collective-permute-start = (f32[128,8,2]{0,2,1:T(2,128)S(1)}, f32[128,8,2]{0,2,1:T(2,128)S(1)}, u32[]{:S(2)}, u32[]{:S(2)}) collective-permute-start(f32[128,8,2]{0,2,1:T(2,128)S(1)} %get-tuple-element.54), channel_id=1, source_target_pairs={{0,4},{4,8},{8,12},{12,16},{16,20},{20,24},{24,28},{28,32},{32,36}... | collective-permute-start | bytes 24584 | tf_op jit(solution)/shard_map/ppermute | solution.py:16
  101.1 7.9 %collective-permute-start.1 = (f32[128,8,2]{0,2,1:T(2,128)S(1)}, f32[128,8,2]{0,2,1:T(2,128)S(1)}, u32[]{:S(2)}, u32[]{:S(2)}) collective-permute-start(f32[128,8,2]{0,2,1:T(2,128)S(1)} %get-tuple-element.53), channel_id=1, source_target_pairs={{4,0},{8,4},{12,8},{16,12},{20,16},{24,20},{28,24},{32,28},{36,32}... | collective-permute-start | bytes 24584 | tf_op jit(solution)/shard_map/ppermute | solution.py:19
  110.3 12.7 %shard_map.86 = f32[8,128,256]{2,1,0:T(8,128)} custom-call(f32[4,64,512]{2,1,0:T(8,128)} %shard_map.84.b0_ref, f32[4,64,512]{2,1,0:T(8,128)} %copy-done.15, f32[4,64,512]{2,1,0:T(8,128)} %copy-done.16, f32[4,64,512]{2,1,0:T(8,128)} %copy-done.17, f32[128,2048]{1,0:T(8,128)} %select_add_fusion.m_ref, f32[8,2048]{1,0:T(8,128)} %get-tuple-element.100.cos_ref, ...), custom_call_target="tpu_custom_call" | custom-call | tf_op jit(solution)/shard_map/pallas_call | solution.py:147
  123.0 2.2 %multiply_subtract_fusion.2 = (f32[128,4,512]{0,2,1:T(8,128)}, f32[128,4,512]{0,2,1:T(8,128)}, f32[128,4,512]{0,2,1:T(8,128)}, f32[128,4,512]{0,2,1:T(8,128)}) fusion(f32[128]{0:T(128)S(1)} %get-tuple-element.108, f32[128]{0:T(128)S(1)} %get-tuple-element.109, f32[128,8,512]{0,2,1:T(8,128)S(1)} %copy.10, f32[128,8,2]{0,2,1:T(2,128)S(1)} %collective-permute-done, ...), kind=kLoop, calls=%fused_computation.37 | loop fusion | flops 4980736 | bytes 6301696 | tf_op jit(solution)/shard_map/sub | solution.py:61
  125.3 2.3 %multiply_subtract_fusion = (f32[128,4,512]{0,2,1:T(8,128)}, f32[128,4,512]{0,2,1:T(8,128)}, f32[128,4,512]{0,2,1:T(8,128)}, f32[128,4,512]{0,2,1:T(8,128)}) fusion(f32[128]{0:T(128)S(1)} %get-tuple-element.112, f32[128]{0:T(128)S(1)} %get-tuple-element.105, f32[128,8,2]{0,2,1:T(2,128)S(1)} %collective-permute-done.1, f32[128,8,512]{0,2,1:T(8,128)S(1)} %copy.10, ...), kind=kLoop, calls=%fused_computation.33 | loop fusion | flops 4980736 | bytes 6301696 | tf_op jit(solution)/shard_map/sub | solution.py:61
  127.6 1.3 copy.17
  128.9 12.7 %shard_map.87 = f32[8,128,256]{2,1,0:T(8,128)} custom-call(f32[4,64,512]{2,1,0:T(8,128)} %shard_map.85.b0_ref, f32[4,64,512]{2,1,0:T(8,128)} %collective-permute-done.13.b1_ref, f32[4,64,512]{2,1,0:T(8,128)} %collective-permute-done.14.b2_ref, f32[4,64,512]{2,1,0:T(8,128)} %collective-permute-done.15.b3_ref, f32[128,2048]{1,0:T(8,128)} %select_add_fusion.m_ref, ...), custom_call_target="tpu_custom_call" | custom-call | tf_op jit(solution)/shard_map/pallas_call | solution.py:147
  141.6 2.7 %copy.18 = f32[8,128,256]{1,2,0:T(8,128)} copy(f32[8,128,256]{2,1,0:T(8,128)} %shard_map.87) | data formatting | bytes 2097152 | tf_op jit(solution)/shard_map/pallas_call | solution.py:147
  144.3 1.6 %maximum_bitcast_fusion = f32[128,2,4,64,8]{0,3,2,1,4:T(8,128)S(1)} fusion(f32[8,128,2,2,64]{1,4,3,2,0:T(8,128)} %bitcast.85, f32[8,128,2,2,64]{1,4,3,2,0:T(8,128)S(1)} %bitcast.82), kind=kLoop, calls=%fused_computation.14 | loop fusion | flops 524288 | bytes 4194304 | tf_op jit(solution)/shard_map/transpose | solution.py:297
  149.4 2.0 %copy.20 = f32[128,8,512]{2,1,0:T(8,128)} copy(f32[128,8,512]{0,2,1:T(8,128)S(1)} %fusion.3) | data formatting | bytes 4194304 | tf_op jit(solution)/shard_map/add | solution.py:299
  (94 shorter events, 21.0 us)
Async XLA Ops:
  17.6 4.5 %copy-start.1 = (f32[4,4,64,512]{3,2,1,0:T(8,128)S(1)}, f32[4,4,64,512]{3,2,1,0:T(8,128)}, u32[]{:S(2)}) copy-start(f32[4,4,64,512]{3,2,1,0:T(8,128)} %shard_map.82) | copy-start | bytes 6291460
  19.1 3.0 %collective-permute-start.2 = (f32[2,4,64,512]{3,2,1,0:T(8,128)S(1)}, f32[2,4,64,512]{3,2,1,0:T(8,128)S(1)}, u32[]{:S(2)}, u32[]{:S(2)}) collective-permute-start(f32[2,4,64,512]{3,2,1,0:T(8,128)S(1)} %slice.346), channel_id=1, source_target_pairs={{0,1},{1,0},{2,3},{3,2},{4,5},{5,4},{6,7},{7,6},{8,9},{9,8},{10,11... | collective-permute-start | bytes 3145736 | tf_op jit(solution)/shard_map/ppermute | solution.py:29
  23.2 21.5 %copy-start.13 = (f32[4,64,512]{2,1,0:T(8,128)}, f32[4,64,512]{2,1,0:T(8,128)S(1)}, u32[]{:S(2)}) copy-start(f32[4,64,512]{2,1,0:T(8,128)S(1)} %get-tuple-element.27.keep_ref) | copy-start | bytes 1572868
  23.2 13.3 %collective-permute-start.3 = (f32[4,64,512]{2,1,0:T(8,128)}, f32[4,64,512]{2,1,0:T(8,128)S(1)}, u32[]{:S(2)}, u32[]{:S(2)}) collective-permute-start(f32[4,64,512]{2,1,0:T(8,128)} %get-tuple-element.63), channel_id=1, source_target_pairs={{0,2},{2,0},{1,3},{3,1},{4,6},{6,4},{5,7},{7,5},{8,10},{10,8},{9,1... | collective-permute-start | bytes 1572872 | tf_op jit(solution)/shard_map/ppermute | solution.py:278
  34.8 6.8 %copy-start = (f32[4,4,64,512]{3,2,1,0:T(8,128)S(1)}, f32[4,4,64,512]{3,2,1,0:T(8,128)}, u32[]{:S(2)}) copy-start(f32[4,4,64,512]{3,2,1,0:T(8,128)} %shard_map.83) | copy-start | bytes 6291460
  36.5 5.3 %copy-start.14 = (f32[4,64,512]{2,1,0:T(8,128)}, f32[4,64,512]{2,1,0:T(8,128)S(1)}, u32[]{:S(2)}) copy-start(f32[4,64,512]{2,1,0:T(8,128)S(1)} %collective-permute-done.3.recv_ref) | copy-start | bytes 1572868
  38.0 5.9 %copy-start.18 = (f32[2,32,2048]{2,1,0:T(8,128)S(1)}, f32[2,32,2048]{2,1,0:T(8,128)}, u32[]{:S(2)}) copy-start(f32[2,32,2048]{2,1,0:T(8,128)} %param.14) | copy-start | bytes 1572868
  38.1 3.6 %collective-permute-start.4 = (f32[2,4,64,512]{3,2,1,0:T(8,128)S(1)}, f32[2,4,64,512]{3,2,1,0:T(8,128)S(1)}, u32[]{:S(2)}, u32[]{:S(2)}) collective-permute-start(f32[2,4,64,512]{3,2,1,0:T(8,128)S(1)} %slice.317), channel_id=1, source_target_pairs={{0,1},{1,0},{2,3},{3,2},{4,5},{5,4},{6,7},{7,6},{8,9},{9,8},{10,11... | collective-permute-start | bytes 3145736 | tf_op jit(solution)/shard_map/ppermute | solution.py:29
  42.8 28.0 %copy-start.12 = (f32[4,64,512]{2,1,0:T(8,128)}, f32[4,64,512]{2,1,0:T(8,128)S(1)}, u32[]{:S(2)}) copy-start(f32[4,64,512]{2,1,0:T(8,128)S(1)} %get-tuple-element.59.keep_ref) | copy-start | bytes 1572868
  42.8 27.9 %collective-permute-start.7 = (f32[4,64,512]{2,1,0:T(8,128)}, f32[4,64,512]{2,1,0:T(8,128)}, u32[]{:S(2)}, u32[]{:S(2)}) collective-permute-start(f32[4,64,512]{2,1,0:T(8,128)} %get-tuple-element.60), channel_id=1, source_target_pairs={{0,2},{2,0},{1,3},{3,1},{4,6},{6,4},{5,7},{7,5},{8,10},{10,8},{9,1... | collective-permute-start | bytes 1572872 | tf_op jit(solution)/shard_map/ppermute | solution.py:284
  46.4 16.7 %collective-permute-start.5 = (f32[4,16,512]{2,1,0:T(8,128)}, f32[4,16,512]{2,1,0:T(8,128)S(1)}, u32[]{:S(2)}, u32[]{:S(2)}) collective-permute-start(f32[4,16,512]{2,1,0:T(8,128)} %get-tuple-element.62), channel_id=1, source_target_pairs={{0,4},{4,8},{8,12},{12,16},{16,20},{20,24},{24,28},{28,32},{32,36}... | collective-permute-start | bytes 393224 | tf_op jit(solution)/shard_map/ppermute | solution.py:271
  49.6 13.5 %collective-permute-start.6 = (f32[4,16,512]{2,1,0:T(8,128)S(1)}, f32[4,16,512]{2,1,0:T(8,128)S(1)}, u32[]{:S(2)}, u32[]{:S(2)}) collective-permute-start(f32[4,16,512]{2,1,0:T(8,128)S(1)} %get-tuple-element.61), channel_id=1, source_target_pairs={{4,0},{8,4},{12,8},{16,12},{20,16},{24,20},{28,24},{32,28},{36,32}... | collective-permute-start | bytes 393224 | tf_op jit(solution)/shard_map/ppermute | solution.py:272
  70.7 38.3 %copy-start.26 = (s32[4,512]{1,0:T(4,128)S(1)}, s32[4,512]{1,0:T(4,128)}, u32[]{:S(2)}) copy-start(s32[4,512]{1,0:T(4,128)} %param.10) | copy-start | bytes 24580
  70.7 38.3 %copy-start.27 = (f32[2,4,128]{2,1,0:T(4,128)S(1)}, f32[2,4,128]{2,1,0:T(4,128)}, u32[]{:S(2)}) copy-start(f32[2,4,128]{2,1,0:T(4,128)} %param.9) | copy-start | bytes 12292
  70.7 23.2 %collective-permute-start.8 = (f32[4,64,512]{2,1,0:T(8,128)}, f32[4,64,512]{2,1,0:T(8,128)S(1)}, u32[]{:S(2)}, u32[]{:S(2)}) collective-permute-start(f32[4,64,512]{2,1,0:T(8,128)} %shard_map.84.b0_ref), channel_id=1, source_target_pairs={{0,2},{2,0},{1,3},{3,1},{4,6},{6,4},{5,7},{7,5},{8,10},{10,8},{9,1... | collective-permute-start | bytes 1572872 | tf_op jit(solution)/shard_map/ppermute | solution.py:287
  71.8 14.5 %collective-permute-start.9 = (f32[4,16,512]{2,1,0:T(8,128)S(1)}, f32[4,16,512]{2,1,0:T(8,128)S(1)}, u32[]{:S(2)}, u32[]{:S(2)}) collective-permute-start(f32[4,16,512]{2,1,0:T(8,128)S(1)} %get-tuple-element.58), channel_id=1, source_target_pairs={{0,4},{4,8},{8,12},{12,16},{16,20},{20,24},{24,28},{28,32},{32,36}... | collective-permute-start | bytes 393224 | tf_op jit(solution)/shard_map/ppermute | solution.py:271
  73.7 12.5 %collective-permute-start.10 = (f32[4,16,512]{2,1,0:T(8,128)S(1)}, f32[4,16,512]{2,1,0:T(8,128)S(1)}, u32[]{:S(2)}, u32[]{:S(2)}) collective-permute-start(f32[4,16,512]{2,1,0:T(8,128)S(1)} %get-tuple-element.57), channel_id=1, source_target_pairs={{4,0},{8,4},{12,8},{16,12},{20,16},{24,20},{28,24},{32,28},{36,32}... | collective-permute-start | bytes 393224 | tf_op jit(solution)/shard_map/ppermute | solution.py:272
  81.6 15.2 %collective-permute-start.11 = (f32[4,64,512]{2,1,0:T(8,128)}, f32[4,64,512]{2,1,0:T(8,128)S(1)}, u32[]{:S(2)}, u32[]{:S(2)}) collective-permute-start(f32[4,64,512]{2,1,0:T(8,128)} %shard_map.84.b0_ref), channel_id=1, source_target_pairs={{0,1},{1,0},{2,3},{3,2},{4,5},{5,4},{6,7},{7,6},{8,9},{9,8},{10,11... | collective-permute-start | bytes 1572872 | tf_op jit(solution)/shard_map/ppermute | solution.py:33
  93.9 16.5 %copy-start.15 = (f32[4,64,512]{2,1,0:T(8,128)}, f32[4,64,512]{2,1,0:T(8,128)S(1)}, u32[]{:S(2)}) copy-start(f32[4,64,512]{2,1,0:T(8,128)S(1)} %collective-permute-done.8.b1_ref) | copy-start | bytes 1572868
  93.9 4.5 %collective-permute-start.12 = (f32[4,64,512]{2,1,0:T(8,128)S(1)}, f32[4,64,512]{2,1,0:T(8,128)S(1)}, u32[]{:S(2)}, u32[]{:S(2)}) collective-permute-start(f32[4,64,512]{2,1,0:T(8,128)S(1)} %collective-permute-done.8.b1_ref), channel_id=1, source_target_pairs={{0,1},{1,0},{2,3},{3,2},{4,5},{5,4},{6,7},{7,6},{8,9},{9,8},{10,11... | collective-permute-start | bytes 1572872 | tf_op jit(solution)/shard_map/ppermute | solution.py:33
  96.8 13.5 %copy-start.16 = (f32[4,64,512]{2,1,0:T(8,128)}, f32[4,64,512]{2,1,0:T(8,128)S(1)}, u32[]{:S(2)}) copy-start(f32[4,64,512]{2,1,0:T(8,128)S(1)} %collective-permute-done.11.b2_ref) | copy-start | bytes 1572868
  99.2 23.8 %collective-permute-start.13 = (f32[4,64,512]{2,1,0:T(8,128)}, f32[4,64,512]{2,1,0:T(8,128)}, u32[]{:S(2)}, u32[]{:S(2)}) collective-permute-start(f32[4,64,512]{2,1,0:T(8,128)} %shard_map.85.b0_ref), channel_id=1, source_target_pairs={{0,2},{2,0},{1,3},{3,1},{4,6},{6,4},{5,7},{7,5},{8,10},{10,8},{9,1... | collective-permute-start | bytes 1572872 | tf_op jit(solution)/shard_map/ppermute | solution.py:292
  99.2 23.9 %collective-permute-start = (f32[128,8,2]{0,2,1:T(2,128)S(1)}, f32[128,8,2]{0,2,1:T(2,128)S(1)}, u32[]{:S(2)}, u32[]{:S(2)}) collective-permute-start(f32[128,8,2]{0,2,1:T(2,128)S(1)} %get-tuple-element.54), channel_id=1, source_target_pairs={{0,4},{4,8},{8,12},{12,16},{16,20},{20,24},{24,28},{28,32},{32,36}... | collective-permute-start | bytes 24584 | tf_op jit(solution)/shard_map/ppermute | solution.py:16
  101.1 24.2 %collective-permute-start.1 = (f32[128,8,2]{0,2,1:T(2,128)S(1)}, f32[128,8,2]{0,2,1:T(2,128)S(1)}, u32[]{:S(2)}, u32[]{:S(2)}) collective-permute-start(f32[128,8,2]{0,2,1:T(2,128)S(1)} %get-tuple-element.53), channel_id=1, source_target_pairs={{4,0},{8,4},{12,8},{16,12},{20,16},{24,20},{28,24},{32,28},{36,32}... | collective-permute-start | bytes 24584 | tf_op jit(solution)/shard_map/ppermute | solution.py:19
  109.0 19.9 %collective-permute-start.14 = (f32[4,64,512]{2,1,0:T(8,128)}, f32[4,64,512]{2,1,0:T(8,128)}, u32[]{:S(2)}, u32[]{:S(2)}) collective-permute-start(f32[4,64,512]{2,1,0:T(8,128)} %shard_map.85.b0_ref), channel_id=1, source_target_pairs={{0,1},{1,0},{2,3},{3,2},{4,5},{5,4},{6,7},{7,6},{8,9},{9,8},{10,11... | collective-permute-start | bytes 1572872 | tf_op jit(solution)/shard_map/ppermute | solution.py:33
  123.0 5.9 %collective-permute-start.15 = (f32[4,64,512]{2,1,0:T(8,128)}, f32[4,64,512]{2,1,0:T(8,128)}, u32[]{:S(2)}, u32[]{:S(2)}) collective-permute-start(f32[4,64,512]{2,1,0:T(8,128)} %collective-permute-done.13.b1_ref), channel_id=1, source_target_pairs={{0,1},{1,0},{2,3},{3,2},{4,5},{5,4},{6,7},{7,6},{8,9},{9,8},{10,11... | collective-permute-start | bytes 1572872 | tf_op jit(solution)/shard_map/ppermute | solution.py:33
  141.6 2.7 %copy-start.3 = (f32[8,128,256]{1,2,0:T(8,128)S(1)}, f32[8,128,256]{1,2,0:T(8,128)}, u32[]{:S(2)}) copy-start(f32[8,128,256]{1,2,0:T(8,128)} %copy.17) | copy-start | bytes 3145732
  144.3 2.8 %copy-start.8 = (f32[128,4,512]{0,2,1:T(8,128)S(1)}, f32[128,4,512]{0,2,1:T(8,128)}, u32[]{:S(2)}) copy-start(f32[128,4,512]{0,2,1:T(8,128)} %get-tuple-element.41) | copy-start | bytes 3145732
  144.3 2.8 %copy-start.9 = (f32[128,4,512]{0,2,1:T(8,128)S(1)}, f32[128,4,512]{0,2,1:T(8,128)}, u32[]{:S(2)}) copy-start(f32[128,4,512]{0,2,1:T(8,128)} %get-tuple-element.42) | copy-start | bytes 3145732
  144.3 2.9 %copy-start.10 = (f32[128,4,512]{0,2,1:T(8,128)S(1)}, f32[128,4,512]{0,2,1:T(8,128)}, u32[]{:S(2)}) copy-start(f32[128,4,512]{0,2,1:T(8,128)} %get-tuple-element.49) | copy-start | bytes 3145732
  144.3 2.9 %copy-start.11 = (f32[128,4,512]{0,2,1:T(8,128)S(1)}, f32[128,4,512]{0,2,1:T(8,128)}, u32[]{:S(2)}) copy-start(f32[128,4,512]{0,2,1:T(8,128)} %get-tuple-element.50) | copy-start | bytes 3145732
  145.9 2.3 %copy-start.7 = (f32[128,4,512]{0,2,1:T(8,128)S(1)}, f32[128,4,512]{0,2,1:T(8,128)}, u32[]{:S(2)}) copy-start(f32[128,4,512]{0,2,1:T(8,128)} %get-tuple-element.52) | copy-start | bytes 3145732
  (12 other events, 16.2 us)

commit v11 on v10

--- a/solution.py
+++ b/solution.py
@@ -26,7 +26,8 @@
 
 
 def reduce_cores(field):
-    return field[:2] + lax.ppermute(field[2:], "dir", CORE_SWAP)
+    keep, send = field
+    return keep + lax.ppermute(send, "dir", CORE_SWAP)
 
 
 def gather_blocks(local, other):
@@ -72,25 +73,26 @@
     return ((rank // 2 + slot % 2) % 2) * 2 + (rank % 2 + slot // 2) % 2
 
 
-def upward_kernel(xt_ref, m_ref, cos_ref, sin_ref, out_ref):
+def upward_kernel(xt_ref, m_ref, cos_ref, sin_ref, keep_ref, send_ref):
     groups = xt_ref.shape[0]
-    comps, slots, width = out_ref.shape[1:]
+    comps, slots, width = keep_ref.shape[1:]
     half = comps // 2
-    first = pl.multiple_of(slot_part(pl.program_id(0)) * width, 128)
-    m = m_ref[:, pl.ds(first, width)]
-    acc_re = jnp.zeros((half, slots, width), jnp.float32)
-    acc_im = jnp.zeros((half, slots, width), jnp.float32)
-    for g in range(groups):
-        r = jnp.dot(xt_ref[g], m, precision=HIGHEST, preferred_element_type=jnp.float32)
-        r = r.reshape(comps, slots, width)
-        c = cos_ref[pl.ds(g, 1), pl.ds(first, width)].reshape(1, 1, width)
-        s = sin_ref[pl.ds(g, 1), pl.ds(first, width)].reshape(1, 1, width)
-        re = r[:half]
-        im = r[half:]
-        acc_re = acc_re + (c * re - s * im)
-        acc_im = acc_im + (c * im + s * re)
-    out_ref[0, :half] = acc_re
-    out_ref[0, half:] = acc_im
+    for slot, out_ref in ((pl.program_id(0), keep_ref), (pl.program_id(0) + 2, send_ref)):
+        first = pl.multiple_of(slot_part(slot) * width, 128)
+        m = m_ref[:, pl.ds(first, width)]
+        acc_re = jnp.zeros((half, slots, width), jnp.float32)
+        acc_im = jnp.zeros((half, slots, width), jnp.float32)
+        for g in range(groups):
+            r = jnp.dot(xt_ref[g], m, precision=HIGHEST, preferred_element_type=jnp.float32)
+            r = r.reshape(comps, slots, width)
+            c = cos_ref[pl.ds(g, 1), pl.ds(first, width)].reshape(1, 1, width)
+            s = sin_ref[pl.ds(g, 1), pl.ds(first, width)].reshape(1, 1, width)
+            re = r[:half]
+            im = r[half:]
+            acc_re = acc_re + (c * re - s * im)
+            acc_im = acc_im + (c * im + s * re)
+        out_ref[0, :half] = acc_re
+        out_ref[0, half:] = acc_im
 
 
 def upward(xt, m, cos, sin, parts, comps):
@@ -98,17 +100,19 @@
     total = m.shape[1]
     width = total // parts
     slots = rows // comps
+    out = jax.ShapeDtypeStruct((parts // 2, comps, slots, width), jnp.float32)
+    block = pl.BlockSpec((1, comps, slots, width), lambda j: (j, 0, 0, 0))
     return pl.pallas_call(
         upward_kernel,
-        grid=(parts,),
+        grid=(parts // 2,),
         in_specs=[
             pl.BlockSpec((groups, rows, q), lambda j: (0, 0, 0)),
             pl.BlockSpec((q, total), lambda j: (0, 0)),
             pl.BlockSpec((groups, total), lambda j: (0, 0)),
             pl.BlockSpec((groups, total), lambda j: (0, 0)),
         ],
-        out_specs=pl.BlockSpec((1, comps, slots, width), lambda j: (j, 0, 0, 0)),
-        out_shape=jax.ShapeDtypeStruct((parts, comps, slots, width), jnp.float32),
+        out_specs=[block, block],
+        out_shape=[out, out],
     )(xt, m, cos, sin)
 
 

time: 152 us -> 148 us (0.974)
  local copies, waits for them, and re-layouts: 24.3 us -> 20.1 us
    slice x2 -> x0, local copies, waits for them, and re-layouts: 2.99 us -> none  [reduce_cores(): return field[:2] + lax.ppermute(field[2:], 'dir', CORE_SWAP)]
    unnamed x57 -> x53, local copies, waits for them, and re-layouts: 5.27 us -> 6.18 us
where the time goes in v11:
time: 148 us; the launch traced here: 147 us
  Pallas kernels  57.9 us (39%)
  starting transfers between devices  40.1 us (27%)
  local copies, waits for them, and re-layouts  20.1 us (14%)
  waiting for transfers between devices  14.7 us (10%)
  other arithmetic  13.7 us (9%)
    pallas_call x2, Pallas kernels, downward(): pl.pallas_call(downward_kernel, grid=(groups,), in_specs=[block] * 4 + [p...  25.3 us
    pallas_call x2, Pallas kernels, upward(): pl.pallas_call(upward_kernel, grid=(parts // 2,), in_specs=[pl.BlockSpec(...  19.9 us
    ppermute x2, starting transfers between devices, translate(): high = lax.ppermute(high, 'box', backward)  14.5 us
    pallas_call x2, Pallas kernels, translate_call(): pl.pallas_call(translate_kernel, out_shape=jax.ShapeDtypeStruct(keep.shap...  12.6 us
    ppermute x1, starting transfers between devices, with_halo(): lax.ppermute(lax.slice_in_dim(block, 0, width, axis=dim), axis, backward)  7.87 us
    ppermute x2, waiting for transfers between devices, translate(): low = lax.ppermute(low, 'box', forward)  7.18 us
    ppermute x4, starting transfers between devices, gather_blocks(): mate_local, mate_other = lax.ppermute((local, other), 'dir', CORE_SWAP)  6.34 us
    unnamed x53, local copies, waits for them, and re-layouts  6.18 us
  transfers between devices with their start and end apart: 16, of which 6 were waited for; matrix products, arithmetic and copies ran while one was open for 9% of the time, Pallas kernels for 24%

profile of v11, /device:TPU:65, one launch (start us, length us, event | category | flops | bytes accessed | tf_op | source)
XLA Modules:
  0.0 146.9 jit_solution(5947808969829448625)
XLA Ops:
  0.0 2.0 %copy.10 = f32[128,8,512]{0,2,1:T(8,128)S(1)} copy(f32[128,8,512]{2,1,0:T(8,128)} %param.8) | data formatting | bytes 4194304 | tf_op args[0]
  4.5 2.7 %select_add_fusion.m_ref = f32[128,2048]{1,0:T(8,128)} fusion(f32[2048]{0:T(1024)S(1)} %bitcast.100, s32[2048]{0:T(1024)S(1)} %bitcast.116, f32[2048]{0:T(1024)S(1)} %bitcast.101, s32[2048]{0:T(1024)S(1)} %bitcast.117, f32[2048]{0:T(1024)S(1)} %bitcast.87, s32[2048]{0:T(1024)S(1)} %bitcast.103, f32[2048]{0:T(1024)S(1)} %bitcast.88, s32[2048]{0:T(1024)S(1)} %bitcast.104, ...), kind=kLoop, calls=%fused_computation.29 | loop fusion | flops 12320768 | bytes 1311232 | tf_op jit(solution)/shard_map/add | solution.py:42
  7.1 10.0 %shard_map.82 = (f32[2,4,64,512]{3,2,1,0:T(8,128)}, f32[2,4,64,512]{3,2,1,0:T(8,128)}) custom-call(f32[8,256,128]{2,1,0:T(8,128)} %bitcast.80, f32[128,2048]{1,0:T(8,128)} %select_add_fusion.m_ref, f32[8,2048]{1,0:T(8,128)} %get-tuple-element.110.cos_ref, f32[8,2048]{1,0:T(8,128)} %get-tuple-element.109.sin_ref), custom_call_target="tpu_custom_call" | custom-call | tf_op jit(solution)/shard_map/pallas_call | solution.py:105
  19.0 1.3 collective-permute-done.2
  22.6 10.0 %shard_map.83 = (f32[2,4,64,512]{3,2,1,0:T(8,128)}, f32[2,4,64,512]{3,2,1,0:T(8,128)}) custom-call(f32[8,256,128]{2,1,0:T(8,128)} %bitcast.81, f32[128,2048]{1,0:T(8,128)} %select_add_fusion.m_ref, f32[8,2048]{1,0:T(8,128)} %get-tuple-element.110.cos_ref, f32[8,2048]{1,0:T(8,128)} %get-tuple-element.109.sin_ref), custom_call_target="tpu_custom_call" | custom-call | tf_op jit(solution)/shard_map/pallas_call | solution.py:105
  32.6 2.1 %collective-permute-done.3.recv_ref = f32[4,64,512]{2,1,0:T(8,128)S(1)} collective-permute-done((f32[4,64,512]{2,1,0:T(8,128)}, f32[4,64,512]{2,1,0:T(8,128)S(1)}, u32[]{:S(2)}, u32[]{:S(2)}) %collective-permute-start.3) | collective-permute-done | bytes 524320 | tf_op jit(solution)/shard_map/ppermute | solution.py:282
  34.7 1.2 collective-permute-start.4
  36.0 2.5 %collective-permute-done.4 = f32[2,4,64,512]{3,2,1,0:T(8,128)S(1)} collective-permute-done((f32[2,4,64,512]{3,2,1,0:T(8,128)}, f32[2,4,64,512]{3,2,1,0:T(8,128)S(1)}, u32[]{:S(2)}, u32[]{:S(2)}) %collective-permute-start.4) | collective-permute-done | bytes 1048608 | tf_op jit(solution)/shard_map/ppermute | solution.py:30
  38.5 1.4 add.129
  42.8 1.6 %slice_add_fusion.2 = (f32[4,16,512]{2,1,0:T(8,128)S(1)}, f32[4,16,512]{2,1,0:T(8,128)}) fusion(f32[4,64,512]{2,1,0:T(8,128)} %copy-done.11, f32[4,64,512]{2,1,0:T(8,128)S(1)} %get-tuple-element.37.keep_ref), kind=kLoop, calls=%fused_computation.44 | loop fusion | flops 65536 | bytes 786432 | tf_op jit(solution)/shard_map/add | solution.py:274
  44.4 3.2 %collective-permute-start.5 = (f32[4,16,512]{2,1,0:T(8,128)}, f32[4,16,512]{2,1,0:T(8,128)S(1)}, u32[]{:S(2)}, u32[]{:S(2)}) collective-permute-start(f32[4,16,512]{2,1,0:T(8,128)} %get-tuple-element.72), channel_id=1, source_target_pairs={{0,4},{4,8},{8,12},{12,16},{16,20},{20,24},{24,28},{28,32},{32,36}... | collective-permute-start | bytes 393224 | tf_op jit(solution)/shard_map/ppermute | solution.py:275
  47.6 6.6 %collective-permute-start.6 = (f32[4,16,512]{2,1,0:T(8,128)S(1)}, f32[4,16,512]{2,1,0:T(8,128)S(1)}, u32[]{:S(2)}, u32[]{:S(2)}) collective-permute-start(f32[4,16,512]{2,1,0:T(8,128)S(1)} %get-tuple-element.71), channel_id=1, source_target_pairs={{4,0},{8,4},{12,8},{16,12},{20,16},{24,20},{28,24},{32,28},{36,32}... | collective-permute-start | bytes 393224 | tf_op jit(solution)/shard_map/ppermute | solution.py:276
  55.0 1.5 %dynamic-slice_bitcast_fusion = (f32[32,512]{1,0:T(8,128)}, f32[32,512]{1,0:T(8,128)}) fusion(f32[1,32,2048]{2,1,0:T(8,128)S(1)} %get-tuple-element.75, s32[]{:T(128)S(6)} %select_n.72, f32[1,32,2048]{2,1,0:T(8,128)} %get-tuple-element.76), kind=kLoop, calls=%fused_computation.46 | loop fusion | bytes 262148 | tf_op jit(solution)/shard_map/dynamic_slice | solution.py:255
  56.5 4.6 %collective-permute-done.5.low_ref = f32[4,16,512]{2,1,0:T(8,128)S(1)} collective-permute-done((f32[4,16,512]{2,1,0:T(8,128)}, f32[4,16,512]{2,1,0:T(8,128)S(1)}, u32[]{:S(2)}, u32[]{:S(2)}) %collective-permute-start.5) | collective-permute-done | bytes 131104 | tf_op jit(solution)/shard_map/ppermute | solution.py:275
  61.1 1.3 broadcast_in_dim.193.mask_ref
  62.4 6.3 %shard_map.84.b0_ref = f32[4,64,512]{2,1,0:T(8,128)} custom-call(f32[4,16,512]{2,1,0:T(8,128)} %copy-done.17, f32[4,64,512]{2,1,0:T(8,128)} %copy-done.10, f32[4,64,512]{2,1,0:T(8,128)} %copy-done.11, f32[4,16,512]{2,1,0:T(8,128)} %copy-done.18, f32[32,512]{1,0:T(8,128)} %get-tuple-element.124.cr_ref, f32[32,512]{1,0:T(8,128)} %get-tuple-element.123.ci_ref, ...), custom_call_target="tpu_custom_call" | custom-call | tf_op jit(solution)/shard_map/pallas_call | solution.py:216
  69.9 1.9 %collective-permute-start.9 = (f32[4,16,512]{2,1,0:T(8,128)S(1)}, f32[4,16,512]{2,1,0:T(8,128)S(1)}, u32[]{:S(2)}, u32[]{:S(2)}) collective-permute-start(f32[4,16,512]{2,1,0:T(8,128)S(1)} %get-tuple-element.68), channel_id=1, source_target_pairs={{0,4},{4,8},{8,12},{12,16},{16,20},{20,24},{24,28},{28,32},{32,36}... | collective-permute-start | bytes 393224 | tf_op jit(solution)/shard_map/ppermute | solution.py:275
  71.8 7.9 %collective-permute-start.10 = (f32[4,16,512]{2,1,0:T(8,128)S(1)}, f32[4,16,512]{2,1,0:T(8,128)S(1)}, u32[]{:S(2)}, u32[]{:S(2)}) collective-permute-start(f32[4,16,512]{2,1,0:T(8,128)S(1)} %get-tuple-element.67), channel_id=1, source_target_pairs={{4,0},{8,4},{12,8},{16,12},{20,16},{24,20},{28,24},{32,28},{36,32}... | collective-permute-start | bytes 393224 | tf_op jit(solution)/shard_map/ppermute | solution.py:276
  79.7 2.1 %collective-permute-start.11 = (f32[4,64,512]{2,1,0:T(8,128)}, f32[4,64,512]{2,1,0:T(8,128)S(1)}, u32[]{:S(2)}, u32[]{:S(2)}) collective-permute-start(f32[4,64,512]{2,1,0:T(8,128)} %shard_map.84.b0_ref), channel_id=1, source_target_pairs={{0,1},{1,0},{2,3},{3,2},{4,5},{5,4},{6,7},{7,6},{8,9},{9,8},{10,11... | collective-permute-start | bytes 1572872 | tf_op jit(solution)/shard_map/ppermute | solution.py:34
  81.7 2.6 %collective-permute-done.9.low_ref = f32[4,16,512]{2,1,0:T(8,128)S(1)} collective-permute-done((f32[4,16,512]{2,1,0:T(8,128)S(1)}, f32[4,16,512]{2,1,0:T(8,128)S(1)}, u32[]{:S(2)}, u32[]{:S(2)}) %collective-permute-start.9) | collective-permute-done | bytes 131104 | tf_op jit(solution)/shard_map/ppermute | solution.py:275
  85.6 6.3 %shard_map.85.b0_ref = f32[4,64,512]{2,1,0:T(8,128)} custom-call(f32[4,16,512]{2,1,0:T(8,128)} %copy-done.19, f32[4,64,512]{2,1,0:T(8,128)} %copy-done.9, f32[4,64,512]{2,1,0:T(8,128)} %collective-permute-done.7.recv_ref, f32[4,16,512]{2,1,0:T(8,128)} %copy-done.20, f32[32,512]{1,0:T(8,128)} %get-tuple-element.124.cr_ref, ...), custom_call_target="tpu_custom_call" | custom-call | tf_op jit(solution)/shard_map/pallas_call | solution.py:216
  91.9 2.9 %collective-permute-start.12 = (f32[4,64,512]{2,1,0:T(8,128)S(1)}, f32[4,64,512]{2,1,0:T(8,128)S(1)}, u32[]{:S(2)}, u32[]{:S(2)}) collective-permute-start(f32[4,64,512]{2,1,0:T(8,128)S(1)} %collective-permute-done.8.b1_ref), channel_id=1, source_target_pairs={{0,1},{1,0},{2,3},{3,2},{4,5},{5,4},{6,7},{7,6},{8,9},{9,8},{10,11... | collective-permute-start | bytes 1572872 | tf_op jit(solution)/shard_map/ppermute | solution.py:34
  94.9 1.5 %collective-permute-done.12.b3_ref = f32[4,64,512]{2,1,0:T(8,128)S(1)} collective-permute-done((f32[4,64,512]{2,1,0:T(8,128)S(1)}, f32[4,64,512]{2,1,0:T(8,128)S(1)}, u32[]{:S(2)}, u32[]{:S(2)}) %collective-permute-start.12) | collective-permute-done | bytes 524320 | tf_op jit(solution)/shard_map/ppermute | solution.py:34
  97.2 1.9 %collective-permute-start = (f32[128,8,2]{0,2,1:T(2,128)S(1)}, f32[128,8,2]{0,2,1:T(2,128)S(1)}, u32[]{:S(2)}, u32[]{:S(2)}) collective-permute-start(f32[128,8,2]{0,2,1:T(2,128)S(1)} %get-tuple-element.64), channel_id=1, source_target_pairs={{0,4},{4,8},{8,12},{12,16},{16,20},{20,24},{24,28},{28,32},{32,36}... | collective-permute-start | bytes 24584 | tf_op jit(solution)/shard_map/ppermute | solution.py:16
  99.2 7.9 %collective-permute-start.1 = (f32[128,8,2]{0,2,1:T(2,128)S(1)}, f32[128,8,2]{0,2,1:T(2,128)S(1)}, u32[]{:S(2)}, u32[]{:S(2)}) collective-permute-start(f32[128,8,2]{0,2,1:T(2,128)S(1)} %get-tuple-element.63), channel_id=1, source_target_pairs={{4,0},{8,4},{12,8},{16,12},{20,16},{24,20},{28,24},{32,28},{36,32}... | collective-permute-start | bytes 24584 | tf_op jit(solution)/shard_map/ppermute | solution.py:19
  107.1 1.3 collective-permute-start.14
  108.4 12.7 %shard_map.86 = f32[8,128,256]{2,1,0:T(8,128)} custom-call(f32[4,64,512]{2,1,0:T(8,128)} %shard_map.84.b0_ref, f32[4,64,512]{2,1,0:T(8,128)} %copy-done.13, f32[4,64,512]{2,1,0:T(8,128)} %copy-done.14, f32[4,64,512]{2,1,0:T(8,128)} %copy-done.15, f32[128,2048]{1,0:T(8,128)} %select_add_fusion.m_ref, f32[8,2048]{1,0:T(8,128)} %get-tuple-element.110.cos_ref, ...), custom_call_target="tpu_custom_call" | custom-call | tf_op jit(solution)/shard_map/pallas_call | solution.py:151
  121.1 2.2 %multiply_subtract_fusion.2 = (f32[128,4,512]{0,2,1:T(8,128)}, f32[128,4,512]{0,2,1:T(8,128)}, f32[128,4,512]{0,2,1:T(8,128)}, f32[128,4,512]{0,2,1:T(8,128)}) fusion(f32[128]{0:T(128)S(1)} %get-tuple-element.118, f32[128]{0:T(128)S(1)} %get-tuple-element.119, f32[128,8,512]{0,2,1:T(8,128)S(1)} %copy.10, f32[128,8,2]{0,2,1:T(2,128)S(1)} %collective-permute-done, ...), kind=kLoop, calls=%fused_computation.35 | loop fusion | flops 4980736 | bytes 6301696 | tf_op jit(solution)/shard_map/sub | solution.py:62
  123.4 2.3 %multiply_subtract_fusion = (f32[128,4,512]{0,2,1:T(8,128)}, f32[128,4,512]{0,2,1:T(8,128)}, f32[128,4,512]{0,2,1:T(8,128)}, f32[128,4,512]{0,2,1:T(8,128)}) fusion(f32[128]{0:T(128)S(1)} %get-tuple-element.122, f32[128]{0:T(128)S(1)} %get-tuple-element.115, f32[128,8,2]{0,2,1:T(2,128)S(1)} %collective-permute-done.1, f32[128,8,512]{0,2,1:T(8,128)S(1)} %copy.10, ...), kind=kLoop, calls=%fused_computation.31 | loop fusion | flops 4980736 | bytes 6301696 | tf_op jit(solution)/shard_map/sub | solution.py:62
  126.0 12.7 %shard_map.87 = f32[8,128,256]{2,1,0:T(8,128)} custom-call(f32[4,64,512]{2,1,0:T(8,128)} %shard_map.85.b0_ref, f32[4,64,512]{2,1,0:T(8,128)} %collective-permute-done.13.b1_ref, f32[4,64,512]{2,1,0:T(8,128)} %collective-permute-done.14.b2_ref, f32[4,64,512]{2,1,0:T(8,128)} %collective-permute-done.15.b3_ref, f32[128,2048]{1,0:T(8,128)} %select_add_fusion.m_ref, ...), custom_call_target="tpu_custom_call" | custom-call | tf_op jit(solution)/shard_map/pallas_call | solution.py:151
  138.7 1.5 %copy.18 = f32[8,128,256]{1,2,0:T(8,128)S(1)} copy(f32[8,128,256]{2,1,0:T(8,128)} %shard_map.87) | data formatting | bytes 2097152 | tf_op jit(solution)/shard_map/pallas_call | solution.py:151
  144.9 2.0 %copy.20 = f32[128,8,512]{2,1,0:T(8,128)} copy(f32[128,8,512]{0,2,1:T(8,128)S(1)} %fusion.3) | data formatting | bytes 4194304 | tf_op jit(solution)/shard_map/add | solution.py:303
  (88 shorter events, 18.4 us)
Async XLA Ops:
  17.1 3.2 %copy-start.12 = (f32[2,4,64,512]{3,2,1,0:T(8,128)S(1)}, f32[2,4,64,512]{3,2,1,0:T(8,128)}, u32[]{:S(2)}) copy-start(f32[2,4,64,512]{3,2,1,0:T(8,128)} %get-tuple-element.28) | copy-start | bytes 3145732
  17.1 3.2 %collective-permute-start.2 = (f32[2,4,64,512]{3,2,1,0:T(8,128)}, f32[2,4,64,512]{3,2,1,0:T(8,128)S(1)}, u32[]{:S(2)}, u32[]{:S(2)}) collective-permute-start(f32[2,4,64,512]{3,2,1,0:T(8,128)} %get-tuple-element.29), channel_id=1, source_target_pairs={{0,1},{1,0},{2,3},{3,2},{4,5},{5,4},{6,7},{7,6},{8,9},{9,8},{10,11... | collective-permute-start | bytes 3145736 | tf_op jit(solution)/shard_map/ppermute | solution.py:30
  21.4 21.4 %copy-start.10 = (f32[4,64,512]{2,1,0:T(8,128)}, f32[4,64,512]{2,1,0:T(8,128)S(1)}, u32[]{:S(2)}) copy-start(f32[4,64,512]{2,1,0:T(8,128)S(1)} %get-tuple-element.37.keep_ref) | copy-start | bytes 1572868
  21.4 13.3 %collective-permute-start.3 = (f32[4,64,512]{2,1,0:T(8,128)}, f32[4,64,512]{2,1,0:T(8,128)S(1)}, u32[]{:S(2)}, u32[]{:S(2)}) collective-permute-start(f32[4,64,512]{2,1,0:T(8,128)} %get-tuple-element.73), channel_id=1, source_target_pairs={{0,2},{2,0},{1,3},{3,1},{4,6},{6,4},{5,7},{7,5},{8,10},{10,8},{9,1... | collective-permute-start | bytes 1572872 | tf_op jit(solution)/shard_map/ppermute | solution.py:282
  34.7 5.2 %copy-start.11 = (f32[4,64,512]{2,1,0:T(8,128)}, f32[4,64,512]{2,1,0:T(8,128)S(1)}, u32[]{:S(2)}) copy-start(f32[4,64,512]{2,1,0:T(8,128)S(1)} %collective-permute-done.3.recv_ref) | copy-start | bytes 1572868
  34.7 7.3 %copy-start.16 = (f32[2,32,2048]{2,1,0:T(8,128)S(1)}, f32[2,32,2048]{2,1,0:T(8,128)}, u32[]{:S(2)}) copy-start(f32[2,32,2048]{2,1,0:T(8,128)} %param.14) | copy-start | bytes 1572868
  34.7 3.7 %collective-permute-start.4 = (f32[2,4,64,512]{3,2,1,0:T(8,128)}, f32[2,4,64,512]{3,2,1,0:T(8,128)S(1)}, u32[]{:S(2)}, u32[]{:S(2)}) collective-permute-start(f32[2,4,64,512]{3,2,1,0:T(8,128)} %get-tuple-element.36), channel_id=1, source_target_pairs={{0,1},{1,0},{2,3},{3,2},{4,5},{5,4},{6,7},{7,6},{8,9},{9,8},{10,11... | collective-permute-start | bytes 3145736 | tf_op jit(solution)/shard_map/ppermute | solution.py:30
  40.8 28.0 %copy-start.9 = (f32[4,64,512]{2,1,0:T(8,128)}, f32[4,64,512]{2,1,0:T(8,128)S(1)}, u32[]{:S(2)}) copy-start(f32[4,64,512]{2,1,0:T(8,128)S(1)} %get-tuple-element.69.keep_ref) | copy-start | bytes 1572868
  40.8 27.9 %collective-permute-start.7 = (f32[4,64,512]{2,1,0:T(8,128)}, f32[4,64,512]{2,1,0:T(8,128)}, u32[]{:S(2)}, u32[]{:S(2)}) collective-permute-start(f32[4,64,512]{2,1,0:T(8,128)} %get-tuple-element.70), channel_id=1, source_target_pairs={{0,2},{2,0},{1,3},{3,1},{4,6},{6,4},{5,7},{7,5},{8,10},{10,8},{9,1... | collective-permute-start | bytes 1572872 | tf_op jit(solution)/shard_map/ppermute | solution.py:288
  44.4 16.7 %collective-permute-start.5 = (f32[4,16,512]{2,1,0:T(8,128)}, f32[4,16,512]{2,1,0:T(8,128)S(1)}, u32[]{:S(2)}, u32[]{:S(2)}) collective-permute-start(f32[4,16,512]{2,1,0:T(8,128)} %get-tuple-element.72), channel_id=1, source_target_pairs={{0,4},{4,8},{8,12},{12,16},{16,20},{20,24},{24,28},{28,32},{32,36}... | collective-permute-start | bytes 393224 | tf_op jit(solution)/shard_map/ppermute | solution.py:275
  47.6 13.5 %collective-permute-start.6 = (f32[4,16,512]{2,1,0:T(8,128)S(1)}, f32[4,16,512]{2,1,0:T(8,128)S(1)}, u32[]{:S(2)}, u32[]{:S(2)}) collective-permute-start(f32[4,16,512]{2,1,0:T(8,128)S(1)} %get-tuple-element.71), channel_id=1, source_target_pairs={{4,0},{8,4},{12,8},{16,12},{20,16},{24,20},{28,24},{32,28},{36,32}... | collective-permute-start | bytes 393224 | tf_op jit(solution)/shard_map/ppermute | solution.py:276
  68.7 38.3 %copy-start.24 = (s32[4,512]{1,0:T(4,128)S(1)}, s32[4,512]{1,0:T(4,128)}, u32[]{:S(2)}) copy-start(s32[4,512]{1,0:T(4,128)} %param.10) | copy-start | bytes 24580
  68.7 38.3 %copy-start.25 = (f32[2,4,128]{2,1,0:T(4,128)S(1)}, f32[2,4,128]{2,1,0:T(4,128)}, u32[]{:S(2)}) copy-start(f32[2,4,128]{2,1,0:T(4,128)} %param.9) | copy-start | bytes 12292
  68.7 23.2 %collective-permute-start.8 = (f32[4,64,512]{2,1,0:T(8,128)}, f32[4,64,512]{2,1,0:T(8,128)S(1)}, u32[]{:S(2)}, u32[]{:S(2)}) collective-permute-start(f32[4,64,512]{2,1,0:T(8,128)} %shard_map.84.b0_ref), channel_id=1, source_target_pairs={{0,2},{2,0},{1,3},{3,1},{4,6},{6,4},{5,7},{7,5},{8,10},{10,8},{9,1... | collective-permute-start | bytes 1572872 | tf_op jit(solution)/shard_map/ppermute | solution.py:291
  69.9 14.4 %collective-permute-start.9 = (f32[4,16,512]{2,1,0:T(8,128)S(1)}, f32[4,16,512]{2,1,0:T(8,128)S(1)}, u32[]{:S(2)}, u32[]{:S(2)}) collective-permute-start(f32[4,16,512]{2,1,0:T(8,128)S(1)} %get-tuple-element.68), channel_id=1, source_target_pairs={{0,4},{4,8},{8,12},{12,16},{16,20},{20,24},{24,28},{28,32},{32,36}... | collective-permute-start | bytes 393224 | tf_op jit(solution)/shard_map/ppermute | solution.py:275
  71.8 12.5 %collective-permute-start.10 = (f32[4,16,512]{2,1,0:T(8,128)S(1)}, f32[4,16,512]{2,1,0:T(8,128)S(1)}, u32[]{:S(2)}, u32[]{:S(2)}) collective-permute-start(f32[4,16,512]{2,1,0:T(8,128)S(1)} %get-tuple-element.67), channel_id=1, source_target_pairs={{4,0},{8,4},{12,8},{16,12},{20,16},{24,20},{28,24},{32,28},{36,32}... | collective-permute-start | bytes 393224 | tf_op jit(solution)/shard_map/ppermute | solution.py:276
  79.7 15.2 %collective-permute-start.11 = (f32[4,64,512]{2,1,0:T(8,128)}, f32[4,64,512]{2,1,0:T(8,128)S(1)}, u32[]{:S(2)}, u32[]{:S(2)}) collective-permute-start(f32[4,64,512]{2,1,0:T(8,128)} %shard_map.84.b0_ref), channel_id=1, source_target_pairs={{0,1},{1,0},{2,3},{3,2},{4,5},{5,4},{6,7},{7,6},{8,9},{9,8},{10,11... | collective-permute-start | bytes 1572872 | tf_op jit(solution)/shard_map/ppermute | solution.py:34
  91.9 16.5 %copy-start.13 = (f32[4,64,512]{2,1,0:T(8,128)}, f32[4,64,512]{2,1,0:T(8,128)S(1)}, u32[]{:S(2)}) copy-start(f32[4,64,512]{2,1,0:T(8,128)S(1)} %collective-permute-done.8.b1_ref) | copy-start | bytes 1572868
  91.9 4.5 %collective-permute-start.12 = (f32[4,64,512]{2,1,0:T(8,128)S(1)}, f32[4,64,512]{2,1,0:T(8,128)S(1)}, u32[]{:S(2)}, u32[]{:S(2)}) collective-permute-start(f32[4,64,512]{2,1,0:T(8,128)S(1)} %collective-permute-done.8.b1_ref), channel_id=1, source_target_pairs={{0,1},{1,0},{2,3},{3,2},{4,5},{5,4},{6,7},{7,6},{8,9},{9,8},{10,11... | collective-permute-start | bytes 1572872 | tf_op jit(solution)/shard_map/ppermute | solution.py:34
  94.9 13.5 %copy-start.14 = (f32[4,64,512]{2,1,0:T(8,128)}, f32[4,64,512]{2,1,0:T(8,128)S(1)}, u32[]{:S(2)}) copy-start(f32[4,64,512]{2,1,0:T(8,128)S(1)} %collective-permute-done.11.b2_ref) | copy-start | bytes 1572868
  97.2 23.9 %collective-permute-start.13 = (f32[4,64,512]{2,1,0:T(8,128)}, f32[4,64,512]{2,1,0:T(8,128)}, u32[]{:S(2)}, u32[]{:S(2)}) collective-permute-start(f32[4,64,512]{2,1,0:T(8,128)} %shard_map.85.b0_ref), channel_id=1, source_target_pairs={{0,2},{2,0},{1,3},{3,1},{4,6},{6,4},{5,7},{7,5},{8,10},{10,8},{9,1... | collective-permute-start | bytes 1572872 | tf_op jit(solution)/shard_map/ppermute | solution.py:296
  97.2 23.9 %collective-permute-start = (f32[128,8,2]{0,2,1:T(2,128)S(1)}, f32[128,8,2]{0,2,1:T(2,128)S(1)}, u32[]{:S(2)}, u32[]{:S(2)}) collective-permute-start(f32[128,8,2]{0,2,1:T(2,128)S(1)} %get-tuple-element.64), channel_id=1, source_target_pairs={{0,4},{4,8},{8,12},{12,16},{16,20},{20,24},{24,28},{28,32},{32,36}... | collective-permute-start | bytes 24584 | tf_op jit(solution)/shard_map/ppermute | solution.py:16
  99.2 24.2 %collective-permute-start.1 = (f32[128,8,2]{0,2,1:T(2,128)S(1)}, f32[128,8,2]{0,2,1:T(2,128)S(1)}, u32[]{:S(2)}, u32[]{:S(2)}) collective-permute-start(f32[128,8,2]{0,2,1:T(2,128)S(1)} %get-tuple-element.63), channel_id=1, source_target_pairs={{4,0},{8,4},{12,8},{16,12},{20,16},{24,20},{28,24},{32,28},{36,32}... | collective-permute-start | bytes 24584 | tf_op jit(solution)/shard_map/ppermute | solution.py:19
  107.1 18.9 %collective-permute-start.14 = (f32[4,64,512]{2,1,0:T(8,128)}, f32[4,64,512]{2,1,0:T(8,128)}, u32[]{:S(2)}, u32[]{:S(2)}) collective-permute-start(f32[4,64,512]{2,1,0:T(8,128)} %shard_map.85.b0_ref), channel_id=1, source_target_pairs={{0,1},{1,0},{2,3},{3,2},{4,5},{5,4},{6,7},{7,6},{8,9},{9,8},{10,11... | collective-permute-start | bytes 1572872 | tf_op jit(solution)/shard_map/ppermute | solution.py:34
  121.1 5.0 %collective-permute-start.15 = (f32[4,64,512]{2,1,0:T(8,128)}, f32[4,64,512]{2,1,0:T(8,128)}, u32[]{:S(2)}, u32[]{:S(2)}) collective-permute-start(f32[4,64,512]{2,1,0:T(8,128)} %collective-permute-done.13.b1_ref), channel_id=1, source_target_pairs={{0,1},{1,0},{2,3},{3,2},{4,5},{5,4},{6,7},{7,6},{8,9},{9,8},{10,11... | collective-permute-start | bytes 1572872 | tf_op jit(solution)/shard_map/ppermute | solution.py:34
  123.3 2.3 %copy-start = (f32[8,128,256]{2,1,0:T(8,128)S(1)}, f32[8,128,256]{2,1,0:T(8,128)}, u32[]{:S(2)}) copy-start(f32[8,128,256]{2,1,0:T(8,128)} %shard_map.86) | copy-start | bytes 3145732
  140.3 1.8 %copy-start.7 = (f32[128,4,512]{0,2,1:T(8,128)S(1)}, f32[128,4,512]{0,2,1:T(8,128)}, u32[]{:S(2)}) copy-start(f32[128,4,512]{0,2,1:T(8,128)} %get-tuple-element.59) | copy-start | bytes 3145732
  140.3 2.2 %copy-start.8 = (f32[128,4,512]{0,2,1:T(8,128)S(1)}, f32[128,4,512]{0,2,1:T(8,128)}, u32[]{:S(2)}) copy-start(f32[128,4,512]{0,2,1:T(8,128)} %get-tuple-element.60) | copy-start | bytes 3145732
  140.5 2.4 %copy-start.1 = (f32[128,4,512]{0,2,1:T(8,128)S(1)}, f32[128,4,512]{0,2,1:T(8,128)}, u32[]{:S(2)}) copy-start(f32[128,4,512]{0,2,1:T(8,128)} %get-tuple-element.55) | copy-start | bytes 3145732
  140.5 2.7 %copy-start.2 = (f32[128,4,512]{0,2,1:T(8,128)S(1)}, f32[128,4,512]{0,2,1:T(8,128)}, u32[]{:S(2)}) copy-start(f32[128,4,512]{0,2,1:T(8,128)} %get-tuple-element.56) | copy-start | bytes 3145732
  140.5 3.0 %copy-start.3 = (f32[128,4,512]{0,2,1:T(8,128)S(1)}, f32[128,4,512]{0,2,1:T(8,128)}, u32[]{:S(2)}) copy-start(f32[128,4,512]{0,2,1:T(8,128)} %get-tuple-element.61) | copy-start | bytes 3145732
  140.5 3.2 %copy-start.4 = (f32[128,4,512]{0,2,1:T(8,128)S(1)}, f32[128,4,512]{0,2,1:T(8,128)}, u32[]{:S(2)}) copy-start(f32[128,4,512]{0,2,1:T(8,128)} %get-tuple-element.62) | copy-start | bytes 3145732
  (10 other events, 11.6 us)

commit v12 on v11

--- a/solution.py
+++ b/solution.py
@@ -246,9 +246,6 @@
 
     child_reach = child_coef.shape[1] // 2
     child_padded = with_halo(pattern, (("box", 2),), child_reach)
-    child_local = translate_padded(
-        child_padded, child_coef[0], child_coef[1], child_mask, child_reach
-    )
 
     parent_reach = parent_coef.shape[1] // 2
     own_real = lax.dynamic_slice_in_dim(parent_coef[0], parent_first, parent_dev, 1)
@@ -276,7 +273,13 @@
         high = lax.ppermute(high, "box", backward)
         return translate_call(low, keep, recv, high, own_real, own_imag, mask_lanes)
 
-    acc_a = reduce_cores(upward(chunk_xt(0), rows, cosine, sine, dir_size, 2 * step))
+    field_a, child_padded = lax.optimization_barrier(
+        (upward(chunk_xt(0), rows, cosine, sine, dir_size, 2 * step), child_padded)
+    )
+    acc_a = reduce_cores(field_a)
+    child_local = translate_padded(
+        child_padded, child_coef[0], child_coef[1], child_mask, child_reach
+    )
     acc_a, xt_b = lax.optimization_barrier((acc_a, chunk_xt(1)))
     keep_a, send_a = acc_a[0], acc_a[1]
     recv_a = lax.ppermute(send_a, "dir", ROW_SWAP)

time: 148 us -> 151 us (1.020)
  other arithmetic: 13.7 us -> 16.2 us
  starting transfers between devices: 40.1 us -> 42.6 us
    ppermute x2, starting transfers between devices: 14.5 us -> 16.7 us  [translate(): high = lax.ppermute(high, 'box', backward)]
    concatenate x0 -> x1, other arithmetic: none -> 1.83 us  [with_halo(): block = jnp.concatenate([low, block, high], axis=dim)]
    unnamed x53 -> x57, local copies, waits for them, and re-layouts: 6.18 us -> 5.59 us
  transfers between devices with their start and end apart: 16 -> 16, of which waited for: 6 -> 6; matrix products, arithmetic and copies ran while one was open for 9% -> 12% of each run, Pallas kernels for 24% -> 30%
where the time goes in v12:
time: 151 us
  Pallas kernels  57.9 us (38%)
  starting transfers between devices  42.6 us (28%)
  local copies, waits for them, and re-layouts  19.5 us (13%)
  other arithmetic  16.2 us (11%)
  waiting for transfers between devices  14.2 us (9%)
    pallas_call x2, Pallas kernels, downward(): pl.pallas_call(downward_kernel, grid=(groups,), in_specs=[block] * 4 + [p...  25.3 us
    pallas_call x2, Pallas kernels, upward(): pl.pallas_call(upward_kernel, grid=(parts // 2,), in_specs=[pl.BlockSpec(...  20 us
    ppermute x2, starting transfers between devices, translate(): high = lax.ppermute(high, 'box', backward)  16.7 us
    pallas_call x2, Pallas kernels, translate_call(): pl.pallas_call(translate_kernel, out_shape=jax.ShapeDtypeStruct(keep.shap...  12.6 us
    ppermute x4, starting transfers between devices, gather_blocks(): mate_local, mate_other = lax.ppermute((local, other), 'dir', CORE_SWAP)  7.22 us
    ppermute x2, waiting for transfers between devices, translate(): low = lax.ppermute(low, 'box', forward)  6.92 us
    ppermute x1, starting transfers between devices, with_halo(): lax.ppermute(lax.slice_in_dim(block, 0, width, axis=dim), axis, backward)  6.59 us
    unnamed x57, local copies, waits for them, and re-layouts  5.59 us
  transfers between devices with their start and end apart: 16, of which 6 were waited for; matrix products, arithmetic and copies ran while one was open for 12% of the time, Pallas kernels for 30%

profile of v12, /device:TPU:65, one launch (start us, length us, event | category | flops | bytes accessed | tf_op | source)
XLA Modules:
  0.0 150.8 jit_solution(3918793419008011582)
XLA Ops:
  0.0 2.0 %copy.10 = f32[128,8,512]{0,2,1:T(8,128)S(1)} copy(f32[128,8,512]{2,1,0:T(8,128)} %param.8) | data formatting | bytes 4194304 | tf_op args[0]
  2.1 3.2 %collective-permute-start = (f32[128,8,2]{0,2,1:T(2,128)S(1)}, f32[128,8,2]{0,2,1:T(2,128)S(1)}, u32[]{:S(2)}, u32[]{:S(2)}) collective-permute-start(f32[128,8,2]{0,2,1:T(2,128)S(1)} %get-tuple-element.71), channel_id=1, source_target_pairs={{0,4},{4,8},{8,12},{12,16},{16,20},{20,24},{24,28},{28,32},{32,36}... | collective-permute-start | bytes 24584 | tf_op jit(solution)/shard_map/ppermute | solution.py:16
  5.3 6.6 %collective-permute-start.1 = (f32[128,8,2]{0,2,1:T(2,128)S(1)}, f32[128,8,2]{0,2,1:T(2,128)S(1)}, u32[]{:S(2)}, u32[]{:S(2)}) collective-permute-start(f32[128,8,2]{0,2,1:T(2,128)S(1)} %get-tuple-element.72), channel_id=1, source_target_pairs={{4,0},{8,4},{12,8},{16,12},{20,16},{24,20},{28,24},{32,28},{36,32}... | collective-permute-start | bytes 24584 | tf_op jit(solution)/shard_map/ppermute | solution.py:19
  13.0 2.7 %select_add_fusion.m_ref = f32[128,2048]{1,0:T(8,128)} fusion(f32[2048]{0:T(1024)S(1)} %bitcast.116, s32[2048]{0:T(1024)S(1)} %bitcast.100, f32[2048]{0:T(1024)S(1)} %bitcast.117, s32[2048]{0:T(1024)S(1)} %bitcast.101, f32[2048]{0:T(1024)S(1)} %bitcast.103, s32[2048]{0:T(1024)S(1)} %bitcast.87, f32[2048]{0:T(1024)S(1)} %bitcast.104, s32[2048]{0:T(1024)S(1)} %bitcast.88, ...), kind=kLoop, calls=%fused_computation.18 | loop fusion | flops 12320768 | bytes 1311232 | tf_op jit(solution)/shard_map/add | solution.py:42
  17.0 10.0 %shard_map.82 = (f32[2,4,64,512]{3,2,1,0:T(8,128)}, f32[2,4,64,512]{3,2,1,0:T(8,128)}) custom-call(f32[8,256,128]{2,1,0:T(8,128)} %bitcast.81, f32[128,2048]{1,0:T(8,128)} %select_add_fusion.m_ref, f32[8,2048]{1,0:T(8,128)} %get-tuple-element.116.cos_ref, f32[8,2048]{1,0:T(8,128)} %get-tuple-element.115.sin_ref), custom_call_target="tpu_custom_call" | custom-call | tf_op jit(solution)/shard_map/pallas_call | solution.py:105
  27.0 1.8 %pad_maximum_fusion = f32[128,8,516]{0,2,1:T(8,128)S(1)} fusion(f32[128,8,2]{0,2,1:T(2,128)S(1)} %collective-permute-done.1, f32[128,8,512]{0,2,1:T(8,128)} %copy-done, f32[128,8,2]{0,2,1:T(2,128)S(1)} %collective-permute-done), kind=kLoop, calls=%fused_computation | loop fusion | flops 1056768 | bytes 4227072 | tf_op jit(solution)/shard_map/concatenate | solution.py:20
  28.9 1.3 collective-permute-start.2
  33.6 1.2 collective-permute-start.3
  34.8 10.0 %shard_map.83 = (f32[2,4,64,512]{3,2,1,0:T(8,128)}, f32[2,4,64,512]{3,2,1,0:T(8,128)}) custom-call(f32[8,256,128]{2,1,0:T(8,128)} %bitcast.80, f32[128,2048]{1,0:T(8,128)} %select_add_fusion.m_ref, f32[8,2048]{1,0:T(8,128)} %get-tuple-element.116.cos_ref, f32[8,2048]{1,0:T(8,128)} %get-tuple-element.115.sin_ref), custom_call_target="tpu_custom_call" | custom-call | tf_op jit(solution)/shard_map/pallas_call | solution.py:105
  44.8 2.1 %collective-permute-done.3.recv_ref = f32[4,64,512]{2,1,0:T(8,128)S(1)} collective-permute-done((f32[4,64,512]{2,1,0:T(8,128)}, f32[4,64,512]{2,1,0:T(8,128)S(1)}, u32[]{:S(2)}, u32[]{:S(2)}) %collective-permute-start.3) | collective-permute-done | bytes 524320 | tf_op jit(solution)/shard_map/ppermute | solution.py:285
  46.9 1.2 collective-permute-start.4
  48.2 2.5 %collective-permute-done.4 = f32[2,4,64,512]{3,2,1,0:T(8,128)S(1)} collective-permute-done((f32[2,4,64,512]{3,2,1,0:T(8,128)}, f32[2,4,64,512]{3,2,1,0:T(8,128)S(1)}, u32[]{:S(2)}, u32[]{:S(2)}) %collective-permute-start.4) | collective-permute-done | bytes 1048608 | tf_op jit(solution)/shard_map/ppermute | solution.py:30
  50.7 1.4 add.129
  55.0 1.7 %slice_add_fusion.2 = (f32[4,16,512]{2,1,0:T(8,128)}, f32[4,16,512]{2,1,0:T(8,128)}) fusion(f32[4,64,512]{2,1,0:T(8,128)} %copy-done.12, f32[4,64,512]{2,1,0:T(8,128)S(1)} %get-tuple-element.43.keep_ref), kind=kLoop, calls=%fused_computation.25 | loop fusion | flops 65536 | bytes 786432 | tf_op jit(solution)/shard_map/add | solution.py:271
  56.7 1.9 %collective-permute-start.5 = (f32[4,16,512]{2,1,0:T(8,128)}, f32[4,16,512]{2,1,0:T(8,128)S(1)}, u32[]{:S(2)}, u32[]{:S(2)}) collective-permute-start(f32[4,16,512]{2,1,0:T(8,128)} %get-tuple-element.78), channel_id=1, source_target_pairs={{0,4},{4,8},{8,12},{12,16},{16,20},{20,24},{24,28},{28,32},{32,36}... | collective-permute-start | bytes 393224 | tf_op jit(solution)/shard_map/ppermute | solution.py:272
  58.6 7.9 %collective-permute-start.6 = (f32[4,16,512]{2,1,0:T(8,128)}, f32[4,16,512]{2,1,0:T(8,128)S(1)}, u32[]{:S(2)}, u32[]{:S(2)}) collective-permute-start(f32[4,16,512]{2,1,0:T(8,128)} %get-tuple-element.77), channel_id=1, source_target_pairs={{4,0},{8,4},{12,8},{16,12},{20,16},{24,20},{28,24},{32,28},{36,32}... | collective-permute-start | bytes 393224 | tf_op jit(solution)/shard_map/ppermute | solution.py:273
  67.3 1.5 dynamic-slice_bitcast_fusion
  69.2 1.3 broadcast_in_dim.193.mask_ref
  70.5 6.3 %shard_map.84.b0_ref = f32[4,64,512]{2,1,0:T(8,128)} custom-call(f32[4,16,512]{2,1,0:T(8,128)} %copy-done.18, f32[4,64,512]{2,1,0:T(8,128)} %copy-done.11, f32[4,64,512]{2,1,0:T(8,128)} %copy-done.12, f32[4,16,512]{2,1,0:T(8,128)} %copy-done.19, f32[32,512]{1,0:T(8,128)} %get-tuple-element.130.cr_ref, f32[32,512]{1,0:T(8,128)} %get-tuple-element.129.ci_ref, ...), custom_call_target="tpu_custom_call" | custom-call | tf_op jit(solution)/shard_map/pallas_call | solution.py:216
  77.9 8.8 %collective-permute-start.10 = (f32[4,16,512]{2,1,0:T(8,128)S(1)}, f32[4,16,512]{2,1,0:T(8,128)S(1)}, u32[]{:S(2)}, u32[]{:S(2)}) collective-permute-start(f32[4,16,512]{2,1,0:T(8,128)S(1)} %get-tuple-element.73), channel_id=1, source_target_pairs={{4,0},{8,4},{12,8},{16,12},{20,16},{24,20},{28,24},{32,28},{36,32}... | collective-permute-start | bytes 393224 | tf_op jit(solution)/shard_map/ppermute | solution.py:273
  86.8 1.9 %collective-permute-start.9 = (f32[4,16,512]{2,1,0:T(8,128)S(1)}, f32[4,16,512]{2,1,0:T(8,128)S(1)}, u32[]{:S(2)}, u32[]{:S(2)}) collective-permute-start(f32[4,16,512]{2,1,0:T(8,128)S(1)} %get-tuple-element.74), channel_id=1, source_target_pairs={{0,4},{4,8},{8,12},{12,16},{16,20},{20,24},{24,28},{28,32},{32,36}... | collective-permute-start | bytes 393224 | tf_op jit(solution)/shard_map/ppermute | solution.py:272
  88.7 2.4 %collective-permute-start.11 = (f32[4,64,512]{2,1,0:T(8,128)}, f32[4,64,512]{2,1,0:T(8,128)S(1)}, u32[]{:S(2)}, u32[]{:S(2)}) collective-permute-start(f32[4,64,512]{2,1,0:T(8,128)} %shard_map.84.b0_ref), channel_id=1, source_target_pairs={{0,1},{1,0},{2,3},{3,2},{4,5},{5,4},{6,7},{7,6},{8,9},{9,8},{10,11... | collective-permute-start | bytes 1572872 | tf_op jit(solution)/shard_map/ppermute | solution.py:34
  91.2 6.5 %collective-permute-done.9.low_ref = f32[4,16,512]{2,1,0:T(8,128)S(1)} collective-permute-done((f32[4,16,512]{2,1,0:T(8,128)S(1)}, f32[4,16,512]{2,1,0:T(8,128)S(1)}, u32[]{:S(2)}, u32[]{:S(2)}) %collective-permute-start.9) | collective-permute-done | bytes 131104 | tf_op jit(solution)/shard_map/ppermute | solution.py:272
  98.3 6.3 %shard_map.85.b0_ref = f32[4,64,512]{2,1,0:T(8,128)} custom-call(f32[4,16,512]{2,1,0:T(8,128)} %copy-done.21, f32[4,64,512]{2,1,0:T(8,128)} %copy-done.10, f32[4,64,512]{2,1,0:T(8,128)} %collective-permute-done.7.recv_ref, f32[4,16,512]{2,1,0:T(8,128)} %copy-done.20, f32[32,512]{1,0:T(8,128)} %get-tuple-element.130.cr_ref, ...), custom_call_target="tpu_custom_call" | custom-call | tf_op jit(solution)/shard_map/pallas_call | solution.py:216
  104.6 2.9 %collective-permute-start.12 = (f32[4,64,512]{2,1,0:T(8,128)S(1)}, f32[4,64,512]{2,1,0:T(8,128)S(1)}, u32[]{:S(2)}, u32[]{:S(2)}) collective-permute-start(f32[4,64,512]{2,1,0:T(8,128)S(1)} %collective-permute-done.8.b1_ref), channel_id=1, source_target_pairs={{0,1},{1,0},{2,3},{3,2},{4,5},{5,4},{6,7},{7,6},{8,9},{9,8},{10,11... | collective-permute-start | bytes 1572872 | tf_op jit(solution)/shard_map/ppermute | solution.py:34
  107.5 1.5 %collective-permute-done.12.b3_ref = f32[4,64,512]{2,1,0:T(8,128)S(1)} collective-permute-done((f32[4,64,512]{2,1,0:T(8,128)S(1)}, f32[4,64,512]{2,1,0:T(8,128)S(1)}, u32[]{:S(2)}, u32[]{:S(2)}) %collective-permute-start.12) | collective-permute-done | bytes 524320 | tf_op jit(solution)/shard_map/ppermute | solution.py:34
  110.6 12.7 %shard_map.86 = f32[8,128,256]{2,1,0:T(8,128)} custom-call(f32[4,64,512]{2,1,0:T(8,128)} %shard_map.84.b0_ref, f32[4,64,512]{2,1,0:T(8,128)} %copy-done.14, f32[4,64,512]{2,1,0:T(8,128)} %copy-done.15, f32[4,64,512]{2,1,0:T(8,128)} %copy-done.16, f32[128,2048]{1,0:T(8,128)} %select_add_fusion.m_ref, f32[8,2048]{1,0:T(8,128)} %get-tuple-element.116.cos_ref, ...), custom_call_target="tpu_custom_call" | custom-call | tf_op jit(solution)/shard_map/pallas_call | solution.py:151
  124.5 1.5 %multiply_subtract_fusion.3 = (f32[128,4,512]{0,2,1:T(8,128)}, f32[128,4,512]{0,2,1:T(8,128)}) fusion(f32[128,8,516]{0,2,1:T(8,128)S(1)} %pad_maximum_fusion, f32[128]{0:T(128)S(1)} %get-tuple-element.126, f32[128]{0:T(128)S(1)} %get-tuple-element.127), kind=kLoop, calls=%fused_computation.17 | loop fusion | flops 1572864 | bytes 4195328 | tf_op jit(solution)/shard_map/sub | solution.py:62
  126.0 3.6 %multiply_subtract_fusion = (f32[128,4,512]{0,2,1:T(8,128)}, f32[128,4,512]{0,2,1:T(8,128)}, f32[128,4,512]{0,2,1:T(8,128)}, f32[128,4,512]{0,2,1:T(8,128)}, f32[128,4,512]{0,2,1:T(8,128)}, /*index=5*/f32[128,4,512]{0,2,1:T(8,128)}) fusion(f32[128,8,516]{0,2,1:T(8,128)S(1)} %pad_maximum_fusion, f32[128]{0:T(128)S(1)} %get-tuple-element.128, ...), kind=kLoop, calls=%fused_computation.11 | loop fusion | flops 4718592 | bytes 12585984 | tf_op jit(solution)/shard_map/sub | solution.py:62
  130.0 12.7 %shard_map.87 = f32[8,128,256]{2,1,0:T(8,128)} custom-call(f32[4,64,512]{2,1,0:T(8,128)} %shard_map.85.b0_ref, f32[4,64,512]{2,1,0:T(8,128)} %collective-permute-done.13.b1_ref, f32[4,64,512]{2,1,0:T(8,128)} %collective-permute-done.14.b2_ref, f32[4,64,512]{2,1,0:T(8,128)} %collective-permute-done.15.b3_ref, f32[128,2048]{1,0:T(8,128)} %select_add_fusion.m_ref, ...), custom_call_target="tpu_custom_call" | custom-call | tf_op jit(solution)/shard_map/pallas_call | solution.py:151
  142.7 1.5 %copy.17 = f32[8,128,256]{1,2,0:T(8,128)S(1)} copy(f32[8,128,256]{2,1,0:T(8,128)} %shard_map.87) | data formatting | bytes 2097152 | tf_op jit(solution)/shard_map/pallas_call | solution.py:151
  148.9 2.0 %copy.19 = f32[128,8,512]{2,1,0:T(8,128)} copy(f32[128,8,512]{0,2,1:T(8,128)S(1)} %fusion.3) | data formatting | bytes 4194304 | tf_op jit(solution)/shard_map/add | solution.py:306
  (93 shorter events, 19.3 us)
Async XLA Ops:
  0.0 11.9 %copy-start.22 = (s32[16,2048]{1,0:T(8,128)S(1)}, s32[16,2048]{1,0:T(8,128)}, u32[]{:S(2)}) copy-start(s32[16,2048]{1,0:T(8,128)} %param.11) | copy-start | bytes 393220
  0.0 12.0 %copy-start.23 = (f32[16,2048]{1,0:T(8,128)S(1)}, f32[16,2048]{1,0:T(8,128)}, u32[]{:S(2)}) copy-start(f32[16,2048]{1,0:T(8,128)} %param.12) | copy-start | bytes 393220
  0.0 12.1 %copy-start.24 = (f32[8,2048]{1,0:T(8,128)S(1)}, f32[8,2048]{1,0:T(8,128)}, u32[]{:S(2)}) copy-start(f32[8,2048]{1,0:T(8,128)} %param.13) | copy-start | bytes 196612
  2.1 13.8 %copy-start = (f32[128,8,512]{0,2,1:T(8,128)}, f32[128,8,512]{0,2,1:T(8,128)S(1)}, u32[]{:S(2)}) copy-start(f32[128,8,512]{0,2,1:T(8,128)S(1)} %copy.10) | copy-start | bytes 6291460
  2.1 24.9 %collective-permute-start = (f32[128,8,2]{0,2,1:T(2,128)S(1)}, f32[128,8,2]{0,2,1:T(2,128)S(1)}, u32[]{:S(2)}, u32[]{:S(2)}) collective-permute-start(f32[128,8,2]{0,2,1:T(2,128)S(1)} %get-tuple-element.71), channel_id=1, source_target_pairs={{0,4},{4,8},{8,12},{12,16},{16,20},{20,24},{24,28},{28,32},{32,36}... | collective-permute-start | bytes 24584 | tf_op jit(solution)/shard_map/ppermute | solution.py:16
  5.3 21.7 %collective-permute-start.1 = (f32[128,8,2]{0,2,1:T(2,128)S(1)}, f32[128,8,2]{0,2,1:T(2,128)S(1)}, u32[]{:S(2)}, u32[]{:S(2)}) collective-permute-start(f32[128,8,2]{0,2,1:T(2,128)S(1)} %get-tuple-element.72), channel_id=1, source_target_pairs={{4,0},{8,4},{12,8},{16,12},{20,16},{24,20},{28,24},{32,28},{36,32}... | collective-permute-start | bytes 24584 | tf_op jit(solution)/shard_map/ppermute | solution.py:19
  28.9 3.6 %copy-start.13 = (f32[2,4,64,512]{3,2,1,0:T(8,128)S(1)}, f32[2,4,64,512]{3,2,1,0:T(8,128)}, u32[]{:S(2)}) copy-start(f32[2,4,64,512]{3,2,1,0:T(8,128)} %get-tuple-element.34) | copy-start | bytes 3145732
  28.9 3.6 %collective-permute-start.2 = (f32[2,4,64,512]{3,2,1,0:T(8,128)S(1)}, f32[2,4,64,512]{3,2,1,0:T(8,128)S(1)}, u32[]{:S(2)}, u32[]{:S(2)}) collective-permute-start(f32[2,4,64,512]{3,2,1,0:T(8,128)S(1)} %copy-done.27), channel_id=1, source_target_pairs={{0,1},{1,0},{2,3},{3,2},{4,5},{5,4},{6,7},{7,6},{8,9},{9,8},{10,11... | collective-permute-start | bytes 3145736 | tf_op jit(solution)/shard_map/ppermute | solution.py:30
  33.6 21.4 %copy-start.11 = (f32[4,64,512]{2,1,0:T(8,128)}, f32[4,64,512]{2,1,0:T(8,128)S(1)}, u32[]{:S(2)}) copy-start(f32[4,64,512]{2,1,0:T(8,128)S(1)} %get-tuple-element.43.keep_ref) | copy-start | bytes 1572868
  33.6 13.3 %collective-permute-start.3 = (f32[4,64,512]{2,1,0:T(8,128)}, f32[4,64,512]{2,1,0:T(8,128)S(1)}, u32[]{:S(2)}, u32[]{:S(2)}) collective-permute-start(f32[4,64,512]{2,1,0:T(8,128)} %get-tuple-element.79), channel_id=1, source_target_pairs={{0,2},{2,0},{1,3},{3,1},{4,6},{6,4},{5,7},{7,5},{8,10},{10,8},{9,1... | collective-permute-start | bytes 1572872 | tf_op jit(solution)/shard_map/ppermute | solution.py:285
  46.9 5.2 %copy-start.12 = (f32[4,64,512]{2,1,0:T(8,128)}, f32[4,64,512]{2,1,0:T(8,128)S(1)}, u32[]{:S(2)}) copy-start(f32[4,64,512]{2,1,0:T(8,128)S(1)} %collective-permute-done.3.recv_ref) | copy-start | bytes 1572868
  46.9 7.3 %copy-start.17 = (f32[2,32,2048]{2,1,0:T(8,128)S(1)}, f32[2,32,2048]{2,1,0:T(8,128)}, u32[]{:S(2)}) copy-start(f32[2,32,2048]{2,1,0:T(8,128)} %param.14) | copy-start | bytes 1572868
  46.9 3.7 %collective-permute-start.4 = (f32[2,4,64,512]{3,2,1,0:T(8,128)}, f32[2,4,64,512]{3,2,1,0:T(8,128)S(1)}, u32[]{:S(2)}, u32[]{:S(2)}) collective-permute-start(f32[2,4,64,512]{3,2,1,0:T(8,128)} %get-tuple-element.42), channel_id=1, source_target_pairs={{0,1},{1,0},{2,3},{3,2},{4,5},{5,4},{6,7},{7,6},{8,9},{9,8},{10,11... | collective-permute-start | bytes 3145736 | tf_op jit(solution)/shard_map/ppermute | solution.py:30
  53.0 23.9 %copy-start.10 = (f32[4,64,512]{2,1,0:T(8,128)}, f32[4,64,512]{2,1,0:T(8,128)S(1)}, u32[]{:S(2)}) copy-start(f32[4,64,512]{2,1,0:T(8,128)S(1)} %get-tuple-element.75.keep_ref) | copy-start | bytes 1572868
  53.0 23.8 %collective-permute-start.7 = (f32[4,64,512]{2,1,0:T(8,128)}, f32[4,64,512]{2,1,0:T(8,128)}, u32[]{:S(2)}, u32[]{:S(2)}) collective-permute-start(f32[4,64,512]{2,1,0:T(8,128)} %get-tuple-element.76), channel_id=1, source_target_pairs={{0,2},{2,0},{1,3},{3,1},{4,6},{6,4},{5,7},{7,5},{8,10},{10,8},{9,1... | collective-permute-start | bytes 1572872 | tf_op jit(solution)/shard_map/ppermute | solution.py:291
  56.7 12.5 %collective-permute-start.5 = (f32[4,16,512]{2,1,0:T(8,128)}, f32[4,16,512]{2,1,0:T(8,128)S(1)}, u32[]{:S(2)}, u32[]{:S(2)}) collective-permute-start(f32[4,16,512]{2,1,0:T(8,128)} %get-tuple-element.78), channel_id=1, source_target_pairs={{0,4},{4,8},{8,12},{12,16},{16,20},{20,24},{24,28},{28,32},{32,36}... | collective-permute-start | bytes 393224 | tf_op jit(solution)/shard_map/ppermute | solution.py:272
  58.6 10.6 %collective-permute-start.6 = (f32[4,16,512]{2,1,0:T(8,128)}, f32[4,16,512]{2,1,0:T(8,128)S(1)}, u32[]{:S(2)}, u32[]{:S(2)}) collective-permute-start(f32[4,16,512]{2,1,0:T(8,128)} %get-tuple-element.77), channel_id=1, source_target_pairs={{4,0},{8,4},{12,8},{16,12},{20,16},{24,20},{28,24},{32,28},{36,32}... | collective-permute-start | bytes 393224 | tf_op jit(solution)/shard_map/ppermute | solution.py:273
  76.8 33.0 %copy-start.26 = (f32[2,4,128]{2,1,0:T(4,128)S(1)}, f32[2,4,128]{2,1,0:T(4,128)}, u32[]{:S(2)}) copy-start(f32[2,4,128]{2,1,0:T(4,128)} %param.9) | copy-start | bytes 12292
  76.8 33.0 %copy-start.25 = (s32[4,512]{1,0:T(4,128)S(1)}, s32[4,512]{1,0:T(4,128)}, u32[]{:S(2)}) copy-start(s32[4,512]{1,0:T(4,128)} %param.10) | copy-start | bytes 24580
  76.8 27.8 %collective-permute-start.8 = (f32[4,64,512]{2,1,0:T(8,128)}, f32[4,64,512]{2,1,0:T(8,128)S(1)}, u32[]{:S(2)}, u32[]{:S(2)}) collective-permute-start(f32[4,64,512]{2,1,0:T(8,128)} %shard_map.84.b0_ref), channel_id=1, source_target_pairs={{0,2},{2,0},{1,3},{3,1},{4,6},{6,4},{5,7},{7,5},{8,10},{10,8},{9,1... | collective-permute-start | bytes 1572872 | tf_op jit(solution)/shard_map/ppermute | solution.py:294
  77.9 13.2 %collective-permute-start.10 = (f32[4,16,512]{2,1,0:T(8,128)S(1)}, f32[4,16,512]{2,1,0:T(8,128)S(1)}, u32[]{:S(2)}, u32[]{:S(2)}) collective-permute-start(f32[4,16,512]{2,1,0:T(8,128)S(1)} %get-tuple-element.73), channel_id=1, source_target_pairs={{4,0},{8,4},{12,8},{16,12},{20,16},{24,20},{28,24},{32,28},{36,32}... | collective-permute-start | bytes 393224 | tf_op jit(solution)/shard_map/ppermute | solution.py:273
  86.8 10.9 %collective-permute-start.9 = (f32[4,16,512]{2,1,0:T(8,128)S(1)}, f32[4,16,512]{2,1,0:T(8,128)S(1)}, u32[]{:S(2)}, u32[]{:S(2)}) collective-permute-start(f32[4,16,512]{2,1,0:T(8,128)S(1)} %get-tuple-element.74), channel_id=1, source_target_pairs={{0,4},{4,8},{8,12},{12,16},{16,20},{20,24},{24,28},{28,32},{32,36}... | collective-permute-start | bytes 393224 | tf_op jit(solution)/shard_map/ppermute | solution.py:272
  88.7 18.8 %collective-permute-start.11 = (f32[4,64,512]{2,1,0:T(8,128)}, f32[4,64,512]{2,1,0:T(8,128)S(1)}, u32[]{:S(2)}, u32[]{:S(2)}) collective-permute-start(f32[4,64,512]{2,1,0:T(8,128)} %shard_map.84.b0_ref), channel_id=1, source_target_pairs={{0,1},{1,0},{2,3},{3,2},{4,5},{5,4},{6,7},{7,6},{8,9},{9,8},{10,11... | collective-permute-start | bytes 1572872 | tf_op jit(solution)/shard_map/ppermute | solution.py:34
  91.2 6.5 %copy-start.20 = (f32[4,16,512]{2,1,0:T(8,128)}, f32[4,16,512]{2,1,0:T(8,128)S(1)}, u32[]{:S(2)}) copy-start(f32[4,16,512]{2,1,0:T(8,128)S(1)} %collective-permute-done.10.high_ref) | copy-start | bytes 393220
  104.6 6.0 %copy-start.14 = (f32[4,64,512]{2,1,0:T(8,128)}, f32[4,64,512]{2,1,0:T(8,128)S(1)}, u32[]{:S(2)}) copy-start(f32[4,64,512]{2,1,0:T(8,128)S(1)} %collective-permute-done.8.b1_ref) | copy-start | bytes 1572868
  104.6 4.4 %collective-permute-start.12 = (f32[4,64,512]{2,1,0:T(8,128)S(1)}, f32[4,64,512]{2,1,0:T(8,128)S(1)}, u32[]{:S(2)}, u32[]{:S(2)}) collective-permute-start(f32[4,64,512]{2,1,0:T(8,128)S(1)} %collective-permute-done.8.b1_ref), channel_id=1, source_target_pairs={{0,1},{1,0},{2,3},{3,2},{4,5},{5,4},{6,7},{7,6},{8,9},{9,8},{10,11... | collective-permute-start | bytes 1572872 | tf_op jit(solution)/shard_map/ppermute | solution.py:34
  107.5 3.1 %copy-start.15 = (f32[4,64,512]{2,1,0:T(8,128)}, f32[4,64,512]{2,1,0:T(8,128)S(1)}, u32[]{:S(2)}) copy-start(f32[4,64,512]{2,1,0:T(8,128)S(1)} %collective-permute-done.11.b2_ref) | copy-start | bytes 1572868
  109.8 13.4 %collective-permute-start.13 = (f32[4,64,512]{2,1,0:T(8,128)}, f32[4,64,512]{2,1,0:T(8,128)}, u32[]{:S(2)}, u32[]{:S(2)}) collective-permute-start(f32[4,64,512]{2,1,0:T(8,128)} %shard_map.85.b0_ref), channel_id=1, source_target_pairs={{0,2},{2,0},{1,3},{3,1},{4,6},{6,4},{5,7},{7,5},{8,10},{10,8},{9,1... | collective-permute-start | bytes 1572872 | tf_op jit(solution)/shard_map/ppermute | solution.py:299
  109.9 20.1 %collective-permute-start.14 = (f32[4,64,512]{2,1,0:T(8,128)}, f32[4,64,512]{2,1,0:T(8,128)}, u32[]{:S(2)}, u32[]{:S(2)}) collective-permute-start(f32[4,64,512]{2,1,0:T(8,128)} %shard_map.85.b0_ref), channel_id=1, source_target_pairs={{0,1},{1,0},{2,3},{3,2},{4,5},{5,4},{6,7},{7,6},{8,9},{9,8},{10,11... | collective-permute-start | bytes 1572872 | tf_op jit(solution)/shard_map/ppermute | solution.py:34
  123.3 6.7 %collective-permute-start.15 = (f32[4,64,512]{2,1,0:T(8,128)}, f32[4,64,512]{2,1,0:T(8,128)}, u32[]{:S(2)}, u32[]{:S(2)}) collective-permute-start(f32[4,64,512]{2,1,0:T(8,128)} %collective-permute-done.13.b1_ref), channel_id=1, source_target_pairs={{0,1},{1,0},{2,3},{3,2},{4,5},{5,4},{6,7},{7,6},{8,9},{9,8},{10,11... | collective-permute-start | bytes 1572872 | tf_op jit(solution)/shard_map/ppermute | solution.py:34
  126.0 3.7 %copy-start.1 = (f32[8,128,256]{2,1,0:T(8,128)S(1)}, f32[8,128,256]{2,1,0:T(8,128)}, u32[]{:S(2)}) copy-start(f32[8,128,256]{2,1,0:T(8,128)} %shard_map.86) | copy-start | bytes 3145732
  144.4 3.2 %copy-start.5 = (f32[128,4,512]{0,2,1:T(8,128)S(1)}, f32[128,4,512]{0,2,1:T(8,128)}, u32[]{:S(2)}) copy-start(f32[128,4,512]{0,2,1:T(8,128)} %get-tuple-element.58) | copy-start | bytes 3145732
  (12 other events, 20.9 us)

commit v13 on v11

--- a/solution.py
+++ b/solution.py
@@ -245,10 +245,6 @@
     rows = interp_matrix(interp_index, interp_weight, child_first, child_dev)
 
     child_reach = child_coef.shape[1] // 2
-    child_padded = with_halo(pattern, (("box", 2),), child_reach)
-    child_local = translate_padded(
-        child_padded, child_coef[0], child_coef[1], child_mask, child_reach
-    )
 
     parent_reach = parent_coef.shape[1] // 2
     own_real = lax.dynamic_slice_in_dim(parent_coef[0], parent_first, parent_dev, 1)
@@ -295,7 +291,11 @@
     all_a, local_b = lax.optimization_barrier((all_a, local_b))
     other_b = lax.ppermute(local_b, "dir", ROW_SWAP)
     far_a = downward(all_a, rows, cosine, sine)
-    far_a, other_b = lax.optimization_barrier((far_a, other_b))
+    far_a, other_b, edges = lax.optimization_barrier((far_a, other_b, pattern))
+    child_padded = with_halo(edges, (("box", 2),), child_reach)
+    child_local = translate_padded(
+        child_padded, child_coef[0], child_coef[1], child_mask, child_reach
+    )
     far_b = downward(gather_blocks(local_b, other_b), rows, cosine, sine)
     fars = [far.reshape(groups, child_dev, 2, step, slots) for far in (far_a, far_b)]
     far = jnp.concatenate(fars, axis=3).transpose(1, 2, 3, 4, 0)

time: 148 us -> 150 us (1.014)
  waiting for transfers between devices: 14.7 us -> 18.8 us
  other arithmetic: 13.7 us -> 11.2 us
    ppermute x2, waiting for transfers between devices: 7.18 us -> 11.5 us  [translate(): low = lax.ppermute(low, 'box', forward)]
    optimization_barrier x1 -> x2, local copies, waits for them, and re-layouts: 0.32 us -> 3.54 us  [body(): far_a, other_b, edges = lax.optimization_barrier((far_a, other_b, pattern))]
    add x2, other arithmetic: 2.66 us -> 0.07 us  [translate(): high = keep[:, :parent_reach] + recv[:, :parent_reach]]
  transfers between devices with their start and end apart: 16 -> 16, of which waited for: 6 -> 6; matrix products, arithmetic and copies ran while one was open for 9% -> 7% of each run, Pallas kernels for 24% -> 24%
where the time goes in v13:
time: 150 us; the launch traced here: 149 us
  Pallas kernels  57.9 us (39%)
  starting transfers between devices  40.3 us (27%)
  local copies, waits for them, and re-layouts  20.1 us (13%)
  waiting for transfers between devices  18.8 us (13%)
  other arithmetic  11.2 us (7%)
    pallas_call x2, Pallas kernels, downward(): pl.pallas_call(downward_kernel, grid=(groups,), in_specs=[block] * 4 + [p...  25.3 us
    pallas_call x2, Pallas kernels, upward(): pl.pallas_call(upward_kernel, grid=(parts // 2,), in_specs=[pl.BlockSpec(...  20 us
    ppermute x2, starting transfers between devices, translate(): high = lax.ppermute(high, 'box', backward)  14.5 us
    pallas_call x2, Pallas kernels, translate_call(): pl.pallas_call(translate_kernel, out_shape=jax.ShapeDtypeStruct(keep.shap...  12.6 us
    ppermute x2, waiting for transfers between devices, translate(): low = lax.ppermute(low, 'box', forward)  11.5 us
    ppermute x1, starting transfers between devices, with_halo(): lax.ppermute(lax.slice_in_dim(block, 0, width, axis=dim), axis, backward)  8.15 us
    unnamed x53, local copies, waits for them, and re-layouts  6.14 us
    ppermute x4, starting transfers between devices, gather_blocks(): mate_local, mate_other = lax.ppermute((local, other), 'dir', CORE_SWAP)  5.83 us
  transfers between devices with their start and end apart: 16, of which 6 were waited for; matrix products, arithmetic and copies ran while one was open for 7% of the time, Pallas kernels for 24%

profile of v13, /device:TPU:65, one launch (start us, length us, event | category | flops | bytes accessed | tf_op | source)
XLA Modules:
  0.0 148.7 jit_solution(10943670961345364143)
XLA Ops:
  0.0 2.0 %copy.10 = f32[128,8,512]{0,2,1:T(8,128)S(1)} copy(f32[128,8,512]{2,1,0:T(8,128)} %param.8) | data formatting | bytes 4194304 | tf_op args[0]
  4.5 2.7 %select_add_fusion.m_ref = f32[128,2048]{1,0:T(8,128)} fusion(f32[2048]{0:T(1024)S(1)} %bitcast.100, s32[2048]{0:T(1024)S(1)} %bitcast.116, f32[2048]{0:T(1024)S(1)} %bitcast.101, s32[2048]{0:T(1024)S(1)} %bitcast.117, f32[2048]{0:T(1024)S(1)} %bitcast.87, s32[2048]{0:T(1024)S(1)} %bitcast.103, f32[2048]{0:T(1024)S(1)} %bitcast.88, s32[2048]{0:T(1024)S(1)} %bitcast.104, ...), kind=kLoop, calls=%fused_computation.37 | loop fusion | flops 12320768 | bytes 1311232 | tf_op jit(solution)/shard_map/add | solution.py:42
  7.1 10.0 %shard_map.82 = (f32[2,4,64,512]{3,2,1,0:T(8,128)}, f32[2,4,64,512]{3,2,1,0:T(8,128)}) custom-call(f32[8,256,128]{2,1,0:T(8,128)} %bitcast.80, f32[128,2048]{1,0:T(8,128)} %select_add_fusion.m_ref, f32[8,2048]{1,0:T(8,128)} %get-tuple-element.112.cos_ref, f32[8,2048]{1,0:T(8,128)} %get-tuple-element.111.sin_ref), custom_call_target="tpu_custom_call" | custom-call | tf_op jit(solution)/shard_map/pallas_call | solution.py:105
  19.0 1.3 collective-permute-done
  20.7 1.3 collective-permute-start.1
  22.0 10.0 %shard_map.83 = (f32[2,4,64,512]{3,2,1,0:T(8,128)}, f32[2,4,64,512]{3,2,1,0:T(8,128)}) custom-call(f32[8,256,128]{2,1,0:T(8,128)} %bitcast.81, f32[128,2048]{1,0:T(8,128)} %select_add_fusion.m_ref, f32[8,2048]{1,0:T(8,128)} %get-tuple-element.112.cos_ref, f32[8,2048]{1,0:T(8,128)} %get-tuple-element.111.sin_ref), custom_call_target="tpu_custom_call" | custom-call | tf_op jit(solution)/shard_map/pallas_call | solution.py:105
  32.0 1.9 %collective-permute-done.1.recv_ref = f32[4,64,512]{2,1,0:T(8,128)S(1)} collective-permute-done((f32[4,64,512]{2,1,0:T(8,128)S(1)}, f32[4,64,512]{2,1,0:T(8,128)S(1)}, u32[]{:S(2)}, u32[]{:S(2)}) %collective-permute-start.1) | collective-permute-done | bytes 524320 | tf_op jit(solution)/shard_map/ppermute | solution.py:278
  35.1 2.5 %collective-permute-done.2 = f32[2,4,64,512]{3,2,1,0:T(8,128)S(1)} collective-permute-done((f32[2,4,64,512]{3,2,1,0:T(8,128)}, f32[2,4,64,512]{3,2,1,0:T(8,128)S(1)}, u32[]{:S(2)}, u32[]{:S(2)}) %collective-permute-start.2) | collective-permute-done | bytes 1048608 | tf_op jit(solution)/shard_map/ppermute | solution.py:30
  37.6 1.5 add.122
  39.2 1.5 collective-permute-start.5
  40.8 3.2 %collective-permute-start.3 = (f32[4,16,512]{2,1,0:T(8,128)S(1)}, f32[4,16,512]{2,1,0:T(8,128)S(1)}, u32[]{:S(2)}, u32[]{:S(2)}) collective-permute-start(f32[4,16,512]{2,1,0:T(8,128)S(1)} %get-tuple-element.74), channel_id=1, source_target_pairs={{0,4},{4,8},{8,12},{12,16},{16,20},{20,24},{24,28},{28,32},{32,36}... | collective-permute-start | bytes 393224 | tf_op jit(solution)/shard_map/ppermute | solution.py:271
  44.0 6.6 %collective-permute-start.4 = (f32[4,16,512]{2,1,0:T(8,128)S(1)}, f32[4,16,512]{2,1,0:T(8,128)S(1)}, u32[]{:S(2)}, u32[]{:S(2)}) collective-permute-start(f32[4,16,512]{2,1,0:T(8,128)S(1)} %get-tuple-element.73), channel_id=1, source_target_pairs={{4,0},{8,4},{12,8},{16,12},{20,16},{24,20},{28,24},{32,28},{36,32}... | collective-permute-start | bytes 393224 | tf_op jit(solution)/shard_map/ppermute | solution.py:272
  52.1 7.5 %collective-permute-done.3.low_ref = f32[4,16,512]{2,1,0:T(8,128)S(1)} collective-permute-done((f32[4,16,512]{2,1,0:T(8,128)S(1)}, f32[4,16,512]{2,1,0:T(8,128)S(1)}, u32[]{:S(2)}, u32[]{:S(2)}) %collective-permute-start.3) | collective-permute-done | bytes 131104 | tf_op jit(solution)/shard_map/ppermute | solution.py:271
  59.6 1.3 broadcast_in_dim.193.mask_ref
  60.9 6.3 %shard_map.84.b0_ref = f32[4,64,512]{2,1,0:T(8,128)} custom-call(f32[4,16,512]{2,1,0:T(8,128)} %copy-done.17, f32[4,64,512]{2,1,0:T(8,128)} %copy-done.9, f32[4,64,512]{2,1,0:T(8,128)} %copy-done.11, f32[4,16,512]{2,1,0:T(8,128)} %copy-done.18, f32[32,512]{1,0:T(8,128)} %get-tuple-element.126.cr_ref, f32[32,512]{1,0:T(8,128)} %get-tuple-element.125.ci_ref, ...), custom_call_target="tpu_custom_call" | custom-call | tf_op jit(solution)/shard_map/pallas_call | solution.py:216
  67.3 1.9 %collective-permute-start.7 = (f32[4,16,512]{2,1,0:T(8,128)S(1)}, f32[4,16,512]{2,1,0:T(8,128)S(1)}, u32[]{:S(2)}, u32[]{:S(2)}) collective-permute-start(f32[4,16,512]{2,1,0:T(8,128)S(1)} %get-tuple-element.70), channel_id=1, source_target_pairs={{0,4},{4,8},{8,12},{12,16},{16,20},{20,24},{24,28},{28,32},{32,36}... | collective-permute-start | bytes 393224 | tf_op jit(solution)/shard_map/ppermute | solution.py:271
  69.3 7.9 %collective-permute-start.8 = (f32[4,16,512]{2,1,0:T(8,128)S(1)}, f32[4,16,512]{2,1,0:T(8,128)S(1)}, u32[]{:S(2)}, u32[]{:S(2)}) collective-permute-start(f32[4,16,512]{2,1,0:T(8,128)S(1)} %get-tuple-element.69), channel_id=1, source_target_pairs={{4,0},{8,4},{12,8},{16,12},{20,16},{24,20},{28,24},{32,28},{36,32}... | collective-permute-start | bytes 393224 | tf_op jit(solution)/shard_map/ppermute | solution.py:272
  77.1 2.1 %collective-permute-start.9 = (f32[4,64,512]{2,1,0:T(8,128)}, f32[4,64,512]{2,1,0:T(8,128)S(1)}, u32[]{:S(2)}, u32[]{:S(2)}) collective-permute-start(f32[4,64,512]{2,1,0:T(8,128)} %shard_map.84.b0_ref), channel_id=1, source_target_pairs={{0,1},{1,0},{2,3},{3,2},{4,5},{5,4},{6,7},{7,6},{8,9},{9,8},{10,11... | collective-permute-start | bytes 1572872 | tf_op jit(solution)/shard_map/ppermute | solution.py:34
  79.2 3.9 %collective-permute-done.7.low_ref = f32[4,16,512]{2,1,0:T(8,128)S(1)} collective-permute-done((f32[4,16,512]{2,1,0:T(8,128)S(1)}, f32[4,16,512]{2,1,0:T(8,128)S(1)}, u32[]{:S(2)}, u32[]{:S(2)}) %collective-permute-start.7) | collective-permute-done | bytes 131104 | tf_op jit(solution)/shard_map/ppermute | solution.py:271
  84.5 6.3 %shard_map.85.b0_ref = f32[4,64,512]{2,1,0:T(8,128)} custom-call(f32[4,16,512]{2,1,0:T(8,128)} %copy-done.19, f32[4,64,512]{2,1,0:T(8,128)} %copy-done.8, f32[4,64,512]{2,1,0:T(8,128)} %copy-done.10, f32[4,16,512]{2,1,0:T(8,128)} %copy-done.20, f32[32,512]{1,0:T(8,128)} %get-tuple-element.126.cr_ref, f32[32,512]{1,0:T(8,128)} %get-tuple-element.125.ci_ref, ...), custom_call_target="tpu_custom_call" | custom-call | tf_op jit(solution)/shard_map/pallas_call | solution.py:216
  90.8 2.4 %collective-permute-start.10 = (f32[4,64,512]{2,1,0:T(8,128)S(1)}, f32[4,64,512]{2,1,0:T(8,128)S(1)}, u32[]{:S(2)}, u32[]{:S(2)}) collective-permute-start(f32[4,64,512]{2,1,0:T(8,128)S(1)} %collective-permute-done.6.b1_ref), channel_id=1, source_target_pairs={{0,1},{1,0},{2,3},{3,2},{4,5},{5,4},{6,7},{7,6},{8,9},{9,8},{10,11... | collective-permute-start | bytes 1572872 | tf_op jit(solution)/shard_map/ppermute | solution.py:34
  93.2 1.5 %collective-permute-done.10.b3_ref = f32[4,64,512]{2,1,0:T(8,128)S(1)} collective-permute-done((f32[4,64,512]{2,1,0:T(8,128)S(1)}, f32[4,64,512]{2,1,0:T(8,128)S(1)}, u32[]{:S(2)}, u32[]{:S(2)}) %collective-permute-start.10) | collective-permute-done | bytes 524320 | tf_op jit(solution)/shard_map/ppermute | solution.py:34
  95.5 12.6 %shard_map.86 = f32[8,128,256]{2,1,0:T(8,128)} custom-call(f32[4,64,512]{2,1,0:T(8,128)} %shard_map.84.b0_ref, f32[4,64,512]{2,1,0:T(8,128)} %copy-done.13, f32[4,64,512]{2,1,0:T(8,128)} %copy-done.14, f32[4,64,512]{2,1,0:T(8,128)} %copy-done.15, f32[128,2048]{1,0:T(8,128)} %select_add_fusion.m_ref, f32[8,2048]{1,0:T(8,128)} %get-tuple-element.112.cos_ref, ...), custom_call_target="tpu_custom_call" | custom-call | tf_op jit(solution)/shard_map/pallas_call | solution.py:151
  108.1 2.0 %copy.13 = f32[128,8,512]{0,2,1:T(8,128)S(1)} copy(f32[128,8,512]{2,1,0:T(8,128)} %param.8) | data formatting | bytes 4194304 | tf_op jit(solution)/shard_map/optimization_barrier | solution.py:294
  110.2 1.9 %collective-permute-start.12 = (f32[128,8,2]{0,2,1:T(2,128)S(1)}, f32[128,8,2]{0,2,1:T(2,128)S(1)}, u32[]{:S(2)}, u32[]{:S(2)}) collective-permute-start(f32[128,8,2]{0,2,1:T(2,128)S(1)} %get-tuple-element.66), channel_id=1, source_target_pairs={{0,4},{4,8},{8,12},{12,16},{16,20},{20,24},{24,28},{28,32},{32,36}... | collective-permute-start | bytes 24584 | tf_op jit(solution)/shard_map/ppermute | solution.py:16
  113.5 1.5 %copy.17 = f32[8,128,256]{1,2,0:T(8,128)S(1)} copy(f32[8,128,256]{2,1,0:T(8,128)} %shard_map.86) | data formatting | bytes 2097152 | tf_op jit(solution)/shard_map/optimization_barrier | solution.py:294
  115.1 8.2 %collective-permute-start.13 = (f32[128,8,2]{0,2,1:T(2,128)S(1)}, f32[128,8,2]{0,2,1:T(2,128)S(1)}, u32[]{:S(2)}, u32[]{:S(2)}) collective-permute-start(f32[128,8,2]{0,2,1:T(2,128)S(1)} %get-tuple-element.65), channel_id=1, source_target_pairs={{4,0},{8,4},{12,8},{16,12},{20,16},{24,20},{28,24},{32,28},{36,32}... | collective-permute-start | bytes 24584 | tf_op jit(solution)/shard_map/ppermute | solution.py:19
  123.2 2.3 %multiply_subtract_fusion.2 = (f32[128,4,512]{0,2,1:T(8,128)}, f32[128,4,512]{0,2,1:T(8,128)}, f32[128,4,512]{0,2,1:T(8,128)}, f32[128,4,512]{0,2,1:T(8,128)}) fusion(f32[128]{0:T(128)S(1)} %get-tuple-element.120, f32[128]{0:T(128)S(1)} %get-tuple-element.121, f32[128,8,512]{0,2,1:T(8,128)S(1)} %copy.13, f32[128,8,2]{0,2,1:T(2,128)S(1)} %collective-permute-done.12, ...), kind=kLoop, calls=%fused_computation.34 | loop fusion | flops 4980736 | bytes 6301696 | tf_op jit(solution)/shard_map/sub | solution.py:62
  125.5 2.3 %multiply_subtract_fusion = (f32[128,4,512]{0,2,1:T(8,128)}, f32[128,4,512]{0,2,1:T(8,128)}, f32[128,4,512]{0,2,1:T(8,128)}, f32[128,4,512]{0,2,1:T(8,128)}) fusion(f32[128]{0:T(128)S(1)} %get-tuple-element.124, f32[128]{0:T(128)S(1)} %get-tuple-element.117, f32[128,8,2]{0,2,1:T(2,128)S(1)} %collective-permute-done.13, f32[128,8,512]{0,2,1:T(8,128)S(1)} %copy.13, ...), kind=kLoop, calls=%fused_computation.30 | loop fusion | flops 4980736 | bytes 6301696 | tf_op jit(solution)/shard_map/sub | solution.py:62
  127.8 12.7 %shard_map.87 = f32[8,128,256]{2,1,0:T(8,128)} custom-call(f32[4,64,512]{2,1,0:T(8,128)} %shard_map.85.b0_ref, f32[4,64,512]{2,1,0:T(8,128)} %collective-permute-done.11.b1_ref, f32[4,64,512]{2,1,0:T(8,128)} %collective-permute-done.14.b2_ref, f32[4,64,512]{2,1,0:T(8,128)} %collective-permute-done.15.b3_ref, f32[128,2048]{1,0:T(8,128)} %select_add_fusion.m_ref, ...), custom_call_target="tpu_custom_call" | custom-call | tf_op jit(solution)/shard_map/pallas_call | solution.py:151
  140.5 1.5 %copy.18 = f32[8,128,256]{1,2,0:T(8,128)S(1)} copy(f32[8,128,256]{2,1,0:T(8,128)} %shard_map.87) | data formatting | bytes 2097152 | tf_op jit(solution)/shard_map/pallas_call | solution.py:151
  146.7 2.0 %copy.20 = f32[128,8,512]{2,1,0:T(8,128)} copy(f32[128,8,512]{0,2,1:T(8,128)S(1)} %fusion.3) | data formatting | bytes 4194304 | tf_op jit(solution)/shard_map/add | solution.py:303
  (89 shorter events, 15.6 us)
Async XLA Ops:
  17.1 3.2 %copy-start.12 = (f32[2,4,64,512]{3,2,1,0:T(8,128)S(1)}, f32[2,4,64,512]{3,2,1,0:T(8,128)}, u32[]{:S(2)}) copy-start(f32[2,4,64,512]{3,2,1,0:T(8,128)} %get-tuple-element.29) | copy-start | bytes 3145732
  17.1 3.2 %collective-permute-start = (f32[2,4,64,512]{3,2,1,0:T(8,128)}, f32[2,4,64,512]{3,2,1,0:T(8,128)S(1)}, u32[]{:S(2)}, u32[]{:S(2)}) collective-permute-start(f32[2,4,64,512]{3,2,1,0:T(8,128)} %get-tuple-element.30), channel_id=1, source_target_pairs={{0,1},{1,0},{2,3},{3,2},{4,5},{5,4},{6,7},{7,6},{8,9},{9,8},{10,11... | collective-permute-start | bytes 3145736 | tf_op jit(solution)/shard_map/ppermute | solution.py:30
  20.7 20.1 %copy-start.9 = (f32[4,64,512]{2,1,0:T(8,128)}, f32[4,64,512]{2,1,0:T(8,128)S(1)}, u32[]{:S(2)}) copy-start(f32[4,64,512]{2,1,0:T(8,128)S(1)} %get-tuple-element.38.keep_ref) | copy-start | bytes 1572868
  20.7 13.2 %collective-permute-start.1 = (f32[4,64,512]{2,1,0:T(8,128)S(1)}, f32[4,64,512]{2,1,0:T(8,128)S(1)}, u32[]{:S(2)}, u32[]{:S(2)}) collective-permute-start(f32[4,64,512]{2,1,0:T(8,128)S(1)} %get-tuple-element.75), channel_id=1, source_target_pairs={{0,2},{2,0},{1,3},{3,1},{4,6},{6,4},{5,7},{7,5},{8,10},{10,8},{9,1... | collective-permute-start | bytes 1572872 | tf_op jit(solution)/shard_map/ppermute | solution.py:278
  33.9 6.9 %copy-start.11 = (f32[4,64,512]{2,1,0:T(8,128)}, f32[4,64,512]{2,1,0:T(8,128)S(1)}, u32[]{:S(2)}) copy-start(f32[4,64,512]{2,1,0:T(8,128)S(1)} %collective-permute-done.1.recv_ref) | copy-start | bytes 1572868
  33.9 6.8 %copy-start.16 = (f32[2,32,2048]{2,1,0:T(8,128)S(1)}, f32[2,32,2048]{2,1,0:T(8,128)}, u32[]{:S(2)}) copy-start(f32[2,32,2048]{2,1,0:T(8,128)} %param.14) | copy-start | bytes 1572868
  33.9 3.7 %collective-permute-start.2 = (f32[2,4,64,512]{3,2,1,0:T(8,128)}, f32[2,4,64,512]{3,2,1,0:T(8,128)S(1)}, u32[]{:S(2)}, u32[]{:S(2)}) collective-permute-start(f32[2,4,64,512]{3,2,1,0:T(8,128)} %get-tuple-element.37), channel_id=1, source_target_pairs={{0,1},{1,0},{2,3},{3,2},{4,5},{5,4},{6,7},{7,6},{8,9},{9,8},{10,11... | collective-permute-start | bytes 3145736 | tf_op jit(solution)/shard_map/ppermute | solution.py:30
  39.2 28.1 %copy-start.8 = (f32[4,64,512]{2,1,0:T(8,128)}, f32[4,64,512]{2,1,0:T(8,128)S(1)}, u32[]{:S(2)}) copy-start(f32[4,64,512]{2,1,0:T(8,128)S(1)} %get-tuple-element.71.keep_ref) | copy-start | bytes 1572868
  39.2 28.0 %collective-permute-start.5 = (f32[4,64,512]{2,1,0:T(8,128)S(1)}, f32[4,64,512]{2,1,0:T(8,128)S(1)}, u32[]{:S(2)}, u32[]{:S(2)}) collective-permute-start(f32[4,64,512]{2,1,0:T(8,128)S(1)} %get-tuple-element.72), channel_id=1, source_target_pairs={{0,2},{2,0},{1,3},{3,1},{4,6},{6,4},{5,7},{7,5},{8,10},{10,8},{9,1... | collective-permute-start | bytes 1572872 | tf_op jit(solution)/shard_map/ppermute | solution.py:284
  40.8 18.8 %collective-permute-start.3 = (f32[4,16,512]{2,1,0:T(8,128)S(1)}, f32[4,16,512]{2,1,0:T(8,128)S(1)}, u32[]{:S(2)}, u32[]{:S(2)}) collective-permute-start(f32[4,16,512]{2,1,0:T(8,128)S(1)} %get-tuple-element.74), channel_id=1, source_target_pairs={{0,4},{4,8},{8,12},{12,16},{16,20},{20,24},{24,28},{28,32},{32,36}... | collective-permute-start | bytes 393224 | tf_op jit(solution)/shard_map/ppermute | solution.py:271
  44.0 15.6 %collective-permute-start.4 = (f32[4,16,512]{2,1,0:T(8,128)S(1)}, f32[4,16,512]{2,1,0:T(8,128)S(1)}, u32[]{:S(2)}, u32[]{:S(2)}) collective-permute-start(f32[4,16,512]{2,1,0:T(8,128)S(1)} %get-tuple-element.73), channel_id=1, source_target_pairs={{4,0},{8,4},{12,8},{16,12},{20,16},{24,20},{28,24},{32,28},{36,32}... | collective-permute-start | bytes 393224 | tf_op jit(solution)/shard_map/ppermute | solution.py:272
  67.2 27.5 %copy-start.24 = (s32[4,512]{1,0:T(4,128)S(1)}, s32[4,512]{1,0:T(4,128)}, u32[]{:S(2)}) copy-start(s32[4,512]{1,0:T(4,128)} %param.10) | copy-start | bytes 24580
  67.2 16.0 %copy-start.10 = (f32[4,64,512]{2,1,0:T(8,128)}, f32[4,64,512]{2,1,0:T(8,128)S(1)}, u32[]{:S(2)}) copy-start(f32[4,64,512]{2,1,0:T(8,128)S(1)} %collective-permute-done.5.recv_ref) | copy-start | bytes 1572868
  67.2 23.6 %collective-permute-start.6 = (f32[4,64,512]{2,1,0:T(8,128)}, f32[4,64,512]{2,1,0:T(8,128)S(1)}, u32[]{:S(2)}, u32[]{:S(2)}) collective-permute-start(f32[4,64,512]{2,1,0:T(8,128)} %shard_map.84.b0_ref), channel_id=1, source_target_pairs={{0,2},{2,0},{1,3},{3,1},{4,6},{6,4},{5,7},{7,5},{8,10},{10,8},{9,1... | collective-permute-start | bytes 1572872 | tf_op jit(solution)/shard_map/ppermute | solution.py:287
  67.3 15.8 %collective-permute-start.7 = (f32[4,16,512]{2,1,0:T(8,128)S(1)}, f32[4,16,512]{2,1,0:T(8,128)S(1)}, u32[]{:S(2)}, u32[]{:S(2)}) collective-permute-start(f32[4,16,512]{2,1,0:T(8,128)S(1)} %get-tuple-element.70), channel_id=1, source_target_pairs={{0,4},{4,8},{8,12},{12,16},{16,20},{20,24},{24,28},{28,32},{32,36}... | collective-permute-start | bytes 393224 | tf_op jit(solution)/shard_map/ppermute | solution.py:271
  69.3 13.9 %collective-permute-start.8 = (f32[4,16,512]{2,1,0:T(8,128)S(1)}, f32[4,16,512]{2,1,0:T(8,128)S(1)}, u32[]{:S(2)}, u32[]{:S(2)}) collective-permute-start(f32[4,16,512]{2,1,0:T(8,128)S(1)} %get-tuple-element.69), channel_id=1, source_target_pairs={{4,0},{8,4},{12,8},{16,12},{20,16},{24,20},{28,24},{32,28},{36,32}... | collective-permute-start | bytes 393224 | tf_op jit(solution)/shard_map/ppermute | solution.py:272
  77.1 16.0 %collective-permute-start.9 = (f32[4,64,512]{2,1,0:T(8,128)}, f32[4,64,512]{2,1,0:T(8,128)S(1)}, u32[]{:S(2)}, u32[]{:S(2)}) collective-permute-start(f32[4,64,512]{2,1,0:T(8,128)} %shard_map.84.b0_ref), channel_id=1, source_target_pairs={{0,1},{1,0},{2,3},{3,2},{4,5},{5,4},{6,7},{7,6},{8,9},{9,8},{10,11... | collective-permute-start | bytes 1572872 | tf_op jit(solution)/shard_map/ppermute | solution.py:34
  90.8 3.9 %copy-start.13 = (f32[4,64,512]{2,1,0:T(8,128)}, f32[4,64,512]{2,1,0:T(8,128)S(1)}, u32[]{:S(2)}) copy-start(f32[4,64,512]{2,1,0:T(8,128)S(1)} %collective-permute-done.6.b1_ref) | copy-start | bytes 1572868
  90.8 3.9 %collective-permute-start.10 = (f32[4,64,512]{2,1,0:T(8,128)S(1)}, f32[4,64,512]{2,1,0:T(8,128)S(1)}, u32[]{:S(2)}, u32[]{:S(2)}) collective-permute-start(f32[4,64,512]{2,1,0:T(8,128)S(1)} %collective-permute-done.6.b1_ref), channel_id=1, source_target_pairs={{0,1},{1,0},{2,3},{3,2},{4,5},{5,4},{6,7},{7,6},{8,9},{9,8},{10,11... | collective-permute-start | bytes 1572872 | tf_op jit(solution)/shard_map/ppermute | solution.py:34
  93.2 1.6 %copy-start.14 = (f32[4,64,512]{2,1,0:T(8,128)}, f32[4,64,512]{2,1,0:T(8,128)S(1)}, u32[]{:S(2)}) copy-start(f32[4,64,512]{2,1,0:T(8,128)S(1)} %collective-permute-done.9.b2_ref) | copy-start | bytes 1572868
  94.7 13.4 %collective-permute-start.11 = (f32[4,64,512]{2,1,0:T(8,128)}, f32[4,64,512]{2,1,0:T(8,128)}, u32[]{:S(2)}, u32[]{:S(2)}) collective-permute-start(f32[4,64,512]{2,1,0:T(8,128)} %shard_map.85.b0_ref), channel_id=1, source_target_pairs={{0,2},{2,0},{1,3},{3,1},{4,6},{6,4},{5,7},{7,5},{8,10},{10,8},{9,1... | collective-permute-start | bytes 1572872 | tf_op jit(solution)/shard_map/ppermute | solution.py:292
  108.1 4.0 %copy-start.25 = (f32[2,4,128]{2,1,0:T(4,128)S(1)}, f32[2,4,128]{2,1,0:T(4,128)}, u32[]{:S(2)}) copy-start(f32[2,4,128]{2,1,0:T(4,128)} %param.9) | copy-start | bytes 12292
  110.2 13.1 %collective-permute-start.12 = (f32[128,8,2]{0,2,1:T(2,128)S(1)}, f32[128,8,2]{0,2,1:T(2,128)S(1)}, u32[]{:S(2)}, u32[]{:S(2)}) collective-permute-start(f32[128,8,2]{0,2,1:T(2,128)S(1)} %get-tuple-element.66), channel_id=1, source_target_pairs={{0,4},{4,8},{8,12},{12,16},{16,20},{20,24},{24,28},{28,32},{32,36}... | collective-permute-start | bytes 24584 | tf_op jit(solution)/shard_map/ppermute | solution.py:16
  112.1 15.7 %collective-permute-start.14 = (f32[4,64,512]{2,1,0:T(8,128)}, f32[4,64,512]{2,1,0:T(8,128)}, u32[]{:S(2)}, u32[]{:S(2)}) collective-permute-start(f32[4,64,512]{2,1,0:T(8,128)} %shard_map.85.b0_ref), channel_id=1, source_target_pairs={{0,1},{1,0},{2,3},{3,2},{4,5},{5,4},{6,7},{7,6},{8,9},{9,8},{10,11... | collective-permute-start | bytes 1572872 | tf_op jit(solution)/shard_map/ppermute | solution.py:34
  113.4 14.4 %collective-permute-start.15 = (f32[4,64,512]{2,1,0:T(8,128)}, f32[4,64,512]{2,1,0:T(8,128)}, u32[]{:S(2)}, u32[]{:S(2)}) collective-permute-start(f32[4,64,512]{2,1,0:T(8,128)} %collective-permute-done.11.b1_ref), channel_id=1, source_target_pairs={{0,1},{1,0},{2,3},{3,2},{4,5},{5,4},{6,7},{7,6},{8,9},{9,8},{10,11... | collective-permute-start | bytes 1572872 | tf_op jit(solution)/shard_map/ppermute | solution.py:34
  115.1 10.4 %collective-permute-start.13 = (f32[128,8,2]{0,2,1:T(2,128)S(1)}, f32[128,8,2]{0,2,1:T(2,128)S(1)}, u32[]{:S(2)}, u32[]{:S(2)}) collective-permute-start(f32[128,8,2]{0,2,1:T(2,128)S(1)} %get-tuple-element.65), channel_id=1, source_target_pairs={{4,0},{8,4},{12,8},{16,12},{20,16},{24,20},{28,24},{32,28},{36,32}... | collective-permute-start | bytes 24584 | tf_op jit(solution)/shard_map/ppermute | solution.py:19
  142.1 1.8 %copy-start.6 = (f32[128,4,512]{0,2,1:T(8,128)S(1)}, f32[128,4,512]{0,2,1:T(8,128)}, u32[]{:S(2)}) copy-start(f32[128,4,512]{0,2,1:T(8,128)} %get-tuple-element.61) | copy-start | bytes 3145732
  142.1 2.2 %copy-start.7 = (f32[128,4,512]{0,2,1:T(8,128)S(1)}, f32[128,4,512]{0,2,1:T(8,128)}, u32[]{:S(2)}) copy-start(f32[128,4,512]{0,2,1:T(8,128)} %get-tuple-element.62) | copy-start | bytes 3145732
  142.2 2.4 %copy-start = (f32[128,4,512]{0,2,1:T(8,128)S(1)}, f32[128,4,512]{0,2,1:T(8,128)}, u32[]{:S(2)}) copy-start(f32[128,4,512]{0,2,1:T(8,128)} %get-tuple-element.57) | copy-start | bytes 3145732
  142.3 2.7 %copy-start.1 = (f32[128,4,512]{0,2,1:T(8,128)S(1)}, f32[128,4,512]{0,2,1:T(8,128)}, u32[]{:S(2)}) copy-start(f32[128,4,512]{0,2,1:T(8,128)} %get-tuple-element.58) | copy-start | bytes 3145732
  142.3 3.0 %copy-start.2 = (f32[128,4,512]{0,2,1:T(8,128)S(1)}, f32[128,4,512]{0,2,1:T(8,128)}, u32[]{:S(2)}) copy-start(f32[128,4,512]{0,2,1:T(8,128)} %get-tuple-element.63) | copy-start | bytes 3145732
  142.3 3.2 %copy-start.3 = (f32[128,4,512]{0,2,1:T(8,128)S(1)}, f32[128,4,512]{0,2,1:T(8,128)}, u32[]{:S(2)}) copy-start(f32[128,4,512]{0,2,1:T(8,128)} %get-tuple-element.64) | copy-start | bytes 3145732
  (10 other events, 11.6 us)

commit v14 on v11

--- a/solution.py
+++ b/solution.py
@@ -11,12 +11,15 @@
 def with_halo(block, sides, width):
     for axis, dim in sides:
         count = lax.axis_size(axis)
-        forward = [(i, i + 1) for i in range(count - 1)]
-        backward = [(target, source) for source, target in forward]
+        rank = lax.axis_index(axis)
+        forward = [(i, (i + 1) % count) for i in range(count)]
+        backward = [((i + 1) % count, i) for i in range(count)]
         low = lax.ppermute(
             lax.slice_in_dim(block, block.shape[dim] - width, None, axis=dim), axis, forward
         )
         high = lax.ppermute(lax.slice_in_dim(block, 0, width, axis=dim), axis, backward)
+        low = jnp.where(rank == 0, jnp.zeros_like(low), low)
+        high = jnp.where(rank == count - 1, jnp.zeros_like(high), high)
         block = jnp.concatenate([low, block, high], axis=dim)
     return block
 
@@ -263,8 +266,8 @@
         return xt.reshape(groups, 2 * step * slots, child_dev)
 
     box_size = lax.axis_size("box")
-    forward = [(i, i + 1) for i in range(box_size - 1)]
-    backward = [(i + 1, i) for i in range(box_size - 1)]
+    forward = [(i, (i + 1) % box_size) for i in range(box_size)]
+    backward = [((i + 1) % box_size, i) for i in range(box_size)]
     mask_lanes = jnp.broadcast_to(
         own_mask.astype(jnp.float32)[:, :, None], own_mask.shape + (128,)
     )
@@ -274,6 +277,8 @@
         high = keep[:, :parent_reach] + recv[:, :parent_reach]
         low = lax.ppermute(low, "box", forward)
         high = lax.ppermute(high, "box", backward)
+        low = jnp.where(box_rank == 0, jnp.zeros_like(low), low)
+        high = jnp.where(box_rank == box_size - 1, jnp.zeros_like(high), high)
         return translate_call(low, keep, recv, high, own_real, own_imag, mask_lanes)
 
     acc_a = reduce_cores(upward(chunk_xt(0), rows, cosine, sine, dir_size, 2 * step))

time: 148 us -> 138 us (0.932)
  starting transfers between devices: 40.1 us -> 31.7 us
  local copies, waits for them, and re-layouts: 20.1 us -> 17.5 us
    ppermute x2, waiting for transfers between devices: 0.01 us -> 9.89 us  [translate(): high = lax.ppermute(high, 'box', backward)]
    ppermute x2, waiting for transfers between devices: 7.18 us -> 0.01 us  [translate(): low = lax.ppermute(low, 'box', forward)]
    ppermute x2, starting transfers between devices: 5.11 us -> 1.44 us  [translate(): low = lax.ppermute(low, 'box', forward)]
    select_n x0 -> x6, other arithmetic: none -> 2.7 us  [the longest x2 1.35 us: translate(): high = jnp.where(box_rank == box_size - 1, jnp.zeros_like(high), high)]
    add x2, other arithmetic: 2.66 us -> 0.07 us  [translate(): high = keep[:, :parent_reach] + recv[:, :parent_reach]]
    unnamed x53 -> x43, local copies, waits for them, and re-layouts: 6.18 us -> 4.08 us
    ppermute x2, starting transfers between devices: 14.5 us -> 12.6 us  [translate(): high = lax.ppermute(high, 'box', backward)]
    ppermute x1, starting transfers between devices: 1.92 us -> 0.08 us  [with_halo(): lax.ppermute(lax.slice_in_dim(block, block.shape[dim] - width, None, axis...]
  transfers between devices with their start and end apart: 16 -> 16, of which waited for: 6 -> 5; matrix products, arithmetic and copies ran while one was open for 9% -> 10% of each run, Pallas kernels for 24% -> 26%
where the time goes in v14:
time: 138 us; the launch traced here: 136 us
  Pallas kernels  57.8 us (42%)
  starting transfers between devices  31.7 us (23%)
  local copies, waits for them, and re-layouts  17.5 us (13%)
  waiting for transfers between devices  14.3 us (10%)
  other arithmetic  14.1 us (10%)
    pallas_call x2, Pallas kernels, downward(): pl.pallas_call(downward_kernel, grid=(groups,), in_specs=[block] * 4 + [p...  25.3 us
    pallas_call x2, Pallas kernels, upward(): pl.pallas_call(upward_kernel, grid=(parts // 2,), in_specs=[pl.BlockSpec(...  19.9 us
    ppermute x2, starting transfers between devices, translate(): high = lax.ppermute(high, 'box', backward)  12.6 us
    pallas_call x2, Pallas kernels, translate_call(): pl.pallas_call(translate_kernel, out_shape=jax.ShapeDtypeStruct(keep.shap...  12.6 us
    ppermute x2, waiting for transfers between devices, translate(): high = lax.ppermute(high, 'box', backward)  9.89 us
    ppermute x1, starting transfers between devices, with_halo(): lax.ppermute(lax.slice_in_dim(block, 0, width, axis=dim), axis, backward)  6.78 us
    ppermute x4, starting transfers between devices, gather_blocks(): mate_local, mate_other = lax.ppermute((local, other), 'dir', CORE_SWAP)  4.86 us
    sub x2, other arithmetic, translate_padded(): scale_real * real_part - scale_imag * imag_part  4.61 us
  transfers between devices with their start and end apart: 16, of which 5 were waited for; matrix products, arithmetic and copies ran while one was open for 10% of the time, Pallas kernels for 26%

profile of v14, /device:TPU:65, one launch (start us, length us, event | category | flops | bytes accessed | tf_op | source)
XLA Modules:
  0.0 135.9 jit_solution(14305792265706430466)
XLA Ops:
  0.0 2.0 %copy.10 = f32[128,8,512]{0,2,1:T(8,128)S(1)} copy(f32[128,8,512]{2,1,0:T(8,128)} %param.8) | data formatting | bytes 4194304 | tf_op args[0]
  2.2 1.2 copy.15
  4.5 2.7 %select_add_fusion.m_ref = f32[128,2048]{1,0:T(8,128)} fusion(f32[2048]{0:T(1024)S(1)} %bitcast.100, s32[2048]{0:T(1024)S(1)} %bitcast.116, f32[2048]{0:T(1024)S(1)} %bitcast.101, s32[2048]{0:T(1024)S(1)} %bitcast.117, f32[2048]{0:T(1024)S(1)} %bitcast.87, s32[2048]{0:T(1024)S(1)} %bitcast.103, f32[2048]{0:T(1024)S(1)} %bitcast.88, s32[2048]{0:T(1024)S(1)} %bitcast.104, ...), kind=kLoop, calls=%fused_computation.29 | loop fusion | flops 12320768 | bytes 1311232 | tf_op jit(solution)/shard_map/add | solution.py:45
  7.1 10.0 %shard_map.82 = (f32[2,4,64,512]{3,2,1,0:T(8,128)}, f32[2,4,64,512]{3,2,1,0:T(8,128)}) custom-call(f32[8,256,128]{2,1,0:T(8,128)} %bitcast.80, f32[128,2048]{1,0:T(8,128)} %select_add_fusion.m_ref, f32[8,2048]{1,0:T(8,128)} %get-tuple-element.110.cos_ref, f32[8,2048]{1,0:T(8,128)} %get-tuple-element.109.sin_ref), custom_call_target="tpu_custom_call" | custom-call | tf_op jit(solution)/shard_map/pallas_call | solution.py:108
  17.8 1.2 copy.16
  18.9 1.3 collective-permute-done.2
  21.4 1.2 collective-permute-start.3
  22.6 10.0 %shard_map.83 = (f32[2,4,64,512]{3,2,1,0:T(8,128)}, f32[2,4,64,512]{3,2,1,0:T(8,128)}) custom-call(f32[8,256,128]{2,1,0:T(8,128)} %bitcast.81, f32[128,2048]{1,0:T(8,128)} %select_add_fusion.m_ref, f32[8,2048]{1,0:T(8,128)} %get-tuple-element.110.cos_ref, f32[8,2048]{1,0:T(8,128)} %get-tuple-element.109.sin_ref), custom_call_target="tpu_custom_call" | custom-call | tf_op jit(solution)/shard_map/pallas_call | solution.py:108
  32.5 2.2 %collective-permute-done.3.recv_ref = f32[4,64,512]{2,1,0:T(8,128)S(1)} collective-permute-done((f32[4,64,512]{2,1,0:T(8,128)}, f32[4,64,512]{2,1,0:T(8,128)S(1)}, u32[]{:S(2)}, u32[]{:S(2)}) %collective-permute-start.3) | collective-permute-done | bytes 524320 | tf_op jit(solution)/shard_map/ppermute | solution.py:287
  34.7 1.2 collective-permute-start.4
  38.5 1.8 %add.129 = f32[2,4,64,512]{3,2,1,0:T(8,128)S(1)} add(f32[2,4,64,512]{3,2,1,0:T(8,128)} %get-tuple-element.35, f32[2,4,64,512]{3,2,1,0:T(8,128)} %collective-permute-done.4) | non-fusion elementwise | flops 262144 | bytes 3145728 | tf_op jit(solution)/shard_map/add | solution.py:33
  40.4 1.4 %collective-permute-start.5 = (f32[4,16,512]{2,1,0:T(8,128)S(1)}, f32[4,16,512]{2,1,0:T(8,128)S(1)}, u32[]{:S(2)}, u32[]{:S(2)}) collective-permute-start(f32[4,16,512]{2,1,0:T(8,128)S(1)} %get-tuple-element.72), channel_id=1, source_target_pairs={{0,4},{4,8},{8,12},{12,16},{16,20},{20,24},{24,28},{28,32},{32,36}... | collective-permute-start | bytes 393224 | tf_op jit(solution)/shard_map/ppermute | solution.py:278
  42.7 1.2 collective-permute-start.7
  44.7 5.3 %collective-permute-start.6 = (f32[4,16,512]{2,1,0:T(8,128)S(1)}, f32[4,16,512]{2,1,0:T(8,128)S(1)}, u32[]{:S(2)}, u32[]{:S(2)}) collective-permute-start(f32[4,16,512]{2,1,0:T(8,128)S(1)} %get-tuple-element.71), channel_id=1, source_target_pairs={{4,0},{8,4},{12,8},{16,12},{20,16},{24,20},{28,24},{32,28},{36,32}... | collective-permute-start | bytes 393224 | tf_op jit(solution)/shard_map/ppermute | solution.py:279
  50.6 6.9 %collective-permute-done.6 = f32[4,16,512]{2,1,0:T(8,128)S(1)} collective-permute-done((f32[4,16,512]{2,1,0:T(8,128)S(1)}, f32[4,16,512]{2,1,0:T(8,128)S(1)}, u32[]{:S(2)}, u32[]{:S(2)}) %collective-permute-start.6) | collective-permute-done | bytes 131104 | tf_op jit(solution)/shard_map/ppermute | solution.py:279
  58.2 1.3 broadcast_in_dim.193.mask_ref
  59.5 6.3 %shard_map.84.b0_ref = f32[4,64,512]{2,1,0:T(8,128)} custom-call(f32[4,16,512]{2,1,0:T(8,128)} %broadcast_select_fusion.3.low_ref, f32[4,64,512]{2,1,0:T(8,128)} %copy-done.9, f32[4,64,512]{2,1,0:T(8,128)} %copy-done.11, f32[4,16,512]{2,1,0:T(8,128)} %broadcast_select_fusion.2.high_ref, f32[32,512]{1,0:T(8,128)} %get-tuple-element.124.cr_ref, ...), custom_call_target="tpu_custom_call" | custom-call | tf_op jit(solution)/shard_map/pallas_call | solution.py:219
  66.3 1.8 %collective-permute-start.11 = (f32[4,64,512]{2,1,0:T(8,128)}, f32[4,64,512]{2,1,0:T(8,128)}, u32[]{:S(2)}, u32[]{:S(2)}) collective-permute-start(f32[4,64,512]{2,1,0:T(8,128)} %shard_map.84.b0_ref), channel_id=1, source_target_pairs={{0,1},{1,0},{2,3},{3,2},{4,5},{5,4},{6,7},{7,6},{8,9},{9,8},{10,11... | collective-permute-start | bytes 1572872 | tf_op jit(solution)/shard_map/ppermute | solution.py:37
  68.1 7.3 %collective-permute-start.10 = (f32[4,16,512]{2,1,0:T(8,128)S(1)}, f32[4,16,512]{2,1,0:T(8,128)S(1)}, u32[]{:S(2)}, u32[]{:S(2)}) collective-permute-start(f32[4,16,512]{2,1,0:T(8,128)S(1)} %get-tuple-element.67), channel_id=1, source_target_pairs={{4,0},{8,4},{12,8},{16,12},{20,16},{24,20},{28,24},{32,28},{36,32}... | collective-permute-start | bytes 393224 | tf_op jit(solution)/shard_map/ppermute | solution.py:279
  76.1 3.0 %collective-permute-done.10 = f32[4,16,512]{2,1,0:T(8,128)S(1)} collective-permute-done((f32[4,16,512]{2,1,0:T(8,128)S(1)}, f32[4,16,512]{2,1,0:T(8,128)S(1)}, u32[]{:S(2)}, u32[]{:S(2)}) %collective-permute-start.10) | collective-permute-done | bytes 131104 | tf_op jit(solution)/shard_map/ppermute | solution.py:279
  79.8 6.3 %shard_map.85.b0_ref = f32[4,64,512]{2,1,0:T(8,128)} custom-call(f32[4,16,512]{2,1,0:T(8,128)} %broadcast_select_fusion.1.low_ref, f32[4,64,512]{2,1,0:T(8,128)} %copy-done.10, f32[4,64,512]{2,1,0:T(8,128)} %copy-done.12, f32[4,16,512]{2,1,0:T(8,128)} %broadcast_select_fusion.high_ref, f32[32,512]{1,0:T(8,128)} %get-tuple-element.124.cr_ref, ...), custom_call_target="tpu_custom_call" | custom-call | tf_op jit(solution)/shard_map/pallas_call | solution.py:219
  86.1 2.4 %collective-permute-start.12 = (f32[4,64,512]{2,1,0:T(8,128)S(1)}, f32[4,64,512]{2,1,0:T(8,128)S(1)}, u32[]{:S(2)}, u32[]{:S(2)}) collective-permute-start(f32[4,64,512]{2,1,0:T(8,128)S(1)} %collective-permute-done.8.b1_ref), channel_id=1, source_target_pairs={{0,1},{1,0},{2,3},{3,2},{4,5},{5,4},{6,7},{7,6},{8,9},{9,8},{10,11... | collective-permute-start | bytes 1572872 | tf_op jit(solution)/shard_map/ppermute | solution.py:37
  88.5 6.8 %collective-permute-start.1 = (f32[128,8,2]{0,2,1:T(2,128)S(1)}, f32[128,8,2]{0,2,1:T(2,128)S(1)}, u32[]{:S(2)}, u32[]{:S(2)}) collective-permute-start(f32[128,8,2]{0,2,1:T(2,128)S(1)} %get-tuple-element.63), channel_id=1, source_target_pairs={{4,0},{8,4},{12,8},{16,12},{20,16},{24,20},{28,24},{32,28},{36,32}... | collective-permute-start | bytes 24584 | tf_op jit(solution)/shard_map/ppermute | solution.py:20
  95.4 1.3 collective-permute-start.13
  96.7 2.3 %multiply_subtract_fusion.2 = (f32[128,4,512]{0,2,1:T(8,128)}, f32[128,4,512]{0,2,1:T(8,128)}, f32[128,4,512]{0,2,1:T(8,128)}, f32[128,4,512]{0,2,1:T(8,128)}) fusion(f32[128]{0:T(128)S(1)} %get-tuple-element.118, f32[128]{0:T(128)S(1)} %get-tuple-element.119, f32[128,8,512]{0,2,1:T(8,128)S(1)} %copy.10, f32[128,8,2]{0,2,1:T(2,128)S(1)} %broadcast_select_fusion.5, ...), kind=kLoop, calls=%fused_computation.35 | loop fusion | flops 4980736 | bytes 6301696 | tf_op jit(solution)/shard_map/sub | solution.py:65
  99.6 12.6 %shard_map.86 = f32[8,128,256]{2,1,0:T(8,128)} custom-call(f32[4,64,512]{2,1,0:T(8,128)} %shard_map.84.b0_ref, f32[4,64,512]{2,1,0:T(8,128)} %copy-done.14, f32[4,64,512]{2,1,0:T(8,128)} %collective-permute-done.11.b2_ref, f32[4,64,512]{2,1,0:T(8,128)} %copy-done.15, f32[128,2048]{1,0:T(8,128)} %select_add_fusion.m_ref, ...), custom_call_target="tpu_custom_call" | custom-call | tf_op jit(solution)/shard_map/pallas_call | solution.py:154
  112.3 2.3 %multiply_subtract_fusion = (f32[128,4,512]{0,2,1:T(8,128)}, f32[128,4,512]{0,2,1:T(8,128)}, f32[128,4,512]{0,2,1:T(8,128)}, f32[128,4,512]{0,2,1:T(8,128)}) fusion(f32[128]{0:T(128)S(1)} %get-tuple-element.122, f32[128]{0:T(128)S(1)} %get-tuple-element.115, f32[128,8,2]{0,2,1:T(2,128)S(1)} %broadcast_select_fusion.4, f32[128,8,512]{0,2,1:T(8,128)S(1)} %copy.10, ...), kind=kLoop, calls=%fused_computation.31 | loop fusion | flops 4980736 | bytes 6301696 | tf_op jit(solution)/shard_map/sub | solution.py:65
  115.0 12.7 %shard_map.87 = f32[8,128,256]{2,1,0:T(8,128)} custom-call(f32[4,64,512]{2,1,0:T(8,128)} %shard_map.85.b0_ref, f32[4,64,512]{2,1,0:T(8,128)} %collective-permute-done.13.b1_ref, f32[4,64,512]{2,1,0:T(8,128)} %collective-permute-done.14.b2_ref, f32[4,64,512]{2,1,0:T(8,128)} %collective-permute-done.15.b3_ref, f32[128,2048]{1,0:T(8,128)} %select_add_fusion.m_ref, ...), custom_call_target="tpu_custom_call" | custom-call | tf_op jit(solution)/shard_map/pallas_call | solution.py:154
  127.7 1.5 %copy.18 = f32[8,128,256]{1,2,0:T(8,128)S(1)} copy(f32[8,128,256]{2,1,0:T(8,128)} %shard_map.87) | data formatting | bytes 2097152 | tf_op jit(solution)/shard_map/pallas_call | solution.py:154
  129.5 1.2 copy.19
  132.7 1.2 fusion.3
  133.9 2.0 %copy.20 = f32[128,8,512]{2,1,0:T(8,128)} copy(f32[128,8,512]{0,2,1:T(8,128)S(1)} %fusion.3) | data formatting | bytes 4194304 | tf_op jit(solution)/shard_map/add | solution.py:308
  (84 shorter events, 13.9 us)
Async XLA Ops:
  17.1 3.2 %copy-start.13 = (f32[2,4,64,512]{3,2,1,0:T(8,128)S(1)}, f32[2,4,64,512]{3,2,1,0:T(8,128)}, u32[]{:S(2)}) copy-start(f32[2,4,64,512]{3,2,1,0:T(8,128)} %get-tuple-element.28) | copy-start | bytes 3145732
  17.1 3.2 %collective-permute-start.2 = (f32[2,4,64,512]{3,2,1,0:T(8,128)}, f32[2,4,64,512]{3,2,1,0:T(8,128)S(1)}, u32[]{:S(2)}, u32[]{:S(2)}) collective-permute-start(f32[2,4,64,512]{3,2,1,0:T(8,128)} %get-tuple-element.29), channel_id=1, source_target_pairs={{0,1},{1,0},{2,3},{3,2},{4,5},{5,4},{6,7},{7,6},{8,9},{9,8},{10,11... | collective-permute-start | bytes 3145736 | tf_op jit(solution)/shard_map/ppermute | solution.py:33
  21.4 19.0 %copy-start.9 = (f32[4,64,512]{2,1,0:T(8,128)}, f32[4,64,512]{2,1,0:T(8,128)S(1)}, u32[]{:S(2)}) copy-start(f32[4,64,512]{2,1,0:T(8,128)S(1)} %get-tuple-element.37.keep_ref) | copy-start | bytes 1572868
  21.4 13.3 %collective-permute-start.3 = (f32[4,64,512]{2,1,0:T(8,128)}, f32[4,64,512]{2,1,0:T(8,128)S(1)}, u32[]{:S(2)}, u32[]{:S(2)}) collective-permute-start(f32[4,64,512]{2,1,0:T(8,128)} %get-tuple-element.73), channel_id=1, source_target_pairs={{0,2},{2,0},{1,3},{3,1},{4,6},{6,4},{5,7},{7,5},{8,10},{10,8},{9,1... | collective-permute-start | bytes 1572872 | tf_op jit(solution)/shard_map/ppermute | solution.py:287
  34.7 5.7 %copy-start.11 = (f32[4,64,512]{2,1,0:T(8,128)}, f32[4,64,512]{2,1,0:T(8,128)S(1)}, u32[]{:S(2)}) copy-start(f32[4,64,512]{2,1,0:T(8,128)S(1)} %collective-permute-done.3.recv_ref) | copy-start | bytes 1572868
  34.7 3.9 %collective-permute-start.4 = (f32[2,4,64,512]{3,2,1,0:T(8,128)}, f32[2,4,64,512]{3,2,1,0:T(8,128)}, u32[]{:S(2)}, u32[]{:S(2)}) collective-permute-start(f32[2,4,64,512]{3,2,1,0:T(8,128)} %get-tuple-element.36), channel_id=1, source_target_pairs={{0,1},{1,0},{2,3},{3,2},{4,5},{5,4},{6,7},{7,6},{8,9},{9,8},{10,11... | collective-permute-start | bytes 3145736 | tf_op jit(solution)/shard_map/ppermute | solution.py:33
  40.4 9.6 %collective-permute-start.5 = (f32[4,16,512]{2,1,0:T(8,128)S(1)}, f32[4,16,512]{2,1,0:T(8,128)S(1)}, u32[]{:S(2)}, u32[]{:S(2)}) collective-permute-start(f32[4,16,512]{2,1,0:T(8,128)S(1)} %get-tuple-element.72), channel_id=1, source_target_pairs={{0,4},{4,8},{8,12},{12,16},{16,20},{20,24},{24,28},{28,32},{32,36}... | collective-permute-start | bytes 393224 | tf_op jit(solution)/shard_map/ppermute | solution.py:278
  42.7 23.1 %copy-start.10 = (f32[4,64,512]{2,1,0:T(8,128)}, f32[4,64,512]{2,1,0:T(8,128)S(1)}, u32[]{:S(2)}) copy-start(f32[4,64,512]{2,1,0:T(8,128)S(1)} %get-tuple-element.69.keep_ref) | copy-start | bytes 1572868
  42.7 23.1 %collective-permute-start.7 = (f32[4,64,512]{2,1,0:T(8,128)}, f32[4,64,512]{2,1,0:T(8,128)S(1)}, u32[]{:S(2)}, u32[]{:S(2)}) collective-permute-start(f32[4,64,512]{2,1,0:T(8,128)} %get-tuple-element.70), channel_id=1, source_target_pairs={{0,2},{2,0},{1,3},{3,1},{4,6},{6,4},{5,7},{7,5},{8,10},{10,8},{9,1... | collective-permute-start | bytes 1572872 | tf_op jit(solution)/shard_map/ppermute | solution.py:293
  44.7 12.9 %collective-permute-start.6 = (f32[4,16,512]{2,1,0:T(8,128)S(1)}, f32[4,16,512]{2,1,0:T(8,128)S(1)}, u32[]{:S(2)}, u32[]{:S(2)}) collective-permute-start(f32[4,16,512]{2,1,0:T(8,128)S(1)} %get-tuple-element.71), channel_id=1, source_target_pairs={{4,0},{8,4},{12,8},{16,12},{20,16},{24,20},{28,24},{32,28},{36,32}... | collective-permute-start | bytes 393224 | tf_op jit(solution)/shard_map/ppermute | solution.py:279
  65.8 14.0 %copy-start.12 = (f32[4,64,512]{2,1,0:T(8,128)}, f32[4,64,512]{2,1,0:T(8,128)S(1)}, u32[]{:S(2)}) copy-start(f32[4,64,512]{2,1,0:T(8,128)S(1)} %collective-permute-done.7.recv_ref) | copy-start | bytes 1572868
  65.8 29.5 %copy-start.19 = (s32[4,512]{1,0:T(4,128)S(1)}, s32[4,512]{1,0:T(4,128)}, u32[]{:S(2)}) copy-start(s32[4,512]{1,0:T(4,128)} %param.10) | copy-start | bytes 24580
  65.8 29.5 %copy-start.20 = (f32[2,4,128]{2,1,0:T(4,128)S(1)}, f32[2,4,128]{2,1,0:T(4,128)}, u32[]{:S(2)}) copy-start(f32[2,4,128]{2,1,0:T(4,128)} %param.9) | copy-start | bytes 12292
  65.9 9.5 %collective-permute-start.9 = (f32[4,16,512]{2,1,0:T(8,128)S(1)}, f32[4,16,512]{2,1,0:T(8,128)S(1)}, u32[]{:S(2)}, u32[]{:S(2)}) collective-permute-start(f32[4,16,512]{2,1,0:T(8,128)S(1)} %get-tuple-element.68), channel_id=1, source_target_pairs={{0,4},{4,8},{8,12},{12,16},{16,20},{20,24},{24,28},{28,32},{32,36}... | collective-permute-start | bytes 393224 | tf_op jit(solution)/shard_map/ppermute | solution.py:278
  66.0 20.1 %collective-permute-start.8 = (f32[4,64,512]{2,1,0:T(8,128)}, f32[4,64,512]{2,1,0:T(8,128)S(1)}, u32[]{:S(2)}, u32[]{:S(2)}) collective-permute-start(f32[4,64,512]{2,1,0:T(8,128)} %shard_map.84.b0_ref), channel_id=1, source_target_pairs={{0,2},{2,0},{1,3},{3,1},{4,6},{6,4},{5,7},{7,5},{8,10},{10,8},{9,1... | collective-permute-start | bytes 1572872 | tf_op jit(solution)/shard_map/ppermute | solution.py:296
  66.3 29.1 %collective-permute-start.11 = (f32[4,64,512]{2,1,0:T(8,128)}, f32[4,64,512]{2,1,0:T(8,128)}, u32[]{:S(2)}, u32[]{:S(2)}) collective-permute-start(f32[4,64,512]{2,1,0:T(8,128)} %shard_map.84.b0_ref), channel_id=1, source_target_pairs={{0,1},{1,0},{2,3},{3,2},{4,5},{5,4},{6,7},{7,6},{8,9},{9,8},{10,11... | collective-permute-start | bytes 1572872 | tf_op jit(solution)/shard_map/ppermute | solution.py:37
  68.1 11.0 %collective-permute-start.10 = (f32[4,16,512]{2,1,0:T(8,128)S(1)}, f32[4,16,512]{2,1,0:T(8,128)S(1)}, u32[]{:S(2)}, u32[]{:S(2)}) collective-permute-start(f32[4,16,512]{2,1,0:T(8,128)S(1)} %get-tuple-element.67), channel_id=1, source_target_pairs={{4,0},{8,4},{12,8},{16,12},{20,16},{24,20},{28,24},{32,28},{36,32}... | collective-permute-start | bytes 393224 | tf_op jit(solution)/shard_map/ppermute | solution.py:279
  86.1 12.9 %copy-start.14 = (f32[4,64,512]{2,1,0:T(8,128)}, f32[4,64,512]{2,1,0:T(8,128)S(1)}, u32[]{:S(2)}) copy-start(f32[4,64,512]{2,1,0:T(8,128)S(1)} %collective-permute-done.8.b1_ref) | copy-start | bytes 1572868
  86.1 9.3 %collective-permute-start.12 = (f32[4,64,512]{2,1,0:T(8,128)S(1)}, f32[4,64,512]{2,1,0:T(8,128)S(1)}, u32[]{:S(2)}, u32[]{:S(2)}) collective-permute-start(f32[4,64,512]{2,1,0:T(8,128)S(1)} %collective-permute-done.8.b1_ref), channel_id=1, source_target_pairs={{0,1},{1,0},{2,3},{3,2},{4,5},{5,4},{6,7},{7,6},{8,9},{9,8},{10,11... | collective-permute-start | bytes 1572872 | tf_op jit(solution)/shard_map/ppermute | solution.py:37
  88.5 8.2 %collective-permute-start = (f32[128,8,2]{0,2,1:T(2,128)S(1)}, f32[128,8,2]{0,2,1:T(2,128)S(1)}, u32[]{:S(2)}, u32[]{:S(2)}) collective-permute-start(f32[128,8,2]{0,2,1:T(2,128)S(1)} %get-tuple-element.64), channel_id=1, source_target_pairs={{0,4},{4,8},{8,12},{12,16},{16,20},{20,24},{24,28},{28,32},{32,36}... | collective-permute-start | bytes 24584 | tf_op jit(solution)/shard_map/ppermute | solution.py:17
  88.5 23.8 %collective-permute-start.1 = (f32[128,8,2]{0,2,1:T(2,128)S(1)}, f32[128,8,2]{0,2,1:T(2,128)S(1)}, u32[]{:S(2)}, u32[]{:S(2)}) collective-permute-start(f32[128,8,2]{0,2,1:T(2,128)S(1)} %get-tuple-element.63), channel_id=1, source_target_pairs={{4,0},{8,4},{12,8},{16,12},{20,16},{24,20},{28,24},{32,28},{36,32}... | collective-permute-start | bytes 24584 | tf_op jit(solution)/shard_map/ppermute | solution.py:20
  95.4 3.6 %copy-start.15 = (f32[4,64,512]{2,1,0:T(8,128)}, f32[4,64,512]{2,1,0:T(8,128)S(1)}, u32[]{:S(2)}) copy-start(f32[4,64,512]{2,1,0:T(8,128)S(1)} %collective-permute-done.12.b3_ref) | copy-start | bytes 1572868
  95.4 16.9 %collective-permute-start.13 = (f32[4,64,512]{2,1,0:T(8,128)}, f32[4,64,512]{2,1,0:T(8,128)}, u32[]{:S(2)}, u32[]{:S(2)}) collective-permute-start(f32[4,64,512]{2,1,0:T(8,128)} %shard_map.85.b0_ref), channel_id=1, source_target_pairs={{0,2},{2,0},{1,3},{3,1},{4,6},{6,4},{5,7},{7,5},{8,10},{10,8},{9,1... | collective-permute-start | bytes 1572872 | tf_op jit(solution)/shard_map/ppermute | solution.py:301
  99.0 16.0 %collective-permute-start.14 = (f32[4,64,512]{2,1,0:T(8,128)}, f32[4,64,512]{2,1,0:T(8,128)}, u32[]{:S(2)}, u32[]{:S(2)}) collective-permute-start(f32[4,64,512]{2,1,0:T(8,128)} %shard_map.85.b0_ref), channel_id=1, source_target_pairs={{0,1},{1,0},{2,3},{3,2},{4,5},{5,4},{6,7},{7,6},{8,9},{9,8},{10,11... | collective-permute-start | bytes 1572872 | tf_op jit(solution)/shard_map/ppermute | solution.py:37
  112.3 2.8 %collective-permute-start.15 = (f32[4,64,512]{2,1,0:T(8,128)}, f32[4,64,512]{2,1,0:T(8,128)}, u32[]{:S(2)}, u32[]{:S(2)}) collective-permute-start(f32[4,64,512]{2,1,0:T(8,128)} %collective-permute-done.13.b1_ref), channel_id=1, source_target_pairs={{0,1},{1,0},{2,3},{3,2},{4,5},{5,4},{6,7},{7,6},{8,9},{9,8},{10,11... | collective-permute-start | bytes 1572872 | tf_op jit(solution)/shard_map/ppermute | solution.py:37
  112.3 2.3 %copy-start = (f32[8,128,256]{2,1,0:T(8,128)S(1)}, f32[8,128,256]{2,1,0:T(8,128)}, u32[]{:S(2)}) copy-start(f32[8,128,256]{2,1,0:T(8,128)} %shard_map.86) | copy-start | bytes 3145732
  129.3 1.8 %copy-start.7 = (f32[128,4,512]{0,2,1:T(8,128)S(1)}, f32[128,4,512]{0,2,1:T(8,128)}, u32[]{:S(2)}) copy-start(f32[128,4,512]{0,2,1:T(8,128)} %get-tuple-element.59) | copy-start | bytes 3145732
  129.3 2.2 %copy-start.8 = (f32[128,4,512]{0,2,1:T(8,128)S(1)}, f32[128,4,512]{0,2,1:T(8,128)}, u32[]{:S(2)}) copy-start(f32[128,4,512]{0,2,1:T(8,128)} %get-tuple-element.60) | copy-start | bytes 3145732
  129.4 2.4 %copy-start.1 = (f32[128,4,512]{0,2,1:T(8,128)S(1)}, f32[128,4,512]{0,2,1:T(8,128)}, u32[]{:S(2)}) copy-start(f32[128,4,512]{0,2,1:T(8,128)} %get-tuple-element.55) | copy-start | bytes 3145732
  129.5 2.7 %copy-start.2 = (f32[128,4,512]{0,2,1:T(8,128)S(1)}, f32[128,4,512]{0,2,1:T(8,128)}, u32[]{:S(2)}) copy-start(f32[128,4,512]{0,2,1:T(8,128)} %get-tuple-element.56) | copy-start | bytes 3145732
  129.5 3.0 %copy-start.3 = (f32[128,4,512]{0,2,1:T(8,128)S(1)}, f32[128,4,512]{0,2,1:T(8,128)}, u32[]{:S(2)}) copy-start(f32[128,4,512]{0,2,1:T(8,128)} %get-tuple-element.61) | copy-start | bytes 3145732
  129.5 3.2 %copy-start.4 = (f32[128,4,512]{0,2,1:T(8,128)S(1)}, f32[128,4,512]{0,2,1:T(8,128)}, u32[]{:S(2)}) copy-start(f32[128,4,512]{0,2,1:T(8,128)} %get-tuple-element.62) | copy-start | bytes 3145732
  (5 other events, 6.8 us)

commit v15 on v14

--- a/solution.py
+++ b/solution.py
@@ -36,6 +36,18 @@
 def gather_blocks(local, other):
     mate_local, mate_other = lax.ppermute((local, other), "dir", CORE_SWAP)
     return (local, other, mate_local, mate_other)
+
+
+def pack(pieces):
+    return jnp.concatenate([piece.reshape(-1) for piece in pieces])
+
+
+def unpack(flat, like):
+    out, first = [], 0
+    for piece in like:
+        out.append(flat[first : first + piece.size].reshape(piece.shape))
+        first += piece.size
+    return out
 
 
 def interp_matrix(index, weight, first_row, row_count):
@@ -248,10 +260,6 @@
     rows = interp_matrix(interp_index, interp_weight, child_first, child_dev)
 
     child_reach = child_coef.shape[1] // 2
-    child_padded = with_halo(pattern, (("box", 2),), child_reach)
-    child_local = translate_padded(
-        child_padded, child_coef[0], child_coef[1], child_mask, child_reach
-    )
 
     parent_reach = parent_coef.shape[1] // 2
     own_real = lax.dynamic_slice_in_dim(parent_coef[0], parent_first, parent_dev, 1)
@@ -272,14 +280,25 @@
         own_mask.astype(jnp.float32)[:, :, None], own_mask.shape + (128,)
     )
 
-    def translate(keep, recv):
+    def translate(keep, recv, extra=None):
         low = keep[:, slots - parent_reach :] + recv[:, slots - parent_reach :]
         high = keep[:, :parent_reach] + recv[:, :parent_reach]
-        low = lax.ppermute(low, "box", forward)
-        high = lax.ppermute(high, "box", backward)
+        if extra is None:
+            low = lax.ppermute(low, "box", forward)
+            high = lax.ppermute(high, "box", backward)
+        else:
+            ups = (low, extra[0])
+            downs = (high, extra[1])
+            low, extra_low = unpack(lax.ppermute(pack(ups), "box", forward), ups)
+            high, extra_high = unpack(lax.ppermute(pack(downs), "box", backward), downs)
         low = jnp.where(box_rank == 0, jnp.zeros_like(low), low)
         high = jnp.where(box_rank == box_size - 1, jnp.zeros_like(high), high)
-        return translate_call(low, keep, recv, high, own_real, own_imag, mask_lanes)
+        local = translate_call(low, keep, recv, high, own_real, own_imag, mask_lanes)
+        if extra is None:
+            return local
+        extra_low = jnp.where(box_rank == 0, jnp.zeros_like(extra_low), extra_low)
+        extra_high = jnp.where(box_rank == box_size - 1, jnp.zeros_like(extra_high), extra_high)
+        return local, extra_low, extra_high
 
     acc_a = reduce_cores(upward(chunk_xt(0), rows, cosine, sine, dir_size, 2 * step))
     acc_a, xt_b = lax.optimization_barrier((acc_a, chunk_xt(1)))
@@ -294,7 +313,12 @@
     local_a = translate(keep_a, recv_a)
     local_a, recv_b = lax.optimization_barrier((local_a, recv_b))
     other_a = lax.ppermute(local_a, "dir", ROW_SWAP)
-    local_b = translate(keep_b, recv_b)
+    edges = (pattern[:, :, box_dev - child_reach :], pattern[:, :, :child_reach])
+    local_b, child_low, child_high = translate(keep_b, recv_b, edges)
+    child_padded = jnp.concatenate([child_low, pattern, child_high], axis=2)
+    child_local = translate_padded(
+        child_padded, child_coef[0], child_coef[1], child_mask, child_reach
+    )
     other_a, local_b = lax.optimization_barrier((other_a, local_b))
     all_a = gather_blocks(local_a, other_a)
     all_a, local_b = lax.optimization_barrier((all_a, local_b))

time: 138 us -> 149 us (1.080)
  the two profiles are of different devices: /device:TPU:65 before, /device:TPU:1 now
where the time goes in v15:
time: 149 us; the launch traced here: 148 us
  Pallas kernels  57.9 us (39%)
  local copies, waits for them, and re-layouts  28.2 us (19%)
  waiting for transfers between devices  27.3 us (18%)
  starting transfers between devices  21.4 us (14%)
  other arithmetic  12.9 us (9%)
    pallas_call x2, Pallas kernels, downward(): pl.pallas_call(downward_kernel, grid=(groups,), in_specs=[block] * 4 + [p...  25.3 us
    pallas_call x2, Pallas kernels, upward(): pl.pallas_call(upward_kernel, grid=(parts // 2,), in_specs=[pl.BlockSpec(...  20 us
    ppermute x1, waiting for transfers between devices, translate(): low = lax.ppermute(low, 'box', forward)  13.2 us
    pallas_call x2, Pallas kernels, translate_call(): pl.pallas_call(translate_kernel, out_shape=jax.ShapeDtypeStruct(keep.shap...  12.6 us
    ppermute x1, starting transfers between devices, translate(): high = lax.ppermute(high, 'box', backward)  8.85 us
    ppermute x1, waiting for transfers between devices, translate(): high, extra_high = unpack(lax.ppermute(pack(downs), 'box', backward), downs)  8.02 us
    ppermute x4, starting transfers between devices, gather_blocks(): mate_local, mate_other = lax.ppermute((local, other), 'dir', CORE_SWAP)  5.4 us
    sub x2, other arithmetic, translate_padded(): scale_real * real_part - scale_imag * imag_part  4.64 us
  transfers between devices with their start and end apart: 14, of which 6 were waited for; matrix products, arithmetic and copies ran while one was open for 13% of the time, Pallas kernels for 24%

profile of v15, /device:TPU:1, one launch (start us, length us, event | category | flops | bytes accessed | tf_op | source)
XLA Modules:
  0.0 148.1 jit_solution(13941859879530380233)
XLA Ops:
  0.0 1.6 %fusion.13 = (s32[1,2048]{1,0:T(1,128)S(1)}, s32[1,2048]{1,0:T(1,128)S(1)}, s32[1,2048]{1,0:T(1,128)S(1)}, s32[1,2048]{1,0:T(1,128)S(1)}, s32[1,2048]{1,0:T(1,12...) fusion(s32[16,2048]{1,0:T(8,128)} %param.11), kind=kLoop, calls=%fused_computation.73 | loop fusion | bytes 262144 | tf_op jit(solution)/shard_map/slice | solution.py:58
  1.6 1.9 %fusion.14 = (f32[1,2048]{1,0:T(1,128)S(1)}, f32[1,2048]{1,0:T(1,128)S(1)}, f32[1,2048]{1,0:T(1,128)S(1)}, f32[1,2048]{1,0:T(1,128)S(1)}, f32[1,2048]{1,0:T(1,12...) fusion(f32[16,2048]{1,0:T(8,128)} %param.12), kind=kLoop, calls=%fused_computation.74 | loop fusion | bytes 262144 | tf_op jit(solution)/shard_map/slice | solution.py:58
  3.6 1.7 %fusion.15 = (f32[8,2048]{1,0:T(8,128)}, f32[8,2048]{1,0:T(8,128)}) fusion(f32[8,2048]{1,0:T(8,128)} %param.13), kind=kLoop, calls=%fused_computation.75 | loop fusion | bytes 196608 | tf_op jit(solution)/shard_map/sin | solution.py:259
  5.3 2.0 %copy.10 = f32[128,8,512]{0,2,1:T(8,128)S(1)} copy(f32[128,8,512]{2,1,0:T(8,128)} %param.8) | data formatting | bytes 4194304 | tf_op args[0]
  8.6 2.7 %select_add_fusion.m_ref = f32[128,2048]{1,0:T(8,128)} fusion(f32[2048]{0:T(1024)S(1)} %bitcast.124, s32[2048]{0:T(1024)S(1)} %bitcast.108, f32[2048]{0:T(1024)S(1)} %bitcast.125, s32[2048]{0:T(1024)S(1)} %bitcast.109, f32[2048]{0:T(1024)S(1)} %bitcast.111, s32[2048]{0:T(1024)S(1)} %bitcast.95, f32[2048]{0:T(1024)S(1)} %bitcast.112, s32[2048]{0:T(1024)S(1)} %bitcast.96, ...), kind=kLoop, calls=%fused_computation.37 | loop fusion | flops 12320768 | bytes 1311232 | tf_op jit(solution)/shard_map/add | solution.py:57
  11.3 10.0 %shard_map.82 = (f32[2,4,64,512]{3,2,1,0:T(8,128)}, f32[2,4,64,512]{3,2,1,0:T(8,128)}) custom-call(f32[8,256,128]{2,1,0:T(8,128)} %bitcast.84, f32[128,2048]{1,0:T(8,128)} %select_add_fusion.m_ref, f32[8,2048]{1,0:T(8,128)} %get-tuple-element.110.cos_ref, f32[8,2048]{1,0:T(8,128)} %get-tuple-element.109.sin_ref), custom_call_target="tpu_custom_call" | custom-call | tf_op jit(solution)/shard_map/pallas_call | solution.py:120
  21.2 1.4 collective-permute-start
  23.8 1.3 collective-permute-done
  26.3 1.3 collective-permute-start.1
  27.6 10.0 %shard_map.83 = (f32[2,4,64,512]{3,2,1,0:T(8,128)}, f32[2,4,64,512]{3,2,1,0:T(8,128)}) custom-call(f32[8,256,128]{2,1,0:T(8,128)} %bitcast.85, f32[128,2048]{1,0:T(8,128)} %select_add_fusion.m_ref, f32[8,2048]{1,0:T(8,128)} %get-tuple-element.110.cos_ref, f32[8,2048]{1,0:T(8,128)} %get-tuple-element.109.sin_ref), custom_call_target="tpu_custom_call" | custom-call | tf_op jit(solution)/shard_map/pallas_call | solution.py:120
  37.5 2.0 %collective-permute-done.1.recv_ref = f32[4,64,512]{2,1,0:T(8,128)S(1)} collective-permute-done((f32[4,64,512]{2,1,0:T(8,128)}, f32[4,64,512]{2,1,0:T(8,128)S(1)}, u32[]{:S(2)}, u32[]{:S(2)}) %collective-permute-start.1) | collective-permute-done | bytes 524320 | tf_op jit(solution)/shard_map/ppermute | solution.py:306
  39.6 1.2 collective-permute-start.2
  40.8 2.1 %fusion.10 = (f32[128,8,2]{2,1,0:T(8,128)}, f32[128,8,2]{2,1,0:T(8,128)S(1)}) fusion(f32[128,8,512]{2,1,0:T(8,128)} %param.8), kind=kLoop, calls=%fused_computation.70 | loop fusion | bytes 32768 | tf_op jit(solution)/shard_map/slice | solution.py:316
  43.0 1.3 reshape.132
  46.3 1.8 %add.122 = f32[2,4,64,512]{3,2,1,0:T(8,128)S(1)} add(f32[2,4,64,512]{3,2,1,0:T(8,128)} %get-tuple-element.35, f32[2,4,64,512]{3,2,1,0:T(8,128)} %collective-permute-done.2) | non-fusion elementwise | flops 262144 | bytes 3145728 | tf_op jit(solution)/shard_map/add | solution.py:33
  48.2 8.9 %collective-permute-start.4 = (f32[4,16,512]{2,1,0:T(8,128)S(1)}, f32[4,16,512]{2,1,0:T(8,128)S(1)}, u32[]{:S(2)}, u32[]{:S(2)}) collective-permute-start(f32[4,16,512]{2,1,0:T(8,128)S(1)} %get-tuple-element.71), channel_id=1, source_target_pairs={{4,0},{8,4},{12,8},{16,12},{20,16},{24,20},{28,24},{32,28},{36,32}... | collective-permute-start | bytes 393224 | tf_op jit(solution)/shard_map/ppermute | solution.py:288
  59.7 13.2 %collective-permute-done.3 = f32[4,16,512]{2,1,0:T(8,128)S(1)} collective-permute-done((f32[4,16,512]{2,1,0:T(8,128)S(1)}, f32[4,16,512]{2,1,0:T(8,128)S(1)}, u32[]{:S(2)}, u32[]{:S(2)}) %collective-permute-start.3) | collective-permute-done | bytes 131104 | tf_op jit(solution)/shard_map/ppermute | solution.py:287
  73.6 1.3 broadcast_in_dim.193.mask_ref
  75.0 6.3 %shard_map.84.b0_ref = f32[4,64,512]{2,1,0:T(8,128)} custom-call(f32[4,16,512]{2,1,0:T(8,128)} %broadcast_select_fusion.1.low_ref, f32[4,64,512]{2,1,0:T(8,128)} %copy-done.9, f32[4,64,512]{2,1,0:T(8,128)} %copy-done.11, f32[4,16,512]{2,1,0:T(8,128)} %broadcast_select_fusion.high_ref, f32[32,512]{1,0:T(8,128)} %get-tuple-element.124.cr_ref, ...), custom_call_target="tpu_custom_call" | custom-call | tf_op jit(solution)/shard_map/pallas_call | solution.py:231
  81.3 2.5 %collective-permute-start.9 = (f32[4,64,512]{2,1,0:T(8,128)}, f32[4,64,512]{2,1,0:T(8,128)}, u32[]{:S(2)}, u32[]{:S(2)}) collective-permute-start(f32[4,64,512]{2,1,0:T(8,128)} %shard_map.84.b0_ref), channel_id=1, source_target_pairs={{0,1},{1,0},{2,3},{3,2},{4,5},{5,4},{6,7},{7,6},{8,9},{9,8},{10,11... | collective-permute-start | bytes 1572872 | tf_op jit(solution)/shard_map/ppermute | solution.py:37
  84.0 1.5 %collective-permute-start.6 = (f32[34816]{0:T(1024)S(1)}, f32[34816]{0:T(1024)S(1)}, u32[]{:S(2)}, u32[]{:S(2)}) collective-permute-start(f32[34816]{0:T(1024)S(1)} %pad_maximum_fusion.2), channel_id=1, source_target_pairs={{0,4},{4,8},{8,12},{12,16},{16,20},{20,24},{24,28},{28,32},{32,36}... | collective-permute-start | bytes 417800 | tf_op jit(solution)/shard_map/ppermute | solution.py:292
  85.5 8.0 %collective-permute-done.7 = f32[34816]{0:T(1024)S(1)} collective-permute-done((f32[34816]{0:T(1024)S(1)}, f32[34816]{0:T(1024)S(1)}, u32[]{:S(2)}, u32[]{:S(2)}) %collective-permute-start.7) | collective-permute-done | bytes 139296 | tf_op jit(solution)/shard_map/ppermute | solution.py:293
  95.9 6.3 %shard_map.85.b0_ref = f32[4,64,512]{2,1,0:T(8,128)} custom-call(f32[4,16,512]{2,1,0:T(8,128)} %select_n.136.low_ref, f32[4,64,512]{2,1,0:T(8,128)} %copy-done.10, f32[4,64,512]{2,1,0:T(8,128)} %copy-done.13, f32[4,16,512]{2,1,0:T(8,128)} %select_n.139.high_ref, f32[32,512]{1,0:T(8,128)} %get-tuple-element.124.cr_ref, f32[32,512]{1,0:T(8,128)} %get-tuple-element.123.ci_ref, ...), custom_call_target="tpu_custom_call" | custom-call | tf_op jit(solution)/shard_map/pallas_call | solution.py:231
  102.2 2.2 %collective-permute-start.10 = (f32[4,64,512]{2,1,0:T(8,128)}, f32[4,64,512]{2,1,0:T(8,128)S(1)}, u32[]{:S(2)}, u32[]{:S(2)}) collective-permute-start(f32[4,64,512]{2,1,0:T(8,128)} %collective-permute-done.8.b1_ref), channel_id=1, source_target_pairs={{0,1},{1,0},{2,3},{3,2},{4,5},{5,4},{6,7},{7,6},{8,9},{9,8},{10,11... | collective-permute-start | bytes 1572872 | tf_op jit(solution)/shard_map/ppermute | solution.py:37
  104.5 1.7 %collective-permute-done.10.b3_ref = f32[4,64,512]{2,1,0:T(8,128)S(1)} collective-permute-done((f32[4,64,512]{2,1,0:T(8,128)}, f32[4,64,512]{2,1,0:T(8,128)S(1)}, u32[]{:S(2)}, u32[]{:S(2)}) %collective-permute-start.10) | collective-permute-done | bytes 524320 | tf_op jit(solution)/shard_map/ppermute | solution.py:37
  106.2 1.3 collective-permute-start.11
  108.2 2.3 %multiply_subtract_fusion = (f32[128,4,512]{0,2,1:T(8,128)}, f32[128,4,512]{0,2,1:T(8,128)}, f32[128,4,512]{0,2,1:T(8,128)}, f32[128,4,512]{0,2,1:T(8,128)}) fusion(f32[128]{0:T(128)S(1)} %get-tuple-element.122, f32[128]{0:T(128)S(1)} %get-tuple-element.115, f32[128,8,2]{0,2,1:T(2,128)S(1)} %copy.16, f32[128,8,512]{0,2,1:T(8,128)S(1)} %copy.10, ...), kind=kLoop, calls=%fused_computation.30 | loop fusion | flops 4980736 | bytes 6301696 | tf_op jit(solution)/shard_map/sub | solution.py:77
  111.2 12.6 %shard_map.86 = f32[8,128,256]{2,1,0:T(8,128)} custom-call(f32[4,64,512]{2,1,0:T(8,128)} %shard_map.84.b0_ref, f32[4,64,512]{2,1,0:T(8,128)} %collective-permute-done.8.b1_ref, f32[4,64,512]{2,1,0:T(8,128)} %collective-permute-done.9.b2_ref, f32[4,64,512]{2,1,0:T(8,128)} %copy-done.15, f32[128,2048]{1,0:T(8,128)} %select_add_fusion.m_ref, ...), custom_call_target="tpu_custom_call" | custom-call | tf_op jit(solution)/shard_map/pallas_call | solution.py:166
  124.6 2.3 %multiply_subtract_fusion.2 = (f32[128,4,512]{0,2,1:T(8,128)}, f32[128,4,512]{0,2,1:T(8,128)}, f32[128,4,512]{0,2,1:T(8,128)}, f32[128,4,512]{0,2,1:T(8,128)}) fusion(f32[128]{0:T(128)S(1)} %get-tuple-element.118, f32[128]{0:T(128)S(1)} %get-tuple-element.119, f32[128,8,512]{0,2,1:T(8,128)S(1)} %copy.10, f32[128,8,2]{0,2,1:T(2,128)S(1)} %copy.13, ...), kind=kLoop, calls=%fused_computation.34 | loop fusion | flops 4980736 | bytes 6301696 | tf_op jit(solution)/shard_map/sub | solution.py:77
  127.2 12.7 %shard_map.87 = f32[8,128,256]{2,1,0:T(8,128)} custom-call(f32[4,64,512]{2,1,0:T(8,128)} %shard_map.85.b0_ref, f32[4,64,512]{2,1,0:T(8,128)} %collective-permute-done.11.b1_ref, f32[4,64,512]{2,1,0:T(8,128)} %collective-permute-done.12.b2_ref, f32[4,64,512]{2,1,0:T(8,128)} %collective-permute-done.13.b3_ref, f32[128,2048]{1,0:T(8,128)} %select_add_fusion.m_ref, ...), custom_call_target="tpu_custom_call" | custom-call | tf_op jit(solution)/shard_map/pallas_call | solution.py:166
  139.9 1.5 %copy.18 = f32[8,128,256]{1,2,0:T(8,128)S(1)} copy(f32[8,128,256]{2,1,0:T(8,128)} %shard_map.87) | data formatting | bytes 2097152 | tf_op jit(solution)/shard_map/pallas_call | solution.py:166
  146.1 2.0 %copy.20 = f32[128,8,512]{2,1,0:T(8,128)} copy(f32[128,8,512]{0,2,1:T(8,128)S(1)} %fusion.3) | data formatting | bytes 4194304 | tf_op jit(solution)/shard_map/add | solution.py:332
  (86 shorter events, 18.5 us)
Async XLA Ops:
  21.2 3.9 %copy-start.14 = (f32[2,4,64,512]{3,2,1,0:T(8,128)S(1)}, f32[2,4,64,512]{3,2,1,0:T(8,128)}, u32[]{:S(2)}) copy-start(f32[2,4,64,512]{3,2,1,0:T(8,128)} %get-tuple-element.28) | copy-start | bytes 3145732
  21.2 3.9 %collective-permute-start = (f32[2,4,64,512]{3,2,1,0:T(8,128)}, f32[2,4,64,512]{3,2,1,0:T(8,128)S(1)}, u32[]{:S(2)}, u32[]{:S(2)}) collective-permute-start(f32[2,4,64,512]{3,2,1,0:T(8,128)} %get-tuple-element.29), channel_id=1, source_target_pairs={{0,1},{1,0},{2,3},{3,2},{4,5},{5,4},{6,7},{7,6},{8,9},{9,8},{10,11... | collective-permute-start | bytes 3145736 | tf_op jit(solution)/shard_map/ppermute | solution.py:33
  26.2 21.9 %copy-start.9 = (f32[4,64,512]{2,1,0:T(8,128)}, f32[4,64,512]{2,1,0:T(8,128)S(1)}, u32[]{:S(2)}) copy-start(f32[4,64,512]{2,1,0:T(8,128)S(1)} %get-tuple-element.38.keep_ref) | copy-start | bytes 1572868
  26.3 13.3 %collective-permute-start.1 = (f32[4,64,512]{2,1,0:T(8,128)}, f32[4,64,512]{2,1,0:T(8,128)S(1)}, u32[]{:S(2)}, u32[]{:S(2)}) collective-permute-start(f32[4,64,512]{2,1,0:T(8,128)} %get-tuple-element.73), channel_id=1, source_target_pairs={{0,2},{2,0},{1,3},{3,1},{4,6},{6,4},{5,7},{7,5},{8,10},{10,8},{9,1... | collective-permute-start | bytes 1572872 | tf_op jit(solution)/shard_map/ppermute | solution.py:306
  39.6 1.2 copy-start.11
  39.6 6.8 %collective-permute-start.2 = (f32[2,4,64,512]{3,2,1,0:T(8,128)}, f32[2,4,64,512]{3,2,1,0:T(8,128)}, u32[]{:S(2)}, u32[]{:S(2)}) collective-permute-start(f32[2,4,64,512]{3,2,1,0:T(8,128)} %get-tuple-element.36), channel_id=1, source_target_pairs={{0,1},{1,0},{2,3},{3,2},{4,5},{5,4},{6,7},{7,6},{8,9},{9,8},{10,11... | collective-permute-start | bytes 3145736 | tf_op jit(solution)/shard_map/ppermute | solution.py:33
  44.5 3.6 %copy-start.12 = (f32[4,64,512]{2,1,0:T(8,128)S(1)}, f32[4,64,512]{2,1,0:T(8,128)}, u32[]{:S(2)}) copy-start(f32[4,64,512]{2,1,0:T(8,128)} %copy-done.11) | copy-start | bytes 1572868
  48.2 10.9 %collective-permute-start.4 = (f32[4,16,512]{2,1,0:T(8,128)S(1)}, f32[4,16,512]{2,1,0:T(8,128)S(1)}, u32[]{:S(2)}, u32[]{:S(2)}) collective-permute-start(f32[4,16,512]{2,1,0:T(8,128)S(1)} %get-tuple-element.71), channel_id=1, source_target_pairs={{4,0},{8,4},{12,8},{16,12},{20,16},{24,20},{28,24},{32,28},{36,32}... | collective-permute-start | bytes 393224 | tf_op jit(solution)/shard_map/ppermute | solution.py:288
  58.0 25.8 %copy-start.10 = (f32[4,64,512]{2,1,0:T(8,128)}, f32[4,64,512]{2,1,0:T(8,128)S(1)}, u32[]{:S(2)}) copy-start(f32[4,64,512]{2,1,0:T(8,128)S(1)} %get-tuple-element.69.keep_ref) | copy-start | bytes 1572868
  58.0 23.3 %collective-permute-start.5 = (f32[4,64,512]{2,1,0:T(8,128)}, f32[4,64,512]{2,1,0:T(8,128)S(1)}, u32[]{:S(2)}, u32[]{:S(2)}) collective-permute-start(f32[4,64,512]{2,1,0:T(8,128)} %get-tuple-element.70), channel_id=1, source_target_pairs={{0,2},{2,0},{1,3},{3,1},{4,6},{6,4},{5,7},{7,5},{8,10},{10,8},{9,1... | collective-permute-start | bytes 1572872 | tf_op jit(solution)/shard_map/ppermute | solution.py:312
  59.1 13.9 %collective-permute-start.3 = (f32[4,16,512]{2,1,0:T(8,128)S(1)}, f32[4,16,512]{2,1,0:T(8,128)S(1)}, u32[]{:S(2)}, u32[]{:S(2)}) collective-permute-start(f32[4,16,512]{2,1,0:T(8,128)S(1)} %get-tuple-element.72), channel_id=1, source_target_pairs={{0,4},{4,8},{8,12},{12,16},{16,20},{20,24},{24,28},{28,32},{32,36}... | collective-permute-start | bytes 393224 | tf_op jit(solution)/shard_map/ppermute | solution.py:287
  81.3 14.6 %copy-start.13 = (f32[4,64,512]{2,1,0:T(8,128)}, f32[4,64,512]{2,1,0:T(8,128)S(1)}, u32[]{:S(2)}) copy-start(f32[4,64,512]{2,1,0:T(8,128)S(1)} %collective-permute-done.5.recv_ref) | copy-start | bytes 1572868
  81.3 20.9 %collective-permute-start.8 = (f32[4,64,512]{2,1,0:T(8,128)}, f32[4,64,512]{2,1,0:T(8,128)}, u32[]{:S(2)}, u32[]{:S(2)}) collective-permute-start(f32[4,64,512]{2,1,0:T(8,128)} %shard_map.84.b0_ref), channel_id=1, source_target_pairs={{0,2},{2,0},{1,3},{3,1},{4,6},{6,4},{5,7},{7,5},{8,10},{10,8},{9,1... | collective-permute-start | bytes 1572872 | tf_op jit(solution)/shard_map/ppermute | solution.py:315
  81.3 23.2 %collective-permute-start.9 = (f32[4,64,512]{2,1,0:T(8,128)}, f32[4,64,512]{2,1,0:T(8,128)}, u32[]{:S(2)}, u32[]{:S(2)}) collective-permute-start(f32[4,64,512]{2,1,0:T(8,128)} %shard_map.84.b0_ref), channel_id=1, source_target_pairs={{0,1},{1,0},{2,3},{3,2},{4,5},{5,4},{6,7},{7,6},{8,9},{9,8},{10,11... | collective-permute-start | bytes 1572872 | tf_op jit(solution)/shard_map/ppermute | solution.py:37
  83.8 9.7 %collective-permute-start.7 = (f32[34816]{0:T(1024)S(1)}, f32[34816]{0:T(1024)S(1)}, u32[]{:S(2)}, u32[]{:S(2)}) collective-permute-start(f32[34816]{0:T(1024)S(1)} %pad_maximum_fusion.3), channel_id=1, source_target_pairs={{4,0},{8,4},{12,8},{16,12},{20,16},{24,20},{28,24},{32,28},{36,32}... | collective-permute-start | bytes 417800 | tf_op jit(solution)/shard_map/ppermute | solution.py:293
  84.0 20.4 %copy-start.17 = (f32[2,4,128]{2,1,0:T(4,128)S(1)}, f32[2,4,128]{2,1,0:T(4,128)}, u32[]{:S(2)}) copy-start(f32[2,4,128]{2,1,0:T(4,128)} %param.9) | copy-start | bytes 12292
  84.0 20.4 %copy-start.16 = (s32[4,512]{1,0:T(4,128)S(1)}, s32[4,512]{1,0:T(4,128)}, u32[]{:S(2)}) copy-start(s32[4,512]{1,0:T(4,128)} %param.10) | copy-start | bytes 24580
  84.0 11.2 %collective-permute-start.6 = (f32[34816]{0:T(1024)S(1)}, f32[34816]{0:T(1024)S(1)}, u32[]{:S(2)}, u32[]{:S(2)}) collective-permute-start(f32[34816]{0:T(1024)S(1)} %pad_maximum_fusion.2), channel_id=1, source_target_pairs={{0,4},{4,8},{8,12},{12,16},{16,20},{20,24},{24,28},{28,32},{32,36}... | collective-permute-start | bytes 417800 | tf_op jit(solution)/shard_map/ppermute | solution.py:292
  102.2 4.0 %collective-permute-start.10 = (f32[4,64,512]{2,1,0:T(8,128)}, f32[4,64,512]{2,1,0:T(8,128)S(1)}, u32[]{:S(2)}, u32[]{:S(2)}) collective-permute-start(f32[4,64,512]{2,1,0:T(8,128)} %collective-permute-done.8.b1_ref), channel_id=1, source_target_pairs={{0,1},{1,0},{2,3},{3,2},{4,5},{5,4},{6,7},{7,6},{8,9},{9,8},{10,11... | collective-permute-start | bytes 1572872 | tf_op jit(solution)/shard_map/ppermute | solution.py:37
  106.2 4.4 %copy-start.15 = (f32[4,64,512]{2,1,0:T(8,128)}, f32[4,64,512]{2,1,0:T(8,128)S(1)}, u32[]{:S(2)}) copy-start(f32[4,64,512]{2,1,0:T(8,128)S(1)} %collective-permute-done.10.b3_ref) | copy-start | bytes 1572868
  106.2 17.7 %collective-permute-start.11 = (f32[4,64,512]{2,1,0:T(8,128)}, f32[4,64,512]{2,1,0:T(8,128)}, u32[]{:S(2)}, u32[]{:S(2)}) collective-permute-start(f32[4,64,512]{2,1,0:T(8,128)} %shard_map.85.b0_ref), channel_id=1, source_target_pairs={{0,2},{2,0},{1,3},{3,1},{4,6},{6,4},{5,7},{7,5},{8,10},{10,8},{9,1... | collective-permute-start | bytes 1572872 | tf_op jit(solution)/shard_map/ppermute | solution.py:325
  110.5 16.7 %collective-permute-start.12 = (f32[4,64,512]{2,1,0:T(8,128)}, f32[4,64,512]{2,1,0:T(8,128)}, u32[]{:S(2)}, u32[]{:S(2)}) collective-permute-start(f32[4,64,512]{2,1,0:T(8,128)} %shard_map.85.b0_ref), channel_id=1, source_target_pairs={{0,1},{1,0},{2,3},{3,2},{4,5},{5,4},{6,7},{7,6},{8,9},{9,8},{10,11... | collective-permute-start | bytes 1572872 | tf_op jit(solution)/shard_map/ppermute | solution.py:37
  123.8 3.4 %collective-permute-start.13 = (f32[4,64,512]{2,1,0:T(8,128)}, f32[4,64,512]{2,1,0:T(8,128)}, u32[]{:S(2)}, u32[]{:S(2)}) collective-permute-start(f32[4,64,512]{2,1,0:T(8,128)} %collective-permute-done.11.b1_ref), channel_id=1, source_target_pairs={{0,1},{1,0},{2,3},{3,2},{4,5},{5,4},{6,7},{7,6},{8,9},{9,8},{10,11... | collective-permute-start | bytes 1572872 | tf_op jit(solution)/shard_map/ppermute | solution.py:37
  124.6 2.3 %copy-start = (f32[8,128,256]{2,1,0:T(8,128)S(1)}, f32[8,128,256]{2,1,0:T(8,128)}, u32[]{:S(2)}) copy-start(f32[8,128,256]{2,1,0:T(8,128)} %shard_map.86) | copy-start | bytes 3145732
  141.5 1.4 copy-start.5
  141.5 1.5 %copy-start.6 = (f32[128,4,512]{0,2,1:T(8,128)S(1)}, f32[128,4,512]{0,2,1:T(8,128)}, u32[]{:S(2)}) copy-start(f32[128,4,512]{0,2,1:T(8,128)} %get-tuple-element.56) | copy-start | bytes 3145732
  141.5 1.8 %copy-start.7 = (f32[128,4,512]{0,2,1:T(8,128)S(1)}, f32[128,4,512]{0,2,1:T(8,128)}, u32[]{:S(2)}) copy-start(f32[128,4,512]{0,2,1:T(8,128)} %get-tuple-element.61) | copy-start | bytes 3145732
  141.5 2.2 %copy-start.8 = (f32[128,4,512]{0,2,1:T(8,128)S(1)}, f32[128,4,512]{0,2,1:T(8,128)}, u32[]{:S(2)}) copy-start(f32[128,4,512]{0,2,1:T(8,128)} %get-tuple-element.62) | copy-start | bytes 3145732
  141.6 2.4 %copy-start.1 = (f32[128,4,512]{0,2,1:T(8,128)S(1)}, f32[128,4,512]{0,2,1:T(8,128)}, u32[]{:S(2)}) copy-start(f32[128,4,512]{0,2,1:T(8,128)} %get-tuple-element.51) | copy-start | bytes 3145732
  141.7 2.7 %copy-start.2 = (f32[128,4,512]{0,2,1:T(8,128)S(1)}, f32[128,4,512]{0,2,1:T(8,128)}, u32[]{:S(2)}) copy-start(f32[128,4,512]{0,2,1:T(8,128)} %get-tuple-element.52) | copy-start | bytes 3145732
  141.7 3.0 %copy-start.3 = (f32[128,4,512]{0,2,1:T(8,128)S(1)}, f32[128,4,512]{0,2,1:T(8,128)}, u32[]{:S(2)}) copy-start(f32[128,4,512]{0,2,1:T(8,128)} %get-tuple-element.59) | copy-start | bytes 3145732
  141.7 3.2 %copy-start.4 = (f32[128,4,512]{0,2,1:T(8,128)S(1)}, f32[128,4,512]{0,2,1:T(8,128)}, u32[]{:S(2)}) copy-start(f32[128,4,512]{0,2,1:T(8,128)} %get-tuple-element.60) | copy-start | bytes 3145732
